TPU v7x, 32 devices: a whole 2x2x4 slice. The times are simulated.
32 devices in a mesh: req: 8 (over z, x), kv: 4 (over y, core).
Axes of the slice: x: 2, y: 2, z: 4, core: 2. Of those that a mesh axis runs over, the one named last changes fastest.
Arguments:
- activations: bfloat16 [4992, 2048], P('req', 'kv'), may hold values from -6 to 6
- span_length: int32 [104], P('req'), may hold values from 1 to 48, as said below
- offsets: int32 [104], P('req'), may hold values from 64 to 8191
- decode_slot: int32 [104], P('req'), may hold values from 0 to 103, as said below
- attention_gain: float32 [2048], replicated, may hold values from 0.1 to 1.9
- query_weight: bfloat16 [2048, 2048], P(None, 'kv'), may hold values from -0.125 to 0.125
- key_projection_matrix: bfloat16 [2048, 1024], P(None, 'kv'), may hold values from -0.125 to 0.125
- value_projection_matrix: bfloat16 [2048, 1024], P(None, 'kv'), may hold values from -0.125 to 0.125
- output_weight: bfloat16 [2048, 2048], P('kv'), may hold values from -0.125 to 0.125
- feedforward_gain: float32 [2048], replicated, may hold values from 0.1 to 1.9
- gate_weight: bfloat16 [2048, 4096], P(None, 'kv'), may hold values from -0.125 to 0.125
- up_weight: bfloat16 [2048, 4096], P(None, 'kv'), may hold values from -0.125 to 0.125
- down_weight: bfloat16 [4096, 2048], P('kv'), may hold values from -0.09375 to 0.09375
- earlier_rotated_keys: bfloat16 [104, 64, 1024], P('req', 'kv'), may hold values from -300 to 300
- earlier_values: bfloat16 [104, 64, 1024], P('req', 'kv'), may hold values from -6 to 6
Outputs:
- layer_out: bfloat16 [4992, 2048], P('req', 'kv')
- decode_keys: bfloat16 [104, 64, 1024], P('req', None, 'kv')
- decode_values: bfloat16 [104, 64, 1024], P('req', None, 'kv')
Inputs may be any that keep to these rules, and one draw needn't show every extreme that they name: `span_length`: on some prefill device every request fills all 48 positions. `decode_slot`: each slot appears once; decode device d owns slots d * 13 to (d + 1) * 13 - 1; at most 2 requests of one prefill device go to one decode device; every prefill device p sends exactly 2 requests to decode device p + 1 (counted round); the differences of decode device minus prefill device, modulo the number of devices of req, form the same multiset on every prefill device.
All inputs are finite; a program needn't handle non-finite values.
Results may differ from a plain program's by a relative error of at most 0.012.
Values may be sent and summed in bfloat16 or wider, within the bound.
No kernel may reach another device: no remote copies, remote signals or barrier semaphores. Data moves between devices by JAX's collectives and lax.ppermute only.
A program may use at most 128 MiB of HBM per device.

v0:
```python
import math

import jax
import jax.numpy as jnp
from jax import lax
from jax.sharding import PartitionSpec as P

HEAD_WIDTH = 256


rope_base = 1000042.0
epsilon = 1e-05


def rms_scale(values, gain_row):
    square_sum = jnp.sum(values * values, axis=-1, keepdims=True)
    return values * lax.rsqrt(square_sum / values.shape[-1] + epsilon) * gain_row


def rotate_pairs(tensor, position):
    half_size = tensor.shape[-1] // 2
    steps_float = jnp.arange(half_size, dtype=jnp.float32)
    inverse = jnp.exp(steps_float * (-2.0 * math.log(rope_base) / tensor.shape[-1]))
    angles = position[:, :, None] * inverse[None, None, :]
    cosine = jnp.cos(angles)[:, :, None, :]
    sine_part = jnp.sin(angles)[:, :, None, :]
    first_half = tensor[..., :half_size]
    second = tensor[..., half_size:]
    return jnp.concatenate(
        [first_half * cosine - second * sine_part, second * cosine + first_half * sine_part],
        axis=-1,
    )


def allowed_keys(span_length, span_size, past_size):
    key_pos = jnp.arange(past_size + span_size, dtype=jnp.int32) - past_size
    query_pos = jnp.arange(span_size, dtype=jnp.int32)
    causal = key_pos[None, :] <= query_pos[:, None]
    live_keys = key_pos[None, None, :] < span_length[:, None, None]
    return (key_pos[None, None, :] < 0) | causal[None, :, :] & live_keys


def local(
    activations,
    span_length,
    offsets,
    decode_slot,
    attention_gain,
    query_weight,
    key_projection_matrix,
    value_projection_matrix,
    output_weight,
    feedforward_gain,
    gate_weight,
    up_weight,
    down_weight,
    earlier_rotated_keys,
    earlier_values,
):
    req_count = lax.axis_size("req")
    kv_index = lax.axis_index("kv")
    req_index = lax.axis_index("req")
    request_list = span_length.shape[0]
    total_rows, width_share = activations.shape
    span_size = total_rows // request_list
    local_kv = key_projection_matrix.shape[1] // HEAD_WIDTH
    local_q = query_weight.shape[1] // HEAD_WIDTH
    query_groups = local_q // local_kv
    x_whole = lax.all_gather(activations, "kv", axis=1, tiled=True)
    x_float = x_whole.astype(jnp.float32)
    normalized_input = rms_scale(x_float, attention_gain).astype(jnp.bfloat16)
    position = (
        offsets[:, None].astype(jnp.float32) + jnp.arange(span_size, dtype=jnp.float32)[None, :]
    )
    query_rows = jnp.dot(
        normalized_input, query_weight, preferred_element_type=jnp.float32
    ).reshape(request_list, span_size, local_q, HEAD_WIDTH)
    query_rows = rotate_pairs(query_rows, position).astype(jnp.bfloat16)
    fresh_keys = jnp.dot(
        normalized_input, key_projection_matrix, preferred_element_type=jnp.float32
    ).reshape(request_list, span_size, local_kv, HEAD_WIDTH)
    fresh_keys = rotate_pairs(fresh_keys, position).astype(jnp.bfloat16)
    fresh_values = (
        jnp.dot(normalized_input, value_projection_matrix, preferred_element_type=jnp.float32)
        .astype(jnp.bfloat16)
        .reshape(request_list, span_size, local_kv, HEAD_WIDTH)
    )
    head_keys, head_values = (
        lax.all_to_all(earlier_rotated_keys, "kv", split_axis=2, concat_axis=1, tiled=True),
        lax.all_to_all(earlier_values, "kv", split_axis=2, concat_axis=1, tiled=True),
    )
    past_size = head_keys.shape[1]
    combined_keys = jnp.concatenate(
        [head_keys.reshape(request_list, past_size, local_kv, HEAD_WIDTH), fresh_keys], axis=1
    )
    combined_values = jnp.concatenate(
        [head_values.reshape(request_list, past_size, local_kv, HEAD_WIDTH), fresh_values], axis=1
    )
    grouped_queries = query_rows.reshape(
        request_list, span_size, local_kv, query_groups, HEAD_WIDTH
    )
    scores = jnp.einsum(
        "rckgd,rskd->rkgcs", grouped_queries, combined_keys, preferred_element_type=jnp.float32
    ) / math.sqrt(HEAD_WIDTH)
    allowed = allowed_keys(span_length, span_size, past_size)[:, None, None, :, :]
    scores = jnp.where(allowed, scores, -jnp.inf)
    weights = jax.nn.softmax(scores, axis=-1).astype(jnp.bfloat16)
    mixed_heads = jnp.einsum(
        "rkgcs,rskd->rckgd", weights, combined_values, preferred_element_type=jnp.float32
    )
    mixed_heads = mixed_heads.astype(jnp.bfloat16).reshape(total_rows, local_q * HEAD_WIDTH)
    head_part = jnp.dot(mixed_heads, output_weight, preferred_element_type=jnp.float32)
    head_total = lax.psum(head_part, "kv")
    residual = x_float + head_total
    normed_two = rms_scale(residual, feedforward_gain).astype(jnp.bfloat16)
    residual_share = lax.dynamic_slice_in_dim(residual, kv_index * width_share, width_share, 1)
    gate_proj = jnp.dot(normed_two, gate_weight, preferred_element_type=jnp.float32)
    upward = jnp.dot(normed_two, up_weight, preferred_element_type=jnp.float32)
    hidden = (jax.nn.silu(gate_proj) * upward).astype(jnp.bfloat16)
    mlp_share = lax.psum_scatter(
        jnp.dot(hidden, down_weight, preferred_element_type=jnp.float32),
        "kv",
        scatter_dimension=1,
        tiled=True,
    )
    live_rows = (jnp.arange(span_size, dtype=jnp.int32)[None, :] < span_length[:, None]).reshape(
        total_rows
    )
    layer_out = jnp.where(live_rows[:, None], residual_share + mlp_share, 0.0).astype(jnp.bfloat16)
    slot_table = lax.all_gather(decode_slot, "req", axis=0, tiled=True)
    capacity = max(2, (request_list + req_count - 1) // req_count)
    order_ids = jnp.arange(request_list, dtype=jnp.int32)
    earlier = order_ids[None, :] < order_ids[:, None]
    own_dest = decode_slot // request_list
    same_dest = own_dest[:, None] == own_dest[None, :]
    own_rank = jnp.sum((same_dest & earlier).astype(jnp.int32), axis=1)
    buffer_place = own_dest * capacity + own_rank
    buffer_ids = jnp.arange(req_count * capacity, dtype=jnp.int32)
    matches = buffer_place[None, :] == buffer_ids[:, None]
    picked = jnp.sum(jnp.where(matches, order_ids[None, :], 0), axis=1)
    filled = jnp.any(matches, axis=1)

    def pack_slots(source_cache):
        taken_rows = jnp.take(source_cache, picked, axis=0)
        taken_rows = jnp.where(filled[:, None, None], taken_rows, jnp.zeros((), source_cache.dtype))
        return taken_rows.reshape((req_count, capacity) + source_cache.shape[1:])

    arrived_keys, arrived_values = (
        lax.all_to_all(pack_slots(head_keys), "req", split_axis=0, concat_axis=0, tiled=True),
        lax.all_to_all(pack_slots(head_values), "req", split_axis=0, concat_axis=0, tiled=True),
    )
    all_dest = (slot_table // request_list).reshape(req_count, request_list)
    same_all = all_dest[:, :, None] == all_dest[:, None, :]
    rank_all = jnp.sum((same_all & earlier[None, :, :]).astype(jnp.int32), axis=2).reshape(-1)
    wanted = req_index * request_list + order_ids
    slot_hits = slot_table[None, :] == wanted[:, None]
    global_ids = jnp.arange(slot_table.shape[0], dtype=jnp.int32)
    source = jnp.sum(jnp.where(slot_hits, global_ids[None, :], 0), axis=1)
    source_rank = jnp.sum(jnp.where(slot_hits, rank_all[None, :], 0), axis=1)
    slot_position = source // request_list * capacity + source_rank
    flat_keys = arrived_keys.reshape((req_count * capacity,) + arrived_keys.shape[2:])
    flat_values = arrived_values.reshape((req_count * capacity,) + arrived_values.shape[2:])
    decode_keys = jnp.take(flat_keys, slot_position, axis=0)
    decode_values = jnp.take(flat_values, slot_position, axis=0)
    return (layer_out, decode_keys, decode_values)


def solution(mesh):
    return jax.shard_map(
        local,
        mesh=mesh,
        in_specs=(
            P("req", "kv"),
            P("req"),
            P("req"),
            P("req"),
            P(),
            P(None, "kv"),
            P(None, "kv"),
            P(None, "kv"),
            P("kv", None),
            P(),
            P(None, "kv"),
            P(None, "kv"),
            P("kv", None),
            P("req", "kv", None),
            P("req", "kv", None),
        ),
        out_specs=(P("req", "kv"), P("req", None, "kv"), P("req", None, "kv")),
        check_vma=False,
    )
```

profile of v0, /device:TPU:0, one launch (start us, length us, event | category | flops | bytes accessed | tf_op | source)
XLA Modules:
  0.0 270.3 jit_solution(3733439131479229272)
XLA Ops:
  7.9 5.7 %copy.36 = bf16[13,16,1024]{1,0,2:T(8,128)(2,1)} copy(bf16[13,16,1024]{2,1,0:T(8,128)(2,1)} %param.32) | data formatting | bytes 851968 | tf_op args[13]
  13.6 5.5 %reshape.332 = bf16[4,2,26624]{2,1,0:T(2,128)(2,1)} reshape(bf16[1024,13,16]{2,1,0:T(8,128)(2,1)} %bitcast.64) | data formatting | bytes 851968
  19.1 4.3 %all-to-all-start.1 = ((bf16[4,2,26624]{2,1,0:T(2,128)(2,1)}), bf16[4,2,26624]{2,1,0:T(2,128)(2,1)S(1)}, u32[]{:S(2)}, u32[]{:S(2)}) async-start(bf16[4,2,26624]{2,1,0:T(2,128)(2,1)} %reshape.332), calls=%async_computation.1 | async-start | bytes 851968 | tf_op jit(solution)/shard_map/all_to_all | solution.py:89
  23.4 4.7 %copy.34 = bf16[13,16,1024]{1,0,2:T(8,128)(2,1)} copy(bf16[13,16,1024]{2,1,0:T(8,128)(2,1)S(1)} %copy-done.9) | data formatting | bytes 851968 | tf_op args[14]
  28.2 5.5 %reshape.330 = bf16[4,2,26624]{2,1,0:T(2,128)(2,1)} reshape(bf16[1024,13,16]{2,1,0:T(8,128)(2,1)} %bitcast.65) | data formatting | bytes 851968
  33.9 2.3 all-to-all-done.1
  36.2 3.5 %all-to-all-start = ((bf16[4,2,26624]{2,1,0:T(2,128)(2,1)}), bf16[4,2,26624]{2,1,0:T(2,128)(2,1)S(1)}, u32[]{:S(2)}, u32[]{:S(2)}) async-start(bf16[4,2,26624]{2,1,0:T(2,128)(2,1)} %reshape.330), calls=%async_computation | async-start | bytes 851968 | tf_op jit(solution)/shard_map/all_to_all | solution.py:90
  39.7 2.0 multiply_cosine_fusion
  41.8 4.4 %reshape.333 = bf16[1024,13,16]{2,1,0:T(8,128)(2,1)} reshape(bf16[4,2,26624]{2,1,0:T(2,128)(2,1)S(1)} %all-to-all-done.1) | data formatting | bytes 851968
  46.2 5.2 %copy.37 = bf16[13,16,4,256]{3,1,2,0:T(8,128)(2,1)} copy(bf16[13,16,4,256]{1,0,3,2:T(8,128)(2,1)} %bitcast.62) | data formatting | bytes 851968 | tf_op jit(solution)/shard_map/all_to_all | solution.py:89
  51.3 4.4 %reshape.331 = bf16[1024,13,16]{2,1,0:T(8,128)(2,1)} reshape(bf16[4,2,26624]{2,1,0:T(2,128)(2,1)S(1)} %all-to-all-done) | data formatting | bytes 851968
  55.7 5.2 %copy.35 = bf16[13,16,4,256]{3,1,2,0:T(8,128)(2,1)} copy(bf16[13,16,4,256]{1,0,3,2:T(8,128)(2,1)} %bitcast.63) | data formatting | bytes 851968 | tf_op jit(solution)/shard_map/all_to_all | solution.py:90
  60.9 2.4 fusion
  63.4 4.2 %fusion.34 = f32[624,512]{1,0:T(8,128)} fusion(bf16[2048,512]{1,0:T(8,128)(2,1)} %param.24, bf16[624,2048]{1,0:T(8,128)(2,1)S(1)} %copy-done.2, f32[2048]{0:T(1024)S(1)} %copy-done.13, f32[624]{0:T(1024)S(1)} %add_rsqrt_fusion.1), kind=kOutput, calls=%fused_computation.90 | convolution fusion | flops 1313734656 | bytes 5941696 | tf_op jit(solution)/shard_map/dot_general | solution.py:75
  67.6 2.1 reshape.272
  70.4 2.9 %fusion.36 = f32[624,256]{1,0:T(8,128)S(1)} fusion(bf16[2048,256]{1,0:T(8,128)(2,1)} %param.25, bf16[624,2048]{1,0:T(8,128)(2,1)} %all-gather.2.cloned.1.call-done, f32[2048]{0:T(1024)S(1)} %copy-done.13, f32[624]{0:T(1024)S(1)} %add_rsqrt_fusion.1), kind=kOutput, calls=%fused_computation.91 | convolution fusion | flops 659423232 | bytes 4254144 | tf_op jit(solution)/shard_map/dot_general | solution.py:79
  73.3 1.6 fusion.22
  77.2 0.9 convolution_convert_fusion.1
  79.4 3.8 %fusion.41 = f32[624,2048]{1,0:T(8,128)} fusion(bf16[624,512]{1,0:T(8,128)(2,1)S(1)} %bitcast.66, bf16[512,2048]{1,0:T(8,128)(2,1)S(1)} %copy-done), kind=kOutput, calls=%fused_computation.94 | convolution fusion | flops 1308622848 | bytes 7847936 | tf_op jit(solution)/shard_map/dot_general | solution.py:112
  83.3 102.7 %all-reduce.3.cloned.1.call-done = f32[624,2048]{1,0:T(8,128)} async-done(((f32[624,2048]{1,0:T(8,128)}), f32[624,2048]{1,0:T(8,128)}) %all-reduce.3.cloned.1.call-update) | async-done | bytes 5111824 | tf_op jit(solution)/shard_map/psum | solution.py:113
  186.0 4.1 %multiply_reduce_fusion = (f32[624]{0:T(1024)S(1)}, f32[624,2048]{1,0:T(8,128)S(1)}) fusion(f32[624,2048]{1,0:T(8,128)} %all-reduce.3.cloned.1.call-done, bf16[624,2048]{1,0:T(8,128)(2,1)} %all-gather.2.cloned.1.call-done), kind=kLoop, calls=%fused_computation.11 | loop fusion | flops 5111184 | bytes 12782016 | tf_op jit(solution)/shard_map/reduce_sum | solution.py:16
  190.1 2.3 copy-done.4
  192.4 4.4 %fusion.33 = f32[624,1024]{1,0:T(8,128)} fusion(bf16[2048,1024]{1,0:T(8,128)(2,1)S(1)} %copy-done.11, f32[624,2048]{1,0:T(8,128)S(1)} %get-tuple-element.10, f32[2048]{0:T(1024)S(1)} %copy-done.14, f32[624]{0:T(1024)S(1)} %add_rsqrt_fusion), kind=kOutput, calls=%fused_computation.89 | convolution fusion | flops 2621079552 | bytes 11872704 | tf_op jit(solution)/shard_map/dot_general | solution.py:117
  196.8 13.5 %fusion.12 = f32[624,2048]{1,0:T(8,128)} fusion(bf16[1024,2048]{1,0:T(8,128)(2,1)} %param.31, f32[624,1024]{1,0:T(8,128)} %fusion.33, bf16[2048,1024]{1,0:T(8,128)(2,1)} %param.30, f32[624,2048]{1,0:T(8,128)} %copy-done.4, f32[2048]{0:T(1024)S(1)} %copy-done.14, f32[624]{0:T(1024)S(1)} %add_rsqrt_fusion), kind=kOutput, calls=%fused_computation.28 | convolution fusion | flops 5242159104 | bytes 21178816 | tf_op jit(solution)/shard_map/dot_general | solution.py:121
  212.6 1.2 select_select_fusion
  213.7 5.5 %all-to-all-start.2 = ((bf16[8,2,64,256]{3,2,1,0:T(8,128)(2,1)}), bf16[8,2,64,256]{3,2,1,0:T(8,128)(2,1)S(1)}, u32[]{:S(2)}, u32[]{:S(2)}) async-start(bf16[8,2,64,256]{3,2,1,0:T(8,128)(2,1)} %bitcast.21), calls=%async_computation.3 | async-start | bytes 1048576 | tf_op jit(solution)/shard_map/all_to_all | solution.py:149
  220.9 13.1 %all-reduce = s32[104]{0:T(128)S(1)} all-reduce(s32[104]{0:T(128)S(1)} %dynamic-update-slice), channel_id=1, replica_groups=mesh['req'=8,'kv'=4] {'req'}, use_global_device_ids=true, to_apply=%add | all-reduce | flops 104 | bytes 832
  234.0 3.5 %all-to-all-start.3 = ((bf16[8,2,64,256]{3,2,1,0:T(8,128)(2,1)}), bf16[8,2,64,256]{3,2,1,0:T(8,128)(2,1)S(1)}, u32[]{:S(2)}, u32[]{:S(2)}) async-start(bf16[8,2,64,256]{3,2,1,0:T(8,128)(2,1)} %bitcast.24), calls=%async_computation.4 | async-start | bytes 1048576 | tf_op jit(solution)/shard_map/all_to_all | solution.py:150
  239.1 12.9 %all-to-all-done.3 = bf16[8,2,64,256]{3,2,1,0:T(8,128)(2,1)S(1)} async-done(((bf16[8,2,64,256]{3,2,1,0:T(8,128)(2,1)}), bf16[8,2,64,256]{3,2,1,0:T(8,128)(2,1)S(1)}, u32[]{:S(2)}, u32[]{:S(2)}) %all-to-all-start.3) | async-done | bytes 524320 | tf_op jit(solution)/shard_map/all_to_all | solution.py:150
  252.6 1.0 broadcast_select_fusion
  253.6 7.5 %reduce-scatter.2.cloned.1.call-done = f32[624,512]{1,0:T(8,128)} async-done(((f32[624,2048]{1,0:T(8,128)}), f32[624,512]{1,0:T(8,128)}) %reduce-scatter.2.cloned.1.call-update) | async-done | bytes 1277968 | tf_op jit(solution)/shard_map/reduce_scatter | solution.py:120
  261.1 2.7 select_convert_fusion
  (89 shorter events, 10.7 us)
Async XLA Ops:
  7.2 72.2 %copy-start = (bf16[512,2048]{1,0:T(8,128)(2,1)S(1)}, bf16[512,2048]{1,0:T(8,128)(2,1)}, u32[]{:S(2)}) copy-start(bf16[512,2048]{1,0:T(8,128)(2,1)} %param.27) | copy-start | bytes 6291460
  7.2 53.7 %all-gather.2.cloned.1.call-start = ((), (), s32[]{:S(2)}) async-start(), calls=%async_computation.5 | async-start | bytes 3194880 | tf_op jit(solution)/shard_map/all_gather | solution.py:69
  13.6 9.8 %copy-start.15 = (s32[13]{0:T(128)S(1)}, s32[13]{0:T(128)}, u32[]{:S(2)}) copy-start(s32[13]{0:T(128)} %param.21) | copy-start | bytes 160
  13.6 9.8 %copy-start.9 = (bf16[13,16,1024]{2,1,0:T(8,128)(2,1)S(1)}, bf16[13,16,1024]{2,1,0:T(8,128)(2,1)}, u32[]{:S(2)}) copy-start(bf16[13,16,1024]{2,1,0:T(8,128)(2,1)} %param.33) | copy-start | bytes 1277956
  19.1 17.1 %all-to-all-start.1 = ((bf16[4,2,26624]{2,1,0:T(2,128)(2,1)}), bf16[4,2,26624]{2,1,0:T(2,128)(2,1)S(1)}, u32[]{:S(2)}, u32[]{:S(2)}) async-start(bf16[4,2,26624]{2,1,0:T(2,128)(2,1)} %reshape.332), calls=%async_computation.1 | async-start | bytes 851968 | tf_op jit(solution)/shard_map/all_to_all | solution.py:89
  28.2 5.5 %copy-start.10 = (s32[13]{0:T(128)S(1)}, s32[13]{0:T(128)}, u32[]{:S(2)}) copy-start(s32[13]{0:T(128)} %param.20) | copy-start | bytes 160
  36.2 15.1 %all-to-all-start = ((bf16[4,2,26624]{2,1,0:T(2,128)(2,1)}), bf16[4,2,26624]{2,1,0:T(2,128)(2,1)S(1)}, u32[]{:S(2)}, u32[]{:S(2)}) async-start(bf16[4,2,26624]{2,1,0:T(2,128)(2,1)} %reshape.330), calls=%async_computation | async-start | bytes 851968 | tf_op jit(solution)/shard_map/all_to_all | solution.py:90
  39.7 146.3 %all-reduce.3.cloned.1.call-start = ((), (), s32[]{:S(2)}) async-start(), calls=%async_computation.6 | async-start | bytes 10223616 | tf_op jit(solution)/shard_map/psum | solution.py:113
  55.7 7.7 %copy-start.13 = (f32[2048]{0:T(1024)S(1)}, f32[2048]{0:T(1024)}, u32[]{:S(2)}) copy-start(f32[2048]{0:T(1024)} %param.23) | copy-start | bytes 24580
  60.9 2.5 copy-start.2
  70.4 4.6 %copy-start.7 = (f32[13,48,128]{2,1,0:T(8,128)S(1)}, f32[13,48,128]{2,1,0:T(8,128)}, u32[]{:S(2)}) copy-start(f32[13,48,128]{2,1,0:T(8,128)} %get-tuple-element.17) | copy-start | bytes 958468
  70.4 4.6 %copy-start.8 = (f32[13,48,128]{2,1,0:T(8,128)S(1)}, f32[13,48,128]{2,1,0:T(8,128)}, u32[]{:S(2)}) copy-start(f32[13,48,128]{2,1,0:T(8,128)} %get-tuple-element.18) | copy-start | bytes 958468
  73.3 1.8 copy-start.5
  75.2 1.7 copy-start.3
  75.2 2.0 copy-start.12
  77.1 1.0 copy-start.6
  83.2 109.2 %copy-start.14 = (f32[2048]{0:T(1024)S(1)}, f32[2048]{0:T(1024)}, u32[]{:S(2)}) copy-start(f32[2048]{0:T(1024)} %param.28) | copy-start | bytes 24580
  83.2 177.9 %reduce-scatter.2.cloned.1.call-start = ((), (), s32[]{:S(2)}) async-start(), calls=%async_computation.7 | async-start | bytes 6389760 | tf_op jit(solution)/shard_map/reduce_scatter | solution.py:120
  186.0 6.4 %copy-start.11 = (bf16[2048,1024]{1,0:T(8,128)(2,1)S(1)}, bf16[2048,1024]{1,0:T(8,128)(2,1)}, u32[]{:S(2)}) copy-start(bf16[2048,1024]{1,0:T(8,128)(2,1)} %param.29) | copy-start | bytes 12582916
  190.1 2.3 copy-start.4
  210.2 0.7 copy-start.16
  211.4 8.0 %copy-start.17 = (u32[32]{0:T(128)S(1)}, u32[32]{0:T(128)}, u32[]{:S(2)}) copy-start(u32[32]{0:T(128)} %constant.89) | copy-start | bytes 388
  213.7 20.2 %all-to-all-start.2 = ((bf16[8,2,64,256]{3,2,1,0:T(8,128)(2,1)}), bf16[8,2,64,256]{3,2,1,0:T(8,128)(2,1)S(1)}, u32[]{:S(2)}, u32[]{:S(2)}) async-start(bf16[8,2,64,256]{3,2,1,0:T(8,128)(2,1)} %bitcast.21), calls=%async_computation.3 | async-start | bytes 1048576 | tf_op jit(solution)/shard_map/all_to_all | solution.py:149
  234.0 18.0 %all-to-all-start.3 = ((bf16[8,2,64,256]{3,2,1,0:T(8,128)(2,1)}), bf16[8,2,64,256]{3,2,1,0:T(8,128)(2,1)S(1)}, u32[]{:S(2)}, u32[]{:S(2)}) async-start(bf16[8,2,64,256]{3,2,1,0:T(8,128)(2,1)} %bitcast.24), calls=%async_computation.4 | async-start | bytes 1048576 | tf_op jit(solution)/shard_map/all_to_all | solution.py:150
  252.0 11.8 %copy-start.1 = (bf16[512,2048]{1,0:T(8,128)(2,1)S(1)}, bf16[512,2048]{1,0:T(8,128)(2,1)}, u32[]{:S(2)}) copy-start(bf16[512,2048]{1,0:T(8,128)(2,1)} %param.27) | copy-start | bytes 6291460
Sparse Core Ops, SparseCore 0:
  9.6 32.4 all-gather.1
  83.3 102.5 all-reduce.2
  210.4 50.6 reduce-scatter.1
where the time goes:
time: 271 us; the launch traced here: 270 us
  waiting for transfers between devices  126 us (46%)
  local copies, waits for them, and re-layouts  51.6 us (19%)
  matrix products  30.7 us (11%)
  other arithmetic  17.2 us (6%)
  starting transfers between devices  16.9 us (6%)
  between operations  14.7 us (5%)
  blocking collectives  13.1 us (5%)
    psum x1, waiting for transfers between devices, local(): head_total = lax.psum(head_part, 'kv')  103 us
    unnamed x46, local copies, waits for them, and re-layouts  35.2 us
    dot_general x1, matrix products, local(): jnp.dot(hidden, down_weight, preferred_element_type=jnp.float32)  13.5 us
    unnamed x1, blocking collectives  13.1 us
    all_to_all x1, waiting for transfers between devices, local(): lax.all_to_all(pack_slots(head_values), 'req', split_axis=0, concat_axis=...  12.9 us
    reduce_scatter x1, waiting for transfers between devices, local(): lax.psum_scatter(jnp.dot(hidden, down_weight, preferred_element_type=jnp....  7.52 us
    reduce_sum x2, other arithmetic, rms_scale(): square_sum = jnp.sum(values * values, axis=-1, keepdims=True)  6.58 us
    all_to_all x1, starting transfers between devices, local(): lax.all_to_all(pack_slots(head_keys), 'req', split_axis=0, concat_axis=0,...  5.5 us
  transfers between devices with their start and end apart: 7, of which 4 were waited for; matrix products, arithmetic and copies ran while one was open for 18% of the time, Pallas kernels for 0%

commit v1 on v0

v1 whole, which is shorter than its diff:
```python
import math

import jax
import jax.numpy as jnp
from jax import lax
from jax.sharding import Mesh
from jax.sharding import PartitionSpec as P

HEAD_WIDTH = 256
CORES = 2


rope_base = 1000042.0
epsilon = 1e-05


def rotate_pairs(tensor, position):
    half_size = tensor.shape[-1] // 2
    steps_float = jnp.arange(half_size, dtype=jnp.float32)
    inverse = jnp.exp(steps_float * (-2.0 * math.log(rope_base) / tensor.shape[-1]))
    angles = position[:, :, None] * inverse[None, None, :]
    cosine = jnp.cos(angles)[:, :, None, :]
    sine_part = jnp.sin(angles)[:, :, None, :]
    first_half = tensor[..., :half_size]
    second = tensor[..., half_size:]
    return jnp.concatenate(
        [first_half * cosine - second * sine_part, second * cosine + first_half * sine_part],
        axis=-1,
    )


def allowed_keys(span_length, span_size, past_size):
    key_pos = jnp.arange(past_size + span_size, dtype=jnp.int32) - past_size
    query_pos = jnp.arange(span_size, dtype=jnp.int32)
    causal = key_pos[None, :] <= query_pos[:, None]
    live_keys = key_pos[None, None, :] < span_length[:, None, None]
    return (key_pos[None, None, :] < 0) | causal[None, :, :] & live_keys


def gather_features(share):
    chips = lax.axis_size("kvy")
    rows, width = share.shape
    pair = lax.all_gather(share, "kvy", axis=1, tiled=True)
    whole = lax.all_gather(pair, "core", axis=1, tiled=True)
    whole = whole.reshape(rows, CORES, chips, width).transpose(0, 2, 1, 3)
    return whole.reshape(rows, CORES * chips * width)


def swap_blocks(matrix):
    chips = lax.axis_size("kvy")
    rows, cols = matrix.shape
    width = cols // (CORES * chips)
    return matrix.reshape(rows, chips, CORES, width).transpose(0, 2, 1, 3).reshape(rows, cols)


def scatter_features(partial):
    on_chip = lax.psum_scatter(partial, "core", scatter_dimension=1, tiled=True)
    return lax.psum_scatter(on_chip, "kvy", scatter_dimension=1, tiled=True)


def row_scale(values, gain_share):
    square_sum = lax.psum(jnp.sum(values * values, axis=-1, keepdims=True), ("kvy", "core"))
    width = values.shape[-1] * lax.axis_size("kvy") * CORES
    return values * lax.rsqrt(square_sum / width + epsilon) * gain_share


def local(
    activations,
    span_length,
    offsets,
    decode_slot,
    attention_gain,
    query_weight,
    key_projection_matrix,
    value_projection_matrix,
    output_weight,
    feedforward_gain,
    gate_weight,
    up_weight,
    down_weight,
    earlier_rotated_keys,
    earlier_values,
):
    req_count = lax.axis_size("req")
    chips = lax.axis_size("kvy")
    kv_count = chips * CORES
    kv_index = lax.axis_index("kvy") * CORES + lax.axis_index("core")
    req_index = lax.axis_index("req")
    request_list = span_length.shape[0]
    total_rows, width_share = activations.shape
    span_size = total_rows // request_list
    local_kv = key_projection_matrix.shape[1] // HEAD_WIDTH
    local_q = query_weight.shape[1] // HEAD_WIDTH
    query_groups = local_q // local_kv

    past_share = earlier_rotated_keys.shape[1]
    stacked = jnp.stack([earlier_rotated_keys, earlier_values])
    stacked = stacked.reshape(2, request_list, past_share, kv_count, local_kv * HEAD_WIDTH)
    stacked = stacked.transpose(0, 3, 1, 2, 4)
    arrived = lax.all_to_all(stacked, ("kvy", "core"), split_axis=1, concat_axis=1, tiled=True)
    head_kv = arrived.transpose(0, 2, 1, 3, 4).reshape(
        2, request_list, kv_count * past_share, local_kv * HEAD_WIDTH
    )
    past_size = head_kv.shape[2]

    capacity = max(2, (request_list + req_count - 1) // req_count)
    order_ids = jnp.arange(request_list, dtype=jnp.int32)
    earlier = order_ids[None, :] < order_ids[:, None]
    own_dest = decode_slot // request_list
    same_dest = own_dest[:, None] == own_dest[None, :]
    own_rank = jnp.sum((same_dest & earlier).astype(jnp.int32), axis=1)
    buffer_place = own_dest * capacity + own_rank
    buffer_ids = jnp.arange(req_count * capacity, dtype=jnp.int32)
    matches = buffer_place[None, :] == buffer_ids[:, None]
    picked = jnp.sum(jnp.where(matches, order_ids[None, :], 0), axis=1)
    filled = jnp.any(matches, axis=1)
    packed = jnp.take(head_kv, picked, axis=1)
    packed = jnp.where(filled[None, :, None, None], packed, jnp.zeros((), packed.dtype))
    packed = packed.reshape((2, req_count, capacity) + packed.shape[2:])
    packed_slots = jnp.where(filled, jnp.take(decode_slot, picked), -1).reshape(req_count, capacity)
    landed = lax.all_to_all(packed, "req", split_axis=1, concat_axis=1, tiled=True)
    landed_slots = lax.all_to_all(packed_slots, "req", split_axis=0, concat_axis=0, tiled=True)
    wanted = req_index * request_list + order_ids
    slot_hits = landed_slots.reshape(1, -1) == wanted[:, None]
    entry_ids = jnp.arange(req_count * capacity, dtype=jnp.int32)
    slot_position = jnp.sum(jnp.where(slot_hits, entry_ids[None, :], 0), axis=1)
    landed = landed.reshape((2, req_count * capacity) + landed.shape[3:])
    decode_kv = jnp.take(landed, slot_position, axis=1)

    x_whole = gather_features(activations)
    x_float = x_whole.astype(jnp.float32)
    square_sum = jnp.sum(x_float * x_float, axis=-1, keepdims=True)
    normalized_input = (
        x_float * lax.rsqrt(square_sum / x_float.shape[-1] + epsilon) * attention_gain
    ).astype(jnp.bfloat16)
    position = (
        offsets[:, None].astype(jnp.float32) + jnp.arange(span_size, dtype=jnp.float32)[None, :]
    )
    query_rows = jnp.dot(
        normalized_input, query_weight, preferred_element_type=jnp.float32
    ).reshape(request_list, span_size, local_q, HEAD_WIDTH)
    query_rows = rotate_pairs(query_rows, position).astype(jnp.bfloat16)
    fresh_keys = jnp.dot(
        normalized_input, key_projection_matrix, preferred_element_type=jnp.float32
    ).reshape(request_list, span_size, local_kv, HEAD_WIDTH)
    fresh_keys = rotate_pairs(fresh_keys, position).astype(jnp.bfloat16)
    fresh_values = (
        jnp.dot(normalized_input, value_projection_matrix, preferred_element_type=jnp.float32)
        .astype(jnp.bfloat16)
        .reshape(request_list, span_size, local_kv, HEAD_WIDTH)
    )
    combined_keys = jnp.concatenate(
        [head_kv[0].reshape(request_list, past_size, local_kv, HEAD_WIDTH), fresh_keys], axis=1
    )
    combined_values = jnp.concatenate(
        [head_kv[1].reshape(request_list, past_size, local_kv, HEAD_WIDTH), fresh_values], axis=1
    )
    grouped_queries = query_rows.reshape(
        request_list, span_size, local_kv, query_groups, HEAD_WIDTH
    )
    scores = jnp.einsum(
        "rckgd,rskd->rkgcs", grouped_queries, combined_keys, preferred_element_type=jnp.float32
    ) / math.sqrt(HEAD_WIDTH)
    allowed = allowed_keys(span_length, span_size, past_size)[:, None, None, :, :]
    scores = jnp.where(allowed, scores, -jnp.inf)
    weights = jax.nn.softmax(scores, axis=-1).astype(jnp.bfloat16)
    mixed_heads = jnp.einsum(
        "rkgcs,rskd->rckgd", weights, combined_values, preferred_element_type=jnp.float32
    )
    mixed_heads = mixed_heads.astype(jnp.bfloat16).reshape(total_rows, local_q * HEAD_WIDTH)
    head_part = jnp.dot(mixed_heads, swap_blocks(output_weight), preferred_element_type=jnp.float32)
    head_share = scatter_features(head_part)
    residual_share = activations.astype(jnp.float32) + head_share

    gain_share = lax.dynamic_slice_in_dim(feedforward_gain, kv_index * width_share, width_share)
    normed_share = row_scale(residual_share, gain_share).astype(jnp.bfloat16)
    normed_two = gather_features(normed_share)
    gate_proj = jnp.dot(normed_two, gate_weight, preferred_element_type=jnp.float32)
    upward = jnp.dot(normed_two, up_weight, preferred_element_type=jnp.float32)
    hidden = (jax.nn.silu(gate_proj) * upward).astype(jnp.bfloat16)
    mlp_share = scatter_features(
        jnp.dot(hidden, swap_blocks(down_weight), preferred_element_type=jnp.float32)
    )
    live_rows = (jnp.arange(span_size, dtype=jnp.int32)[None, :] < span_length[:, None]).reshape(
        total_rows
    )
    layer_out = jnp.where(live_rows[:, None], residual_share + mlp_share, 0.0).astype(jnp.bfloat16)
    return (layer_out, decode_kv[0], decode_kv[1])


def solution(mesh):
    req_size, kv_size = mesh.devices.shape
    split_mesh = Mesh(
        mesh.devices.reshape(req_size, kv_size // CORES, CORES), ("req", "kvy", "core")
    )
    kv = ("kvy", "core")
    return jax.shard_map(
        local,
        mesh=split_mesh,
        in_specs=(
            P("req", kv),
            P("req"),
            P("req"),
            P("req"),
            P(),
            P(None, kv),
            P(None, kv),
            P(None, kv),
            P(kv, None),
            P(),
            P(None, kv),
            P(None, kv),
            P(kv, None),
            P("req", kv, None),
            P("req", kv, None),
        ),
        out_specs=(P("req", kv), P("req", None, kv), P("req", None, kv)),
        check_vma=False,
    )
```

time: 271 us -> 340 us (1.25)
  local copies, waits for them, and re-layouts: 51.6 us -> 97.2 us
  waiting for transfers between devices: 126 us -> 152 us
  blocking collectives: 13.1 us -> 5.76 us
  other arithmetic: 17.2 us -> 23.4 us
    psum x1 -> x0, waiting for transfers between devices: 103 us -> none  [local(): head_total = lax.psum(head_part, 'kv')]
    reduce_scatter x1 -> x4, waiting for transfers between devices: 7.52 us -> 67 us  [the longest x2 39.5 us: scatter_features(): return lax.psum_scatter(on_chip, 'kvy', scatter_dimension=1, tiled=True)]
    all_gather x1 -> x4, waiting for transfers between devices: 0.01 us -> 54.3 us  [the longest x2 53.3 us: gather_features(): pair = lax.all_gather(share, 'kvy', axis=1, tiled=True)]
    convert_element_type x0 -> x7, local copies, waits for them, and re-layouts: none -> 43.9 us  [the longest x5 32.7 us: local(): x_float = x_whole.astype(jnp.float32)]
    unnamed x46 -> x35, local copies, waits for them, and re-layouts: 35.2 us -> 12 us
    all_to_all x4 -> x3, waiting for transfers between devices: 15.2 us -> 29.9 us  [the longest x1 24.1 us: local(): lax.all_to_all(packed, 'req', split_axis=1, concat_axis=1, tiled=True)]
    unnamed x1 -> x0, blocking collectives: 13.1 us -> none
    reshape x1 -> x2, local copies, waits for them, and re-layouts: 2.07 us -> 14.6 us  [gather_features(): whole = whole.reshape(rows, CORES, chips, width).transpose(0, 2, 1, 3)]
  transfers between devices with their start and end apart: 7 -> 11, of which waited for: 4 -> 9; matrix products, arithmetic and copies ran while one was open for 18% -> 13% of each run, Pallas kernels for 0% -> 0%
where the time goes in v1:
time: 340 us; the launch traced here: 338 us
  waiting for transfers between devices  152 us (45%)
  local copies, waits for them, and re-layouts  97.2 us (29%)
  matrix products  30.8 us (9%)
  other arithmetic  23.4 us (7%)
  starting transfers between devices  14.7 us (4%)
  between operations  14.5 us (4%)
  blocking collectives  5.76 us (2%)
    all_gather x2, waiting for transfers between devices, gather_features(): pair = lax.all_gather(share, 'kvy', axis=1, tiled=True)  53.3 us
    reduce_scatter x2, waiting for transfers between devices, scatter_features(): return lax.psum_scatter(on_chip, 'kvy', scatter_dimension=1, tiled=True)  39.5 us
    convert_element_type x5, local copies, waits for them, and re-layouts, local(): x_float = x_whole.astype(jnp.float32)  32.7 us
    reduce_scatter x2, waiting for transfers between devices, scatter_features(): on_chip = lax.psum_scatter(partial, 'core', scatter_dimension=1, tiled=True)  27.5 us
    all_to_all x1, waiting for transfers between devices, local(): lax.all_to_all(packed, 'req', split_axis=1, concat_axis=1, tiled=True)  24.1 us
    reshape x2, local copies, waits for them, and re-layouts, gather_features(): whole = whole.reshape(rows, CORES, chips, width).transpose(0, 2, 1, 3)  14.6 us
    dot_general x1, matrix products, local(): jnp.dot(hidden, swap_blocks(down_weight), preferred_element_type=jnp.floa...  13 us
    unnamed x35, local copies, waits for them, and re-layouts  12 us
  transfers between devices with their start and end apart: 11, of which 9 were waited for; matrix products, arithmetic and copies ran while one was open for 13% of the time, Pallas kernels for 0%

profile of v1, /device:TPU:0, one launch (start us, length us, event | category | flops | bytes accessed | tf_op | source)
XLA Modules:
  0.0 338.3 jit_solution(16456305696777216266)
XLA Ops:
  8.0 28.2 %all-gather.5.cloned.1.call-done = bf16[624,1024]{1,0:T(8,128)(2,1)} async-done(((bf16[624,512]{1,0:T(8,128)(2,1)}), bf16[624,1024]{1,0:T(8,128)(2,1)}) %all-gather.5.cloned.1.call-update) | async-done | bytes 1277968 | tf_op jit(solution)/shard_map/all_gather | solution.py:43
  42.3 4.4 %all-to-all-start = ((bf16[2,4,13,16,256]{4,3,2,0,1:T(8,128)(2,1)}), bf16[2,4,13,16,256]{4,3,2,0,1:T(8,128)(2,1)}, u32[]{:S(2)}, u32[]{:S(2)}) async-start(bf16[2,4,13,16,256]{4,3,2,0,1:T(8,128)(2,1)} %copy.111), calls=%async_computation | async-start | bytes 1703936 | tf_op jit(solution)/shard_map/all_to_all | solution.py:100
  46.8 2.5 copy.132
  49.3 2.9 copy.120
  55.1 4.0 %all-to-all-done = bf16[2,4,13,16,256]{4,3,2,0,1:T(8,128)(2,1)} async-done(((bf16[2,4,13,16,256]{4,3,2,0,1:T(8,128)(2,1)}), bf16[2,4,13,16,256]{4,3,2,0,1:T(8,128)(2,1)}, u32[]{:S(2)}, u32[]{:S(2)}) %all-to-all-start) | async-done | bytes 852000 | tf_op jit(solution)/shard_map/all_to_all | solution.py:100
  61.5 4.8 %copy.113 = f32[624,2048]{0,1:T(8,128)} copy(bf16[624,2048]{1,0:T(8,128)(2,1)} %all-gather.7.cloned.1.call-done) | data formatting | bytes 7667712 | tf_op jit(solution)/shard_map/convert_element_type | solution.py:131
  66.3 3.0 multiply_reduce_fusion
  69.3 8.9 %copy.115 = f32[624,2,2,512]{3,2,1,0:T(2,128)} copy(f32[624,2,2,512]{0,3,1,2:T(8,128)} %bitcast.105) | data formatting | bytes 10223616 | tf_op jit(solution)/shard_map/convert_element_type | solution.py:131
  78.2 5.1 %copy.114 = f32[624,2,2,512]{0,3,2,1:T(8,128)} copy(f32[624,2,2,512]{0,3,1,2:T(8,128)} %bitcast.106) | data formatting | bytes 10223616 | tf_op jit(solution)/shard_map/convert_element_type | solution.py:131
  83.4 5.8 %copy.116 = f32[624,2,2,512]{3,0,1,2:T(8,128)} copy(f32[624,2,2,512]{0,3,2,1:T(8,128)} %bitcast.107) | data formatting | bytes 10223616 | tf_op jit(solution)/shard_map/convert_element_type | solution.py:131
  89.3 3.0 fusion.2
  92.3 4.1 %copy.117 = bf16[624,2,2,512]{3,2,1,0:T(2,128)(2,1)} copy(bf16[624,2,2,512]{3,0,2,1:T(8,128)(2,1)S(1)} %fusion.2) | data formatting | bytes 5111808 | tf_op jit(solution)/shard_map/convert_element_type | solution.py:135
  96.4 7.1 %reshape.453 = bf16[13,48,2048,1]{2,1,0,3:T(8,128)(2,1)} reshape(bf16[624,2,2,512]{3,2,1,0:T(2,128)(2,1)} %copy.117) | data formatting | bytes 5111808 | tf_op jit(solution)/shard_map/convert_element_type | solution.py:135
  103.4 8.0 %reshape.424 = f32[13,48,2048]{2,1,0:T(8,128)} reshape(f32[624,2,2,512]{3,2,1,0:T(2,128)} %copy.115) | data formatting | bytes 10223616 | tf_op jit(solution)/shard_map/convert_element_type | solution.py:131
  111.4 3.3 fusion.9
  116.4 3.2 fusion.1
  125.7 3.8 %fusion.44 = f32[624,2048]{1,0:T(8,128)} fusion(bf16[624,512]{1,0:T(8,128)(2,1)S(1)} %bitcast.117, bf16[512,2048]{0,1:T(8,128)(2,1)S(1)} %bitcast.112), kind=kOutput, calls=%fused_computation.103 | convolution fusion | flops 1308622848 | bytes 7847936 | tf_op jit(solution)/shard_map/dot_general | solution.py:171
  129.6 13.2 %reduce-scatter.5.cloned.1.call-done = f32[624,1024]{1,0:T(8,128)} async-done(((f32[624,2048]{1,0:T(8,128)}), f32[624,1024]{1,0:T(8,128)}) %reduce-scatter.5.cloned.1.call-update) | async-done | bytes 2555920 | tf_op jit(solution)/shard_map/reduce_scatter | solution.py:57
  143.6 39.5 %reduce-scatter.7.cloned.1.call-done = f32[624,512]{1,0:T(8,128)} async-done(((f32[624,1024]{1,0:T(8,128)}), f32[624,512]{1,0:T(8,128)}) %reduce-scatter.7.cloned.1.call-update) | async-done | bytes 1277968 | tf_op jit(solution)/shard_map/reduce_scatter | solution.py:58
  184.7 5.8 %psum.7 = f32[624,1]{0,1:T(1,128)S(1)} all-reduce(f32[624,1]{0,1:T(1,128)S(1)} %broadcast_in_dim.128), channel_id=1, replica_groups=mesh['req'=8,'kvy'=2,'core'=2] {'kvy','core'}, use_global_device_ids=true, to_apply=%region_6.7 | all-reduce | flops 624 | bytes 4992 | tf_op jit(solution)/shard_map/psum | solution.py:62
  191.6 25.1 %all-gather.9.cloned.1.call-done = bf16[624,1024]{1,0:T(8,128)(2,1)} async-done(((bf16[624,512]{1,0:T(8,128)(2,1)}), bf16[624,1024]{1,0:T(8,128)(2,1)}) %all-gather.9.cloned.1.call-update) | async-done | bytes 1277968 | tf_op jit(solution)/shard_map/all_gather | solution.py:43
  216.8 6.6 %copy.123 = bf16[1024,2048]{0,1:T(8,128)(2,1)} copy(bf16[1024,2048]{1,0:T(8,128)(2,1)} %param.27) | data formatting | bytes 8388608 | tf_op args[12]
  223.4 5.1 %copy.124 = bf16[1024,2,2,512]{0,3,2,1:T(8,128)(2,1)} copy(bf16[1024,2,2,512]{0,3,1,2:T(8,128)(2,1)} %bitcast.108) | data formatting | bytes 8388608 | tf_op jit(solution)/shard_map/transpose | solution.py:53
  229.4 7.1 %reshape.417 = bf16[624,2,2,512]{3,2,1,0:T(2,128)(2,1)} reshape(bf16[624,2048]{1,0:T(8,128)(2,1)} %all-gather.11.cloned.1.call-done) | data formatting | bytes 5111808 | tf_op jit(solution)/shard_map/reshape | solution.py:45
  236.5 7.5 %copy.122 = bf16[624,2,2,512]{0,3,1,2:T(8,128)(2,1)} copy(bf16[624,2,2,512]{3,2,1,0:T(2,128)(2,1)} %reshape.417) | data formatting | bytes 5111808 | tf_op jit(solution)/shard_map/reshape | solution.py:45
  244.0 7.3 %fusion.45 = f32[624,1024]{1,0:T(8,128)} fusion(bf16[624,2048]{0,1:T(8,128)(2,1)} %bitcast.118, bf16[2048,1024]{1,0:T(8,128)(2,1)} %param.25), kind=kOutput, calls=%fused_computation.104 | convolution fusion | flops 2617245696 | bytes 9306112 | tf_op jit(solution)/shard_map/dot_general | solution.py:178
  251.4 13.0 %fusion.19 = f32[624,2048]{1,0:T(8,128)} fusion(bf16[1024,2048]{0,1:T(8,128)(2,1)} %bitcast.115, f32[624,1024]{1,0:T(8,128)} %fusion.45, bf16[624,2048]{0,1:T(8,128)(2,1)} %bitcast.119, bf16[2048,1024]{1,0:T(8,128)(2,1)} %param.26), kind=kOutput, calls=%fused_computation.39 | convolution fusion | flops 5238325248 | bytes 18612224 | tf_op jit(solution)/shard_map/dot_general | solution.py:182
  264.5 14.3 %reduce-scatter.9.cloned.1.call-done = f32[624,1024]{1,0:T(8,128)} async-done(((f32[624,2048]{1,0:T(8,128)}), f32[624,1024]{1,0:T(8,128)}) %reduce-scatter.9.cloned.1.call-update) | async-done | bytes 2555920 | tf_op jit(solution)/shard_map/reduce_scatter | solution.py:57
  280.8 5.8 %all-to-all-start.1 = ((s32[8,1,2]{2,1,0:T(1,128)}), s32[8,1,2]{2,1,0:T(1,128)S(1)}, u32[]{:S(2)}, u32[]{:S(2)}) async-start(s32[8,1,2]{2,1,0:T(1,128)} %bitcast.38), calls=%async_computation.5 | async-start | bytes 8192 | tf_op jit(solution)/shard_map/all_to_all | solution.py:122
  293.0 4.2 %all-to-all-start.2 = ((bf16[2,8,2,64,256]{4,3,2,0,1:T(8,128)(2,1)}), bf16[2,8,2,64,256]{4,3,2,0,1:T(8,128)(2,1)S(1)}, u32[]{:S(2)}, u32[]{:S(2)}) async-start(bf16[2,8,2,64,256]{4,3,2,0,1:T(8,128)(2,1)} %copy.127), calls=%async_computation.6 | async-start | bytes 2097152 | tf_op jit(solution)/shard_map/all_to_all | solution.py:121
  298.9 24.1 %all-to-all-done.2 = bf16[2,8,2,64,256]{4,3,2,0,1:T(8,128)(2,1)S(1)} async-done(((bf16[2,8,2,64,256]{4,3,2,0,1:T(8,128)(2,1)}), bf16[2,8,2,64,256]{4,3,2,0,1:T(8,128)(2,1)S(1)}, u32[]{:S(2)}, u32[]{:S(2)}) %all-to-all-start.2) | async-done | bytes 1048608 | tf_op jit(solution)/shard_map/all_to_all | solution.py:121
  324.1 2.7 gather_fusion.2
  (118 shorter events, 40.4 us)
Async XLA Ops:
  7.2 104.3 %copy-start = (bf16[2048,256]{1,0:T(8,128)(2,1)S(1)}, bf16[2048,256]{1,0:T(8,128)(2,1)}, u32[]{:S(2)}) copy-start(bf16[2048,256]{1,0:T(8,128)(2,1)} %param.21) | copy-start | bytes 3145732
  7.2 31.1 %copy-start.11 = (bf16[13,16,1024]{2,1,0:T(8,128)(2,1)S(1)}, bf16[13,16,1024]{2,1,0:T(8,128)(2,1)}, u32[]{:S(2)}) copy-start(bf16[13,16,1024]{2,1,0:T(8,128)(2,1)} %param.28) | copy-start | bytes 1277956
  7.2 29.0 %all-gather.5.cloned.1.call-start = ((), (), s32[]{:S(2)}) async-start(), calls=%async_computation.7 | async-start | bytes 1916928 | tf_op jit(solution)/shard_map/all_gather | solution.py:43
  7.9 53.6 %all-gather.7.cloned.1.call-start = ((), (), s32[]{:S(2)}) async-start(), calls=%async_computation.8 | async-start | bytes 3833856 | tf_op jit(solution)/shard_map/all_gather | solution.py:44
  39.4 7.4 %copy-start.12 = (f32[2048]{0:T(1024)S(1)}, f32[2048]{0:T(1024)}, u32[]{:S(2)}) copy-start(f32[2048]{0:T(1024)} %param.19) | copy-start | bytes 24580
  39.4 7.5 %copy-start.9 = (bf16[2048,512]{1,0:T(8,128)(2,1)S(1)}, bf16[2048,512]{1,0:T(8,128)(2,1)}, u32[]{:S(2)}) copy-start(bf16[2048,512]{1,0:T(8,128)(2,1)} %param.20) | copy-start | bytes 6291460
  42.3 7.0 %copy-start.15 = (s32[13]{0:T(128)S(1)}, s32[13]{0:T(128)}, u32[]{:S(2)}) copy-start(s32[13]{0:T(128)} %param.17) | copy-start | bytes 160
  42.3 16.8 %all-to-all-start = ((bf16[2,4,13,16,256]{4,3,2,0,1:T(8,128)(2,1)}), bf16[2,4,13,16,256]{4,3,2,0,1:T(8,128)(2,1)}, u32[]{:S(2)}, u32[]{:S(2)}) async-start(bf16[2,4,13,16,256]{4,3,2,0,1:T(8,128)(2,1)} %copy.111), calls=%async_computation | async-start | bytes 1703936 | tf_op jit(solution)/shard_map/all_to_all | solution.py:100
  46.7 96.0 %reduce-scatter.5.cloned.1.call-start = ((), (), s32[]{:S(2)}) async-start(), calls=%async_computation.9 | async-start | bytes 7667712 | tf_op jit(solution)/shard_map/reduce_scatter | solution.py:57
  52.2 1.6 copy-start.13
  60.4 1.0 copy-start.5
  116.3 3.3 copy-start.8
  116.4 3.9 %copy-start.10 = (bf16[512,2048]{1,0:T(8,128)(2,1)S(1)}, bf16[512,2048]{1,0:T(8,128)(2,1)}, u32[]{:S(2)}) copy-start(bf16[512,2048]{1,0:T(8,128)(2,1)} %copy.132) | copy-start | bytes 6291460
  122.0 1.2 copy-start.14
  124.1 1.6 copy-start.7
  129.5 53.6 %copy-start.4 = (bf16[624,512]{1,0:T(8,128)(2,1)S(1)}, bf16[624,512]{1,0:T(8,128)(2,1)}, u32[]{:S(2)}) copy-start(bf16[624,512]{1,0:T(8,128)(2,1)} %param.15) | copy-start | bytes 1916932
  129.5 53.5 %reduce-scatter.7.cloned.1.call-start = ((), (), s32[]{:S(2)}) async-start(), calls=%async_computation.10 | async-start | bytes 3833856 | tf_op jit(solution)/shard_map/reduce_scatter | solution.py:58
  142.8 74.0 %all-gather.9.cloned.1.call-start = ((), (), s32[]{:S(2)}) async-start(), calls=%async_computation.11 | async-start | bytes 1916928 | tf_op jit(solution)/shard_map/all_gather | solution.py:43
  183.1 7.5 %copy-start.3 = (f32[624,512]{1,0:T(8,128)S(1)}, f32[624,512]{1,0:T(8,128)}, u32[]{:S(2)}) copy-start(f32[624,512]{1,0:T(8,128)} %reduce-scatter.7.cloned.1.call-done) | copy-start | bytes 3833860
  191.6 37.8 %all-gather.11.cloned.1.call-start = ((), (), s32[]{:S(2)}) async-start(), calls=%async_computation.12 | async-start | bytes 3833856 | tf_op jit(solution)/shard_map/all_gather | solution.py:44
  216.8 62.0 %reduce-scatter.9.cloned.1.call-start = ((), (), s32[]{:S(2)}) async-start(), calls=%async_computation.13 | async-start | bytes 7667712 | tf_op jit(solution)/shard_map/reduce_scatter | solution.py:57
  264.4 14.4 %copy-start.2 = (s32[13]{0:T(128)S(1)}, s32[13]{0:T(128)}, u32[]{:S(2)}) copy-start(s32[13]{0:T(128)} %param.18) | copy-start | bytes 160
  264.4 22.4 %copy-start.6 = (bf16[2,4,13,16,256]{4,3,1,2,0:T(8,128)(2,1)S(1)}, bf16[2,4,13,16,256]{4,3,1,2,0:T(8,128)(2,1)}, u32[]{:S(2)}) copy-start(bf16[2,4,13,16,256]{4,3,1,2,0:T(8,128)(2,1)} %copy-done.5) | copy-start | bytes 2555908
  264.4 64.7 %reduce-scatter.11.cloned.1.call-start = ((), (), s32[]{:S(2)}) async-start(), calls=%async_computation.14 | async-start | bytes 3833856 | tf_op jit(solution)/shard_map/reduce_scatter | solution.py:58
  280.8 12.2 %all-to-all-start.1 = ((s32[8,1,2]{2,1,0:T(1,128)}), s32[8,1,2]{2,1,0:T(1,128)S(1)}, u32[]{:S(2)}, u32[]{:S(2)}) async-start(s32[8,1,2]{2,1,0:T(1,128)} %bitcast.38), calls=%async_computation.5 | async-start | bytes 8192 | tf_op jit(solution)/shard_map/all_to_all | solution.py:122
  293.0 29.9 %all-to-all-start.2 = ((bf16[2,8,2,64,256]{4,3,2,0,1:T(8,128)(2,1)}), bf16[2,8,2,64,256]{4,3,2,0,1:T(8,128)(2,1)S(1)}, u32[]{:S(2)}, u32[]{:S(2)}) async-start(bf16[2,8,2,64,256]{4,3,2,0,1:T(8,128)(2,1)} %copy.127), calls=%async_computation.6 | async-start | bytes 2097152 | tf_op jit(solution)/shard_map/all_to_all | solution.py:121
  326.8 4.7 %copy-start.1 = (bf16[2048,256]{1,0:T(8,128)(2,1)S(1)}, bf16[2048,256]{1,0:T(8,128)(2,1)}, u32[]{:S(2)}) copy-start(bf16[2048,256]{1,0:T(8,128)(2,1)} %param.21) | copy-start | bytes 3145732
Sparse Core Ops, SparseCore 0:
  9.6 26.5 all-gather.4
  37.7 11.5 all-gather.6
  129.6 13.0 reduce-scatter.4
  144.9 38.0 reduce-scatter.6
  191.7 24.9 all-gather.8
  218.1 11.2 all-gather.10
  264.5 14.2 reduce-scatter.8
  281.1 38.1 reduce-scatter.10

commit v2 on v1

--- a/solution.py
+++ b/solution.py
@@ -37,30 +37,47 @@
     return (key_pos[None, None, :] < 0) | causal[None, :, :] & live_keys
 
 
+def swap(values, axis_name):
+    return lax.ppermute(values, axis_name, [(0, 1), (1, 0)])
+
+
 def gather_features(share):
-    chips = lax.axis_size("kvy")
-    rows, width = share.shape
-    pair = lax.all_gather(share, "kvy", axis=1, tiled=True)
-    whole = lax.all_gather(pair, "core", axis=1, tiled=True)
-    whole = whole.reshape(rows, CORES, chips, width).transpose(0, 2, 1, 3)
-    return whole.reshape(rows, CORES * chips * width)
-
-
-def swap_blocks(matrix):
-    chips = lax.axis_size("kvy")
-    rows, cols = matrix.shape
-    width = cols // (CORES * chips)
-    return matrix.reshape(rows, chips, CORES, width).transpose(0, 2, 1, 3).reshape(rows, cols)
-
-
-def scatter_features(partial):
-    on_chip = lax.psum_scatter(partial, "core", scatter_dimension=1, tiled=True)
-    return lax.psum_scatter(on_chip, "kvy", scatter_dimension=1, tiled=True)
+    chip = lax.axis_index("kvy")
+    core = lax.axis_index("core")
+    partner = swap(share, "kvy")
+    pair = jnp.where(chip == 0, jnp.stack([share, partner]), jnp.stack([partner, share]))
+    other = swap(pair, "core")
+    blocks = []
+    for chip_block in range(2):
+        for core_block in range(2):
+            blocks.append(jnp.where(core == core_block, pair[chip_block], other[chip_block]))
+    return jnp.concatenate(blocks, axis=1)
+
+
+def scatter_features(matrix_in, weight):
+    chip = lax.axis_index("kvy")
+    core = lax.axis_index("core")
+    rows, cols = weight.shape
+    width = cols // (2 * CORES)
+    blocks = jnp.einsum(
+        "rd,dkcf->ckrf",
+        matrix_in,
+        weight.reshape(rows, 2, CORES, width),
+        preferred_element_type=jnp.float32,
+    )
+    keep = jnp.where(core == 0, blocks[0], blocks[1])
+    give = jnp.where(core == 0, blocks[1], blocks[0])
+    chip_sum = keep + swap(give, "core")
+    mine = jnp.where(chip == 0, chip_sum[0], chip_sum[1])
+    theirs = jnp.where(chip == 0, chip_sum[1], chip_sum[0])
+    return mine + swap(theirs, "kvy")
 
 
 def row_scale(values, gain_share):
-    square_sum = lax.psum(jnp.sum(values * values, axis=-1, keepdims=True), ("kvy", "core"))
-    width = values.shape[-1] * lax.axis_size("kvy") * CORES
+    square_sum = jnp.sum(values * values, axis=-1, keepdims=True)
+    square_sum = square_sum + swap(square_sum, "core")
+    square_sum = square_sum + swap(square_sum, "kvy")
+    width = values.shape[-1] * 2 * CORES
     return values * lax.rsqrt(square_sum / width + epsilon) * gain_share
 
 
@@ -168,8 +185,7 @@
         "rkgcs,rskd->rckgd", weights, combined_values, preferred_element_type=jnp.float32
     )
     mixed_heads = mixed_heads.astype(jnp.bfloat16).reshape(total_rows, local_q * HEAD_WIDTH)
-    head_part = jnp.dot(mixed_heads, swap_blocks(output_weight), preferred_element_type=jnp.float32)
-    head_share = scatter_features(head_part)
+    head_share = scatter_features(mixed_heads, output_weight)
     residual_share = activations.astype(jnp.float32) + head_share
 
     gain_share = lax.dynamic_slice_in_dim(feedforward_gain, kv_index * width_share, width_share)
@@ -178,9 +194,7 @@
     gate_proj = jnp.dot(normed_two, gate_weight, preferred_element_type=jnp.float32)
     upward = jnp.dot(normed_two, up_weight, preferred_element_type=jnp.float32)
     hidden = (jax.nn.silu(gate_proj) * upward).astype(jnp.bfloat16)
-    mlp_share = scatter_features(
-        jnp.dot(hidden, swap_blocks(down_weight), preferred_element_type=jnp.float32)
-    )
+    mlp_share = scatter_features(hidden, down_weight)
     live_rows = (jnp.arange(span_size, dtype=jnp.int32)[None, :] < span_length[:, None]).reshape(
         total_rows
     )

time: 340 us -> 191 us (0.56)
  waiting for transfers between devices: 152 us -> 83.5 us
  local copies, waits for them, and re-layouts: 97.2 us -> 35.6 us
  matrix products: 30.8 us -> 17.4 us
  between operations: 14.5 us -> 1.24 us
  starting transfers between devices: 14.7 us -> 24.5 us
  blocking collectives: 5.76 us -> 0 us
  other arithmetic: 23.4 us -> 28.3 us
    reduce_scatter x4 -> x0, waiting for transfers between devices: 67 us -> none  [the longest x2 39.5 us: scatter_features(): return lax.psum_scatter(on_chip, 'kvy', scatter_dimension=1, tiled=True)]
    ppermute x0 -> x10, waiting for transfers between devices: none -> 60.5 us  [swap(): return lax.ppermute(values, axis_name, [(0, 1), (1, 0)])]
    all_gather x4 -> x0, waiting for transfers between devices: 54.3 us -> none  [the longest x2 53.3 us: gather_features(): pair = lax.all_gather(share, 'kvy', axis=1, tiled=True)]
    convert_element_type x7 -> x0, local copies, waits for them, and re-layouts: 43.9 us -> none  [the longest x5 32.7 us: local(): x_float = x_whole.astype(jnp.float32)]
    ppermute x0 -> x10, starting transfers between devices: none -> 10.7 us  [swap(): return lax.ppermute(values, axis_name, [(0, 1), (1, 0)])]
    select_n x0 -> x8, other arithmetic: none -> 9.45 us  [the longest x2 3.04 us: gather_features(): jnp.where(core == core_block, pair[chip_block], other[chip_block])]
    all_to_all x1, waiting for transfers between devices: 24.1 us -> 14.7 us  [local(): lax.all_to_all(packed, 'req', split_axis=1, concat_axis=1, tiled=True)]
    dot_general x2 -> x3, matrix products: 16.8 us -> 8.02 us  [the longest x2 4.42 us: scatter_features(): jnp.einsum('rd,dkcf->ckrf', matrix_in, weight.reshape(rows, 2, CORES, wid...]
  transfers between devices with their start and end apart: 11 -> 13, of which waited for: 9 -> 10; matrix products, arithmetic and copies ran while one was open for 13% -> 19% of each run, Pallas kernels for 0% -> 0%
where the time goes in v2:
time: 191 us; the launch traced here: 190 us
  waiting for transfers between devices  83.5 us (44%)
  local copies, waits for them, and re-layouts  35.6 us (19%)
  other arithmetic  28.3 us (15%)
  starting transfers between devices  24.5 us (13%)
  matrix products  17.4 us (9%)
    ppermute x10, waiting for transfers between devices, swap(): return lax.ppermute(values, axis_name, [(0, 1), (1, 0)])  60.5 us
    all_to_all x1, waiting for transfers between devices, local(): lax.all_to_all(packed, 'req', split_axis=1, concat_axis=1, tiled=True)  14.7 us
    reshape x2, local copies, waits for them, and re-layouts, scatter_features(): weight.reshape(rows, 2, CORES, width)  12.3 us
    ppermute x10, starting transfers between devices, swap(): return lax.ppermute(values, axis_name, [(0, 1), (1, 0)])  10.7 us
    unnamed x46, local copies, waits for them, and re-layouts  7.67 us
    all_to_all x1, starting transfers between devices, local(): lax.all_to_all(packed_slots, 'req', split_axis=0, concat_axis=0, tiled=True)  6.03 us
    add x2, other arithmetic, scatter_features(): chip_sum = keep + swap(give, 'core')  5.12 us
    dot_general x2, matrix products, scatter_features(): jnp.einsum('rd,dkcf->ckrf', matrix_in, weight.reshape(rows, 2, CORES, wid...  4.42 us
  transfers between devices with their start and end apart: 13, of which 10 were waited for; matrix products, arithmetic and copies ran while one was open for 19% of the time, Pallas kernels for 0%

profile of v2, /device:TPU:0, one launch (start us, length us, event | category | flops | bytes accessed | tf_op | source)
XLA Modules:
  0.0 190.4 jit_solution(14881923914795494855)
XLA Ops:
  0.6 3.0 %collective-permute-start = (bf16[624,512]{1,0:T(8,128)(2,1)}, bf16[624,512]{1,0:T(8,128)(2,1)}, u32[]{:S(2)}, u32[]{:S(2)}) collective-permute-start(bf16[624,512]{1,0:T(8,128)(2,1)} %param.15), channel_id=1, source_target_pairs={{0,2},{2,0},{1,3},{3,1},{4,6},{6,4},{5,7},{7,5},{8,10},{10,8},{9,1... | collective-permute-start | bytes 1916936 | tf_op jit(solution)/shard_map/ppermute | solution.py:41
  8.0 4.2 %all-to-all-start = ((bf16[2,4,13,16,256]{4,3,2,0,1:T(8,128)(2,1)}), bf16[2,4,13,16,256]{4,3,2,0,1:T(8,128)(2,1)}, u32[]{:S(2)}, u32[]{:S(2)}) async-start(bf16[2,4,13,16,256]{4,3,2,0,1:T(8,128)(2,1)} %copy.72), calls=%async_computation | async-start | bytes 1703936 | tf_op jit(solution)/shard_map/all_to_all | solution.py:117
  12.3 4.5 %reshape.380 = bf16[512,2,2,512]{3,2,1,0:T(2,128)(2,1)} reshape(bf16[512,2048]{1,0:T(8,128)(2,1)} %param.23) | data formatting | bytes 4194304 | tf_op jit(solution)/shard_map/reshape | solution.py:65
  16.8 2.4 %collective-permute-done = bf16[624,512]{1,0:T(8,128)(2,1)} collective-permute-done((bf16[624,512]{1,0:T(8,128)(2,1)}, bf16[624,512]{1,0:T(8,128)(2,1)}, u32[]{:S(2)}, u32[]{:S(2)}) %collective-permute-start) | collective-permute-done | bytes 639008 | tf_op jit(solution)/shard_map/ppermute | solution.py:41
  19.2 1.9 maximum_select_fusion
  21.4 2.0 %multiply_cosine_fusion = (f32[13,48,128]{2,1,0:T(8,128)}, f32[13,48,128]{2,1,0:T(8,128)}) fusion(f32[128]{0:T(128)S(1)} %multiply_exponential_fusion, f32[13,48]{1,0:T(8,128)S(1)} %iota_add_fusion), kind=kLoop, calls=%fused_computation.70 | loop fusion | flops 79872 | bytes 641984 | tf_op jit(solution)/shard_map/cos | solution.py:22
  23.4 4.1 %all-to-all-done = bf16[2,4,13,16,256]{4,3,2,0,1:T(8,128)(2,1)} async-done(((bf16[2,4,13,16,256]{4,3,2,0,1:T(8,128)(2,1)}), bf16[2,4,13,16,256]{4,3,2,0,1:T(8,128)(2,1)}, u32[]{:S(2)}, u32[]{:S(2)}) %all-to-all-start) | async-done | bytes 852000 | tf_op jit(solution)/shard_map/all_to_all | solution.py:117
  32.1 2.0 %fusion = f32[624]{0:T(1024)S(1)} fusion(bf16[624,512]{1,0:T(8,128)(2,1)S(1)} %get-tuple-element.11, bf16[624,512]{1,0:T(8,128)(2,1)S(1)} %get-tuple-element.12, bf16[624,512]{1,0:T(8,128)(2,1)S(1)} %get-tuple-element.10, bf16[624,512]{1,0:T(8,128)(2,1)S(1)} %get-tuple-element.9), kind=kLoop, calls=%fused_computation.5 | loop fusion | flops 12778896 | bytes 2558400 | tf_op jit(solution)/shard_map/reduce_sum | solution.py:149
  36.5 2.6 %fusion.55 = f32[624,512]{1,0:T(8,128)} fusion(bf16[624,2048]{1,0:T(8,128)(2,1)S(1)} %fusion.2, bf16[2048,512]{1,0:T(8,128)(2,1)S(1)} %copy-done), kind=kOutput, calls=%fused_computation.128 | convolution fusion | flops 1308622848 | bytes 5931008 | tf_op jit(solution)/shard_map/dot_general | solution.py:156
  39.1 2.1 %reshape.377 = f32[13,48,2,256]{3,2,1,0:T(2,128)S(1)} reshape(f32[624,512]{1,0:T(8,128)} %fusion.55) | data formatting | bytes 2555904 | tf_op jit(solution)/shard_map/reshape | solution.py:158
  42.9 2.1 %fusion.54 = f32[624,256]{1,0:T(8,128)S(1)} fusion(bf16[624,2048]{1,0:T(8,128)(2,1)S(1)} %copy-done.12, bf16[2048,256]{1,0:T(8,128)(2,1)} %param.21), kind=kOutput, calls=%fused_computation.127 | convolution fusion | flops 654311424 | bytes 4243456 | tf_op jit(solution)/shard_map/dot_general | solution.py:160
  45.0 1.6 fusion.36
  51.1 1.6 convolution_bitcast_fusion
  53.3 4.8 %collective-permute-done.2 = f32[2,624,512]{2,1,0:T(8,128)S(1)} collective-permute-done((f32[2,624,512]{2,1,0:T(8,128)S(1)}, f32[2,624,512]{2,1,0:T(8,128)S(1)}, u32[]{:S(2)}, u32[]{:S(2)}) %collective-permute-start.2) | collective-permute-done | bytes 2555936 | tf_op jit(solution)/shard_map/ppermute | solution.py:41
  59.4 1.8 collective-permute-start.3
  61.2 28.4 %collective-permute-done.3 = f32[624,512]{1,0:T(8,128)S(1)} collective-permute-done((f32[624,512]{1,0:T(8,128)S(1)}, f32[624,512]{1,0:T(8,128)S(1)}, u32[]{:S(2)}, u32[]{:S(2)}) %collective-permute-start.3) | collective-permute-done | bytes 1277984 | tf_op jit(solution)/shard_map/ppermute | solution.py:41
  91.2 1.7 collective-permute-start.5
  95.0 1.8 collective-permute-start.6
  97.0 13.4 %collective-permute-done.6 = bf16[624,512]{1,0:T(8,128)(2,1)S(1)} collective-permute-done((bf16[624,512]{1,0:T(8,128)(2,1)S(1)}, bf16[624,512]{1,0:T(8,128)(2,1)S(1)}, u32[]{:S(2)}, u32[]{:S(2)}) %collective-permute-start.6) | collective-permute-done | bytes 639008 | tf_op jit(solution)/shard_map/ppermute | solution.py:41
  110.7 7.8 %reshape.381 = bf16[1024,2,2,512]{3,2,1,0:T(2,128)(2,1)} reshape(bf16[1024,2048]{1,0:T(8,128)(2,1)} %param.27) | data formatting | bytes 8388608 | tf_op jit(solution)/shard_map/reshape | solution.py:65
  118.5 1.6 select_bitcast_fusion.8
  121.1 2.8 %fusion.34 = f32[624,1024]{1,0:T(8,128)S(1)} fusion(bf16[2048,1024]{1,0:T(8,128)(2,1)S(1)} %copy-done.19, bf16[624,512]{1,0:T(8,128)(2,1)S(1)} %get-tuple-element.7, bf16[624,512]{1,0:T(8,128)(2,1)S(1)} %get-tuple-element.8, bf16[624,512]{1,0:T(8,128)(2,1)S(1)} %get-tuple-element.6, bf16[624,512]{1,0:T(8,128)(2,1)S(1)} %get-tuple-element.5), kind=kOutput, calls=%fused_computation.77 | convolution fusion | flops 2627469312 | bytes 9306112 | tf_op jit(solution)/shard_map/dot_general | solution.py:194
  123.9 3.6 %fusion.11 = bf16[624,1024,1,1]{1,0,2,3:T(8,128)(2,1)S(1)} fusion(bf16[2048,1024]{1,0:T(8,128)(2,1)S(1)} %copy-done.20, f32[624,1024]{1,0:T(8,128)S(1)} %fusion.34, bf16[624,512]{1,0:T(8,128)(2,1)S(1)} %get-tuple-element.7, bf16[624,512]{1,0:T(8,128)(2,1)S(1)} %get-tuple-element.8, bf16[624,512]{1,0:T(8,128)(2,1)S(1)} %get-tuple-element.6, ...), kind=kOutput, calls=%fused_computation.22 | convolution fusion | flops 2631303168 | bytes 10584064 | tf_op jit(solution)/shard_map/dot_general | solution.py:195
  127.5 2.9 %fusion.7 = f32[2,2,624,512]{3,2,1,0:T(8,128)S(1)} fusion(bf16[624,1024,1,1]{1,0,2,3:T(8,128)(2,1)S(1)} %fusion.11, bf16[1024,2,2,512]{3,2,1,0:T(2,128)(2,1)S(1)} %copy-done.9), kind=kOutput, calls=%fused_computation.19 | convolution fusion | flops 2617245696 | bytes 10584064 | tf_op jit(solution)/shard_map/rd,dkcf->ckrf/dot_general | solution.py:62
  130.5 2.1 %select_bitcast_fusion = f32[2,624,512]{2,1,0:T(8,128)} fusion(f32[2,2,624,512]{3,2,1,0:T(8,128)S(1)} %fusion.7, pred[]{:T(512)S(6)} %eq.27), kind=kLoop, calls=%fused_computation.16 | loop fusion | flops 638976 | bytes 7667713 | tf_op jit(solution)/shard_map/jit(_where)/select_n | solution.py:69
  135.9 6.0 %all-to-all-start.1 = ((s32[8,1,2]{2,1,0:T(1,128)}), s32[8,1,2]{2,1,0:T(1,128)S(1)}, u32[]{:S(2)}, u32[]{:S(2)}) async-start(s32[8,1,2]{2,1,0:T(1,128)} %bitcast.46), calls=%async_computation.1 | async-start | bytes 8192 | tf_op jit(solution)/shard_map/all_to_all | solution.py:139
  144.2 4.2 %all-to-all-done.1 = s32[8,1,2]{2,1,0:T(1,128)S(1)} async-done(((s32[8,1,2]{2,1,0:T(1,128)}), s32[8,1,2]{2,1,0:T(1,128)S(1)}, u32[]{:S(2)}, u32[]{:S(2)}) %all-to-all-start.1) | async-done | bytes 96 | tf_op jit(solution)/shard_map/all_to_all | solution.py:139
  148.4 3.6 %all-to-all-start.2 = ((bf16[2,8,2,64,256]{4,3,2,0,1:T(8,128)(2,1)}), bf16[2,8,2,64,256]{4,3,2,0,1:T(8,128)(2,1)S(1)}, u32[]{:S(2)}, u32[]{:S(2)}) async-start(bf16[2,8,2,64,256]{4,3,2,0,1:T(8,128)(2,1)} %copy.86), calls=%async_computation.2 | async-start | bytes 2097152 | tf_op jit(solution)/shard_map/all_to_all | solution.py:138
  152.1 4.2 %bitcast_add_fusion = f32[2,624,512]{2,1,0:T(8,128)S(1)} fusion(f32[2,624,512]{2,1,0:T(8,128)} %collective-permute-done.8, f32[2,2,624,512]{3,2,1,0:T(8,128)} %copy-done.5, pred[]{:T(512)S(6)} %eq.27), kind=kLoop, calls=%fused_computation.15 | loop fusion | flops 1277952 | bytes 10223617 | tf_op jit(solution)/shard_map/add | solution.py:70
  162.1 14.7 %all-to-all-done.2 = bf16[2,8,2,64,256]{4,3,2,0,1:T(8,128)(2,1)S(1)} async-done(((bf16[2,8,2,64,256]{4,3,2,0,1:T(8,128)(2,1)}), bf16[2,8,2,64,256]{4,3,2,0,1:T(8,128)(2,1)S(1)}, u32[]{:S(2)}, u32[]{:S(2)}) %all-to-all-start.2) | async-done | bytes 1048608 | tf_op jit(solution)/shard_map/all_to_all | solution.py:138
  178.7 9.3 %collective-permute-done.9 = f32[624,512]{1,0:T(8,128)} collective-permute-done((f32[624,512]{1,0:T(8,128)}, f32[624,512]{1,0:T(8,128)}, u32[]{:S(2)}, u32[]{:S(2)}) %collective-permute-start.9) | collective-permute-done | bytes 1277984 | tf_op jit(solution)/shard_map/ppermute | solution.py:41
  187.9 2.4 %fusion.14 = bf16[624,512]{1,0:T(8,128)(2,1)} fusion(f32[624,512]{1,0:T(8,128)S(1)} %get-tuple-element.4, f32[624,512]{1,0:T(8,128)} %collective-permute-done.9, f32[2,624,512]{2,1,0:T(8,128)S(1)} %copy-done.4, pred[624]{0:T(1024)(128)(4,1)S(1)} %lt.111, pred[]{:T(512)S(6)} %eq.26), kind=kLoop, calls=%fused_computation.29 | loop fusion | flops 1597440 | bytes 5751409 | tf_op jit(solution)/shard_map/convert_element_type | solution.py:201
  (127 shorter events, 37.9 us)
Async XLA Ops:
  0.6 35.9 %copy-start = (bf16[2048,512]{1,0:T(8,128)(2,1)S(1)}, bf16[2048,512]{1,0:T(8,128)(2,1)}, u32[]{:S(2)}) copy-start(bf16[2048,512]{1,0:T(8,128)(2,1)} %param.20) | copy-start | bytes 6291460
  0.6 18.6 %collective-permute-start = (bf16[624,512]{1,0:T(8,128)(2,1)}, bf16[624,512]{1,0:T(8,128)(2,1)}, u32[]{:S(2)}, u32[]{:S(2)}) collective-permute-start(bf16[624,512]{1,0:T(8,128)(2,1)} %param.15), channel_id=1, source_target_pairs={{0,2},{2,0},{1,3},{3,1},{4,6},{6,4},{5,7},{7,5},{8,10},{10,8},{9,1... | collective-permute-start | bytes 1916936 | tf_op jit(solution)/shard_map/ppermute | solution.py:41
  6.3 5.9 %copy-start.22 = (s32[13]{0:T(128)S(1)}, s32[13]{0:T(128)}, u32[]{:S(2)}) copy-start(s32[13]{0:T(128)} %param.17) | copy-start | bytes 160
  8.0 19.5 %all-to-all-start = ((bf16[2,4,13,16,256]{4,3,2,0,1:T(8,128)(2,1)}), bf16[2,4,13,16,256]{4,3,2,0,1:T(8,128)(2,1)}, u32[]{:S(2)}, u32[]{:S(2)}) async-start(bf16[2,4,13,16,256]{4,3,2,0,1:T(8,128)(2,1)} %copy.72), calls=%async_computation | async-start | bytes 1703936 | tf_op jit(solution)/shard_map/all_to_all | solution.py:117
  12.3 9.0 %copy-start.18 = (s32[13]{0:T(128)S(1)}, s32[13]{0:T(128)}, u32[]{:S(2)}) copy-start(s32[13]{0:T(128)} %param.16) | copy-start | bytes 160
  21.1 9.5 %collective-permute-start.1 = (bf16[2,624,512]{2,1,0:T(8,128)(2,1)S(1)}, bf16[2,624,512]{2,1,0:T(8,128)(2,1)}, u32[]{:S(2)}, u32[]{:S(2)}) collective-permute-start(bf16[2,624,512]{2,1,0:T(8,128)(2,1)S(1)} %maximum_select_fusion), channel_id=1, source_target_pairs={{0,1},{1,0},{2,3},{3,2},{4,5},{5,4},{6,7},{7,6},{8,9},{9,8},{10,11... | collective-permute-start | bytes 3833864 | tf_op jit(solution)/shard_map/ppermute | solution.py:41
  32.1 2.1 %copy-start.17 = (f32[2048]{0:T(1024)S(1)}, f32[2048]{0:T(1024)}, u32[]{:S(2)}) copy-start(f32[2048]{0:T(1024)} %param.19) | copy-start | bytes 24580
  35.0 1.5 copy-start.11
  41.2 1.7 copy-start.12
  42.9 3.7 %copy-start.21 = (bf16[2048,256]{1,0:T(8,128)(2,1)S(1)}, bf16[2048,256]{1,0:T(8,128)(2,1)}, u32[]{:S(2)}) copy-start(bf16[2048,256]{1,0:T(8,128)(2,1)} %param.22) | copy-start | bytes 3145732
  47.9 1.6 copy-start.15
  49.5 1.6 copy-start.8
  53.3 4.9 %collective-permute-start.2 = (f32[2,624,512]{2,1,0:T(8,128)S(1)}, f32[2,624,512]{2,1,0:T(8,128)S(1)}, u32[]{:S(2)}, u32[]{:S(2)}) collective-permute-start(f32[2,624,512]{2,1,0:T(8,128)S(1)} %select_bitcast_fusion.1), channel_id=1, source_target_pairs={{0,1},{1,0},{2,3},{3,2},{4,5},{5,4},{6,7},{7,6},{8,9},{9,8},{10,11... | collective-permute-start | bytes 7667720 | tf_op jit(solution)/shard_map/ppermute | solution.py:41
  59.1 30.5 %copy-start.10 = (bf16[624,512]{1,0:T(8,128)(2,1)S(1)}, bf16[624,512]{1,0:T(8,128)(2,1)}, u32[]{:S(2)}) copy-start(bf16[624,512]{1,0:T(8,128)(2,1)} %param.15) | copy-start | bytes 1916932
  59.4 30.2 %collective-permute-start.3 = (f32[624,512]{1,0:T(8,128)S(1)}, f32[624,512]{1,0:T(8,128)S(1)}, u32[]{:S(2)}, u32[]{:S(2)}) collective-permute-start(f32[624,512]{1,0:T(8,128)S(1)} %select_bitcast_fusion.3), channel_id=1, source_target_pairs={{0,2},{2,0},{1,3},{3,1},{4,6},{6,4},{5,7},{7,5},{8,10},{10,8},{9,1... | collective-permute-start | bytes 3833864 | tf_op jit(solution)/shard_map/ppermute | solution.py:41
  90.0 1.2 collective-permute-start.4
  91.2 3.6 %collective-permute-start.5 = (f32[624,1]{0,1:T(1,128)S(1)}, f32[624,1]{0,1:T(1,128)S(1)}, u32[]{:S(2)}, u32[]{:S(2)}) collective-permute-start(f32[624,1]{0,1:T(1,128)S(1)} %reshape_add_fusion), channel_id=1, source_target_pairs={{0,2},{2,0},{1,3},{3,1},{4,6},{6,4},{5,7},{7,5},{8,10},{10,8},{9,1... | collective-permute-start | bytes 7496 | tf_op jit(solution)/shard_map/ppermute | solution.py:41
  95.0 15.4 %collective-permute-start.6 = (bf16[624,512]{1,0:T(8,128)(2,1)S(1)}, bf16[624,512]{1,0:T(8,128)(2,1)S(1)}, u32[]{:S(2)}, u32[]{:S(2)}) collective-permute-start(bf16[624,512]{1,0:T(8,128)(2,1)S(1)} %multiply_convert_fusion.1), channel_id=1, source_target_pairs={{0,2},{2,0},{1,3},{3,1},{4,6},{6,4},{5,7},{7,5},{8,10},{10,8},{9,1... | collective-permute-start | bytes 1916936 | tf_op jit(solution)/shard_map/ppermute | solution.py:41
  110.6 7.9 %collective-permute-start.7 = (bf16[2,624,512]{2,1,0:T(8,128)(2,1)S(1)}, bf16[2,624,512]{2,1,0:T(8,128)(2,1)}, u32[]{:S(2)}, u32[]{:S(2)}) collective-permute-start(bf16[2,624,512]{2,1,0:T(8,128)(2,1)S(1)} %maximum_select_fusion.1), channel_id=1, source_target_pairs={{0,1},{1,0},{2,3},{3,2},{4,5},{5,4},{6,7},{7,6},{8,9},{9,8},{10,11... | collective-permute-start | bytes 3833864 | tf_op jit(solution)/shard_map/ppermute | solution.py:41
  118.5 2.6 %copy-start.19 = (bf16[2048,1024]{1,0:T(8,128)(2,1)S(1)}, bf16[2048,1024]{1,0:T(8,128)(2,1)}, u32[]{:S(2)}) copy-start(bf16[2048,1024]{1,0:T(8,128)(2,1)} %param.25) | copy-start | bytes 12582916
  121.1 2.9 %copy-start.20 = (bf16[2048,1024]{1,0:T(8,128)(2,1)S(1)}, bf16[2048,1024]{1,0:T(8,128)(2,1)}, u32[]{:S(2)}) copy-start(bf16[2048,1024]{1,0:T(8,128)(2,1)} %param.26) | copy-start | bytes 12582916
  123.9 3.6 %copy-start.9 = (bf16[1024,2,2,512]{3,2,1,0:T(2,128)(2,1)S(1)}, bf16[1024,2,2,512]{3,2,1,0:T(2,128)(2,1)}, u32[]{:S(2)}) copy-start(bf16[1024,2,2,512]{3,2,1,0:T(2,128)(2,1)} %reshape.381) | copy-start | bytes 12582916
  130.4 3.0 %copy-start.5 = (f32[2,2,624,512]{3,2,1,0:T(8,128)}, f32[2,2,624,512]{3,2,1,0:T(8,128)S(1)}, u32[]{:S(2)}) copy-start(f32[2,2,624,512]{3,2,1,0:T(8,128)S(1)} %fusion.7) | copy-start | bytes 15335428
  130.4 3.5 %copy-start.2 = (s32[13]{0:T(128)S(1)}, s32[13]{0:T(128)}, u32[]{:S(2)}) copy-start(s32[13]{0:T(128)} %param.18) | copy-start | bytes 160
  130.4 11.7 %copy-start.7 = (bf16[2,4,13,16,256]{4,3,1,2,0:T(8,128)(2,1)S(1)}, bf16[2,4,13,16,256]{4,3,1,2,0:T(8,128)(2,1)}, u32[]{:S(2)}) copy-start(bf16[2,4,13,16,256]{4,3,1,2,0:T(8,128)(2,1)} %copy-done.6) | copy-start | bytes 2555908
  133.4 18.6 %collective-permute-start.8 = (f32[2,624,512]{2,1,0:T(8,128)}, f32[2,624,512]{2,1,0:T(8,128)}, u32[]{:S(2)}, u32[]{:S(2)}) collective-permute-start(f32[2,624,512]{2,1,0:T(8,128)} %select_bitcast_fusion), channel_id=1, source_target_pairs={{0,1},{1,0},{2,3},{3,2},{4,5},{5,4},{6,7},{7,6},{8,9},{9,8},{10,11... | collective-permute-start | bytes 7667720 | tf_op jit(solution)/shard_map/ppermute | solution.py:41
  135.9 12.4 %all-to-all-start.1 = ((s32[8,1,2]{2,1,0:T(1,128)}), s32[8,1,2]{2,1,0:T(1,128)S(1)}, u32[]{:S(2)}, u32[]{:S(2)}) async-start(s32[8,1,2]{2,1,0:T(1,128)} %bitcast.46), calls=%async_computation.1 | async-start | bytes 8192 | tf_op jit(solution)/shard_map/all_to_all | solution.py:139
  148.4 28.5 %all-to-all-start.2 = ((bf16[2,8,2,64,256]{4,3,2,0,1:T(8,128)(2,1)}), bf16[2,8,2,64,256]{4,3,2,0,1:T(8,128)(2,1)S(1)}, u32[]{:S(2)}, u32[]{:S(2)}) async-start(bf16[2,8,2,64,256]{4,3,2,0,1:T(8,128)(2,1)} %copy.86), calls=%async_computation.2 | async-start | bytes 2097152 | tf_op jit(solution)/shard_map/all_to_all | solution.py:138
  156.3 1.5 copy-start.3
  159.1 28.9 %collective-permute-start.9 = (f32[624,512]{1,0:T(8,128)}, f32[624,512]{1,0:T(8,128)}, u32[]{:S(2)}, u32[]{:S(2)}) collective-permute-start(f32[624,512]{1,0:T(8,128)} %select_bitcast_fusion.2), channel_id=1, source_target_pairs={{0,2},{2,0},{1,3},{3,1},{4,6},{6,4},{5,7},{7,5},{8,10},{10,8},{9,1... | collective-permute-start | bytes 3833864 | tf_op jit(solution)/shard_map/ppermute | solution.py:41
  177.5 10.4 %copy-start.4 = (f32[2,624,512]{2,1,0:T(8,128)S(1)}, f32[2,624,512]{2,1,0:T(8,128)}, u32[]{:S(2)}) copy-start(f32[2,624,512]{2,1,0:T(8,128)} %copy-done.3) | copy-start | bytes 7667716
  177.7 12.7 %copy-start.1 = (bf16[2048,512]{1,0:T(8,128)(2,1)S(1)}, bf16[2048,512]{1,0:T(8,128)(2,1)}, u32[]{:S(2)}) copy-start(bf16[2048,512]{1,0:T(8,128)(2,1)} %param.20) | copy-start | bytes 6291460
  (4 other events, 4.0 us)

commit v3 on v2

--- a/solution.py
+++ b/solution.py
@@ -57,16 +57,15 @@
 def scatter_features(matrix_in, weight):
     chip = lax.axis_index("kvy")
     core = lax.axis_index("core")
-    rows, cols = weight.shape
-    width = cols // (2 * CORES)
-    blocks = jnp.einsum(
-        "rd,dkcf->ckrf",
-        matrix_in,
-        weight.reshape(rows, 2, CORES, width),
-        preferred_element_type=jnp.float32,
-    )
-    keep = jnp.where(core == 0, blocks[0], blocks[1])
-    give = jnp.where(core == 0, blocks[1], blocks[0])
+    product = jnp.dot(matrix_in, weight, preferred_element_type=jnp.float32)
+    width = product.shape[1] // (2 * CORES)
+
+    def block(chip_block, core_block):
+        start = (chip_block * CORES + core_block) * width
+        return product[:, start:start + width]
+
+    keep = jnp.stack([jnp.where(core == 0, block(k, 0), block(k, 1)) for k in range(2)])
+    give = jnp.stack([jnp.where(core == 0, block(k, 1), block(k, 0)) for k in range(2)])
     chip_sum = keep + swap(give, "core")
     mine = jnp.where(chip == 0, chip_sum[0], chip_sum[1])
     theirs = jnp.where(chip == 0, chip_sum[1], chip_sum[0])
@@ -131,18 +130,24 @@
     matches = buffer_place[None, :] == buffer_ids[:, None]
     picked = jnp.sum(jnp.where(matches, order_ids[None, :], 0), axis=1)
     filled = jnp.any(matches, axis=1)
-    packed = jnp.take(head_kv, picked, axis=1)
-    packed = jnp.where(filled[None, :, None, None], packed, jnp.zeros((), packed.dtype))
-    packed = packed.reshape((2, req_count, capacity) + packed.shape[2:])
-    packed_slots = jnp.where(filled, jnp.take(decode_slot, picked), -1).reshape(req_count, capacity)
-    landed = lax.all_to_all(packed, "req", split_axis=1, concat_axis=1, tiled=True)
-    landed_slots = lax.all_to_all(packed_slots, "req", split_axis=0, concat_axis=0, tiled=True)
+    lanes = local_kv * HEAD_WIDTH
+    rows_kv = jnp.moveaxis(head_kv, 0, 1).reshape(request_list, 2 * past_size * lanes)
+    slot_code = jnp.stack([decode_slot // 16, decode_slot % 16], axis=1).astype(jnp.bfloat16)
+    trailer = jnp.pad(slot_code, ((0, 0), (0, lanes - 2)))
+    payload = jnp.concatenate([rows_kv, trailer], axis=1)
+    packed = jnp.take(payload, picked, axis=0)
+    packed = jnp.where(filled[:, None], packed, -jnp.ones((), packed.dtype))
+    packed = packed.reshape(req_count, capacity, payload.shape[1])
+    landed = lax.all_to_all(packed, "req", split_axis=0, concat_axis=0, tiled=True)
+    landed = landed.reshape(req_count * capacity, payload.shape[1])
+    code = landed[:, 2 * past_size * lanes:2 * past_size * lanes + 2].astype(jnp.int32)
+    landed_slots = code[:, 0] * 16 + code[:, 1]
     wanted = req_index * request_list + order_ids
-    slot_hits = landed_slots.reshape(1, -1) == wanted[:, None]
+    slot_hits = landed_slots[None, :] == wanted[:, None]
     entry_ids = jnp.arange(req_count * capacity, dtype=jnp.int32)
     slot_position = jnp.sum(jnp.where(slot_hits, entry_ids[None, :], 0), axis=1)
-    landed = landed.reshape((2, req_count * capacity) + landed.shape[3:])
-    decode_kv = jnp.take(landed, slot_position, axis=1)
+    decode_rows = jnp.take(landed[:, :2 * past_size * lanes], slot_position, axis=0)
+    decode_kv = jnp.moveaxis(decode_rows.reshape(request_list, 2, past_size, lanes), 1, 0)
 
     x_whole = gather_features(activations)
     x_float = x_whole.astype(jnp.float32)

time: 191 us -> 221 us (1.16)
  waiting for transfers between devices: 83.5 us -> 109 us
  other arithmetic: 28.3 us -> 36.7 us
  local copies, waits for them, and re-layouts: 35.6 us -> 27.5 us
  matrix products: 17.4 us -> 24.5 us
  starting transfers between devices: 24.5 us -> 20.9 us
    ppermute x10, waiting for transfers between devices: 60.5 us -> 79.1 us  [swap(): return lax.ppermute(values, axis_name, [(0, 1), (1, 0)])]
    reshape x3 -> x1, local copies, waits for them, and re-layouts: 12.7 us -> 1.29 us  [local(): landed = landed.reshape(req_count * capacity, payload.shape[1])]
    another operation x2 -> x8, other arithmetic: 1.77 us -> 9.24 us  [the longest x2 5.44 us: scatter_features(): jnp.stack([jnp.where(core == 0, block(k, 0), block(k, 1)) for k in range(...]
    all_to_all x2 -> x1, waiting for transfers between devices: 18.9 us -> 25.9 us  [local(): lax.all_to_all(packed, 'req', split_axis=0, concat_axis=0, tiled=True)]
    dot_general x3 -> x2, matrix products: 8.02 us -> 13.7 us  [scatter_features(): product = jnp.dot(matrix_in, weight, preferred_element_type=jnp.float32)]
    gather x5 -> x3, local copies, waits for them, and re-layouts: 2.06 us -> 5.69 us  [the longest x2 4.56 us: local(): packed = jnp.take(payload, picked, axis=0)]
    all_to_all x2 -> x1, starting transfers between devices: 9.59 us -> 6 us  [local(): lax.all_to_all(packed, 'req', split_axis=0, concat_axis=0, tiled=True)]
    select_n x2, other arithmetic: 2.09 us -> 4.44 us  [gather_features(): jnp.where(chip == 0, jnp.stack([share, partner]), jnp.stack([partner, sha...]
  transfers between devices with their start and end apart: 13 -> 12, of which waited for: 10 -> 9; matrix products, arithmetic and copies ran while one was open for 19% -> 12% of each run, Pallas kernels for 0% -> 0%
where the time goes in v3:
time: 221 us; the launch traced here: 220 us
  waiting for transfers between devices  109 us (49%)
  other arithmetic  36.7 us (17%)
  local copies, waits for them, and re-layouts  27.5 us (12%)
  matrix products  24.5 us (11%)
  starting transfers between devices  20.9 us (9%)
    ppermute x10, waiting for transfers between devices, swap(): return lax.ppermute(values, axis_name, [(0, 1), (1, 0)])  79.1 us
    all_to_all x1, waiting for transfers between devices, local(): lax.all_to_all(packed, 'req', split_axis=0, concat_axis=0, tiled=True)  25.9 us
    dot_general x2, matrix products, scatter_features(): product = jnp.dot(matrix_in, weight, preferred_element_type=jnp.float32)  13.7 us
    ppermute x10, starting transfers between devices, swap(): return lax.ppermute(values, axis_name, [(0, 1), (1, 0)])  10.5 us
    unnamed x49, local copies, waits for them, and re-layouts  7.94 us
    all_to_all x1, starting transfers between devices, local(): lax.all_to_all(packed, 'req', split_axis=0, concat_axis=0, tiled=True)  6 us
    another operation x2, other arithmetic, scatter_features(): jnp.stack([jnp.where(core == 0, block(k, 0), block(k, 1)) for k in range(...  5.44 us
    gather x2, local copies, waits for them, and re-layouts, local(): packed = jnp.take(payload, picked, axis=0)  4.56 us
  transfers between devices with their start and end apart: 12, of which 9 were waited for; matrix products, arithmetic and copies ran while one was open for 12% of the time, Pallas kernels for 0%

profile of v3, /device:TPU:0, one launch (start us, length us, event | category | flops | bytes accessed | tf_op | source)
XLA Modules:
  0.0 219.9 jit_solution(15142087049285046663)
XLA Ops:
  0.6 3.0 %collective-permute-start = (bf16[624,512]{1,0:T(8,128)(2,1)}, bf16[624,512]{1,0:T(8,128)(2,1)}, u32[]{:S(2)}, u32[]{:S(2)}) collective-permute-start(bf16[624,512]{1,0:T(8,128)(2,1)} %param.15), channel_id=1, source_target_pairs={{0,2},{2,0},{1,3},{3,1},{4,6},{6,4},{5,7},{7,5},{8,10},{10,8},{9,1... | collective-permute-start | bytes 1916936 | tf_op jit(solution)/shard_map/ppermute | solution.py:41
  8.0 4.3 %all-to-all-start = ((bf16[2,4,13,16,256]{4,3,2,0,1:T(8,128)(2,1)}), bf16[2,4,13,16,256]{4,3,2,0,1:T(8,128)(2,1)}, u32[]{:S(2)}, u32[]{:S(2)}) async-start(bf16[2,4,13,16,256]{4,3,2,0,1:T(8,128)(2,1)} %copy.50), calls=%async_computation | async-start | bytes 1703936 | tf_op jit(solution)/shard_map/all_to_all | solution.py:116
  12.4 6.8 %collective-permute-done = bf16[624,512]{1,0:T(8,128)(2,1)} collective-permute-done((bf16[624,512]{1,0:T(8,128)(2,1)}, bf16[624,512]{1,0:T(8,128)(2,1)}, u32[]{:S(2)}, u32[]{:S(2)}) %collective-permute-start) | collective-permute-done | bytes 639008 | tf_op jit(solution)/shard_map/ppermute | solution.py:41
  19.2 1.9 maximum_select_fusion
  21.4 2.0 multiply_cosine_fusion
  23.4 4.1 %all-to-all-done = bf16[2,4,13,16,256]{4,3,2,0,1:T(8,128)(2,1)} async-done(((bf16[2,4,13,16,256]{4,3,2,0,1:T(8,128)(2,1)}), bf16[2,4,13,16,256]{4,3,2,0,1:T(8,128)(2,1)}, u32[]{:S(2)}, u32[]{:S(2)}) %all-to-all-start) | async-done | bytes 852000 | tf_op jit(solution)/shard_map/all_to_all | solution.py:116
  32.1 2.0 fusion
  36.5 2.6 %fusion.54 = f32[624,512]{1,0:T(8,128)} fusion(bf16[624,2048]{1,0:T(8,128)(2,1)S(1)} %fusion.2, bf16[2048,512]{1,0:T(8,128)(2,1)S(1)} %copy-done.19), kind=kOutput, calls=%fused_computation.144 | convolution fusion | flops 1308622848 | bytes 5931008 | tf_op jit(solution)/shard_map/dot_general | solution.py:161
  39.1 2.1 reshape.325
  42.9 2.2 fusion.53
  45.1 1.6 fusion.30
  50.8 1.5 fusion.55
  53.4 4.8 %collective-permute-done.2 = f32[2,624,512]{2,1,0:T(8,128)S(1)} collective-permute-done((f32[2,624,512]{2,1,0:T(8,128)S(1)}, f32[2,624,512]{2,1,0:T(8,128)S(1)}, u32[]{:S(2)}, u32[]{:S(2)}) %collective-permute-start.2) | collective-permute-done | bytes 2555936 | tf_op jit(solution)/shard_map/ppermute | solution.py:41
  59.1 1.8 collective-permute-start.3
  61.2 28.1 %collective-permute-done.3 = f32[624,512]{1,0:T(8,128)S(1)} collective-permute-done((f32[624,512]{1,0:T(8,128)S(1)}, f32[624,512]{1,0:T(8,128)S(1)}, u32[]{:S(2)}, u32[]{:S(2)}) %collective-permute-start.3) | collective-permute-done | bytes 1277984 | tf_op jit(solution)/shard_map/ppermute | solution.py:41
  90.9 1.7 collective-permute-start.5
  95.5 1.7 collective-permute-start.6
  98.5 12.6 %collective-permute-done.6 = bf16[624,512]{1,0:T(8,128)(2,1)} collective-permute-done((bf16[624,512]{1,0:T(8,128)(2,1)}, bf16[624,512]{1,0:T(8,128)(2,1)}, u32[]{:S(2)}, u32[]{:S(2)}) %collective-permute-start.6) | collective-permute-done | bytes 639008 | tf_op jit(solution)/shard_map/ppermute | solution.py:41
  111.1 2.6 %maximum_select_fusion.1 = bf16[2,624,512]{2,1,0:T(8,128)(2,1)} fusion(bf16[1,624,512]{2,1,0:T(8,128)(2,1)} %bitcast.30, bf16[1,624,512]{2,1,0:T(8,128)(2,1)S(1)} %fusion.67, pred[]{:T(512)S(6)} %eq.26), kind=kLoop, calls=%fused_computation.20 | loop fusion | flops 1916928 | bytes 2555905 | tf_op jit(solution)/shard_map/jit(_where)/select_n | solution.py:48
  113.8 2.2 %gather_fusion = bf16[16,33024]{1,0:T(8,128)(2,1)} fusion(bf16[13,33024]{1,0:T(8,128)(2,1)S(1)} %fusion.11, s32[1024]{0:T(1024)S(1)} %pad_clamp_fusion.1), kind=kCustom, calls=%fused_computation | custom fusion | bytes 2113600 | tf_op jit(solution)/shard_map/jit(_take)/gather | solution.py:138
  116.0 2.3 %gather.13 = bf16[8,2,33024]{2,1,0:T(2,128)(2,1)} reshape(bf16[16,33024]{1,0:T(8,128)(2,1)} %gather_fusion) | data formatting | bytes 2113536 | tf_op jit(solution)/shard_map/jit(_take)/gather | solution.py:138
  118.3 2.0 select_bitcast_fusion.13
  121.3 4.3 %fusion.28 = f32[624,1024]{1,0:T(8,128)} fusion(bf16[2048,1024]{1,0:T(8,128)(2,1)S(1)} %copy-done.18, bf16[624,512]{1,0:T(8,128)(2,1)S(1)} %get-tuple-element.15, bf16[624,512]{1,0:T(8,128)(2,1)S(1)} %get-tuple-element.16, bf16[624,512]{1,0:T(8,128)(2,1)S(1)} %get-tuple-element.14, bf16[624,512]{1,0:T(8,128)(2,1)S(1)} %get-tuple-element.13), kind=kOutput, calls=%fused_computation.81 | convolution fusion | flops 2627469312 | bytes 9306112 | tf_op jit(solution)/shard_map/dot_general | solution.py:199
  125.6 12.2 %fusion.19 = f32[624,2048]{1,0:T(8,128)} fusion(bf16[1024,2048]{1,0:T(8,128)(2,1)} %param.27, f32[624,1024]{1,0:T(8,128)} %fusion.28, bf16[2048,1024]{1,0:T(8,128)(2,1)} %param.26, bf16[624,512]{1,0:T(8,128)(2,1)S(1)} %get-tuple-element.15, bf16[624,512]{1,0:T(8,128)(2,1)} %copy-done.12, bf16[624,512]{1,0:T(8,128)(2,1)S(1)} %get-tuple-element.14, ...), kind=kOutput, calls=%fused_computation.56 | convolution fusion | flops 5248548864 | bytes 18612224 | tf_op jit(solution)/shard_map/dot_general | solution.py:60
  137.8 4.8 %select_bitcast_fusion.4 = (f32[1,624,512]{2,1,0:T(8,128)}, f32[1,624,512]{2,1,0:T(8,128)}, f32[1,624,512]{2,1,0:T(8,128)S(1)}, f32[1,624,512]{2,1,0:T(8,128)S(1)}) fusion(f32[624,2048]{1,0:T(8,128)} %fusion.19, pred[]{:T(512)S(6)} %eq.27), kind=kLoop, calls=%fused_computation.31 | loop fusion | flops 1277952 | bytes 10223617 | tf_op jit(solution)/shard_map/stack | solution.py:67
  142.5 1.8 pad_maximum_fusion.3
  144.8 2.2 %broadcast_select_fusion.1 = bf16[8,2,33024]{2,1,0:T(2,128)(2,1)} fusion(pred[8,2]{1,0:T(8,128)(4,1)S(1)} %broadcast_in_dim.125, bf16[8,2,33024]{2,1,0:T(2,128)(2,1)S(1)} %copy-done.6, pred[8,2]{1,0:T(8,128)(4,1)S(1)} %compare_and_fusion), kind=kLoop, calls=%fused_computation.17 | loop fusion | flops 1056768 | bytes 2113568 | tf_op jit(solution)/shard_map/jit(_where)/select_n | solution.py:139
  147.1 6.0 %all-to-all-start.1 = ((bf16[8,2,33024]{2,1,0:T(2,128)(2,1)}), bf16[8,2,33024]{2,1,0:T(2,128)(2,1)S(1)}, u32[]{:S(2)}, u32[]{:S(2)}) async-start(bf16[8,2,33024]{2,1,0:T(2,128)(2,1)} %broadcast_select_fusion.1), calls=%async_computation.1 | async-start | bytes 2113536 | tf_op jit(solution)/shard_map/all_to_all | solution.py:141
  153.2 25.9 %all-to-all-done.1 = bf16[8,2,33024]{2,1,0:T(2,128)(2,1)S(1)} async-done(((bf16[8,2,33024]{2,1,0:T(2,128)(2,1)}), bf16[8,2,33024]{2,1,0:T(2,128)(2,1)S(1)}, u32[]{:S(2)}, u32[]{:S(2)}) %all-to-all-start.1) | async-done | bytes 1056800 | tf_op jit(solution)/shard_map/all_to_all | solution.py:141
  182.5 3.1 %maximum_add_fusion.1 = f32[2,624,512]{2,1,0:T(8,128)S(1)} fusion(f32[2,624,512]{2,1,0:T(8,128)} %collective-permute-done.8, f32[1,624,512]{2,1,0:T(8,128)} %get-tuple-element.6, f32[1,624,512]{2,1,0:T(8,128)} %get-tuple-element.5), kind=kLoop, calls=%fused_computation.11 | loop fusion | flops 1277952 | bytes 7667712 | tf_op jit(solution)/shard_map/add | solution.py:69
  192.8 24.7 %collective-permute-done.9 = f32[624,512]{1,0:T(8,128)} collective-permute-done((f32[624,512]{1,0:T(8,128)}, f32[624,512]{1,0:T(8,128)}, u32[]{:S(2)}, u32[]{:S(2)}) %collective-permute-start.9) | collective-permute-done | bytes 1277984 | tf_op jit(solution)/shard_map/ppermute | solution.py:41
  217.5 2.4 %fusion.6 = bf16[624,512]{1,0:T(8,128)(2,1)} fusion(f32[624,512]{1,0:T(8,128)S(1)} %get-tuple-element.4, f32[624,512]{1,0:T(8,128)} %collective-permute-done.9, f32[2,624,512]{2,1,0:T(8,128)S(1)} %copy-done.3, pred[624]{0:T(1024)(128)(4,1)S(1)} %lt.105, pred[]{:T(512)S(6)} %eq.26), kind=kLoop, calls=%fused_computation.24 | loop fusion | flops 1597440 | bytes 5751409 | tf_op jit(solution)/shard_map/convert_element_type | solution.py:206
  (124 shorter events, 37.4 us)
Async XLA Ops:
  0.6 50.2 %copy-start = (bf16[512,2048]{1,0:T(8,128)(2,1)S(1)}, bf16[512,2048]{1,0:T(8,128)(2,1)}, u32[]{:S(2)}) copy-start(bf16[512,2048]{1,0:T(8,128)(2,1)} %param.23) | copy-start | bytes 6291460
  0.6 18.6 %collective-permute-start = (bf16[624,512]{1,0:T(8,128)(2,1)}, bf16[624,512]{1,0:T(8,128)(2,1)}, u32[]{:S(2)}, u32[]{:S(2)}) collective-permute-start(bf16[624,512]{1,0:T(8,128)(2,1)} %param.15), channel_id=1, source_target_pairs={{0,2},{2,0},{1,3},{3,1},{4,6},{6,4},{5,7},{7,5},{8,10},{10,8},{9,1... | collective-permute-start | bytes 1916936 | tf_op jit(solution)/shard_map/ppermute | solution.py:41
  6.9 5.4 %copy-start.21 = (s32[13]{0:T(128)S(1)}, s32[13]{0:T(128)}, u32[]{:S(2)}) copy-start(s32[13]{0:T(128)} %param.17) | copy-start | bytes 160
  8.0 13.3 %copy-start.16 = (s32[13]{0:T(128)S(1)}, s32[13]{0:T(128)}, u32[]{:S(2)}) copy-start(s32[13]{0:T(128)} %param.16) | copy-start | bytes 160
  8.0 19.5 %all-to-all-start = ((bf16[2,4,13,16,256]{4,3,2,0,1:T(8,128)(2,1)}), bf16[2,4,13,16,256]{4,3,2,0,1:T(8,128)(2,1)}, u32[]{:S(2)}, u32[]{:S(2)}) async-start(bf16[2,4,13,16,256]{4,3,2,0,1:T(8,128)(2,1)} %copy.50), calls=%async_computation | async-start | bytes 1703936 | tf_op jit(solution)/shard_map/all_to_all | solution.py:116
  21.1 9.6 %collective-permute-start.1 = (bf16[2,624,512]{2,1,0:T(8,128)(2,1)S(1)}, bf16[2,624,512]{2,1,0:T(8,128)(2,1)}, u32[]{:S(2)}, u32[]{:S(2)}) collective-permute-start(bf16[2,624,512]{2,1,0:T(8,128)(2,1)S(1)} %maximum_select_fusion), channel_id=1, source_target_pairs={{0,1},{1,0},{2,3},{3,2},{4,5},{5,4},{6,7},{7,6},{8,9},{9,8},{10,11... | collective-permute-start | bytes 3833864 | tf_op jit(solution)/shard_map/ppermute | solution.py:41
  32.1 2.1 copy-start.15
  34.2 2.4 %copy-start.19 = (bf16[2048,512]{1,0:T(8,128)(2,1)S(1)}, bf16[2048,512]{1,0:T(8,128)(2,1)}, u32[]{:S(2)}) copy-start(bf16[2048,512]{1,0:T(8,128)(2,1)} %param.20) | copy-start | bytes 6291460
  35.1 1.5 copy-start.8
  41.2 1.7 copy-start.9
  42.9 3.7 %copy-start.20 = (bf16[2048,256]{1,0:T(8,128)(2,1)S(1)}, bf16[2048,256]{1,0:T(8,128)(2,1)}, u32[]{:S(2)}) copy-start(bf16[2048,256]{1,0:T(8,128)(2,1)} %param.22) | copy-start | bytes 3145732
  46.7 1.0 copy-start.10
  46.7 1.1 copy-start.11
  47.6 1.1 copy-start.14
  48.6 1.0 copy-start.13
  53.3 4.9 %collective-permute-start.2 = (f32[2,624,512]{2,1,0:T(8,128)S(1)}, f32[2,624,512]{2,1,0:T(8,128)S(1)}, u32[]{:S(2)}, u32[]{:S(2)}) collective-permute-start(f32[2,624,512]{2,1,0:T(8,128)S(1)} %pad_maximum_fusion.1), channel_id=1, source_target_pairs={{0,1},{1,0},{2,3},{3,2},{4,5},{5,4},{6,7},{7,6},{8,9},{9,8},{10,11... | collective-permute-start | bytes 7667720 | tf_op jit(solution)/shard_map/ppermute | solution.py:41
  58.8 2.1 copy-start.17
  58.8 30.5 %copy-start.7 = (bf16[624,512]{1,0:T(8,128)(2,1)S(1)}, bf16[624,512]{1,0:T(8,128)(2,1)}, u32[]{:S(2)}) copy-start(bf16[624,512]{1,0:T(8,128)(2,1)} %param.15) | copy-start | bytes 1916932
  59.1 30.2 %collective-permute-start.3 = (f32[624,512]{1,0:T(8,128)S(1)}, f32[624,512]{1,0:T(8,128)S(1)}, u32[]{:S(2)}, u32[]{:S(2)}) collective-permute-start(f32[624,512]{1,0:T(8,128)S(1)} %select_bitcast_fusion.5), channel_id=1, source_target_pairs={{0,2},{2,0},{1,3},{3,1},{4,6},{6,4},{5,7},{7,5},{8,10},{10,8},{9,1... | collective-permute-start | bytes 3833864 | tf_op jit(solution)/shard_map/ppermute | solution.py:41
  89.6 7.9 %copy-start.5 = (bf16[2,4,13,16,256]{4,3,1,2,0:T(8,128)(2,1)S(1)}, bf16[2,4,13,16,256]{4,3,1,2,0:T(8,128)(2,1)}, u32[]{:S(2)}) copy-start(bf16[2,4,13,16,256]{4,3,1,2,0:T(8,128)(2,1)} %copy-done.4) | copy-start | bytes 2555908
  89.6 1.2 collective-permute-start.4
  90.9 3.6 %collective-permute-start.5 = (f32[624,1]{0,1:T(1,128)S(1)}, f32[624,1]{0,1:T(1,128)S(1)}, u32[]{:S(2)}, u32[]{:S(2)}) collective-permute-start(f32[624,1]{0,1:T(1,128)S(1)} %reshape_add_fusion), channel_id=1, source_target_pairs={{0,2},{2,0},{1,3},{3,1},{4,6},{6,4},{5,7},{7,5},{8,10},{10,8},{9,1... | collective-permute-start | bytes 7496 | tf_op jit(solution)/shard_map/ppermute | solution.py:41
  95.5 15.6 %collective-permute-start.6 = (bf16[624,512]{1,0:T(8,128)(2,1)}, bf16[624,512]{1,0:T(8,128)(2,1)}, u32[]{:S(2)}, u32[]{:S(2)}) collective-permute-start(bf16[624,512]{1,0:T(8,128)(2,1)} %multiply_convert_fusion.1), channel_id=1, source_target_pairs={{0,2},{2,0},{1,3},{3,1},{4,6},{6,4},{5,7},{7,5},{8,10},{10,8},{9,1... | collective-permute-start | bytes 1916936 | tf_op jit(solution)/shard_map/ppermute | solution.py:41
  113.7 4.7 %collective-permute-start.7 = (bf16[2,624,512]{2,1,0:T(8,128)(2,1)}, bf16[2,624,512]{2,1,0:T(8,128)(2,1)}, u32[]{:S(2)}, u32[]{:S(2)}) collective-permute-start(bf16[2,624,512]{2,1,0:T(8,128)(2,1)} %maximum_select_fusion.1), channel_id=1, source_target_pairs={{0,1},{1,0},{2,3},{3,2},{4,5},{5,4},{6,7},{7,6},{8,9},{9,8},{10,11... | collective-permute-start | bytes 3833864 | tf_op jit(solution)/shard_map/ppermute | solution.py:41
  118.3 3.0 %copy-start.18 = (bf16[2048,1024]{1,0:T(8,128)(2,1)S(1)}, bf16[2048,1024]{1,0:T(8,128)(2,1)}, u32[]{:S(2)}) copy-start(bf16[2048,1024]{1,0:T(8,128)(2,1)} %param.25) | copy-start | bytes 12582916
  142.5 2.3 %copy-start.6 = (bf16[8,2,33024]{2,1,0:T(2,128)(2,1)S(1)}, bf16[8,2,33024]{2,1,0:T(2,128)(2,1)}, u32[]{:S(2)}) copy-start(bf16[8,2,33024]{2,1,0:T(2,128)(2,1)} %gather.13) | copy-start | bytes 3170308
  144.3 38.1 %collective-permute-start.8 = (f32[2,624,512]{2,1,0:T(8,128)}, f32[2,624,512]{2,1,0:T(8,128)}, u32[]{:S(2)}, u32[]{:S(2)}) collective-permute-start(f32[2,624,512]{2,1,0:T(8,128)} %pad_maximum_fusion.3), channel_id=1, source_target_pairs={{0,1},{1,0},{2,3},{3,2},{4,5},{5,4},{6,7},{7,6},{8,9},{9,8},{10,11... | collective-permute-start | bytes 7667720 | tf_op jit(solution)/shard_map/ppermute | solution.py:41
  147.1 32.1 %all-to-all-start.1 = ((bf16[8,2,33024]{2,1,0:T(2,128)(2,1)}), bf16[8,2,33024]{2,1,0:T(2,128)(2,1)S(1)}, u32[]{:S(2)}, u32[]{:S(2)}) async-start(bf16[8,2,33024]{2,1,0:T(2,128)(2,1)} %broadcast_select_fusion.1), calls=%async_computation.1 | async-start | bytes 2113536 | tf_op jit(solution)/shard_map/all_to_all | solution.py:141
  185.5 1.5 copy-start.2
  188.3 29.2 %collective-permute-start.9 = (f32[624,512]{1,0:T(8,128)}, f32[624,512]{1,0:T(8,128)}, u32[]{:S(2)}, u32[]{:S(2)}) collective-permute-start(f32[624,512]{1,0:T(8,128)} %select_bitcast_fusion), channel_id=1, source_target_pairs={{0,2},{2,0},{1,3},{3,1},{4,6},{6,4},{5,7},{7,5},{8,10},{10,8},{9,1... | collective-permute-start | bytes 3833864 | tf_op jit(solution)/shard_map/ppermute | solution.py:41
  191.6 25.9 %copy-start.3 = (f32[2,624,512]{2,1,0:T(8,128)S(1)}, f32[2,624,512]{2,1,0:T(8,128)}, u32[]{:S(2)}) copy-start(f32[2,624,512]{2,1,0:T(8,128)} %copy-done.2) | copy-start | bytes 7667716
  191.8 28.1 %copy-start.1 = (bf16[512,2048]{1,0:T(8,128)(2,1)S(1)}, bf16[512,2048]{1,0:T(8,128)(2,1)}, u32[]{:S(2)}) copy-start(bf16[512,2048]{1,0:T(8,128)(2,1)} %param.23) | copy-start | bytes 6291460
  (2 other events, 1.7 us)

commit v4 on v3

--- a/solution.py
+++ b/solution.py
@@ -138,8 +138,12 @@
     packed = jnp.take(payload, picked, axis=0)
     packed = jnp.where(filled[:, None], packed, -jnp.ones((), packed.dtype))
     packed = packed.reshape(req_count, capacity, payload.shape[1])
-    landed = lax.all_to_all(packed, "req", split_axis=0, concat_axis=0, tiled=True)
-    landed = landed.reshape(req_count * capacity, payload.shape[1])
+    pieces = [lax.dynamic_index_in_dim(packed, req_index, 0, keepdims=False)]
+    for shift in range(1, req_count):
+        outgoing = lax.dynamic_index_in_dim(packed, (req_index + shift) % req_count, 0, keepdims=False)
+        pairs = [(source, (source + shift) % req_count) for source in range(req_count)]
+        pieces.append(lax.ppermute(outgoing, "req", pairs))
+    landed = jnp.stack(pieces).reshape(req_count * capacity, payload.shape[1])
     code = landed[:, 2 * past_size * lanes:2 * past_size * lanes + 2].astype(jnp.int32)
     landed_slots = code[:, 0] * 16 + code[:, 1]
     wanted = req_index * request_list + order_ids

time: 221 us -> 206 us (0.932)
  waiting for transfers between devices: 109 us -> 88.7 us
  local copies, waits for them, and re-layouts: 27.5 us -> 38.2 us
  other arithmetic: 36.7 us -> 29.8 us
    all_to_all x1 -> x0, waiting for transfers between devices: 25.9 us -> none  [local(): lax.all_to_all(packed, 'req', split_axis=0, concat_axis=0, tiled=True)]
    ppermute x0 -> x7, starting transfers between devices: none -> 12.9 us  [local(): pieces.append(lax.ppermute(outgoing, 'req', pairs))]
    unnamed x49 -> x63, local copies, waits for them, and re-layouts: 7.94 us -> 16.1 us
    all_to_all x1 -> x0, starting transfers between devices: 6 us -> none  [local(): lax.all_to_all(packed, 'req', split_axis=0, concat_axis=0, tiled=True)]
    ppermute x10, starting transfers between devices: 10.5 us -> 4.97 us  [swap(): return lax.ppermute(values, axis_name, [(0, 1), (1, 0)])]
    ppermute x10, waiting for transfers between devices: 79.1 us -> 82.6 us  [swap(): return lax.ppermute(values, axis_name, [(0, 1), (1, 0)])]
    select_n x2, other arithmetic: 3.42 us -> 0.35 us  [gather_features(): jnp.where(core == core_block, pair[chip_block], other[chip_block])]
    select_n x2, other arithmetic: 4.44 us -> 2.1 us  [gather_features(): jnp.where(chip == 0, jnp.stack([share, partner]), jnp.stack([partner, sha...]
  transfers between devices with their start and end apart: 12 -> 18, of which waited for: 9 -> 8; matrix products, arithmetic and copies ran while one was open for 12% -> 36% of each run, Pallas kernels for 0% -> 0%
where the time goes in v4:
time: 206 us; the launch traced here: 205 us
  waiting for transfers between devices  88.7 us (43%)
  local copies, waits for them, and re-layouts  38.2 us (19%)
  other arithmetic  29.8 us (14%)
  matrix products  24.9 us (12%)
  starting transfers between devices  22.3 us (11%)
    ppermute x10, waiting for transfers between devices, swap(): return lax.ppermute(values, axis_name, [(0, 1), (1, 0)])  82.6 us
    unnamed x63, local copies, waits for them, and re-layouts  16.1 us
    dot_general x2, matrix products, scatter_features(): product = jnp.dot(matrix_in, weight, preferred_element_type=jnp.float32)  14.1 us
    ppermute x7, starting transfers between devices, local(): pieces.append(lax.ppermute(outgoing, 'req', pairs))  12.9 us
    all_to_all x1, waiting for transfers between devices, local(): lax.all_to_all(stacked, ('kvy', 'core'), split_axis=1, concat_axis=1, til...  6.12 us
    another operation x2, other arithmetic, scatter_features(): jnp.stack([jnp.where(core == 0, block(k, 0), block(k, 1)) for k in range(...  5.43 us
    ppermute x10, starting transfers between devices, swap(): return lax.ppermute(values, axis_name, [(0, 1), (1, 0)])  4.97 us
    all_to_all x1, starting transfers between devices, local(): lax.all_to_all(stacked, ('kvy', 'core'), split_axis=1, concat_axis=1, til...  4.37 us
  transfers between devices with their start and end apart: 18, of which 8 were waited for; matrix products, arithmetic and copies ran while one was open for 36% of the time, Pallas kernels for 0%

profile of v4, /device:TPU:0, one launch (start us, length us, event | category | flops | bytes accessed | tf_op | source)
XLA Modules:
  0.0 205.1 jit_solution(12378151175570591222)
XLA Ops:
  5.1 4.4 %all-to-all-start = ((bf16[2,4,13,16,256]{4,3,2,0,1:T(8,128)(2,1)}), bf16[2,4,13,16,256]{4,3,2,0,1:T(8,128)(2,1)S(1)}, u32[]{:S(2)}, u32[]{:S(2)}) async-start(bf16[2,4,13,16,256]{4,3,2,0,1:T(8,128)(2,1)} %copy.50), calls=%async_computation | async-start | bytes 1703936 | tf_op jit(solution)/shard_map/all_to_all | solution.py:116
  9.5 2.3 %collective-permute-start = (bf16[624,512]{1,0:T(8,128)(2,1)}, bf16[624,512]{1,0:T(8,128)(2,1)}, u32[]{:S(2)}, u32[]{:S(2)}) collective-permute-start(bf16[624,512]{1,0:T(8,128)(2,1)} %param.15), channel_id=1, source_target_pairs={{0,2},{2,0},{1,3},{3,1},{4,6},{6,4},{5,7},{7,5},{8,10},{10,8},{9,1... | collective-permute-start | bytes 1916936 | tf_op jit(solution)/shard_map/ppermute | solution.py:41
  14.4 2.0 multiply_cosine_fusion
  16.4 6.1 %all-to-all-done = bf16[2,4,13,16,256]{4,3,2,0,1:T(8,128)(2,1)S(1)} async-done(((bf16[2,4,13,16,256]{4,3,2,0,1:T(8,128)(2,1)}), bf16[2,4,13,16,256]{4,3,2,0,1:T(8,128)(2,1)S(1)}, u32[]{:S(2)}, u32[]{:S(2)}) %all-to-all-start) | async-done | bytes 852000 | tf_op jit(solution)/shard_map/all_to_all | solution.py:116
  24.2 2.3 %gather_fusion = bf16[16,33024]{1,0:T(8,128)(2,1)} fusion(bf16[13,33024]{1,0:T(8,128)(2,1)S(1)} %fusion.11, s32[1024]{0:T(1024)S(1)} %pad_clamp_fusion.1), kind=kCustom, calls=%fused_computation | custom fusion | bytes 2113600 | tf_op jit(solution)/shard_map/jit(_take)/gather | solution.py:138
  28.0 7.7 %collective-permute-done = bf16[624,512]{1,0:T(8,128)(2,1)} collective-permute-done((bf16[624,512]{1,0:T(8,128)(2,1)}, bf16[624,512]{1,0:T(8,128)(2,1)}, u32[]{:S(2)}, u32[]{:S(2)}) %collective-permute-start) | collective-permute-done | bytes 639008 | tf_op jit(solution)/shard_map/ppermute | solution.py:41
  35.6 1.9 maximum_select_fusion
  40.3 2.2 %collective-permute-start.10 = (bf16[2,33024]{1,0:T(2,128)(2,1)}, bf16[2,33024]{1,0:T(2,128)(2,1)}, u32[]{:S(2)}, u32[]{:S(2)}) collective-permute-start(bf16[2,33024]{1,0:T(2,128)(2,1)} %get-tuple-element.31), channel_id=1, source_target_pairs={{0,4},{4,8},{8,12},{12,16},{16,20},{20,24},{24,28},{28,0},{1,5},{5... | collective-permute-start | bytes 396296 | tf_op jit(solution)/shard_map/ppermute | solution.py:145
  44.1 2.6 %collective-permute-start.12 = (bf16[2,33024]{1,0:T(2,128)(2,1)}, bf16[2,33024]{1,0:T(2,128)(2,1)}, u32[]{:S(2)}, u32[]{:S(2)}) collective-permute-start(bf16[2,33024]{1,0:T(2,128)(2,1)} %get-tuple-element.29), channel_id=1, source_target_pairs={{0,12},{4,16},{8,20},{12,24},{16,28},{20,0},{24,4},{28,8},{1,13},{... | collective-permute-start | bytes 396296 | tf_op jit(solution)/shard_map/ppermute | solution.py:145
  48.9 2.6 %collective-permute-start.14 = (bf16[2,33024]{1,0:T(2,128)(2,1)}, bf16[2,33024]{1,0:T(2,128)(2,1)}, u32[]{:S(2)}, u32[]{:S(2)}) collective-permute-start(bf16[2,33024]{1,0:T(2,128)(2,1)} %get-tuple-element.27), channel_id=1, source_target_pairs={{0,20},{4,24},{8,28},{12,0},{16,4},{20,8},{24,12},{28,16},{1,21},{... | collective-permute-start | bytes 396296 | tf_op jit(solution)/shard_map/ppermute | solution.py:145
  51.7 2.0 fusion
  56.1 2.6 %fusion.54 = f32[624,512]{1,0:T(8,128)} fusion(bf16[624,2048]{1,0:T(8,128)(2,1)S(1)} %fusion.2, bf16[2048,512]{1,0:T(8,128)(2,1)S(1)} %copy-done.23), kind=kOutput, calls=%fused_computation.159 | convolution fusion | flops 1308622848 | bytes 5931008 | tf_op jit(solution)/shard_map/dot_general | solution.py:165
  58.7 2.1 %reshape.325 = f32[13,48,2,256]{3,2,1,0:T(2,128)S(1)} reshape(f32[624,512]{1,0:T(8,128)} %fusion.54) | data formatting | bytes 2555904 | tf_op jit(solution)/shard_map/reshape | solution.py:167
  62.5 2.1 %fusion.53 = f32[624,256]{1,0:T(8,128)S(1)} fusion(bf16[624,2048]{1,0:T(8,128)(2,1)S(1)} %copy-done.9, bf16[2048,256]{1,0:T(8,128)(2,1)} %param.21), kind=kOutput, calls=%fused_computation.158 | convolution fusion | flops 654311424 | bytes 4243456 | tf_op jit(solution)/shard_map/dot_general | solution.py:169
  72.9 1.7 bitcast_dynamic-update-slice_fusion.6
  74.6 3.1 %collective-permute-done.2 = f32[2,624,512]{2,1,0:T(8,128)S(1)} collective-permute-done((f32[2,624,512]{2,1,0:T(8,128)S(1)}, f32[2,624,512]{2,1,0:T(8,128)S(1)}, u32[]{:S(2)}, u32[]{:S(2)}) %collective-permute-start.2) | collective-permute-done | bytes 2555936 | tf_op jit(solution)/shard_map/ppermute | solution.py:41
  80.4 1.6 bitcast_dynamic-update-slice_fusion.5
  82.1 27.8 %collective-permute-done.3 = f32[624,512]{1,0:T(8,128)S(1)} collective-permute-done((f32[624,512]{1,0:T(8,128)S(1)}, f32[624,512]{1,0:T(8,128)S(1)}, u32[]{:S(2)}, u32[]{:S(2)}) %collective-permute-start.3) | collective-permute-done | bytes 1277984 | tf_op jit(solution)/shard_map/ppermute | solution.py:41
  111.8 1.7 bitcast_dynamic-update-slice_fusion.4
  113.9 1.6 bitcast_dynamic-update-slice_fusion.3
  117.7 1.7 bitcast_dynamic-update-slice_fusion.2
  119.6 13.4 %collective-permute-done.6 = bf16[624,512]{1,0:T(8,128)(2,1)S(1)} collective-permute-done((bf16[624,512]{1,0:T(8,128)(2,1)S(1)}, bf16[624,512]{1,0:T(8,128)(2,1)S(1)}, u32[]{:S(2)}, u32[]{:S(2)}) %collective-permute-start.6) | collective-permute-done | bytes 639008 | tf_op jit(solution)/shard_map/ppermute | solution.py:41
  134.0 2.2 %collective-permute-done.7 = bf16[2,624,512]{2,1,0:T(8,128)(2,1)S(1)} collective-permute-done((bf16[2,624,512]{2,1,0:T(8,128)(2,1)S(1)}, bf16[2,624,512]{2,1,0:T(8,128)(2,1)S(1)}, u32[]{:S(2)}, u32[]{:S(2)}) %collective-permute-start.7) | collective-permute-done | bytes 1277984 | tf_op jit(solution)/shard_map/ppermute | solution.py:41
  137.7 4.2 %fusion.28 = f32[624,1024]{1,0:T(8,128)} fusion(bf16[2048,1024]{1,0:T(8,128)(2,1)S(1)} %copy-done.22, bf16[624,512]{1,0:T(8,128)(2,1)S(1)} %get-tuple-element.15, bf16[624,512]{1,0:T(8,128)(2,1)S(1)} %get-tuple-element.16, bf16[624,512]{1,0:T(8,128)(2,1)S(1)} %get-tuple-element.14, bf16[624,512]{1,0:T(8,128)(2,1)S(1)} %get-tuple-element.13), kind=kOutput, calls=%fused_computation.81 | convolution fusion | flops 2627469312 | bytes 9306112 | tf_op jit(solution)/shard_map/dot_general | solution.py:203
  142.0 12.6 %fusion.19 = f32[624,2048]{1,0:T(8,128)} fusion(bf16[1024,2048]{1,0:T(8,128)(2,1)} %param.27, f32[624,1024]{1,0:T(8,128)} %fusion.28, bf16[2048,1024]{1,0:T(8,128)(2,1)} %param.26, bf16[624,512]{1,0:T(8,128)(2,1)} %copy-done.13, bf16[624,512]{1,0:T(8,128)(2,1)} %copy-done.14, bf16[624,512]{1,0:T(8,128)(2,1)} %copy-done.12, ...), kind=kOutput, calls=%fused_computation.56 | convolution fusion | flops 5248548864 | bytes 18612224 | tf_op jit(solution)/shard_map/dot_general | solution.py:60
  154.6 4.7 %select_bitcast_fusion.4 = (f32[1,624,512]{2,1,0:T(8,128)}, f32[1,624,512]{2,1,0:T(8,128)}, f32[1,624,512]{2,1,0:T(8,128)S(1)}, f32[1,624,512]{2,1,0:T(8,128)S(1)}) fusion(f32[624,2048]{1,0:T(8,128)} %fusion.19, pred[]{:T(512)S(6)} %eq.35), kind=kLoop, calls=%fused_computation.31 | loop fusion | flops 1277952 | bytes 10223617 | tf_op jit(solution)/shard_map/stack | solution.py:67
  159.3 1.8 pad_maximum_fusion.3
  161.2 1.7 bitcast_dynamic-update-slice_fusion
  162.9 2.3 %reshape.330 = bf16[16,33024]{1,0:T(8,128)(2,1)} reshape(bf16[8,2,33024]{2,1,0:T(2,128)(2,1)} %bitcast_dynamic-update-slice_fusion) | data formatting | bytes 2113536 | tf_op jit(solution)/shard_map/reshape | solution.py:146
  167.3 2.7 %maximum_add_fusion.1 = f32[2,624,512]{2,1,0:T(8,128)S(1)} fusion(f32[2,624,512]{2,1,0:T(8,128)} %collective-permute-done.8, f32[1,624,512]{2,1,0:T(8,128)} %get-tuple-element.6, f32[1,624,512]{2,1,0:T(8,128)S(1)} %copy-done.6), kind=kLoop, calls=%fused_computation.11 | loop fusion | flops 1277952 | bytes 7667712 | tf_op jit(solution)/shard_map/add | solution.py:69
  175.8 26.7 %collective-permute-done.9 = f32[624,512]{1,0:T(8,128)} collective-permute-done((f32[624,512]{1,0:T(8,128)}, f32[624,512]{1,0:T(8,128)}, u32[]{:S(2)}, u32[]{:S(2)}) %collective-permute-start.9) | collective-permute-done | bytes 1277984 | tf_op jit(solution)/shard_map/ppermute | solution.py:41
  202.5 2.6 %fusion.6 = bf16[624,512]{1,0:T(8,128)(2,1)} fusion(f32[624,512]{1,0:T(8,128)S(1)} %get-tuple-element.4, f32[624,512]{1,0:T(8,128)} %collective-permute-done.9, f32[2,624,512]{2,1,0:T(8,128)S(1)} %copy-done.3, pred[624]{0:T(1024)(128)(4,1)S(1)} %lt.160, pred[]{:T(512)S(6)} %eq.34), kind=kLoop, calls=%fused_computation.24 | loop fusion | flops 1597440 | bytes 5751409 | tf_op jit(solution)/shard_map/convert_element_type | solution.py:210
  (152 shorter events, 46.9 us)
Async XLA Ops:
  0.6 69.7 %copy-start = (bf16[512,2048]{1,0:T(8,128)(2,1)S(1)}, bf16[512,2048]{1,0:T(8,128)(2,1)}, u32[]{:S(2)}) copy-start(bf16[512,2048]{1,0:T(8,128)(2,1)} %param.23) | copy-start | bytes 6291460
  5.1 6.7 %copy-start.21 = (s32[13]{0:T(128)S(1)}, s32[13]{0:T(128)}, u32[]{:S(2)}) copy-start(s32[13]{0:T(128)} %param.18) | copy-start | bytes 160
  5.1 7.5 %copy-start.25 = (s32[13]{0:T(128)S(1)}, s32[13]{0:T(128)}, u32[]{:S(2)}) copy-start(s32[13]{0:T(128)} %param.17) | copy-start | bytes 160
  5.1 7.6 %copy-start.20 = (s32[13]{0:T(128)S(1)}, s32[13]{0:T(128)}, u32[]{:S(2)}) copy-start(s32[13]{0:T(128)} %param.16) | copy-start | bytes 160
  5.1 17.4 %all-to-all-start = ((bf16[2,4,13,16,256]{4,3,2,0,1:T(8,128)(2,1)}), bf16[2,4,13,16,256]{4,3,2,0,1:T(8,128)(2,1)S(1)}, u32[]{:S(2)}, u32[]{:S(2)}) async-start(bf16[2,4,13,16,256]{4,3,2,0,1:T(8,128)(2,1)} %copy.50), calls=%async_computation | async-start | bytes 1703936 | tf_op jit(solution)/shard_map/all_to_all | solution.py:116
  9.5 26.2 %collective-permute-start = (bf16[624,512]{1,0:T(8,128)(2,1)}, bf16[624,512]{1,0:T(8,128)(2,1)}, u32[]{:S(2)}, u32[]{:S(2)}) collective-permute-start(bf16[624,512]{1,0:T(8,128)(2,1)} %param.15), channel_id=1, source_target_pairs={{0,2},{2,0},{1,3},{3,1},{4,6},{6,4},{5,7},{7,5},{8,10},{10,8},{9,1... | collective-permute-start | bytes 1916936 | tf_op jit(solution)/shard_map/ppermute | solution.py:41
  37.5 11.3 %collective-permute-start.1 = (bf16[2,624,512]{2,1,0:T(8,128)(2,1)S(1)}, bf16[2,624,512]{2,1,0:T(8,128)(2,1)S(1)}, u32[]{:S(2)}, u32[]{:S(2)}) collective-permute-start(bf16[2,624,512]{2,1,0:T(8,128)(2,1)S(1)} %maximum_select_fusion), channel_id=1, source_target_pairs={{0,1},{1,0},{2,3},{3,2},{4,5},{5,4},{6,7},{7,6},{8,9},{9,8},{10,11... | collective-permute-start | bytes 3833864 | tf_op jit(solution)/shard_map/ppermute | solution.py:41
  38.8 9.1 %copy-start.5 = (bf16[2,4,13,16,256]{4,3,1,2,0:T(8,128)(2,1)S(1)}, bf16[2,4,13,16,256]{4,3,1,2,0:T(8,128)(2,1)}, u32[]{:S(2)}) copy-start(bf16[2,4,13,16,256]{4,3,1,2,0:T(8,128)(2,1)} %copy-done.4) | copy-start | bytes 2555908
  40.3 32.5 %collective-permute-start.10 = (bf16[2,33024]{1,0:T(2,128)(2,1)}, bf16[2,33024]{1,0:T(2,128)(2,1)}, u32[]{:S(2)}, u32[]{:S(2)}) collective-permute-start(bf16[2,33024]{1,0:T(2,128)(2,1)} %get-tuple-element.31), channel_id=1, source_target_pairs={{0,4},{4,8},{8,12},{12,16},{16,20},{20,24},{24,28},{28,0},{1,5},{5... | collective-permute-start | bytes 396296 | tf_op jit(solution)/shard_map/ppermute | solution.py:145
  42.5 37.5 %collective-permute-start.11 = (bf16[2,33024]{1,0:T(2,128)(2,1)}, bf16[2,33024]{1,0:T(2,128)(2,1)}, u32[]{:S(2)}, u32[]{:S(2)}) collective-permute-start(bf16[2,33024]{1,0:T(2,128)(2,1)} %get-tuple-element.30), channel_id=1, source_target_pairs={{0,8},{4,12},{8,16},{12,20},{16,24},{20,28},{24,0},{28,4},{1,9},{5... | collective-permute-start | bytes 396296 | tf_op jit(solution)/shard_map/ppermute | solution.py:145
  44.1 67.6 %collective-permute-start.12 = (bf16[2,33024]{1,0:T(2,128)(2,1)}, bf16[2,33024]{1,0:T(2,128)(2,1)}, u32[]{:S(2)}, u32[]{:S(2)}) collective-permute-start(bf16[2,33024]{1,0:T(2,128)(2,1)} %get-tuple-element.29), channel_id=1, source_target_pairs={{0,12},{4,16},{8,20},{12,24},{16,28},{20,0},{24,4},{28,8},{1,13},{... | collective-permute-start | bytes 396296 | tf_op jit(solution)/shard_map/ppermute | solution.py:145
  46.7 67.2 %collective-permute-start.13 = (bf16[2,33024]{1,0:T(2,128)(2,1)}, bf16[2,33024]{1,0:T(2,128)(2,1)}, u32[]{:S(2)}, u32[]{:S(2)}) collective-permute-start(bf16[2,33024]{1,0:T(2,128)(2,1)} %get-tuple-element.28), channel_id=1, source_target_pairs={{0,16},{4,20},{8,24},{12,28},{16,0},{20,4},{24,8},{28,12},{1,17},{... | collective-permute-start | bytes 396296 | tf_op jit(solution)/shard_map/ppermute | solution.py:145
  48.9 68.9 %collective-permute-start.14 = (bf16[2,33024]{1,0:T(2,128)(2,1)}, bf16[2,33024]{1,0:T(2,128)(2,1)}, u32[]{:S(2)}, u32[]{:S(2)}) collective-permute-start(bf16[2,33024]{1,0:T(2,128)(2,1)} %get-tuple-element.27), channel_id=1, source_target_pairs={{0,20},{4,24},{8,28},{12,0},{16,4},{20,8},{24,12},{28,16},{1,21},{... | collective-permute-start | bytes 396296 | tf_op jit(solution)/shard_map/ppermute | solution.py:145
  51.6 2.1 %copy-start.19 = (f32[2048]{0:T(1024)S(1)}, f32[2048]{0:T(1024)}, u32[]{:S(2)}) copy-start(f32[2048]{0:T(1024)} %param.19) | copy-start | bytes 24580
  53.7 2.4 %copy-start.23 = (bf16[2048,512]{1,0:T(8,128)(2,1)S(1)}, bf16[2048,512]{1,0:T(8,128)(2,1)}, u32[]{:S(2)}) copy-start(bf16[2048,512]{1,0:T(8,128)(2,1)} %param.20) | copy-start | bytes 6291460
  62.5 3.6 %copy-start.24 = (bf16[2048,256]{1,0:T(8,128)(2,1)S(1)}, bf16[2048,256]{1,0:T(8,128)(2,1)}, u32[]{:S(2)}) copy-start(bf16[2048,256]{1,0:T(8,128)(2,1)} %param.22) | copy-start | bytes 3145732
  72.6 5.1 %copy-start.17 = (bf16[2,33024]{1,0:T(2,128)(2,1)S(1)}, bf16[2,33024]{1,0:T(2,128)(2,1)}, u32[]{:S(2)}) copy-start(bf16[2,33024]{1,0:T(2,128)(2,1)} %get-tuple-element.26) | copy-start | bytes 396292
  72.8 4.9 %collective-permute-start.2 = (f32[2,624,512]{2,1,0:T(8,128)S(1)}, f32[2,624,512]{2,1,0:T(8,128)S(1)}, u32[]{:S(2)}, u32[]{:S(2)}) collective-permute-start(f32[2,624,512]{2,1,0:T(8,128)S(1)} %pad_maximum_fusion.1), channel_id=1, source_target_pairs={{0,1},{1,0},{2,3},{3,2},{4,5},{5,4},{6,7},{7,6},{8,9},{9,8},{10,11... | collective-permute-start | bytes 7667720 | tf_op jit(solution)/shard_map/ppermute | solution.py:41
  77.7 55.6 %collective-permute-start.15 = (bf16[2,33024]{1,0:T(2,128)(2,1)S(1)}, bf16[2,33024]{1,0:T(2,128)(2,1)S(1)}, u32[]{:S(2)}, u32[]{:S(2)}) collective-permute-start(bf16[2,33024]{1,0:T(2,128)(2,1)S(1)} %copy-done.17), channel_id=1, source_target_pairs={{0,24},{4,28},{8,0},{12,4},{16,8},{20,12},{24,16},{28,20},{1,25},{... | collective-permute-start | bytes 396296 | tf_op jit(solution)/shard_map/ppermute | solution.py:145
  79.7 31.6 %copy-start.7 = (bf16[624,512]{1,0:T(8,128)(2,1)S(1)}, bf16[624,512]{1,0:T(8,128)(2,1)}, u32[]{:S(2)}) copy-start(bf16[624,512]{1,0:T(8,128)(2,1)} %param.15) | copy-start | bytes 1916932
  80.0 29.9 %collective-permute-start.3 = (f32[624,512]{1,0:T(8,128)S(1)}, f32[624,512]{1,0:T(8,128)S(1)}, u32[]{:S(2)}, u32[]{:S(2)}) collective-permute-start(f32[624,512]{1,0:T(8,128)S(1)} %select_bitcast_fusion.5), channel_id=1, source_target_pairs={{0,2},{2,0},{1,3},{3,1},{4,6},{6,4},{5,7},{7,5},{8,10},{10,8},{9,1... | collective-permute-start | bytes 3833864 | tf_op jit(solution)/shard_map/ppermute | solution.py:41
  109.9 51.4 %collective-permute-start.16 = (bf16[2,33024]{1,0:T(2,128)(2,1)S(1)}, bf16[2,33024]{1,0:T(2,128)(2,1)}, u32[]{:S(2)}, u32[]{:S(2)}) collective-permute-start(bf16[2,33024]{1,0:T(2,128)(2,1)S(1)} %get-tuple-element.25), channel_id=1, source_target_pairs={{0,28},{4,0},{8,4},{12,8},{16,12},{20,16},{24,20},{28,24},{1,29},{... | collective-permute-start | bytes 396296 | tf_op jit(solution)/shard_map/ppermute | solution.py:145
  111.7 1.7 collective-permute-start.4
  113.4 3.7 %collective-permute-start.5 = (f32[624,1]{0,1:T(1,128)S(1)}, f32[624,1]{0,1:T(1,128)S(1)}, u32[]{:S(2)}, u32[]{:S(2)}) collective-permute-start(f32[624,1]{0,1:T(1,128)S(1)} %reshape_add_fusion), channel_id=1, source_target_pairs={{0,2},{2,0},{1,3},{3,1},{4,6},{6,4},{5,7},{7,5},{8,10},{10,8},{9,1... | collective-permute-start | bytes 7496 | tf_op jit(solution)/shard_map/ppermute | solution.py:41
  117.3 15.7 %collective-permute-start.6 = (bf16[624,512]{1,0:T(8,128)(2,1)S(1)}, bf16[624,512]{1,0:T(8,128)(2,1)S(1)}, u32[]{:S(2)}, u32[]{:S(2)}) collective-permute-start(bf16[624,512]{1,0:T(8,128)(2,1)S(1)} %multiply_convert_fusion.1), channel_id=1, source_target_pairs={{0,2},{2,0},{1,3},{3,1},{4,6},{6,4},{5,7},{7,5},{8,10},{10,8},{9,1... | collective-permute-start | bytes 1916936 | tf_op jit(solution)/shard_map/ppermute | solution.py:41
  133.2 3.1 %collective-permute-start.7 = (bf16[2,624,512]{2,1,0:T(8,128)(2,1)S(1)}, bf16[2,624,512]{2,1,0:T(8,128)(2,1)S(1)}, u32[]{:S(2)}, u32[]{:S(2)}) collective-permute-start(bf16[2,624,512]{2,1,0:T(8,128)(2,1)S(1)} %maximum_select_fusion.1), channel_id=1, source_target_pairs={{0,1},{1,0},{2,3},{3,2},{4,5},{5,4},{6,7},{7,6},{8,9},{9,8},{10,11... | collective-permute-start | bytes 3833864 | tf_op jit(solution)/shard_map/ppermute | solution.py:41
  134.0 3.7 %copy-start.22 = (bf16[2048,1024]{1,0:T(8,128)(2,1)S(1)}, bf16[2048,1024]{1,0:T(8,128)(2,1)}, u32[]{:S(2)}) copy-start(bf16[2048,1024]{1,0:T(8,128)(2,1)} %param.25) | copy-start | bytes 12582916
  161.1 6.1 %collective-permute-start.8 = (f32[2,624,512]{2,1,0:T(8,128)}, f32[2,624,512]{2,1,0:T(8,128)}, u32[]{:S(2)}, u32[]{:S(2)}) collective-permute-start(f32[2,624,512]{2,1,0:T(8,128)} %pad_maximum_fusion.3), channel_id=1, source_target_pairs={{0,1},{1,0},{2,3},{3,2},{4,5},{5,4},{6,7},{7,6},{8,9},{9,8},{10,11... | collective-permute-start | bytes 7667720 | tf_op jit(solution)/shard_map/ppermute | solution.py:41
  165.2 2.1 %copy-start.6 = (f32[1,624,512]{2,1,0:T(8,128)S(1)}, f32[1,624,512]{2,1,0:T(8,128)}, u32[]{:S(2)}) copy-start(f32[1,624,512]{2,1,0:T(8,128)} %get-tuple-element.5) | copy-start | bytes 3833860
  171.8 30.7 %collective-permute-start.9 = (f32[624,512]{1,0:T(8,128)}, f32[624,512]{1,0:T(8,128)}, u32[]{:S(2)}, u32[]{:S(2)}) collective-permute-start(f32[624,512]{1,0:T(8,128)} %select_bitcast_fusion), channel_id=1, source_target_pairs={{0,2},{2,0},{1,3},{3,1},{4,6},{6,4},{5,7},{7,5},{8,10},{10,8},{9,1... | collective-permute-start | bytes 3833864 | tf_op jit(solution)/shard_map/ppermute | solution.py:41
  174.7 27.9 %copy-start.3 = (f32[2,624,512]{2,1,0:T(8,128)S(1)}, f32[2,624,512]{2,1,0:T(8,128)}, u32[]{:S(2)}) copy-start(f32[2,624,512]{2,1,0:T(8,128)} %copy-done.2) | copy-start | bytes 7667716
  202.5 2.6 %copy-start.1 = (bf16[512,2048]{1,0:T(8,128)(2,1)S(1)}, bf16[512,2048]{1,0:T(8,128)(2,1)}, u32[]{:S(2)}) copy-start(bf16[512,2048]{1,0:T(8,128)(2,1)} %param.23) | copy-start | bytes 6291460
  (12 other events, 14.2 us)

commit v5 on v3

--- a/solution.py
+++ b/solution.py
@@ -54,7 +54,7 @@
     return jnp.concatenate(blocks, axis=1)
 
 
-def scatter_features(matrix_in, weight):
+def scatter_features(matrix_in, weight, link_type=None):
     chip = lax.axis_index("kvy")
     core = lax.axis_index("core")
     product = jnp.dot(matrix_in, weight, preferred_element_type=jnp.float32)
@@ -69,7 +69,9 @@
     chip_sum = keep + swap(give, "core")
     mine = jnp.where(chip == 0, chip_sum[0], chip_sum[1])
     theirs = jnp.where(chip == 0, chip_sum[1], chip_sum[0])
-    return mine + swap(theirs, "kvy")
+    if link_type is not None:
+        theirs = theirs.astype(link_type)
+    return mine + swap(theirs, "kvy").astype(jnp.float32)
 
 
 def row_scale(values, gain_share):
@@ -131,23 +133,22 @@
     picked = jnp.sum(jnp.where(matches, order_ids[None, :], 0), axis=1)
     filled = jnp.any(matches, axis=1)
     lanes = local_kv * HEAD_WIDTH
-    rows_kv = jnp.moveaxis(head_kv, 0, 1).reshape(request_list, 2 * past_size * lanes)
     slot_code = jnp.stack([decode_slot // 16, decode_slot % 16], axis=1).astype(jnp.bfloat16)
-    trailer = jnp.pad(slot_code, ((0, 0), (0, lanes - 2)))
-    payload = jnp.concatenate([rows_kv, trailer], axis=1)
+    trailer = jnp.pad(slot_code, ((0, 0), (0, lanes - 2)))[:, None, :]
+    payload = jnp.concatenate([head_kv[0], head_kv[1], trailer], axis=1)
     packed = jnp.take(payload, picked, axis=0)
-    packed = jnp.where(filled[:, None], packed, -jnp.ones((), packed.dtype))
-    packed = packed.reshape(req_count, capacity, payload.shape[1])
+    packed = jnp.where(filled[:, None, None], packed, -jnp.ones((), packed.dtype))
+    packed = packed.reshape((req_count, capacity) + payload.shape[1:])
     landed = lax.all_to_all(packed, "req", split_axis=0, concat_axis=0, tiled=True)
-    landed = landed.reshape(req_count * capacity, payload.shape[1])
-    code = landed[:, 2 * past_size * lanes:2 * past_size * lanes + 2].astype(jnp.int32)
+    landed = landed.reshape((req_count * capacity,) + payload.shape[1:])
+    code = landed[:, 2 * past_size, :2].astype(jnp.int32)
     landed_slots = code[:, 0] * 16 + code[:, 1]
     wanted = req_index * request_list + order_ids
     slot_hits = landed_slots[None, :] == wanted[:, None]
     entry_ids = jnp.arange(req_count * capacity, dtype=jnp.int32)
     slot_position = jnp.sum(jnp.where(slot_hits, entry_ids[None, :], 0), axis=1)
-    decode_rows = jnp.take(landed[:, :2 * past_size * lanes], slot_position, axis=0)
-    decode_kv = jnp.moveaxis(decode_rows.reshape(request_list, 2, past_size, lanes), 1, 0)
+    decode_rows = jnp.take(landed, slot_position, axis=0)
+    decode_kv = (decode_rows[:, :past_size], decode_rows[:, past_size:2 * past_size])
 
     x_whole = gather_features(activations)
     x_float = x_whole.astype(jnp.float32)
@@ -199,7 +200,7 @@
     gate_proj = jnp.dot(normed_two, gate_weight, preferred_element_type=jnp.float32)
     upward = jnp.dot(normed_two, up_weight, preferred_element_type=jnp.float32)
     hidden = (jax.nn.silu(gate_proj) * upward).astype(jnp.bfloat16)
-    mlp_share = scatter_features(hidden, down_weight)
+    mlp_share = scatter_features(hidden, down_weight, jnp.bfloat16)
     live_rows = (jnp.arange(span_size, dtype=jnp.int32)[None, :] < span_length[:, None]).reshape(
         total_rows
     )

time: 221 us -> 178 us (0.81)
  waiting for transfers between devices: 109 us -> 73.3 us
  other arithmetic: 36.7 us -> 30.8 us
    all_to_all x1, waiting for transfers between devices: 25.9 us -> 0.02 us  [local(): lax.all_to_all(packed, 'req', split_axis=0, concat_axis=0, tiled=True)]
    ppermute x10, waiting for transfers between devices: 79.1 us -> 69.3 us  [swap(): return lax.ppermute(values, axis_name, [(0, 1), (1, 0)])]
    select_n x2, other arithmetic: 4.44 us -> 2.11 us  [gather_features(): jnp.where(chip == 0, jnp.stack([share, partner]), jnp.stack([partner, sha...]
    unnamed x49 -> x46, local copies, waits for them, and re-layouts: 7.94 us -> 6.01 us
    gather x2 -> x1, local copies, waits for them, and re-layouts: 4.56 us -> 2.78 us  [local(): packed = jnp.take(payload, picked, axis=0)]
  transfers between devices with their start and end apart: 12 -> 12, of which waited for: 9 -> 8; matrix products, arithmetic and copies ran while one was open for 12% -> 29% of each run, Pallas kernels for 0% -> 0%
where the time goes in v5:
time: 178 us; the launch traced here: 177 us
  waiting for transfers between devices  73.3 us (41%)
  other arithmetic  30.8 us (17%)
  local copies, waits for them, and re-layouts  26.1 us (15%)
  matrix products  24.9 us (14%)
  starting transfers between devices  20.8 us (12%)
    ppermute x10, waiting for transfers between devices, swap(): return lax.ppermute(values, axis_name, [(0, 1), (1, 0)])  69.3 us
    dot_general x2, matrix products, scatter_features(): product = jnp.dot(matrix_in, weight, preferred_element_type=jnp.float32)  14.1 us
    ppermute x10, starting transfers between devices, swap(): return lax.ppermute(values, axis_name, [(0, 1), (1, 0)])  10.5 us
    all_to_all x1, starting transfers between devices, local(): lax.all_to_all(packed, 'req', split_axis=0, concat_axis=0, tiled=True)  6.02 us
    unnamed x46, local copies, waits for them, and re-layouts  6.01 us
    another operation x2, other arithmetic, scatter_features(): jnp.stack([jnp.where(core == 0, block(k, 0), block(k, 1)) for k in range(...  5.46 us
    all_to_all x1, starting transfers between devices, local(): lax.all_to_all(stacked, ('kvy', 'core'), split_axis=1, concat_axis=1, til...  4.34 us
    dot_general x1, matrix products, local(): jnp.dot(normed_two, gate_weight, preferred_element_type=jnp.float32)  4.27 us
  transfers between devices with their start and end apart: 12, of which 8 were waited for; matrix products, arithmetic and copies ran while one was open for 29% of the time, Pallas kernels for 0%

profile of v5, /device:TPU:0, one launch (start us, length us, event | category | flops | bytes accessed | tf_op | source)
XLA Modules:
  0.0 177.2 jit_solution(9100115716542251003)
XLA Ops:
  0.6 3.0 %collective-permute-start = (bf16[624,512]{1,0:T(8,128)(2,1)}, bf16[624,512]{1,0:T(8,128)(2,1)}, u32[]{:S(2)}, u32[]{:S(2)}) collective-permute-start(bf16[624,512]{1,0:T(8,128)(2,1)} %param.15), channel_id=1, source_target_pairs={{0,2},{2,0},{1,3},{3,1},{4,6},{6,4},{5,7},{7,5},{8,10},{10,8},{9,1... | collective-permute-start | bytes 1916936 | tf_op jit(solution)/shard_map/ppermute | solution.py:41
  8.0 4.3 %all-to-all-start = ((bf16[2,4,13,16,256]{4,3,2,0,1:T(8,128)(2,1)}), bf16[2,4,13,16,256]{4,3,2,0,1:T(8,128)(2,1)}, u32[]{:S(2)}, u32[]{:S(2)}) async-start(bf16[2,4,13,16,256]{4,3,2,0,1:T(8,128)(2,1)} %copy.70), calls=%async_computation | async-start | bytes 1703936 | tf_op jit(solution)/shard_map/all_to_all | solution.py:118
  12.4 6.8 %collective-permute-done = bf16[624,512]{1,0:T(8,128)(2,1)} collective-permute-done((bf16[624,512]{1,0:T(8,128)(2,1)}, bf16[624,512]{1,0:T(8,128)(2,1)}, u32[]{:S(2)}, u32[]{:S(2)}) %collective-permute-start) | collective-permute-done | bytes 639008 | tf_op jit(solution)/shard_map/ppermute | solution.py:41
  19.2 1.9 %maximum_select_fusion = bf16[2,624,512]{2,1,0:T(8,128)(2,1)S(1)} fusion(bf16[1,624,512]{2,1,0:T(8,128)(2,1)} %bitcast.4, bf16[1,624,512]{2,1,0:T(8,128)(2,1)} %bitcast.133, pred[]{:T(512)S(6)} %eq.26), kind=kLoop, calls=%fused_computation.15 | loop fusion | flops 1916928 | bytes 2555905 | tf_op jit(solution)/shard_map/jit(_where)/select_n | solution.py:48
  21.4 2.1 %multiply_cosine_fusion = (f32[13,48,128]{2,1,0:T(8,128)}, f32[13,48,128]{2,1,0:T(8,128)}) fusion(f32[128]{0:T(128)S(1)} %multiply_exponential_fusion, f32[13,48]{1,0:T(8,128)S(1)} %iota_add_fusion), kind=kLoop, calls=%fused_computation.72 | loop fusion | flops 79872 | bytes 641984 | tf_op jit(solution)/shard_map/cos | solution.py:22
  23.5 4.0 %all-to-all-done = bf16[2,4,13,16,256]{4,3,2,0,1:T(8,128)(2,1)} async-done(((bf16[2,4,13,16,256]{4,3,2,0,1:T(8,128)(2,1)}), bf16[2,4,13,16,256]{4,3,2,0,1:T(8,128)(2,1)}, u32[]{:S(2)}, u32[]{:S(2)}) %all-to-all-start) | async-done | bytes 852000 | tf_op jit(solution)/shard_map/all_to_all | solution.py:118
  31.2 2.0 %fusion = f32[624]{0:T(1024)S(1)} fusion(bf16[624,512]{1,0:T(8,128)(2,1)S(1)} %get-tuple-element.19, bf16[624,512]{1,0:T(8,128)(2,1)S(1)} %get-tuple-element.20, bf16[624,512]{1,0:T(8,128)(2,1)S(1)} %get-tuple-element.18, bf16[624,512]{1,0:T(8,128)(2,1)S(1)} %get-tuple-element.17), kind=kLoop, calls=%fused_computation.4 | loop fusion | flops 12778896 | bytes 2558400 | tf_op jit(solution)/shard_map/reduce_sum | solution.py:155
  35.6 2.6 %fusion.55 = f32[624,512]{1,0:T(8,128)} fusion(bf16[624,2048]{1,0:T(8,128)(2,1)S(1)} %fusion.2, bf16[2048,512]{1,0:T(8,128)(2,1)S(1)} %copy-done.19), kind=kOutput, calls=%fused_computation.141 | convolution fusion | flops 1308622848 | bytes 5931008 | tf_op jit(solution)/shard_map/dot_general | solution.py:162
  38.2 2.1 %reshape.313 = f32[13,48,2,256]{3,2,1,0:T(2,128)S(1)} reshape(f32[624,512]{1,0:T(8,128)} %fusion.55) | data formatting | bytes 2555904 | tf_op jit(solution)/shard_map/reshape | solution.py:164
  42.0 2.2 %fusion.54 = f32[624,256]{1,0:T(8,128)S(1)} fusion(bf16[624,2048]{1,0:T(8,128)(2,1)S(1)} %copy-done.7, bf16[2048,256]{1,0:T(8,128)(2,1)} %param.21), kind=kOutput, calls=%fused_computation.140 | convolution fusion | flops 654311424 | bytes 4243456 | tf_op jit(solution)/shard_map/dot_general | solution.py:166
  44.2 1.6 fusion.28
  49.9 1.5 fusion.56
  52.5 4.8 %collective-permute-done.2 = f32[2,624,512]{2,1,0:T(8,128)S(1)} collective-permute-done((f32[2,624,512]{2,1,0:T(8,128)S(1)}, f32[2,624,512]{2,1,0:T(8,128)S(1)}, u32[]{:S(2)}, u32[]{:S(2)}) %collective-permute-start.2) | collective-permute-done | bytes 2555936 | tf_op jit(solution)/shard_map/ppermute | solution.py:41
  58.2 1.8 %collective-permute-start.3 = (f32[624,512]{1,0:T(8,128)S(1)}, f32[624,512]{1,0:T(8,128)S(1)}, u32[]{:S(2)}, u32[]{:S(2)}) collective-permute-start(f32[624,512]{1,0:T(8,128)S(1)} %select_bitcast_fusion.4), channel_id=1, source_target_pairs={{0,2},{2,0},{1,3},{3,1},{4,6},{6,4},{5,7},{7,5},{8,10},{10,8},{9,1... | collective-permute-start | bytes 3833864 | tf_op jit(solution)/shard_map/ppermute | solution.py:41
  60.0 28.4 %collective-permute-done.3 = f32[624,512]{1,0:T(8,128)S(1)} collective-permute-done((f32[624,512]{1,0:T(8,128)S(1)}, f32[624,512]{1,0:T(8,128)S(1)}, u32[]{:S(2)}, u32[]{:S(2)}) %collective-permute-start.3) | collective-permute-done | bytes 1277984 | tf_op jit(solution)/shard_map/ppermute | solution.py:41
  90.0 1.7 collective-permute-start.5
  93.8 1.8 %collective-permute-start.6 = (bf16[624,512]{1,0:T(8,128)(2,1)S(1)}, bf16[624,512]{1,0:T(8,128)(2,1)S(1)}, u32[]{:S(2)}, u32[]{:S(2)}) collective-permute-start(bf16[624,512]{1,0:T(8,128)(2,1)S(1)} %multiply_convert_fusion.1), channel_id=1, source_target_pairs={{0,2},{2,0},{1,3},{3,1},{4,6},{6,4},{5,7},{7,5},{8,10},{10,8},{9,1... | collective-permute-start | bytes 1916936 | tf_op jit(solution)/shard_map/ppermute | solution.py:41
  96.0 13.2 %collective-permute-done.6 = bf16[624,512]{1,0:T(8,128)(2,1)S(1)} collective-permute-done((bf16[624,512]{1,0:T(8,128)(2,1)S(1)}, bf16[624,512]{1,0:T(8,128)(2,1)S(1)}, u32[]{:S(2)}, u32[]{:S(2)}) %collective-permute-start.6) | collective-permute-done | bytes 639008 | tf_op jit(solution)/shard_map/ppermute | solution.py:41
  110.0 2.1 %pad_maximum_fusion.4 = bf16[13,129,256]{2,1,0:T(8,128)(2,1)} fusion(bf16[13,1,256]{2,1,0:T(2,128)(2,1)S(1)} %copy.76, bf16[13,64,256]{2,1,0:T(8,128)(2,1)} %bitcast.137, bf16[13,64,256]{2,1,0:T(8,128)(2,1)} %bitcast.135), kind=kLoop, calls=%fused_computation.41 | loop fusion | flops 2575872 | bytes 1717248 | tf_op jit(solution)/shard_map/concatenate | solution.py:138
  112.2 2.8 %gather_fusion = bf16[16,129,256]{2,1,0:T(8,128)(2,1)} fusion(bf16[13,129,256]{2,1,0:T(8,128)(2,1)} %pad_maximum_fusion.4, s32[1024]{0:T(1024)S(1)} %pad_clamp_fusion.1), kind=kCustom, calls=%fused_computation | custom fusion | bytes 2113600 | tf_op jit(solution)/shard_map/jit(_take)/gather | solution.py:139
  114.9 1.5 select_select_fusion
  116.5 1.8 %copy.77 = bf16[8,2,129,256]{3,1,2,0:T(2,128)(2,1)} copy(bf16[8,2,129,256]{3,2,1,0:T(8,128)(2,1)S(1)} %select_select_fusion) | data formatting | bytes 2113536 | tf_op jit(solution)/shard_map/jit(_where)/select_n | solution.py:140
  118.2 6.0 %all-to-all-start.1 = ((bf16[8,2,129,256]{3,1,2,0:T(2,128)(2,1)}), bf16[8,2,129,256]{3,1,2,0:T(2,128)(2,1)}, u32[]{:S(2)}, u32[]{:S(2)}) async-start(bf16[8,2,129,256]{3,1,2,0:T(2,128)(2,1)} %copy.77), calls=%async_computation.1 | async-start | bytes 2113536 | tf_op jit(solution)/shard_map/all_to_all | solution.py:142
  124.3 1.6 select_bitcast_fusion.12
  127.1 4.3 %fusion.26 = f32[624,1024]{1,0:T(8,128)} fusion(bf16[2048,1024]{1,0:T(8,128)(2,1)S(1)} %copy-done.18, bf16[624,512]{1,0:T(8,128)(2,1)S(1)} %get-tuple-element.15, bf16[624,512]{1,0:T(8,128)(2,1)S(1)} %get-tuple-element.16, bf16[624,512]{1,0:T(8,128)(2,1)S(1)} %get-tuple-element.14, bf16[624,512]{1,0:T(8,128)(2,1)S(1)} %get-tuple-element.13), kind=kOutput, calls=%fused_computation.79 | convolution fusion | flops 2627469312 | bytes 9306112 | tf_op jit(solution)/shard_map/dot_general | solution.py:200
  131.4 12.6 %fusion.16 = f32[624,2048]{1,0:T(8,128)} fusion(bf16[1024,2048]{1,0:T(8,128)(2,1)} %param.27, f32[624,1024]{1,0:T(8,128)} %fusion.26, bf16[2048,1024]{1,0:T(8,128)(2,1)} %param.26, bf16[624,512]{1,0:T(8,128)(2,1)} %copy-done.13, bf16[624,512]{1,0:T(8,128)(2,1)} %copy-done.14, bf16[624,512]{1,0:T(8,128)(2,1)} %copy-done.12, ...), kind=kOutput, calls=%fused_computation.53 | convolution fusion | flops 5248548864 | bytes 18612224 | tf_op jit(solution)/shard_map/dot_general | solution.py:60
  144.0 4.8 %select_bitcast_fusion.3 = (f32[1,624,512]{2,1,0:T(8,128)}, f32[1,624,512]{2,1,0:T(8,128)}, f32[1,624,512]{2,1,0:T(8,128)S(1)}, f32[1,624,512]{2,1,0:T(8,128)S(1)}) fusion(f32[624,2048]{1,0:T(8,128)} %fusion.16, pred[]{:T(512)S(6)} %eq.27), kind=kLoop, calls=%fused_computation.27 | loop fusion | flops 1277952 | bytes 10223617 | tf_op jit(solution)/shard_map/stack | solution.py:67
  148.8 1.8 %pad_maximum_fusion.3 = f32[2,624,512]{2,1,0:T(8,128)} fusion(f32[1,624,512]{2,1,0:T(8,128)S(1)} %get-tuple-element.7, f32[1,624,512]{2,1,0:T(8,128)S(1)} %get-tuple-element.8), kind=kLoop, calls=%fused_computation.12 | loop fusion | flops 638976 | bytes 5111808 | tf_op jit(solution)/shard_map/stack | solution.py:68
  153.8 2.8 %gather_fusion.1 = bf16[13,129,256]{2,1,0:T(8,128)(2,1)} fusion(bf16[16,129,256]{2,1,0:T(8,128)(2,1)} %bitcast.130, s32[1024]{0:T(1024)S(1)} %pad_clamp_fusion), kind=kCustom, calls=%fused_computation.1 | custom fusion | bytes 1717300 | tf_op jit(solution)/shard_map/jit(_take)/gather | solution.py:150
  156.6 2.7 %maximum_add_fusion.1 = f32[2,624,512]{2,1,0:T(8,128)S(1)} fusion(f32[2,624,512]{2,1,0:T(8,128)} %collective-permute-done.8, f32[1,624,512]{2,1,0:T(8,128)} %get-tuple-element.6, f32[1,624,512]{2,1,0:T(8,128)S(1)} %copy-done.2), kind=kLoop, calls=%fused_computation.11 | loop fusion | flops 1277952 | bytes 7667712 | tf_op jit(solution)/shard_map/add | solution.py:69
  159.4 1.6 collective-permute-start.9
  162.1 13.9 %collective-permute-done.9 = bf16[624,512]{1,0:T(8,128)(2,1)S(1)} collective-permute-done((bf16[624,512]{1,0:T(8,128)(2,1)S(1)}, bf16[624,512]{1,0:T(8,128)(2,1)S(1)}, u32[]{:S(2)}, u32[]{:S(2)}) %collective-permute-start.9) | collective-permute-done | bytes 639008 | tf_op jit(solution)/shard_map/ppermute | solution.py:41
  (120 shorter events, 30.0 us)
Async XLA Ops:
  0.6 49.3 %copy-start = (bf16[512,2048]{1,0:T(8,128)(2,1)S(1)}, bf16[512,2048]{1,0:T(8,128)(2,1)}, u32[]{:S(2)}) copy-start(bf16[512,2048]{1,0:T(8,128)(2,1)} %param.23) | copy-start | bytes 6291460
  0.6 18.6 %collective-permute-start = (bf16[624,512]{1,0:T(8,128)(2,1)}, bf16[624,512]{1,0:T(8,128)(2,1)}, u32[]{:S(2)}, u32[]{:S(2)}) collective-permute-start(bf16[624,512]{1,0:T(8,128)(2,1)} %param.15), channel_id=1, source_target_pairs={{0,2},{2,0},{1,3},{3,1},{4,6},{6,4},{5,7},{7,5},{8,10},{10,8},{9,1... | collective-permute-start | bytes 1916936 | tf_op jit(solution)/shard_map/ppermute | solution.py:41
  6.9 5.4 %copy-start.21 = (s32[13]{0:T(128)S(1)}, s32[13]{0:T(128)}, u32[]{:S(2)}) copy-start(s32[13]{0:T(128)} %param.17) | copy-start | bytes 160
  8.0 13.3 %copy-start.16 = (s32[13]{0:T(128)S(1)}, s32[13]{0:T(128)}, u32[]{:S(2)}) copy-start(s32[13]{0:T(128)} %param.16) | copy-start | bytes 160
  8.0 19.5 %all-to-all-start = ((bf16[2,4,13,16,256]{4,3,2,0,1:T(8,128)(2,1)}), bf16[2,4,13,16,256]{4,3,2,0,1:T(8,128)(2,1)}, u32[]{:S(2)}, u32[]{:S(2)}) async-start(bf16[2,4,13,16,256]{4,3,2,0,1:T(8,128)(2,1)} %copy.70), calls=%async_computation | async-start | bytes 1703936 | tf_op jit(solution)/shard_map/all_to_all | solution.py:118
  21.1 8.6 %collective-permute-start.1 = (bf16[2,624,512]{2,1,0:T(8,128)(2,1)S(1)}, bf16[2,624,512]{2,1,0:T(8,128)(2,1)}, u32[]{:S(2)}, u32[]{:S(2)}) collective-permute-start(bf16[2,624,512]{2,1,0:T(8,128)(2,1)S(1)} %maximum_select_fusion), channel_id=1, source_target_pairs={{0,1},{1,0},{2,3},{3,2},{4,5},{5,4},{6,7},{7,6},{8,9},{9,8},{10,11... | collective-permute-start | bytes 3833864 | tf_op jit(solution)/shard_map/ppermute | solution.py:41
  31.2 2.1 %copy-start.15 = (f32[2048]{0:T(1024)S(1)}, f32[2048]{0:T(1024)}, u32[]{:S(2)}) copy-start(f32[2048]{0:T(1024)} %param.19) | copy-start | bytes 24580
  33.3 2.4 %copy-start.19 = (bf16[2048,512]{1,0:T(8,128)(2,1)S(1)}, bf16[2048,512]{1,0:T(8,128)(2,1)}, u32[]{:S(2)}) copy-start(bf16[2048,512]{1,0:T(8,128)(2,1)} %param.20) | copy-start | bytes 6291460
  34.2 1.5 copy-start.6
  40.3 1.7 copy-start.7
  42.0 3.7 %copy-start.20 = (bf16[2048,256]{1,0:T(8,128)(2,1)S(1)}, bf16[2048,256]{1,0:T(8,128)(2,1)}, u32[]{:S(2)}) copy-start(bf16[2048,256]{1,0:T(8,128)(2,1)} %param.22) | copy-start | bytes 3145732
  45.8 1.1 copy-start.11
  46.7 1.1 copy-start.8
  47.7 1.0 copy-start.9
  52.4 4.9 %collective-permute-start.2 = (f32[2,624,512]{2,1,0:T(8,128)S(1)}, f32[2,624,512]{2,1,0:T(8,128)S(1)}, u32[]{:S(2)}, u32[]{:S(2)}) collective-permute-start(f32[2,624,512]{2,1,0:T(8,128)S(1)} %pad_maximum_fusion.1), channel_id=1, source_target_pairs={{0,1},{1,0},{2,3},{3,2},{4,5},{5,4},{6,7},{7,6},{8,9},{9,8},{10,11... | collective-permute-start | bytes 7667720 | tf_op jit(solution)/shard_map/ppermute | solution.py:41
  57.9 30.5 %copy-start.5 = (bf16[624,512]{1,0:T(8,128)(2,1)S(1)}, bf16[624,512]{1,0:T(8,128)(2,1)}, u32[]{:S(2)}) copy-start(bf16[624,512]{1,0:T(8,128)(2,1)} %param.15) | copy-start | bytes 1916932
  58.2 37.4 %copy-start.17 = (s32[13]{0:T(128)S(1)}, s32[13]{0:T(128)}, u32[]{:S(2)}) copy-start(s32[13]{0:T(128)} %param.18) | copy-start | bytes 160
  58.2 30.2 %collective-permute-start.3 = (f32[624,512]{1,0:T(8,128)S(1)}, f32[624,512]{1,0:T(8,128)S(1)}, u32[]{:S(2)}, u32[]{:S(2)}) collective-permute-start(f32[624,512]{1,0:T(8,128)S(1)} %select_bitcast_fusion.4), channel_id=1, source_target_pairs={{0,2},{2,0},{1,3},{3,1},{4,6},{6,4},{5,7},{7,5},{8,10},{10,8},{9,1... | collective-permute-start | bytes 3833864 | tf_op jit(solution)/shard_map/ppermute | solution.py:41
  88.7 1.2 collective-permute-start.4
  90.0 3.6 %collective-permute-start.5 = (f32[624,1]{0,1:T(1,128)S(1)}, f32[624,1]{0,1:T(1,128)S(1)}, u32[]{:S(2)}, u32[]{:S(2)}) collective-permute-start(f32[624,1]{0,1:T(1,128)S(1)} %reshape_add_fusion), channel_id=1, source_target_pairs={{0,2},{2,0},{1,3},{3,1},{4,6},{6,4},{5,7},{7,5},{8,10},{10,8},{9,1... | collective-permute-start | bytes 7496 | tf_op jit(solution)/shard_map/ppermute | solution.py:41
  93.8 15.4 %collective-permute-start.6 = (bf16[624,512]{1,0:T(8,128)(2,1)S(1)}, bf16[624,512]{1,0:T(8,128)(2,1)S(1)}, u32[]{:S(2)}, u32[]{:S(2)}) collective-permute-start(bf16[624,512]{1,0:T(8,128)(2,1)S(1)} %multiply_convert_fusion.1), channel_id=1, source_target_pairs={{0,2},{2,0},{1,3},{3,1},{4,6},{6,4},{5,7},{7,5},{8,10},{10,8},{9,1... | collective-permute-start | bytes 1916936 | tf_op jit(solution)/shard_map/ppermute | solution.py:41
  109.3 14.9 %collective-permute-start.7 = (bf16[2,624,512]{2,1,0:T(8,128)(2,1)S(1)}, bf16[2,624,512]{2,1,0:T(8,128)(2,1)}, u32[]{:S(2)}, u32[]{:S(2)}) collective-permute-start(bf16[2,624,512]{2,1,0:T(8,128)(2,1)S(1)} %maximum_select_fusion.1), channel_id=1, source_target_pairs={{0,1},{1,0},{2,3},{3,2},{4,5},{5,4},{6,7},{7,6},{8,9},{9,8},{10,11... | collective-permute-start | bytes 3833864 | tf_op jit(solution)/shard_map/ppermute | solution.py:41
  118.2 32.7 %all-to-all-start.1 = ((bf16[8,2,129,256]{3,1,2,0:T(2,128)(2,1)}), bf16[8,2,129,256]{3,1,2,0:T(2,128)(2,1)}, u32[]{:S(2)}, u32[]{:S(2)}) async-start(bf16[8,2,129,256]{3,1,2,0:T(2,128)(2,1)} %copy.77), calls=%async_computation.1 | async-start | bytes 2113536 | tf_op jit(solution)/shard_map/all_to_all | solution.py:142
  124.3 2.9 %copy-start.18 = (bf16[2048,1024]{1,0:T(8,128)(2,1)S(1)}, bf16[2048,1024]{1,0:T(8,128)(2,1)}, u32[]{:S(2)}) copy-start(bf16[2048,1024]{1,0:T(8,128)(2,1)} %param.25) | copy-start | bytes 12582916
  125.9 1.0 copy-start.13
  125.9 1.2 copy-start.14
  150.6 6.0 %copy-start.2 = (f32[1,624,512]{2,1,0:T(8,128)S(1)}, f32[1,624,512]{2,1,0:T(8,128)}, u32[]{:S(2)}) copy-start(f32[1,624,512]{2,1,0:T(8,128)} %get-tuple-element.5) | copy-start | bytes 3833860
  150.6 6.0 %collective-permute-start.8 = (f32[2,624,512]{2,1,0:T(8,128)}, f32[2,624,512]{2,1,0:T(8,128)}, u32[]{:S(2)}, u32[]{:S(2)}) collective-permute-start(f32[2,624,512]{2,1,0:T(8,128)} %pad_maximum_fusion.3), channel_id=1, source_target_pairs={{0,1},{1,0},{2,3},{3,2},{4,5},{5,4},{6,7},{7,6},{8,9},{9,8},{10,11... | collective-permute-start | bytes 7667720 | tf_op jit(solution)/shard_map/ppermute | solution.py:41
  152.3 1.1 copy-start.3
  159.2 1.7 copy-start.4
  159.4 16.6 %collective-permute-start.9 = (bf16[624,512]{1,0:T(8,128)(2,1)S(1)}, bf16[624,512]{1,0:T(8,128)(2,1)S(1)}, u32[]{:S(2)}, u32[]{:S(2)}) collective-permute-start(bf16[624,512]{1,0:T(8,128)(2,1)S(1)} %fusion.17), channel_id=1, source_target_pairs={{0,2},{2,0},{1,3},{3,1},{4,6},{6,4},{5,7},{7,5},{8,10},{10,8},{9,1... | collective-permute-start | bytes 1916936 | tf_op jit(solution)/shard_map/ppermute | solution.py:41
  161.1 16.0 %copy-start.1 = (bf16[512,2048]{1,0:T(8,128)(2,1)S(1)}, bf16[512,2048]{1,0:T(8,128)(2,1)}, u32[]{:S(2)}) copy-start(bf16[512,2048]{1,0:T(8,128)(2,1)} %param.23) | copy-start | bytes 6291460
  (2 other events, 1.8 us)

commit v6 on v5

--- a/solution.py
+++ b/solution.py
@@ -150,61 +150,80 @@
     decode_rows = jnp.take(landed, slot_position, axis=0)
     decode_kv = (decode_rows[:, :past_size], decode_rows[:, past_size:2 * past_size])
 
-    x_whole = gather_features(activations)
-    x_float = x_whole.astype(jnp.float32)
-    square_sum = jnp.sum(x_float * x_float, axis=-1, keepdims=True)
-    normalized_input = (
-        x_float * lax.rsqrt(square_sum / x_float.shape[-1] + epsilon) * attention_gain
-    ).astype(jnp.bfloat16)
-    position = (
-        offsets[:, None].astype(jnp.float32) + jnp.arange(span_size, dtype=jnp.float32)[None, :]
-    )
-    query_rows = jnp.dot(
-        normalized_input, query_weight, preferred_element_type=jnp.float32
-    ).reshape(request_list, span_size, local_q, HEAD_WIDTH)
-    query_rows = rotate_pairs(query_rows, position).astype(jnp.bfloat16)
-    fresh_keys = jnp.dot(
-        normalized_input, key_projection_matrix, preferred_element_type=jnp.float32
-    ).reshape(request_list, span_size, local_kv, HEAD_WIDTH)
-    fresh_keys = rotate_pairs(fresh_keys, position).astype(jnp.bfloat16)
-    fresh_values = (
-        jnp.dot(normalized_input, value_projection_matrix, preferred_element_type=jnp.float32)
-        .astype(jnp.bfloat16)
-        .reshape(request_list, span_size, local_kv, HEAD_WIDTH)
-    )
-    combined_keys = jnp.concatenate(
-        [head_kv[0].reshape(request_list, past_size, local_kv, HEAD_WIDTH), fresh_keys], axis=1
-    )
-    combined_values = jnp.concatenate(
-        [head_kv[1].reshape(request_list, past_size, local_kv, HEAD_WIDTH), fresh_values], axis=1
-    )
-    grouped_queries = query_rows.reshape(
-        request_list, span_size, local_kv, query_groups, HEAD_WIDTH
-    )
-    scores = jnp.einsum(
-        "rckgd,rskd->rkgcs", grouped_queries, combined_keys, preferred_element_type=jnp.float32
-    ) / math.sqrt(HEAD_WIDTH)
-    allowed = allowed_keys(span_length, span_size, past_size)[:, None, None, :, :]
-    scores = jnp.where(allowed, scores, -jnp.inf)
-    weights = jax.nn.softmax(scores, axis=-1).astype(jnp.bfloat16)
-    mixed_heads = jnp.einsum(
-        "rkgcs,rskd->rckgd", weights, combined_values, preferred_element_type=jnp.float32
-    )
-    mixed_heads = mixed_heads.astype(jnp.bfloat16).reshape(total_rows, local_q * HEAD_WIDTH)
-    head_share = scatter_features(mixed_heads, output_weight)
-    residual_share = activations.astype(jnp.float32) + head_share
-
     gain_share = lax.dynamic_slice_in_dim(feedforward_gain, kv_index * width_share, width_share)
-    normed_share = row_scale(residual_share, gain_share).astype(jnp.bfloat16)
-    normed_two = gather_features(normed_share)
-    gate_proj = jnp.dot(normed_two, gate_weight, preferred_element_type=jnp.float32)
-    upward = jnp.dot(normed_two, up_weight, preferred_element_type=jnp.float32)
-    hidden = (jax.nn.silu(gate_proj) * upward).astype(jnp.bfloat16)
-    mlp_share = scatter_features(hidden, down_weight, jnp.bfloat16)
-    live_rows = (jnp.arange(span_size, dtype=jnp.int32)[None, :] < span_length[:, None]).reshape(
-        total_rows
-    )
-    layer_out = jnp.where(live_rows[:, None], residual_share + mlp_share, 0.0).astype(jnp.bfloat16)
+
+    def layer_rows(activations, span_length, offsets, past_keys, past_values):
+        request_list = span_length.shape[0]
+        total_rows = activations.shape[0]
+        x_whole = gather_features(activations)
+        x_float = x_whole.astype(jnp.float32)
+        square_sum = jnp.sum(x_float * x_float, axis=-1, keepdims=True)
+        normalized_input = (
+            x_float * lax.rsqrt(square_sum / x_float.shape[-1] + epsilon) * attention_gain
+        ).astype(jnp.bfloat16)
+        position = (
+            offsets[:, None].astype(jnp.float32) + jnp.arange(span_size, dtype=jnp.float32)[None, :]
+        )
+        query_rows = jnp.dot(
+            normalized_input, query_weight, preferred_element_type=jnp.float32
+        ).reshape(request_list, span_size, local_q, HEAD_WIDTH)
+        query_rows = rotate_pairs(query_rows, position).astype(jnp.bfloat16)
+        fresh_keys = jnp.dot(
+            normalized_input, key_projection_matrix, preferred_element_type=jnp.float32
+        ).reshape(request_list, span_size, local_kv, HEAD_WIDTH)
+        fresh_keys = rotate_pairs(fresh_keys, position).astype(jnp.bfloat16)
+        fresh_values = (
+            jnp.dot(normalized_input, value_projection_matrix, preferred_element_type=jnp.float32)
+            .astype(jnp.bfloat16)
+            .reshape(request_list, span_size, local_kv, HEAD_WIDTH)
+        )
+        combined_keys = jnp.concatenate(
+            [past_keys.reshape(request_list, past_size, local_kv, HEAD_WIDTH), fresh_keys], axis=1
+        )
+        combined_values = jnp.concatenate(
+            [past_values.reshape(request_list, past_size, local_kv, HEAD_WIDTH), fresh_values], axis=1
+        )
+        grouped_queries = query_rows.reshape(
+            request_list, span_size, local_kv, query_groups, HEAD_WIDTH
+        )
+        scores = jnp.einsum(
+            "rckgd,rskd->rkgcs", grouped_queries, combined_keys, preferred_element_type=jnp.float32
+        ) / math.sqrt(HEAD_WIDTH)
+        allowed = allowed_keys(span_length, span_size, past_size)[:, None, None, :, :]
+        scores = jnp.where(allowed, scores, -jnp.inf)
+        weights = jax.nn.softmax(scores, axis=-1).astype(jnp.bfloat16)
+        mixed_heads = jnp.einsum(
+            "rkgcs,rskd->rckgd", weights, combined_values, preferred_element_type=jnp.float32
+        )
+        mixed_heads = mixed_heads.astype(jnp.bfloat16).reshape(total_rows, local_q * HEAD_WIDTH)
+        head_share = scatter_features(mixed_heads, output_weight)
+        residual_share = activations.astype(jnp.float32) + head_share
+
+        normed_share = row_scale(residual_share, gain_share).astype(jnp.bfloat16)
+        normed_two = gather_features(normed_share)
+        gate_proj = jnp.dot(normed_two, gate_weight, preferred_element_type=jnp.float32)
+        upward = jnp.dot(normed_two, up_weight, preferred_element_type=jnp.float32)
+        hidden = (jax.nn.silu(gate_proj) * upward).astype(jnp.bfloat16)
+        mlp_share = scatter_features(hidden, down_weight, jnp.bfloat16)
+        live_rows = (jnp.arange(span_size, dtype=jnp.int32)[None, :] < span_length[:, None]).reshape(
+            total_rows
+        )
+        layer_out = jnp.where(live_rows[:, None], residual_share + mlp_share, 0.0).astype(jnp.bfloat16)
+        return layer_out
+
+    first = (request_list + 1) // 2
+    outputs = []
+    for low, high in ((0, first), (first, request_list)):
+        outputs.append(
+            layer_rows(
+                activations[low * span_size:high * span_size],
+                span_length[low:high],
+                offsets[low:high],
+                head_kv[0, low:high],
+                head_kv[1, low:high],
+            )
+        )
+    layer_out = jnp.concatenate(outputs, axis=0)
     return (layer_out, decode_kv[0], decode_kv[1])
 
 

time: 178 us -> 195 us (1.096)
  other arithmetic: 30.8 us -> 45.8 us
  waiting for transfers between devices: 73.3 us -> 63.6 us
  matrix products: 24.9 us -> 31.7 us
  starting transfers between devices: 20.8 us -> 23.4 us
    ppermute x10 -> x20, waiting for transfers between devices: 69.3 us -> 58.1 us  [swap(): return lax.ppermute(values, axis_name, [(0, 1), (1, 0)])]
    all_to_all x1, waiting for transfers between devices: 0.02 us -> 5.55 us  [local(): lax.all_to_all(packed, 'req', split_axis=0, concat_axis=0, tiled=True)]
    another operation x0 -> x4, local copies, waits for them, and re-layouts: none -> 4.64 us  [the longest x2 3.08 us: gather_features(): jnp.stack([share, partner])]
    dot_general x2 -> x4, matrix products: 14.1 us -> 18.2 us  [scatter_features(): product = jnp.dot(matrix_in, weight, preferred_element_type=jnp.float32)]
    all_to_all x1, waiting for transfers between devices: 4.04 us -> 0.01 us  [local(): lax.all_to_all(stacked, ('kvy', 'core'), split_axis=1, concat_axis=1, til...]
    add x2 -> x4, other arithmetic: 3.27 us -> 6.57 us  [scatter_features(): chip_sum = keep + swap(give, 'core')]
    another operation x2 -> x4, other arithmetic: 5.46 us -> 8.68 us  [scatter_features(): jnp.stack([jnp.where(core == 0, block(k, 0), block(k, 1)) for k in range(...]
    dot_general x6 -> x12, matrix products: 10.8 us -> 13.5 us  [the longest x2 5.11 us: layer_rows(): jnp.dot(normed_two, gate_weight, preferred_element_type=jnp.float32)]
  transfers between devices with their start and end apart: 12 -> 22, of which waited for: 8 -> 9; matrix products, arithmetic and copies ran while one was open for 29% -> 49% of each run, Pallas kernels for 0% -> 0%
where the time goes in v6:
time: 195 us; the launch traced here: 194 us
  waiting for transfers between devices  63.6 us (33%)
  other arithmetic  45.8 us (23%)
  matrix products  31.7 us (16%)
  local copies, waits for them, and re-layouts  27.7 us (14%)
  starting transfers between devices  23.4 us (12%)
    ppermute x20, waiting for transfers between devices, swap(): return lax.ppermute(values, axis_name, [(0, 1), (1, 0)])  58.1 us
    dot_general x4, matrix products, scatter_features(): product = jnp.dot(matrix_in, weight, preferred_element_type=jnp.float32)  18.2 us
    ppermute x20, starting transfers between devices, swap(): return lax.ppermute(values, axis_name, [(0, 1), (1, 0)])  13.1 us
    another operation x4, other arithmetic, scatter_features(): jnp.stack([jnp.where(core == 0, block(k, 0), block(k, 1)) for k in range(...  8.68 us
    unnamed x105, local copies, waits for them, and re-layouts  7.6 us
    add x4, other arithmetic, scatter_features(): chip_sum = keep + swap(give, 'core')  6.57 us
    all_to_all x1, starting transfers between devices, local(): lax.all_to_all(packed, 'req', split_axis=0, concat_axis=0, tiled=True)  5.94 us
    all_to_all x1, waiting for transfers between devices, local(): lax.all_to_all(packed, 'req', split_axis=0, concat_axis=0, tiled=True)  5.55 us
  transfers between devices with their start and end apart: 22, of which 9 were waited for; matrix products, arithmetic and copies ran while one was open for 49% of the time, Pallas kernels for 0%

profile of v6, /device:TPU:0, one launch (start us, length us, event | category | flops | bytes accessed | tf_op | source)
XLA Modules:
  0.0 193.8 jit_solution(4094699158322242989)
XLA Ops:
  0.7 2.0 %slice_bitcast_fusion.5 = (bf16[1,336,512]{2,1,0:T(8,128)(2,1)}, bf16[336,512]{1,0:T(8,128)(2,1)}) fusion(bf16[624,512]{1,0:T(8,128)(2,1)} %param.15), kind=kLoop, calls=%fused_computation.236 | loop fusion | bytes 1032192 | tf_op jit(solution)/shard_map/stack | solution.py:48
  2.7 3.0 %collective-permute-start = (bf16[336,512]{1,0:T(8,128)(2,1)}, bf16[336,512]{1,0:T(8,128)(2,1)}, u32[]{:S(2)}, u32[]{:S(2)}) collective-permute-start(bf16[336,512]{1,0:T(8,128)(2,1)} %get-tuple-element.56), channel_id=1, source_target_pairs={{0,2},{2,0},{1,3},{3,1},{4,6},{6,4},{5,7},{7,5},{8,10},{10,8},{9,1... | collective-permute-start | bytes 1032200 | tf_op jit(solution)/shard_map/ppermute | solution.py:41
  8.9 4.3 %all-to-all-start = ((bf16[2,4,13,16,256]{4,3,2,0,1:T(8,128)(2,1)}), bf16[2,4,13,16,256]{4,3,2,0,1:T(8,128)(2,1)}, u32[]{:S(2)}, u32[]{:S(2)}) async-start(bf16[2,4,13,16,256]{4,3,2,0,1:T(8,128)(2,1)} %copy.86), calls=%async_computation | async-start | bytes 1703936 | tf_op jit(solution)/shard_map/all_to_all | solution.py:118
  14.3 2.0 %collective-permute-start.10 = (bf16[288,512]{1,0:T(8,128)(2,1)S(1)}, bf16[288,512]{1,0:T(8,128)(2,1)S(1)}, u32[]{:S(2)}, u32[]{:S(2)}) collective-permute-start(bf16[288,512]{1,0:T(8,128)(2,1)S(1)} %get-tuple-element.58), channel_id=1, source_target_pairs={{0,2},{2,0},{1,3},{3,1},{4,6},{6,4},{5,7},{7,5},{8,10},{10,8},{9,1... | collective-permute-start | bytes 884744 | tf_op jit(solution)/shard_map/ppermute | solution.py:41
  16.8 1.4 multiply_cosine_fusion
  23.4 8.5 %collective-permute-done.10 = bf16[288,512]{1,0:T(8,128)(2,1)S(1)} collective-permute-done((bf16[288,512]{1,0:T(8,128)(2,1)S(1)}, bf16[288,512]{1,0:T(8,128)(2,1)S(1)}, u32[]{:S(2)}, u32[]{:S(2)}) %collective-permute-start.10) | collective-permute-done | bytes 294944 | tf_op jit(solution)/shard_map/ppermute | solution.py:41
  33.9 2.1 %maximum_select_fusion = bf16[2,336,512]{2,1,0:T(8,128)(2,1)} fusion(bf16[1,336,512]{2,1,0:T(8,128)(2,1)} %bitcast.5, bf16[1,336,512]{2,1,0:T(8,128)(2,1)S(1)} %copy-done.11, pred[]{:T(512)S(6)} %eq.26), kind=kLoop, calls=%fused_computation.44 | loop fusion | flops 1032192 | bytes 1376257 | tf_op jit(solution)/shard_map/jit(_where)/select_n | solution.py:48
  38.8 2.9 %gather_fusion = bf16[16,129,256]{2,1,0:T(8,128)(2,1)} fusion(bf16[13,129,256]{2,1,0:T(8,128)(2,1)} %pad_maximum_fusion.8, s32[1024]{0:T(1024)} %pad_clamp_fusion.1), kind=kCustom, calls=%fused_computation | custom fusion | bytes 2113600 | tf_op jit(solution)/shard_map/jit(_take)/gather | solution.py:139
  48.3 2.2 %fusion.102 = f32[288,256]{1,0:T(8,128)S(1)} fusion(bf16[288,2048]{1,0:T(8,128)(2,1)} %copy-done.12, bf16[2048,256]{1,0:T(8,128)(2,1)} %param.21), kind=kOutput, calls=%fused_computation.247 | convolution fusion | flops 301989888 | bytes 2523136 | tf_op jit(solution)/shard_map/dot_general | solution.py:171
  57.1 1.4 select_bitcast_fusion.25
  72.3 1.8 copy.96
  74.1 5.9 %all-to-all-start.1 = ((bf16[8,2,129,256]{3,1,2,0:T(2,128)(2,1)}), bf16[8,2,129,256]{3,1,2,0:T(2,128)(2,1)}, u32[]{:S(2)}, u32[]{:S(2)}) async-start(bf16[8,2,129,256]{3,1,2,0:T(2,128)(2,1)} %copy.96), calls=%async_computation.1 | async-start | bytes 2113536 | tf_op jit(solution)/shard_map/all_to_all | solution.py:142
  80.3 1.5 maximum_add_fusion.2
  84.0 1.8 maximum_add_fusion
  85.8 12.7 %collective-permute-done.13 = f32[288,512]{1,0:T(8,128)} collective-permute-done((f32[288,512]{1,0:T(8,128)}, f32[288,512]{1,0:T(8,128)}, u32[]{:S(2)}, u32[]{:S(2)}) %collective-permute-start.13) | collective-permute-done | bytes 589856 | tf_op jit(solution)/shard_map/ppermute | solution.py:41
  101.2 5.6 %all-to-all-done.1 = bf16[8,2,129,256]{3,1,2,0:T(2,128)(2,1)} async-done(((bf16[8,2,129,256]{3,1,2,0:T(2,128)(2,1)}), bf16[8,2,129,256]{3,1,2,0:T(2,128)(2,1)}, u32[]{:S(2)}, u32[]{:S(2)}) %all-to-all-start.1) | async-done | bytes 1056800 | tf_op jit(solution)/shard_map/all_to_all | solution.py:142
  108.7 10.3 %collective-permute-done.15 = f32[288,1]{0,1:T(1,128)S(1)} collective-permute-done((f32[288,1]{0,1:T(1,128)S(1)}, f32[288,1]{0,1:T(1,128)S(1)}, u32[]{:S(2)}, u32[]{:S(2)}) %collective-permute-start.15) | collective-permute-done | bytes 1184 | tf_op jit(solution)/shard_map/ppermute | solution.py:41
  119.6 1.4 multiply_reduce_fusion
  122.3 1.7 collective-permute-start.5
  123.9 4.0 %collective-permute-done.16 = bf16[288,512]{1,0:T(8,128)(2,1)S(1)} collective-permute-done((bf16[288,512]{1,0:T(8,128)(2,1)S(1)}, bf16[288,512]{1,0:T(8,128)(2,1)S(1)}, u32[]{:S(2)}, u32[]{:S(2)}) %collective-permute-start.16) | collective-permute-done | bytes 294944 | tf_op jit(solution)/shard_map/ppermute | solution.py:41
  128.8 10.0 %collective-permute-done.6 = bf16[336,512]{1,0:T(8,128)(2,1)S(1)} collective-permute-done((bf16[336,512]{1,0:T(8,128)(2,1)S(1)}, bf16[336,512]{1,0:T(8,128)(2,1)S(1)}, u32[]{:S(2)}, u32[]{:S(2)}) %collective-permute-start.6) | collective-permute-done | bytes 344096 | tf_op jit(solution)/shard_map/ppermute | solution.py:41
  139.9 2.4 %fusion.56 = f32[288,1024]{1,0:T(8,128)} fusion(bf16[2048,1024]{1,0:T(8,128)(2,1)S(1)} %copy-done.43, bf16[288,512]{1,0:T(8,128)(2,1)S(1)} %get-tuple-element.33, bf16[288,512]{1,0:T(8,128)(2,1)S(1)} %get-tuple-element.34, bf16[288,512]{1,0:T(8,128)(2,1)S(1)} %get-tuple-element.32, bf16[288,512]{1,0:T(8,128)(2,1)S(1)} %get-tuple-element.31), kind=kOutput, calls=%fused_computation.157 | convolution fusion | flops 1212678144 | bytes 6553600 | tf_op jit(solution)/shard_map/dot_general | solution.py:204
  142.3 8.1 %fusion.19 = f32[288,2048]{1,0:T(8,128)} fusion(bf16[1024,2048]{1,0:T(8,128)(2,1)} %param.27, bf16[2048,1024]{1,0:T(8,128)(2,1)} %param.26, f32[288,1024]{1,0:T(8,128)} %fusion.56, bf16[288,512]{1,0:T(8,128)(2,1)} %copy-done.21, bf16[288,512]{1,0:T(8,128)(2,1)} %copy-done.22, bf16[288,512]{1,0:T(8,128)(2,1)S(1)} %get-tuple-element.32, ...), kind=kOutput, calls=%fused_computation.66 | convolution fusion | flops 2422407168 | bytes 13107200 | tf_op jit(solution)/shard_map/dot_general | solution.py:60
  150.4 3.0 %select_bitcast_fusion.12 = (f32[1,288,512]{2,1,0:T(8,128)}, f32[1,288,512]{2,1,0:T(8,128)}, f32[1,288,512]{2,1,0:T(8,128)S(1)}, f32[1,288,512]{2,1,0:T(8,128)S(1)}) fusion(f32[288,2048]{1,0:T(8,128)} %fusion.19, pred[]{:T(512)S(6)} %eq.27), kind=kLoop, calls=%fused_computation.79 | loop fusion | flops 589824 | bytes 4718593 | tf_op jit(solution)/shard_map/stack | solution.py:67
  156.3 2.7 %fusion.51 = f32[336,1024]{1,0:T(8,128)} fusion(bf16[2048,1024]{1,0:T(8,128)(2,1)S(1)} %copy-done.44, bf16[336,512]{1,0:T(8,128)(2,1)S(1)} %get-tuple-element.25, bf16[336,512]{1,0:T(8,128)(2,1)S(1)} %get-tuple-element.26, bf16[336,512]{1,0:T(8,128)(2,1)S(1)} %get-tuple-element.24, bf16[336,512]{1,0:T(8,128)(2,1)S(1)} %get-tuple-element.23), kind=kOutput, calls=%fused_computation.146 | convolution fusion | flops 1414791168 | bytes 6946816 | tf_op jit(solution)/shard_map/dot_general | solution.py:204
  159.0 8.5 %fusion.18 = f32[336,2048]{1,0:T(8,128)} fusion(bf16[1024,2048]{1,0:T(8,128)(2,1)} %param.27, bf16[2048,1024]{1,0:T(8,128)(2,1)} %param.26, f32[336,1024]{1,0:T(8,128)} %fusion.51, bf16[336,512]{1,0:T(8,128)(2,1)S(1)} %get-tuple-element.25, bf16[336,512]{1,0:T(8,128)(2,1)S(1)} %get-tuple-element.26, bf16[336,512]{1,0:T(8,128)(2,1)S(1)} %get-tuple-element.24, ...), kind=kOutput, calls=%fused_computation.65 | convolution fusion | flops 2826141696 | bytes 13893632 | tf_op jit(solution)/shard_map/dot_general | solution.py:60
  167.4 3.1 %select_bitcast_fusion.3 = (f32[1,336,512]{2,1,0:T(8,128)}, f32[1,336,512]{2,1,0:T(8,128)}, f32[1,336,512]{2,1,0:T(8,128)S(1)}, f32[1,336,512]{2,1,0:T(8,128)S(1)}) fusion(f32[336,2048]{1,0:T(8,128)} %fusion.18, pred[]{:T(512)S(6)} %eq.27), kind=kLoop, calls=%fused_computation.56 | loop fusion | flops 688128 | bytes 5505025 | tf_op jit(solution)/shard_map/stack | solution.py:67
  174.3 1.6 maximum_add_fusion.3
  176.4 1.6 maximum_add_fusion.1
  178.2 1.7 collective-permute-start.9
  180.9 5.0 %collective-permute-done.19 = bf16[288,512]{1,0:T(8,128)(2,1)S(1)} collective-permute-done((bf16[288,512]{1,0:T(8,128)(2,1)S(1)}, bf16[288,512]{1,0:T(8,128)(2,1)S(1)}, u32[]{:S(2)}, u32[]{:S(2)}) %collective-permute-start.19) | collective-permute-done | bytes 294944 | tf_op jit(solution)/shard_map/ppermute | solution.py:41
  186.1 6.6 %collective-permute-done.9 = bf16[336,512]{1,0:T(8,128)(2,1)S(1)} collective-permute-done((bf16[336,512]{1,0:T(8,128)(2,1)S(1)}, bf16[336,512]{1,0:T(8,128)(2,1)S(1)}, u32[]{:S(2)}, u32[]{:S(2)}) %collective-permute-start.9) | collective-permute-done | bytes 344096 | tf_op jit(solution)/shard_map/ppermute | solution.py:41
  (248 shorter events, 61.4 us)
Async XLA Ops:
  0.6 53.2 %copy-start = (bf16[512,2048]{1,0:T(8,128)(2,1)S(1)}, bf16[512,2048]{1,0:T(8,128)(2,1)}, u32[]{:S(2)}) copy-start(bf16[512,2048]{1,0:T(8,128)(2,1)} %param.23) | copy-start | bytes 6291460
  0.6 6.3 %copy-start.18 = (bf16[13,16,1024]{2,1,0:T(8,128)(2,1)S(1)}, bf16[13,16,1024]{2,1,0:T(8,128)(2,1)}, u32[]{:S(2)}) copy-start(bf16[13,16,1024]{2,1,0:T(8,128)(2,1)} %param.29) | copy-start | bytes 1277956
  2.7 31.2 %collective-permute-start = (bf16[336,512]{1,0:T(8,128)(2,1)}, bf16[336,512]{1,0:T(8,128)(2,1)}, u32[]{:S(2)}, u32[]{:S(2)}) collective-permute-start(bf16[336,512]{1,0:T(8,128)(2,1)} %get-tuple-element.56), channel_id=1, source_target_pairs={{0,2},{2,0},{1,3},{3,1},{4,6},{6,4},{5,7},{7,5},{8,10},{10,8},{9,1... | collective-permute-start | bytes 1032200 | tf_op jit(solution)/shard_map/ppermute | solution.py:41
  8.9 7.5 %copy-start.49 = (s32[13]{0:T(128)S(1)}, s32[13]{0:T(128)}, u32[]{:S(2)}) copy-start(s32[13]{0:T(128)} %param.17) | copy-start | bytes 160
  8.9 7.7 %copy-start.39 = (s32[13]{0:T(128)S(1)}, s32[13]{0:T(128)}, u32[]{:S(2)}) copy-start(s32[13]{0:T(128)} %param.16) | copy-start | bytes 160
  8.9 12.0 %copy-start.38 = (s32[13]{0:T(128)S(1)}, s32[13]{0:T(128)}, u32[]{:S(2)}) copy-start(s32[13]{0:T(128)} %param.18) | copy-start | bytes 160
  8.9 27.5 %all-to-all-start = ((bf16[2,4,13,16,256]{4,3,2,0,1:T(8,128)(2,1)}), bf16[2,4,13,16,256]{4,3,2,0,1:T(8,128)(2,1)}, u32[]{:S(2)}, u32[]{:S(2)}) async-start(bf16[2,4,13,16,256]{4,3,2,0,1:T(8,128)(2,1)} %copy.86), calls=%async_computation | async-start | bytes 1703936 | tf_op jit(solution)/shard_map/all_to_all | solution.py:118
  13.3 20.6 %copy-start.11 = (bf16[1,336,512]{2,1,0:T(8,128)(2,1)S(1)}, bf16[1,336,512]{2,1,0:T(8,128)(2,1)}, u32[]{:S(2)}) copy-start(bf16[1,336,512]{2,1,0:T(8,128)(2,1)} %get-tuple-element.55) | copy-start | bytes 1032196
  14.3 17.6 %collective-permute-start.10 = (bf16[288,512]{1,0:T(8,128)(2,1)S(1)}, bf16[288,512]{1,0:T(8,128)(2,1)S(1)}, u32[]{:S(2)}, u32[]{:S(2)}) collective-permute-start(bf16[288,512]{1,0:T(8,128)(2,1)S(1)} %get-tuple-element.58), channel_id=1, source_target_pairs={{0,2},{2,0},{1,3},{3,1},{4,6},{6,4},{5,7},{7,5},{8,10},{10,8},{9,1... | collective-permute-start | bytes 884744 | tf_op jit(solution)/shard_map/ppermute | solution.py:41
  33.8 9.5 %collective-permute-start.11 = (bf16[2,288,512]{2,1,0:T(8,128)(2,1)S(1)}, bf16[2,288,512]{2,1,0:T(8,128)(2,1)}, u32[]{:S(2)}, u32[]{:S(2)}) collective-permute-start(bf16[2,288,512]{2,1,0:T(8,128)(2,1)S(1)} %maximum_select_fusion.2), channel_id=1, source_target_pairs={{0,1},{1,0},{2,3},{3,2},{4,5},{5,4},{6,7},{7,6},{8,9},{9,8},{10,11... | collective-permute-start | bytes 1769480 | tf_op jit(solution)/shard_map/ppermute | solution.py:41
  35.9 21.2 %collective-permute-start.1 = (bf16[2,336,512]{2,1,0:T(8,128)(2,1)}, bf16[2,336,512]{2,1,0:T(8,128)(2,1)}, u32[]{:S(2)}, u32[]{:S(2)}) collective-permute-start(bf16[2,336,512]{2,1,0:T(8,128)(2,1)} %maximum_select_fusion), channel_id=1, source_target_pairs={{0,1},{1,0},{2,3},{3,2},{4,5},{5,4},{6,7},{7,6},{8,9},{9,8},{10,11... | collective-permute-start | bytes 2064392 | tf_op jit(solution)/shard_map/ppermute | solution.py:41
  57.1 23.2 %collective-permute-start.12 = (f32[2,288,512]{2,1,0:T(8,128)}, f32[2,288,512]{2,1,0:T(8,128)}, u32[]{:S(2)}, u32[]{:S(2)}) collective-permute-start(f32[2,288,512]{2,1,0:T(8,128)} %pad_maximum_fusion.5), channel_id=1, source_target_pairs={{0,1},{1,0},{2,3},{3,2},{4,5},{5,4},{6,7},{7,6},{8,9},{9,8},{10,11... | collective-permute-start | bytes 3538952 | tf_op jit(solution)/shard_map/ppermute | solution.py:41
  71.5 12.5 %collective-permute-start.2 = (f32[2,336,512]{2,1,0:T(8,128)}, f32[2,336,512]{2,1,0:T(8,128)}, u32[]{:S(2)}, u32[]{:S(2)}) collective-permute-start(f32[2,336,512]{2,1,0:T(8,128)} %pad_maximum_fusion.1), channel_id=1, source_target_pairs={{0,1},{1,0},{2,3},{3,2},{4,5},{5,4},{6,7},{7,6},{8,9},{9,8},{10,11... | collective-permute-start | bytes 4128776 | tf_op jit(solution)/shard_map/ppermute | solution.py:41
  74.1 6.1 %copy-start.8 = (f32[1,288,512]{2,1,0:T(8,128)S(1)}, f32[1,288,512]{2,1,0:T(8,128)}, u32[]{:S(2)}) copy-start(f32[1,288,512]{2,1,0:T(8,128)} %get-tuple-element.20) | copy-start | bytes 1769476
  74.1 32.6 %all-to-all-start.1 = ((bf16[8,2,129,256]{3,1,2,0:T(2,128)(2,1)}), bf16[8,2,129,256]{3,1,2,0:T(2,128)(2,1)}, u32[]{:S(2)}, u32[]{:S(2)}) async-start(bf16[8,2,129,256]{3,1,2,0:T(2,128)(2,1)} %copy.96), calls=%async_computation.1 | async-start | bytes 2113536 | tf_op jit(solution)/shard_map/all_to_all | solution.py:142
  82.7 15.8 %collective-permute-start.13 = (f32[288,512]{1,0:T(8,128)}, f32[288,512]{1,0:T(8,128)}, u32[]{:S(2)}, u32[]{:S(2)}) collective-permute-start(f32[288,512]{1,0:T(8,128)} %select_bitcast_fusion.13), channel_id=1, source_target_pairs={{0,2},{2,0},{1,3},{3,1},{4,6},{6,4},{5,7},{7,5},{8,10},{10,8},{9,1... | collective-permute-start | bytes 1769480 | tf_op jit(solution)/shard_map/ppermute | solution.py:41
  99.8 8.5 %collective-permute-start.14 = (f32[288,1]{0,1:T(1,128)S(1)}, f32[288,1]{0,1:T(1,128)S(1)}, u32[]{:S(2)}, u32[]{:S(2)}) collective-permute-start(f32[288,1]{0,1:T(1,128)S(1)} %broadcast_in_dim.116), channel_id=1, source_target_pairs={{0,1},{1,0},{2,3},{3,2},{4,5},{5,4},{6,7},{7,6},{8,9},{9,8},{10,11... | collective-permute-start | bytes 3464 | tf_op jit(solution)/shard_map/ppermute | solution.py:41
  100.9 18.8 %collective-permute-start.3 = (f32[336,512]{1,0:T(8,128)}, f32[336,512]{1,0:T(8,128)}, u32[]{:S(2)}, u32[]{:S(2)}) collective-permute-start(f32[336,512]{1,0:T(8,128)} %select_bitcast_fusion.4), channel_id=1, source_target_pairs={{0,2},{2,0},{1,3},{3,1},{4,6},{6,4},{5,7},{7,5},{8,10},{10,8},{9,1... | collective-permute-start | bytes 2064392 | tf_op jit(solution)/shard_map/ppermute | solution.py:41
  108.2 11.5 %copy-start.3 = (bf16[8,2,129,256]{3,2,1,0:T(8,128)(2,1)}, bf16[8,2,129,256]{3,2,1,0:T(8,128)(2,1)S(1)}, u32[]{:S(2)}) copy-start(bf16[8,2,129,256]{3,2,1,0:T(8,128)(2,1)S(1)} %copy.97) | copy-start | bytes 3170308
  108.3 10.7 %collective-permute-start.15 = (f32[288,1]{0,1:T(1,128)S(1)}, f32[288,1]{0,1:T(1,128)S(1)}, u32[]{:S(2)}, u32[]{:S(2)}) collective-permute-start(f32[288,1]{0,1:T(1,128)S(1)} %reshape_add_fusion.1), channel_id=1, source_target_pairs={{0,2},{2,0},{1,3},{3,1},{4,6},{6,4},{5,7},{7,5},{8,10},{10,8},{9,1... | collective-permute-start | bytes 3464 | tf_op jit(solution)/shard_map/ppermute | solution.py:41
  119.2 8.7 %collective-permute-start.16 = (bf16[288,512]{1,0:T(8,128)(2,1)S(1)}, bf16[288,512]{1,0:T(8,128)(2,1)S(1)}, u32[]{:S(2)}, u32[]{:S(2)}) collective-permute-start(bf16[288,512]{1,0:T(8,128)(2,1)S(1)} %multiply_convert_fusion.1), channel_id=1, source_target_pairs={{0,2},{2,0},{1,3},{3,1},{4,6},{6,4},{5,7},{7,5},{8,10},{10,8},{9,1... | collective-permute-start | bytes 884744 | tf_op jit(solution)/shard_map/ppermute | solution.py:41
  121.0 1.2 collective-permute-start.4
  122.3 5.8 %collective-permute-start.5 = (f32[336,1]{0,1:T(1,128)S(1)}, f32[336,1]{0,1:T(1,128)S(1)}, u32[]{:S(2)}, u32[]{:S(2)}) collective-permute-start(f32[336,1]{0,1:T(1,128)S(1)} %reshape_add_fusion), channel_id=1, source_target_pairs={{0,2},{2,0},{1,3},{3,1},{4,6},{6,4},{5,7},{7,5},{8,10},{10,8},{9,1... | collective-permute-start | bytes 4040 | tf_op jit(solution)/shard_map/ppermute | solution.py:41
  128.0 11.0 %collective-permute-start.17 = (bf16[2,288,512]{2,1,0:T(8,128)(2,1)S(1)}, bf16[2,288,512]{2,1,0:T(8,128)(2,1)S(1)}, u32[]{:S(2)}, u32[]{:S(2)}) collective-permute-start(bf16[2,288,512]{2,1,0:T(8,128)(2,1)S(1)} %maximum_select_fusion.3), channel_id=1, source_target_pairs={{0,1},{1,0},{2,3},{3,2},{4,5},{5,4},{6,7},{7,6},{8,9},{9,8},{10,11... | collective-permute-start | bytes 1769480 | tf_op jit(solution)/shard_map/ppermute | solution.py:41
  128.3 10.5 %collective-permute-start.6 = (bf16[336,512]{1,0:T(8,128)(2,1)S(1)}, bf16[336,512]{1,0:T(8,128)(2,1)S(1)}, u32[]{:S(2)}, u32[]{:S(2)}) collective-permute-start(bf16[336,512]{1,0:T(8,128)(2,1)S(1)} %multiply_convert_fusion), channel_id=1, source_target_pairs={{0,2},{2,0},{1,3},{3,1},{4,6},{6,4},{5,7},{7,5},{8,10},{10,8},{9,1... | collective-permute-start | bytes 1032200 | tf_op jit(solution)/shard_map/ppermute | solution.py:41
  128.7 11.2 %copy-start.43 = (bf16[2048,1024]{1,0:T(8,128)(2,1)S(1)}, bf16[2048,1024]{1,0:T(8,128)(2,1)}, u32[]{:S(2)}) copy-start(bf16[2048,1024]{1,0:T(8,128)(2,1)} %param.25) | copy-start | bytes 12582916
  138.9 16.1 %collective-permute-start.7 = (bf16[2,336,512]{2,1,0:T(8,128)(2,1)S(1)}, bf16[2,336,512]{2,1,0:T(8,128)(2,1)}, u32[]{:S(2)}, u32[]{:S(2)}) collective-permute-start(bf16[2,336,512]{2,1,0:T(8,128)(2,1)S(1)} %maximum_select_fusion.1), channel_id=1, source_target_pairs={{0,1},{1,0},{2,3},{3,2},{4,5},{5,4},{6,7},{7,6},{8,9},{9,8},{10,11... | collective-permute-start | bytes 2064392 | tf_op jit(solution)/shard_map/ppermute | solution.py:41
  154.5 18.7 %collective-permute-start.18 = (f32[2,288,512]{2,1,0:T(8,128)}, f32[2,288,512]{2,1,0:T(8,128)}, u32[]{:S(2)}, u32[]{:S(2)}) collective-permute-start(f32[2,288,512]{2,1,0:T(8,128)} %pad_maximum_fusion.7), channel_id=1, source_target_pairs={{0,1},{1,0},{2,3},{3,2},{4,5},{5,4},{6,7},{7,6},{8,9},{9,8},{10,11... | collective-permute-start | bytes 3538952 | tf_op jit(solution)/shard_map/ppermute | solution.py:41
  171.8 4.7 %collective-permute-start.8 = (f32[2,336,512]{2,1,0:T(8,128)}, f32[2,336,512]{2,1,0:T(8,128)}, u32[]{:S(2)}, u32[]{:S(2)}) collective-permute-start(f32[2,336,512]{2,1,0:T(8,128)} %pad_maximum_fusion.3), channel_id=1, source_target_pairs={{0,1},{1,0},{2,3},{3,2},{4,5},{5,4},{6,7},{7,6},{8,9},{9,8},{10,11... | collective-permute-start | bytes 4128776 | tf_op jit(solution)/shard_map/ppermute | solution.py:41
  176.0 9.9 %collective-permute-start.19 = (bf16[288,512]{1,0:T(8,128)(2,1)S(1)}, bf16[288,512]{1,0:T(8,128)(2,1)S(1)}, u32[]{:S(2)}, u32[]{:S(2)}) collective-permute-start(bf16[288,512]{1,0:T(8,128)(2,1)S(1)} %fusion.42), channel_id=1, source_target_pairs={{0,2},{2,0},{1,3},{3,1},{4,6},{6,4},{5,7},{7,5},{8,10},{10,8},{9,1... | collective-permute-start | bytes 884744 | tf_op jit(solution)/shard_map/ppermute | solution.py:41
  178.2 14.5 %collective-permute-start.9 = (bf16[336,512]{1,0:T(8,128)(2,1)S(1)}, bf16[336,512]{1,0:T(8,128)(2,1)S(1)}, u32[]{:S(2)}, u32[]{:S(2)}) collective-permute-start(bf16[336,512]{1,0:T(8,128)(2,1)S(1)} %fusion.31), channel_id=1, source_target_pairs={{0,2},{2,0},{1,3},{3,1},{4,6},{6,4},{5,7},{7,5},{8,10},{10,8},{9,1... | collective-permute-start | bytes 1032200 | tf_op jit(solution)/shard_map/ppermute | solution.py:41
  185.9 7.9 %copy-start.1 = (bf16[512,2048]{1,0:T(8,128)(2,1)S(1)}, bf16[512,2048]{1,0:T(8,128)(2,1)}, u32[]{:S(2)}) copy-start(bf16[512,2048]{1,0:T(8,128)(2,1)} %param.23) | copy-start | bytes 6291460
  (41 other events, 84.2 us)

commit v7 on v5

--- a/solution.py
+++ b/solution.py
@@ -54,7 +54,7 @@
     return jnp.concatenate(blocks, axis=1)
 
 
-def scatter_features(matrix_in, weight, link_type=None):
+def scatter_features(matrix_in, weight, link_type=None, ride=None):
     chip = lax.axis_index("kvy")
     core = lax.axis_index("core")
     product = jnp.dot(matrix_in, weight, preferred_element_type=jnp.float32)
@@ -71,7 +71,14 @@
     theirs = jnp.where(chip == 0, chip_sum[1], chip_sum[0])
     if link_type is not None:
         theirs = theirs.astype(link_type)
-    return mine + swap(theirs, "kvy").astype(jnp.float32)
+    if ride is None:
+        return mine + swap(theirs, "kvy").astype(jnp.float32)
+    ride_input, work = ride
+    ride_input, theirs = lax.optimization_barrier((ride_input, theirs))
+    arrived = swap(theirs, "kvy")
+    ride_output = work(ride_input)
+    ride_output, arrived = lax.optimization_barrier((ride_output, arrived))
+    return mine + arrived.astype(jnp.float32), ride_output
 
 
 def row_scale(values, gain_share):
@@ -132,23 +139,26 @@
     matches = buffer_place[None, :] == buffer_ids[:, None]
     picked = jnp.sum(jnp.where(matches, order_ids[None, :], 0), axis=1)
     filled = jnp.any(matches, axis=1)
-    lanes = local_kv * HEAD_WIDTH
-    slot_code = jnp.stack([decode_slot // 16, decode_slot % 16], axis=1).astype(jnp.bfloat16)
-    trailer = jnp.pad(slot_code, ((0, 0), (0, lanes - 2)))[:, None, :]
-    payload = jnp.concatenate([head_kv[0], head_kv[1], trailer], axis=1)
-    packed = jnp.take(payload, picked, axis=0)
-    packed = jnp.where(filled[:, None, None], packed, -jnp.ones((), packed.dtype))
-    packed = packed.reshape((req_count, capacity) + payload.shape[1:])
-    landed = lax.all_to_all(packed, "req", split_axis=0, concat_axis=0, tiled=True)
-    landed = landed.reshape((req_count * capacity,) + payload.shape[1:])
-    code = landed[:, 2 * past_size, :2].astype(jnp.int32)
-    landed_slots = code[:, 0] * 16 + code[:, 1]
-    wanted = req_index * request_list + order_ids
-    slot_hits = landed_slots[None, :] == wanted[:, None]
-    entry_ids = jnp.arange(req_count * capacity, dtype=jnp.int32)
-    slot_position = jnp.sum(jnp.where(slot_hits, entry_ids[None, :], 0), axis=1)
-    decode_rows = jnp.take(landed, slot_position, axis=0)
-    decode_kv = (decode_rows[:, :past_size], decode_rows[:, past_size:2 * past_size])
+    def hand_off(ride_input):
+        head_kv, decode_slot, picked, filled = ride_input
+        lanes = local_kv * HEAD_WIDTH
+        slot_code = jnp.stack([decode_slot // 16, decode_slot % 16], axis=1).astype(jnp.bfloat16)
+        trailer = jnp.pad(slot_code, ((0, 0), (0, lanes - 2)))[:, None, :]
+        payload = jnp.concatenate([head_kv[0], head_kv[1], trailer], axis=1)
+        packed = jnp.take(payload, picked, axis=0)
+        packed = jnp.where(filled[:, None, None], packed, -jnp.ones((), packed.dtype))
+        packed = packed.reshape((req_count, capacity) + payload.shape[1:])
+        landed = lax.all_to_all(packed, "req", split_axis=0, concat_axis=0, tiled=True)
+        landed = landed.reshape((req_count * capacity,) + payload.shape[1:])
+        code = landed[:, 2 * past_size, :2].astype(jnp.int32)
+        landed_slots = code[:, 0] * 16 + code[:, 1]
+        wanted = req_index * request_list + order_ids
+        slot_hits = landed_slots[None, :] == wanted[:, None]
+        entry_ids = jnp.arange(req_count * capacity, dtype=jnp.int32)
+        slot_position = jnp.sum(jnp.where(slot_hits, entry_ids[None, :], 0), axis=1)
+        decode_rows = jnp.take(landed, slot_position, axis=0)
+        return decode_rows[:, :past_size], decode_rows[:, past_size:2 * past_size]
+
 
     x_whole = gather_features(activations)
     x_float = x_whole.astype(jnp.float32)
@@ -191,7 +201,9 @@
         "rkgcs,rskd->rckgd", weights, combined_values, preferred_element_type=jnp.float32
     )
     mixed_heads = mixed_heads.astype(jnp.bfloat16).reshape(total_rows, local_q * HEAD_WIDTH)
-    head_share = scatter_features(mixed_heads, output_weight)
+    head_share, decode_kv = scatter_features(
+        mixed_heads, output_weight, ride=((head_kv, decode_slot, picked, filled), hand_off)
+    )
     residual_share = activations.astype(jnp.float32) + head_share
 
     gain_share = lax.dynamic_slice_in_dim(feedforward_gain, kv_index * width_share, width_share)

time: 178 us -> 185 us (1.039)
  waiting for transfers between devices: 73.3 us -> 77.9 us
  other arithmetic: 30.8 us -> 34.8 us
    all_to_all x1, waiting for transfers between devices: 0.02 us -> 24.8 us  [hand_off(): lax.all_to_all(packed, 'req', split_axis=0, concat_axis=0, tiled=True)]
    ppermute x10, waiting for transfers between devices: 69.3 us -> 49.6 us  [swap(): return lax.ppermute(values, axis_name, [(0, 1), (1, 0)])]
    convert_element_type x1, other arithmetic: 0.11 us -> 2.63 us  [scatter_features(): theirs = theirs.astype(link_type)]
    reduce_sum x1, other arithmetic: 0.36 us -> 2.69 us  [row_scale(): square_sum = jnp.sum(values * values, axis=-1, keepdims=True)]
    gather x2, local copies, waits for them, and re-layouts: 5.59 us -> 3.47 us  [the longest x1 1.85 us: hand_off(): decode_rows = jnp.take(landed, slot_position, axis=0)]
    unnamed x46 -> x40, local copies, waits for them, and re-layouts: 6.01 us -> 5.39 us
  transfers between devices with their start and end apart: 12 -> 12, of which waited for: 8 -> 10; matrix products, arithmetic and copies ran while one was open for 29% -> 9% of each run, Pallas kernels for 0% -> 0%
where the time goes in v7:
time: 185 us; the launch traced here: 184 us
  waiting for transfers between devices  77.9 us (42%)
  other arithmetic  34.8 us (19%)
  local copies, waits for them, and re-layouts  26 us (14%)
  matrix products  24.5 us (13%)
  starting transfers between devices  20 us (11%)
    ppermute x10, waiting for transfers between devices, swap(): return lax.ppermute(values, axis_name, [(0, 1), (1, 0)])  49.6 us
    all_to_all x1, waiting for transfers between devices, hand_off(): lax.all_to_all(packed, 'req', split_axis=0, concat_axis=0, tiled=True)  24.8 us
    dot_general x2, matrix products, scatter_features(): product = jnp.dot(matrix_in, weight, preferred_element_type=jnp.float32)  13.7 us
    ppermute x10, starting transfers between devices, swap(): return lax.ppermute(values, axis_name, [(0, 1), (1, 0)])  9.59 us
    all_to_all x1, starting transfers between devices, hand_off(): lax.all_to_all(packed, 'req', split_axis=0, concat_axis=0, tiled=True)  6.01 us
    unnamed x40, local copies, waits for them, and re-layouts  5.39 us
    all_to_all x1, starting transfers between devices, local(): lax.all_to_all(stacked, ('kvy', 'core'), split_axis=1, concat_axis=1, til...  4.35 us
    dot_general x1, matrix products, local(): jnp.dot(normed_two, gate_weight, preferred_element_type=jnp.float32)  4.25 us
  transfers between devices with their start and end apart: 12, of which 10 were waited for; matrix products, arithmetic and copies ran while one was open for 9% of the time, Pallas kernels for 0%

profile of v7, /device:TPU:0, one launch (start us, length us, event | category | flops | bytes accessed | tf_op | source)
XLA Modules:
  0.0 184.2 jit_solution(14832835484982761400)
XLA Ops:
  0.6 3.0 %collective-permute-start = (bf16[624,512]{1,0:T(8,128)(2,1)}, bf16[624,512]{1,0:T(8,128)(2,1)}, u32[]{:S(2)}, u32[]{:S(2)}) collective-permute-start(bf16[624,512]{1,0:T(8,128)(2,1)} %param.15), channel_id=1, source_target_pairs={{0,2},{2,0},{1,3},{3,1},{4,6},{6,4},{5,7},{7,5},{8,10},{10,8},{9,1... | collective-permute-start | bytes 1916936 | tf_op jit(solution)/shard_map/ppermute | solution.py:41
  8.0 4.3 %all-to-all-start = ((bf16[2,4,13,16,256]{4,3,2,0,1:T(8,128)(2,1)}), bf16[2,4,13,16,256]{4,3,2,0,1:T(8,128)(2,1)}, u32[]{:S(2)}, u32[]{:S(2)}) async-start(bf16[2,4,13,16,256]{4,3,2,0,1:T(8,128)(2,1)} %copy.70), calls=%async_computation | async-start | bytes 1703936 | tf_op jit(solution)/shard_map/all_to_all | solution.py:125
  12.4 6.8 %collective-permute-done = bf16[624,512]{1,0:T(8,128)(2,1)} collective-permute-done((bf16[624,512]{1,0:T(8,128)(2,1)}, bf16[624,512]{1,0:T(8,128)(2,1)}, u32[]{:S(2)}, u32[]{:S(2)}) %collective-permute-start) | collective-permute-done | bytes 639008 | tf_op jit(solution)/shard_map/ppermute | solution.py:41
  19.2 2.6 %maximum_select_fusion = bf16[2,624,512]{2,1,0:T(8,128)(2,1)} fusion(bf16[1,624,512]{2,1,0:T(8,128)(2,1)} %bitcast.4, bf16[1,624,512]{2,1,0:T(8,128)(2,1)S(1)} %bitcast.134, pred[]{:T(512)S(6)} %eq.25), kind=kLoop, calls=%fused_computation.15 | loop fusion | flops 1916928 | bytes 2555905 | tf_op jit(solution)/shard_map/jit(_where)/select_n | solution.py:48
  22.0 2.0 %multiply_cosine_fusion = (f32[13,48,128]{2,1,0:T(8,128)S(1)}, f32[13,48,128]{2,1,0:T(8,128)}) fusion(f32[128]{0:T(128)S(1)} %multiply_exponential_fusion, f32[13,48]{1,0:T(8,128)S(1)} %iota_add_fusion), kind=kLoop, calls=%fused_computation.71 | loop fusion | flops 79872 | bytes 641984 | tf_op jit(solution)/shard_map/cos | solution.py:22
  24.0 3.6 %all-to-all-done = bf16[2,4,13,16,256]{4,3,2,0,1:T(8,128)(2,1)} async-done(((bf16[2,4,13,16,256]{4,3,2,0,1:T(8,128)(2,1)}), bf16[2,4,13,16,256]{4,3,2,0,1:T(8,128)(2,1)}, u32[]{:S(2)}, u32[]{:S(2)}) %all-to-all-start) | async-done | bytes 852000 | tf_op jit(solution)/shard_map/all_to_all | solution.py:125
  29.7 1.8 select_bitcast_fusion.16
  31.6 2.0 %fusion = f32[624]{0:T(1024)S(1)} fusion(bf16[624,512]{1,0:T(8,128)(2,1)S(1)} %get-tuple-element.35, bf16[624,512]{1,0:T(8,128)(2,1)S(1)} %get-tuple-element.36, bf16[624,512]{1,0:T(8,128)(2,1)S(1)} %get-tuple-element.34, bf16[624,512]{1,0:T(8,128)(2,1)S(1)} %get-tuple-element.33), kind=kLoop, calls=%fused_computation.4 | loop fusion | flops 12778896 | bytes 2558400 | tf_op jit(solution)/shard_map/reduce_sum | solution.py:165
  36.0 2.5 %fusion.54 = f32[624,512]{1,0:T(8,128)} fusion(bf16[624,2048]{1,0:T(8,128)(2,1)S(1)} %fusion.2, bf16[2048,512]{1,0:T(8,128)(2,1)S(1)} %copy-done.15), kind=kOutput, calls=%fused_computation.141 | convolution fusion | flops 1308622848 | bytes 5931008 | tf_op jit(solution)/shard_map/dot_general | solution.py:172
  38.6 2.9 %reshape.300 = f32[13,48,2,256]{3,2,1,0:T(2,128)} reshape(f32[624,512]{1,0:T(8,128)} %fusion.54) | data formatting | bytes 2555904 | tf_op jit(solution)/shard_map/reshape | solution.py:174
  43.6 2.2 %fusion.53 = f32[624,256]{1,0:T(8,128)S(1)} fusion(bf16[624,2048]{1,0:T(8,128)(2,1)S(1)} %copy-done.7, bf16[2048,256]{1,0:T(8,128)(2,1)} %param.21), kind=kOutput, calls=%fused_computation.140 | convolution fusion | flops 654311424 | bytes 4243456 | tf_op jit(solution)/shard_map/dot_general | solution.py:176
  45.7 1.6 fusion.28
  51.4 1.5 fusion.55
  54.9 4.0 %collective-permute-done.2 = f32[2,624,512]{2,1,0:T(8,128)S(1)} collective-permute-done((f32[2,624,512]{2,1,0:T(8,128)S(1)}, f32[2,624,512]{2,1,0:T(8,128)S(1)}, u32[]{:S(2)}, u32[]{:S(2)}) %collective-permute-start.2) | collective-permute-done | bytes 2555936 | tf_op jit(solution)/shard_map/ppermute | solution.py:41
  63.4 1.6 gather_fusion
  66.6 1.8 copy.77
  68.4 6.0 %all-to-all-start.1 = ((bf16[8,2,129,256]{3,1,2,0:T(2,128)(2,1)}), bf16[8,2,129,256]{3,1,2,0:T(2,128)(2,1)}, u32[]{:S(2)}, u32[]{:S(2)}) async-start(bf16[8,2,129,256]{3,1,2,0:T(2,128)(2,1)} %copy.77), calls=%async_computation.1 | async-start | bytes 2113536 | tf_op jit(solution)/shard_map/all_to_all | solution.py:151
  74.4 1.6 collective-permute-start.3
  76.0 24.8 %all-to-all-done.1 = bf16[8,2,129,256]{3,1,2,0:T(2,128)(2,1)} async-done(((bf16[8,2,129,256]{3,1,2,0:T(2,128)(2,1)}), bf16[8,2,129,256]{3,1,2,0:T(2,128)(2,1)}, u32[]{:S(2)}, u32[]{:S(2)}) %all-to-all-start.1) | async-done | bytes 1056800 | tf_op jit(solution)/shard_map/all_to_all | solution.py:151
  103.4 1.9 %gather_fusion.1 = bf16[13,129,256]{2,1,0:T(8,128)(2,1)S(1)} fusion(bf16[16,129,256]{2,1,0:T(8,128)(2,1)} %bitcast.132, s32[1024]{0:T(1024)S(1)} %pad_clamp_fusion), kind=kCustom, calls=%fused_computation.1 | custom fusion | bytes 1717300 | tf_op jit(solution)/shard_map/jit(_take)/gather | solution.py:159
  106.5 2.7 %multiply_reduce_fusion = (f32[624]{0:T(1024)S(1)}, f32[624,512]{1,0:T(8,128)}) fusion(f32[624,512]{1,0:T(8,128)} %collective-permute-done.3, f32[2,624,512]{2,1,0:T(8,128)S(1)} %maximum_add_fusion, pred[]{:T(512)S(6)} %eq.25, bf16[624,512]{1,0:T(8,128)(2,1)S(1)} %copy-done.5), kind=kLoop, calls=%fused_computation.29 | loop fusion | flops 1916304 | bytes 5753281 | tf_op jit(solution)/shard_map/reduce_sum | solution.py:85
  115.5 1.6 collective-permute-start.6
  117.2 13.6 %collective-permute-done.6 = bf16[624,512]{1,0:T(8,128)(2,1)S(1)} collective-permute-done((bf16[624,512]{1,0:T(8,128)(2,1)S(1)}, bf16[624,512]{1,0:T(8,128)(2,1)S(1)}, u32[]{:S(2)}, u32[]{:S(2)}) %collective-permute-start.6) | collective-permute-done | bytes 639008 | tf_op jit(solution)/shard_map/ppermute | solution.py:41
  131.1 3.0 %collective-permute-done.7 = bf16[2,624,512]{2,1,0:T(8,128)(2,1)S(1)} collective-permute-done((bf16[2,624,512]{2,1,0:T(8,128)(2,1)S(1)}, bf16[2,624,512]{2,1,0:T(8,128)(2,1)S(1)}, u32[]{:S(2)}, u32[]{:S(2)}) %collective-permute-start.7) | collective-permute-done | bytes 1277984 | tf_op jit(solution)/shard_map/ppermute | solution.py:41
  135.1 4.3 %fusion.26 = f32[624,1024]{1,0:T(8,128)} fusion(bf16[2048,1024]{1,0:T(8,128)(2,1)S(1)} %copy-done.14, bf16[624,512]{1,0:T(8,128)(2,1)S(1)} %get-tuple-element.31, bf16[624,512]{1,0:T(8,128)(2,1)S(1)} %get-tuple-element.32, bf16[624,512]{1,0:T(8,128)(2,1)S(1)} %get-tuple-element.30, bf16[624,512]{1,0:T(8,128)(2,1)S(1)} %get-tuple-element.29), kind=kOutput, calls=%fused_computation.78 | convolution fusion | flops 2627469312 | bytes 9306112 | tf_op jit(solution)/shard_map/dot_general | solution.py:212
  139.4 12.2 %fusion.16 = f32[624,2048]{1,0:T(8,128)} fusion(bf16[1024,2048]{1,0:T(8,128)(2,1)} %param.27, f32[624,1024]{1,0:T(8,128)} %fusion.26, bf16[2048,1024]{1,0:T(8,128)(2,1)} %param.26, bf16[624,512]{1,0:T(8,128)(2,1)S(1)} %get-tuple-element.31, bf16[624,512]{1,0:T(8,128)(2,1)} %copy-done.9, bf16[624,512]{1,0:T(8,128)(2,1)S(1)} %get-tuple-element.30, ...), kind=kOutput, calls=%fused_computation.52 | convolution fusion | flops 5248548864 | bytes 18612224 | tf_op jit(solution)/shard_map/dot_general | solution.py:60
  151.6 3.1 %select_bitcast_fusion.3 = (f32[1,624,512]{2,1,0:T(8,128)S(1)}, f32[1,624,512]{2,1,0:T(8,128)S(1)}, f32[1,624,512]{2,1,0:T(8,128)S(1)}, f32[1,624,512]{2,1,0:T(8,128)S(1)}) fusion(f32[624,2048]{1,0:T(8,128)} %fusion.16, pred[]{:T(512)S(6)} %eq.27), kind=kLoop, calls=%fused_computation.27 | loop fusion | flops 1277952 | bytes 10223617 | tf_op jit(solution)/shard_map/stack | solution.py:67
  155.1 4.7 %collective-permute-done.8 = f32[2,624,512]{2,1,0:T(8,128)S(1)} collective-permute-done((f32[2,624,512]{2,1,0:T(8,128)S(1)}, f32[2,624,512]{2,1,0:T(8,128)S(1)}, u32[]{:S(2)}, u32[]{:S(2)}) %collective-permute-start.8) | collective-permute-done | bytes 2555936 | tf_op jit(solution)/shard_map/ppermute | solution.py:41
  159.8 2.1 %maximum_add_fusion.1 = f32[2,624,512]{2,1,0:T(8,128)} fusion(f32[2,624,512]{2,1,0:T(8,128)S(1)} %collective-permute-done.8, f32[1,624,512]{2,1,0:T(8,128)S(1)} %get-tuple-element.22, f32[1,624,512]{2,1,0:T(8,128)S(1)} %get-tuple-element.21), kind=kLoop, calls=%fused_computation.11 | loop fusion | flops 1277952 | bytes 7667712 | tf_op jit(solution)/shard_map/add | solution.py:69
  161.9 2.6 %fusion.17 = bf16[624,512]{1,0:T(8,128)(2,1)} fusion(f32[2,624,512]{2,1,0:T(8,128)} %maximum_add_fusion.1, pred[]{:T(512)S(6)} %eq.25), kind=kLoop, calls=%fused_computation.53 | loop fusion | flops 319488 | bytes 1916929 | tf_op jit(solution)/shard_map/convert_element_type | solution.py:73
  166.2 15.1 %collective-permute-done.9 = bf16[624,512]{1,0:T(8,128)(2,1)} collective-permute-done((bf16[624,512]{1,0:T(8,128)(2,1)}, bf16[624,512]{1,0:T(8,128)(2,1)}, u32[]{:S(2)}, u32[]{:S(2)}) %collective-permute-start.9) | collective-permute-done | bytes 639008 | tf_op jit(solution)/shard_map/ppermute | solution.py:41
  181.2 3.0 %fusion.5 = bf16[624,512]{1,0:T(8,128)(2,1)} fusion(f32[624,512]{1,0:T(8,128)S(1)} %copy-done.2, bf16[624,512]{1,0:T(8,128)(2,1)} %collective-permute-done.9, f32[2,624,512]{2,1,0:T(8,128)} %maximum_add_fusion.1, pred[624]{0:T(1024)(128)(4,1)S(1)} %lt.93, pred[]{:T(512)S(6)} %eq.25), kind=kLoop, calls=%fused_computation.20 | loop fusion | flops 1916928 | bytes 5112433 | tf_op jit(solution)/shard_map/convert_element_type | solution.py:219
  (116 shorter events, 36.8 us)
Async XLA Ops:
  0.6 50.8 %copy-start = (bf16[512,2048]{1,0:T(8,128)(2,1)S(1)}, bf16[512,2048]{1,0:T(8,128)(2,1)}, u32[]{:S(2)}) copy-start(bf16[512,2048]{1,0:T(8,128)(2,1)} %param.23) | copy-start | bytes 6291460
  0.6 18.6 %collective-permute-start = (bf16[624,512]{1,0:T(8,128)(2,1)}, bf16[624,512]{1,0:T(8,128)(2,1)}, u32[]{:S(2)}, u32[]{:S(2)}) collective-permute-start(bf16[624,512]{1,0:T(8,128)(2,1)} %param.15), channel_id=1, source_target_pairs={{0,2},{2,0},{1,3},{3,1},{4,6},{6,4},{5,7},{7,5},{8,10},{10,8},{9,1... | collective-permute-start | bytes 1916936 | tf_op jit(solution)/shard_map/ppermute | solution.py:41
  6.9 5.4 %copy-start.17 = (s32[13]{0:T(128)S(1)}, s32[13]{0:T(128)}, u32[]{:S(2)}) copy-start(s32[13]{0:T(128)} %param.17) | copy-start | bytes 160
  7.0 12.3 %copy-start.4 = (bf16[624,512]{1,0:T(8,128)(2,1)S(1)}, bf16[624,512]{1,0:T(8,128)(2,1)}, u32[]{:S(2)}) copy-start(bf16[624,512]{1,0:T(8,128)(2,1)} %param.15) | copy-start | bytes 1916932
  8.0 13.9 %copy-start.13 = (s32[13]{0:T(128)S(1)}, s32[13]{0:T(128)}, u32[]{:S(2)}) copy-start(s32[13]{0:T(128)} %param.16) | copy-start | bytes 160
  8.0 19.5 %all-to-all-start = ((bf16[2,4,13,16,256]{4,3,2,0,1:T(8,128)(2,1)}), bf16[2,4,13,16,256]{4,3,2,0,1:T(8,128)(2,1)}, u32[]{:S(2)}, u32[]{:S(2)}) async-start(bf16[2,4,13,16,256]{4,3,2,0,1:T(8,128)(2,1)} %copy.70), calls=%async_computation | async-start | bytes 1703936 | tf_op jit(solution)/shard_map/all_to_all | solution.py:125
  21.8 8.0 %collective-permute-start.1 = (bf16[2,624,512]{2,1,0:T(8,128)(2,1)}, bf16[2,624,512]{2,1,0:T(8,128)(2,1)}, u32[]{:S(2)}, u32[]{:S(2)}) collective-permute-start(bf16[2,624,512]{2,1,0:T(8,128)(2,1)} %maximum_select_fusion), channel_id=1, source_target_pairs={{0,1},{1,0},{2,3},{3,2},{4,5},{5,4},{6,7},{7,6},{8,9},{9,8},{10,11... | collective-permute-start | bytes 3833864 | tf_op jit(solution)/shard_map/ppermute | solution.py:41
  31.6 2.1 %copy-start.12 = (f32[2048]{0:T(1024)S(1)}, f32[2048]{0:T(1024)}, u32[]{:S(2)}) copy-start(f32[2048]{0:T(1024)} %param.19) | copy-start | bytes 24580
  33.6 2.4 %copy-start.15 = (bf16[2048,512]{1,0:T(8,128)(2,1)S(1)}, bf16[2048,512]{1,0:T(8,128)(2,1)}, u32[]{:S(2)}) copy-start(bf16[2048,512]{1,0:T(8,128)(2,1)} %param.20) | copy-start | bytes 6291460
  34.5 1.5 copy-start.6
  41.5 2.1 %copy-start.7 = (bf16[624,2048]{1,0:T(8,128)(2,1)S(1)}, bf16[624,2048]{1,0:T(8,128)(2,1)}, u32[]{:S(2)}) copy-start(bf16[624,2048]{1,0:T(8,128)(2,1)} %copy-done.6) | copy-start | bytes 7667716
  43.6 3.7 %copy-start.16 = (bf16[2048,256]{1,0:T(8,128)(2,1)S(1)}, bf16[2048,256]{1,0:T(8,128)(2,1)}, u32[]{:S(2)}) copy-start(bf16[2048,256]{1,0:T(8,128)(2,1)} %param.22) | copy-start | bytes 3145732
  47.3 1.0 copy-start.8
  48.2 1.0 copy-start.11
  49.2 1.0 copy-start.10
  53.8 0.7 copy-start.18
  54.1 4.9 %collective-permute-start.2 = (f32[2,624,512]{2,1,0:T(8,128)S(1)}, f32[2,624,512]{2,1,0:T(8,128)S(1)}, u32[]{:S(2)}, u32[]{:S(2)}) collective-permute-start(f32[2,624,512]{2,1,0:T(8,128)S(1)} %pad_maximum_fusion.1), channel_id=1, source_target_pairs={{0,1},{1,0},{2,3},{3,2},{4,5},{5,4},{6,7},{7,6},{8,9},{9,8},{10,11... | collective-permute-start | bytes 7667720 | tf_op jit(solution)/shard_map/ppermute | solution.py:41
  68.4 32.4 %all-to-all-start.1 = ((bf16[8,2,129,256]{3,1,2,0:T(2,128)(2,1)}), bf16[8,2,129,256]{3,1,2,0:T(2,128)(2,1)}, u32[]{:S(2)}, u32[]{:S(2)}) async-start(bf16[8,2,129,256]{3,1,2,0:T(2,128)(2,1)} %copy.77), calls=%async_computation.1 | async-start | bytes 2113536 | tf_op jit(solution)/shard_map/all_to_all | solution.py:151
  74.4 32.1 %collective-permute-start.3 = (f32[624,512]{1,0:T(8,128)}, f32[624,512]{1,0:T(8,128)}, u32[]{:S(2)}, u32[]{:S(2)}) collective-permute-start(f32[624,512]{1,0:T(8,128)} %select_bitcast_fusion.4), channel_id=1, source_target_pairs={{0,2},{2,0},{1,3},{3,1},{4,6},{6,4},{5,7},{7,5},{8,10},{10,8},{9,1... | collective-permute-start | bytes 3833864 | tf_op jit(solution)/shard_map/ppermute | solution.py:41
  102.1 1.0 copy-start.3
  105.3 1.2 copy-start.5
  109.2 7.9 %copy-start.2 = (f32[624,512]{1,0:T(8,128)S(1)}, f32[624,512]{1,0:T(8,128)}, u32[]{:S(2)}) copy-start(f32[624,512]{1,0:T(8,128)} %get-tuple-element.20) | copy-start | bytes 3833860
  109.2 1.2 collective-permute-start.4
  110.4 3.6 %collective-permute-start.5 = (f32[624,1]{0,1:T(1,128)S(1)}, f32[624,1]{0,1:T(1,128)S(1)}, u32[]{:S(2)}, u32[]{:S(2)}) collective-permute-start(f32[624,1]{0,1:T(1,128)S(1)} %reshape_add_fusion), channel_id=1, source_target_pairs={{0,2},{2,0},{1,3},{3,1},{4,6},{6,4},{5,7},{7,5},{8,10},{10,8},{9,1... | collective-permute-start | bytes 7496 | tf_op jit(solution)/shard_map/ppermute | solution.py:41
  115.5 15.4 %collective-permute-start.6 = (bf16[624,512]{1,0:T(8,128)(2,1)S(1)}, bf16[624,512]{1,0:T(8,128)(2,1)S(1)}, u32[]{:S(2)}, u32[]{:S(2)}) collective-permute-start(bf16[624,512]{1,0:T(8,128)(2,1)S(1)} %multiply_convert_fusion.1), channel_id=1, source_target_pairs={{0,2},{2,0},{1,3},{3,1},{4,6},{6,4},{5,7},{7,5},{8,10},{10,8},{9,1... | collective-permute-start | bytes 1916936 | tf_op jit(solution)/shard_map/ppermute | solution.py:41
  131.0 4.1 %copy-start.14 = (bf16[2048,1024]{1,0:T(8,128)(2,1)S(1)}, bf16[2048,1024]{1,0:T(8,128)(2,1)}, u32[]{:S(2)}) copy-start(bf16[2048,1024]{1,0:T(8,128)(2,1)} %param.25) | copy-start | bytes 12582916
  131.1 3.1 %collective-permute-start.7 = (bf16[2,624,512]{2,1,0:T(8,128)(2,1)S(1)}, bf16[2,624,512]{2,1,0:T(8,128)(2,1)S(1)}, u32[]{:S(2)}, u32[]{:S(2)}) collective-permute-start(bf16[2,624,512]{2,1,0:T(8,128)(2,1)S(1)} %maximum_select_fusion.1), channel_id=1, source_target_pairs={{0,1},{1,0},{2,3},{3,2},{4,5},{5,4},{6,7},{7,6},{8,9},{9,8},{10,11... | collective-permute-start | bytes 3833864 | tf_op jit(solution)/shard_map/ppermute | solution.py:41
  134.3 0.8 copy-start.9
  154.9 4.9 %collective-permute-start.8 = (f32[2,624,512]{2,1,0:T(8,128)S(1)}, f32[2,624,512]{2,1,0:T(8,128)S(1)}, u32[]{:S(2)}, u32[]{:S(2)}) collective-permute-start(f32[2,624,512]{2,1,0:T(8,128)S(1)} %pad_maximum_fusion.3), channel_id=1, source_target_pairs={{0,1},{1,0},{2,3},{3,2},{4,5},{5,4},{6,7},{7,6},{8,9},{9,8},{10,11... | collective-permute-start | bytes 7667720 | tf_op jit(solution)/shard_map/ppermute | solution.py:41
  164.5 16.7 %collective-permute-start.9 = (bf16[624,512]{1,0:T(8,128)(2,1)}, bf16[624,512]{1,0:T(8,128)(2,1)}, u32[]{:S(2)}, u32[]{:S(2)}) collective-permute-start(bf16[624,512]{1,0:T(8,128)(2,1)} %fusion.17), channel_id=1, source_target_pairs={{0,2},{2,0},{1,3},{3,1},{4,6},{6,4},{5,7},{7,5},{8,10},{10,8},{9,1... | collective-permute-start | bytes 1916936 | tf_op jit(solution)/shard_map/ppermute | solution.py:41
  166.1 18.1 %copy-start.1 = (bf16[512,2048]{1,0:T(8,128)(2,1)S(1)}, bf16[512,2048]{1,0:T(8,128)(2,1)}, u32[]{:S(2)}) copy-start(bf16[512,2048]{1,0:T(8,128)(2,1)} %param.23) | copy-start | bytes 6291460

commit v8 on v5

--- a/solution.py
+++ b/solution.py
@@ -52,6 +52,43 @@
         for core_block in range(2):
             blocks.append(jnp.where(core == core_block, pair[chip_block], other[chip_block]))
     return jnp.concatenate(blocks, axis=1)
+
+
+def gather_project(share, weights):
+    chip = lax.axis_index("kvy")
+    core = lax.axis_index("core")
+    from_core = swap(share, "core")
+    from_chip = swap(share, "kvy")
+    local_pair = jnp.where(
+        core == 0,
+        jnp.concatenate([share, from_core], axis=1),
+        jnp.concatenate([from_core, share], axis=1),
+    )
+    half = local_pair.shape[1]
+    local_parts = tuple(
+        jnp.dot(
+            local_pair,
+            lax.dynamic_slice_in_dim(weight, chip * half, half, 0),
+            preferred_element_type=jnp.float32,
+        )
+        for weight in weights
+    )
+    from_chip, local_parts = lax.optimization_barrier((from_chip, local_parts))
+    from_diagonal = swap(from_chip, "core")
+    remote_pair = jnp.where(
+        core == 0,
+        jnp.concatenate([from_chip, from_diagonal], axis=1),
+        jnp.concatenate([from_diagonal, from_chip], axis=1),
+    )
+    return [
+        part
+        + jnp.dot(
+            remote_pair,
+            lax.dynamic_slice_in_dim(weight, (1 - chip) * half, half, 0),
+            preferred_element_type=jnp.float32,
+        )
+        for part, weight in zip(local_parts, weights)
+    ]
 
 
 def scatter_features(matrix_in, weight, link_type=None):
@@ -196,9 +233,7 @@
 
     gain_share = lax.dynamic_slice_in_dim(feedforward_gain, kv_index * width_share, width_share)
     normed_share = row_scale(residual_share, gain_share).astype(jnp.bfloat16)
-    normed_two = gather_features(normed_share)
-    gate_proj = jnp.dot(normed_two, gate_weight, preferred_element_type=jnp.float32)
-    upward = jnp.dot(normed_two, up_weight, preferred_element_type=jnp.float32)
+    gate_proj, upward = gather_project(normed_share, (gate_weight, up_weight))
     hidden = (jax.nn.silu(gate_proj) * upward).astype(jnp.bfloat16)
     mlp_share = scatter_features(hidden, down_weight, jnp.bfloat16)
     live_rows = (jnp.arange(span_size, dtype=jnp.int32)[None, :] < span_length[:, None]).reshape(

time: 178 us -> 173 us (0.972)
  matrix products: 24.9 us -> 35.7 us
  waiting for transfers between devices: 73.3 us -> 64.9 us
  other arithmetic: 30.8 us -> 25.6 us
  local copies, waits for them, and re-layouts: 26.1 us -> 23.5 us
    dot_general x1 -> x3, matrix products: 4.27 us -> 15 us  [the longest x2 9.61 us: gather_project(): jnp.dot(local_pair, lax.dynamic_slice_in_dim(weight, chip * half, half, 0...]
    ppermute x10 -> x11, waiting for transfers between devices: 69.3 us -> 59.3 us  [swap(): return lax.ppermute(values, axis_name, [(0, 1), (1, 0)])]
    gather x1, local copies, waits for them, and re-layouts: 2.78 us -> 0.62 us  [local(): packed = jnp.take(payload, picked, axis=0)]
    concatenate x1, other arithmetic: 2.15 us -> 0.07 us  [local(): payload = jnp.concatenate([head_kv[0], head_kv[1], trailer], axis=1)]
    ppermute x10 -> x11, starting transfers between devices: 10.5 us -> 10.5 us  [swap(): return lax.ppermute(values, axis_name, [(0, 1), (1, 0)])]
  transfers between devices with their start and end apart: 12 -> 13, of which waited for: 8 -> 9; matrix products, arithmetic and copies ran while one was open for 29% -> 32% of each run, Pallas kernels for 0% -> 0%
where the time goes in v8:
time: 173 us; the launch traced here: 172 us
  waiting for transfers between devices  64.9 us (38%)
  matrix products  35.7 us (21%)
  other arithmetic  25.6 us (15%)
  local copies, waits for them, and re-layouts  23.5 us (14%)
  starting transfers between devices  20.8 us (12%)
    ppermute x11, waiting for transfers between devices, swap(): return lax.ppermute(values, axis_name, [(0, 1), (1, 0)])  59.3 us
    dot_general x2, matrix products, scatter_features(): product = jnp.dot(matrix_in, weight, preferred_element_type=jnp.float32)  14.1 us
    ppermute x11, starting transfers between devices, swap(): return lax.ppermute(values, axis_name, [(0, 1), (1, 0)])  10.5 us
    dot_general x2, matrix products, gather_project(): jnp.dot(local_pair, lax.dynamic_slice_in_dim(weight, chip * half, half, 0...  9.61 us
    all_to_all x1, starting transfers between devices, local(): lax.all_to_all(packed, 'req', split_axis=0, concat_axis=0, tiled=True)  6.02 us
    unnamed x46, local copies, waits for them, and re-layouts  5.61 us
    another operation x2, other arithmetic, scatter_features(): jnp.stack([jnp.where(core == 0, block(k, 0), block(k, 1)) for k in range(...  5.46 us
    dot_general x1, matrix products, gather_project(): jnp.dot(remote_pair, lax.dynamic_slice_in_dim(weight, (1 - chip) * half,...  5.41 us
  transfers between devices with their start and end apart: 13, of which 9 were waited for; matrix products, arithmetic and copies ran while one was open for 32% of the time, Pallas kernels for 0%

profile of v8, /device:TPU:0, one launch (start us, length us, event | category | flops | bytes accessed | tf_op | source)
XLA Modules:
  0.0 171.8 jit_solution(17538750744319716351)
XLA Ops:
  0.6 3.0 %collective-permute-start = (bf16[624,512]{1,0:T(8,128)(2,1)}, bf16[624,512]{1,0:T(8,128)(2,1)}, u32[]{:S(2)}, u32[]{:S(2)}) collective-permute-start(bf16[624,512]{1,0:T(8,128)(2,1)} %param.15), channel_id=1, source_target_pairs={{0,2},{2,0},{1,3},{3,1},{4,6},{6,4},{5,7},{7,5},{8,10},{10,8},{9,1... | collective-permute-start | bytes 1916936 | tf_op jit(solution)/shard_map/ppermute | solution.py:41
  8.0 4.3 %all-to-all-start = ((bf16[2,4,13,16,256]{4,3,2,0,1:T(8,128)(2,1)}), bf16[2,4,13,16,256]{4,3,2,0,1:T(8,128)(2,1)}, u32[]{:S(2)}, u32[]{:S(2)}) async-start(bf16[2,4,13,16,256]{4,3,2,0,1:T(8,128)(2,1)} %copy.70), calls=%async_computation | async-start | bytes 1703936 | tf_op jit(solution)/shard_map/all_to_all | solution.py:155
  12.4 6.8 %collective-permute-done = bf16[624,512]{1,0:T(8,128)(2,1)} collective-permute-done((bf16[624,512]{1,0:T(8,128)(2,1)}, bf16[624,512]{1,0:T(8,128)(2,1)}, u32[]{:S(2)}, u32[]{:S(2)}) %collective-permute-start) | collective-permute-done | bytes 639008 | tf_op jit(solution)/shard_map/ppermute | solution.py:41
  19.2 2.0 %maximum_select_fusion = bf16[2,624,512]{2,1,0:T(8,128)(2,1)S(1)} fusion(bf16[1,624,512]{2,1,0:T(8,128)(2,1)} %bitcast.4, bf16[1,624,512]{2,1,0:T(8,128)(2,1)} %bitcast.120, pred[]{:T(512)S(6)} %eq.26), kind=kLoop, calls=%fused_computation.23 | loop fusion | flops 1916928 | bytes 2555905 | tf_op jit(solution)/shard_map/jit(_where)/select_n | solution.py:48
  21.5 2.1 %multiply_cosine_fusion = (f32[13,48,128]{2,1,0:T(8,128)}, f32[13,48,128]{2,1,0:T(8,128)}) fusion(f32[128]{0:T(128)S(1)} %multiply_exponential_fusion, f32[13,48]{1,0:T(8,128)S(1)} %iota_add_fusion), kind=kLoop, calls=%fused_computation.77 | loop fusion | flops 79872 | bytes 641984 | tf_op jit(solution)/shard_map/cos | solution.py:22
  23.6 3.9 %all-to-all-done = bf16[2,4,13,16,256]{4,3,2,0,1:T(8,128)(2,1)} async-done(((bf16[2,4,13,16,256]{4,3,2,0,1:T(8,128)(2,1)}), bf16[2,4,13,16,256]{4,3,2,0,1:T(8,128)(2,1)}, u32[]{:S(2)}, u32[]{:S(2)}) %all-to-all-start) | async-done | bytes 852000 | tf_op jit(solution)/shard_map/all_to_all | solution.py:155
  31.2 2.0 %fusion = f32[624]{0:T(1024)S(1)} fusion(bf16[624,512]{1,0:T(8,128)(2,1)S(1)} %get-tuple-element.21, bf16[624,512]{1,0:T(8,128)(2,1)S(1)} %get-tuple-element.22, bf16[624,512]{1,0:T(8,128)(2,1)S(1)} %get-tuple-element.20, bf16[624,512]{1,0:T(8,128)(2,1)S(1)} %get-tuple-element.19), kind=kLoop, calls=%fused_computation.4 | loop fusion | flops 12778896 | bytes 2558400 | tf_op jit(solution)/shard_map/reduce_sum | solution.py:192
  34.2 1.5 copy-done.6
  35.6 2.6 %fusion.74 = f32[624,512]{1,0:T(8,128)} fusion(bf16[624,2048]{1,0:T(8,128)(2,1)S(1)} %fusion.2, bf16[2048,512]{1,0:T(8,128)(2,1)S(1)} %copy-done.18), kind=kOutput, calls=%fused_computation.151 | convolution fusion | flops 1308622848 | bytes 5931008 | tf_op jit(solution)/shard_map/dot_general | solution.py:199
  38.2 2.1 %reshape.305 = f32[13,48,2,256]{3,2,1,0:T(2,128)S(1)} reshape(f32[624,512]{1,0:T(8,128)} %fusion.74) | data formatting | bytes 2555904 | tf_op jit(solution)/shard_map/reshape | solution.py:201
  42.0 2.2 %fusion.73 = f32[624,256]{1,0:T(8,128)S(1)} fusion(bf16[624,2048]{1,0:T(8,128)(2,1)S(1)} %copy-done.7, bf16[2048,256]{1,0:T(8,128)(2,1)} %param.21), kind=kOutput, calls=%fused_computation.150 | convolution fusion | flops 654311424 | bytes 4243456 | tf_op jit(solution)/shard_map/dot_general | solution.py:203
  44.2 1.6 fusion.40
  49.9 1.5 fusion.75
  52.5 4.8 %collective-permute-done.2 = f32[2,624,512]{2,1,0:T(8,128)S(1)} collective-permute-done((f32[2,624,512]{2,1,0:T(8,128)S(1)}, f32[2,624,512]{2,1,0:T(8,128)S(1)}, u32[]{:S(2)}, u32[]{:S(2)}) %collective-permute-start.2) | collective-permute-done | bytes 2555936 | tf_op jit(solution)/shard_map/ppermute | solution.py:41
  58.2 1.8 %collective-permute-start.3 = (f32[624,512]{1,0:T(8,128)S(1)}, f32[624,512]{1,0:T(8,128)S(1)}, u32[]{:S(2)}, u32[]{:S(2)}) collective-permute-start(f32[624,512]{1,0:T(8,128)S(1)} %select_bitcast_fusion.4), channel_id=1, source_target_pairs={{0,2},{2,0},{1,3},{3,1},{4,6},{6,4},{5,7},{7,5},{8,10},{10,8},{9,1... | collective-permute-start | bytes 3833864 | tf_op jit(solution)/shard_map/ppermute | solution.py:41
  60.0 28.4 %collective-permute-done.3 = f32[624,512]{1,0:T(8,128)S(1)} collective-permute-done((f32[624,512]{1,0:T(8,128)S(1)}, f32[624,512]{1,0:T(8,128)S(1)}, u32[]{:S(2)}, u32[]{:S(2)}) %collective-permute-start.3) | collective-permute-done | bytes 1277984 | tf_op jit(solution)/shard_map/ppermute | solution.py:41
  90.0 1.7 %collective-permute-start.5 = (f32[624,1]{0,1:T(1,128)S(1)}, f32[624,1]{0,1:T(1,128)S(1)}, u32[]{:S(2)}, u32[]{:S(2)}) collective-permute-start(f32[624,1]{0,1:T(1,128)S(1)} %reshape_add_fusion), channel_id=1, source_target_pairs={{0,2},{2,0},{1,3},{3,1},{4,6},{6,4},{5,7},{7,5},{8,10},{10,8},{9,1... | collective-permute-start | bytes 7496 | tf_op jit(solution)/shard_map/ppermute | solution.py:41
  94.0 1.8 %collective-permute-start.6 = (bf16[624,512]{1,0:T(8,128)(2,1)S(1)}, bf16[624,512]{1,0:T(8,128)(2,1)}, u32[]{:S(2)}, u32[]{:S(2)}) collective-permute-start(bf16[624,512]{1,0:T(8,128)(2,1)S(1)} %multiply_convert_fusion.2), channel_id=1, source_target_pairs={{0,2},{2,0},{1,3},{3,1},{4,6},{6,4},{5,7},{7,5},{8,10},{10,8},{9,1... | collective-permute-start | bytes 1916936 | tf_op jit(solution)/shard_map/ppermute | solution.py:41
  97.1 5.2 %fusion.7 = f32[624,1024]{1,0:T(8,128)} fusion(bf16[2048,1024]{1,0:T(8,128)(2,1)} %param.26, s32[]{:T(128)S(6)} %select_n.232, bf16[624,512]{1,0:T(8,128)(2,1)S(1)} %collective-permute-done.7, bf16[624,512]{1,0:T(8,128)(2,1)S(1)} %multiply_convert_fusion.2, pred[]{:T(512)S(6)} %eq.27), kind=kOutput, calls=%fused_computation.17 | convolution fusion | flops 1314373632 | bytes 5931013 | tf_op jit(solution)/shard_map/dot_general | solution.py:69
  102.3 4.4 %fusion.9 = f32[624,1024]{1,0:T(8,128)} fusion(bf16[2048,1024]{1,0:T(8,128)(2,1)S(1)} %copy-done.17, s32[]{:T(128)S(6)} %select_n.232, bf16[624,512]{1,0:T(8,128)(2,1)} %copy-done.20, bf16[624,512]{1,0:T(8,128)(2,1)S(1)} %multiply_convert_fusion.2, pred[]{:T(512)S(6)} %eq.27), kind=kOutput, calls=%fused_computation.19 | convolution fusion | flops 1314373632 | bytes 5931013 | tf_op jit(solution)/shard_map/dot_general | solution.py:69
  106.7 4.3 %collective-permute-done.6 = bf16[624,512]{1,0:T(8,128)(2,1)} collective-permute-done((bf16[624,512]{1,0:T(8,128)(2,1)S(1)}, bf16[624,512]{1,0:T(8,128)(2,1)}, u32[]{:S(2)}, u32[]{:S(2)}) %collective-permute-start.6) | collective-permute-done | bytes 639008 | tf_op jit(solution)/shard_map/ppermute | solution.py:41
  111.9 1.8 %copy.77 = bf16[8,2,129,256]{3,1,2,0:T(2,128)(2,1)} copy(bf16[8,2,129,256]{3,2,1,0:T(8,128)(2,1)S(1)} %select_select_fusion) | data formatting | bytes 2113536 | tf_op jit(solution)/shard_map/jit(_where)/select_n | solution.py:177
  113.7 6.0 %all-to-all-start.1 = ((bf16[8,2,129,256]{3,1,2,0:T(2,128)(2,1)}), bf16[8,2,129,256]{3,1,2,0:T(2,128)(2,1)}, u32[]{:S(2)}, u32[]{:S(2)}) async-start(bf16[8,2,129,256]{3,1,2,0:T(2,128)(2,1)} %copy.77), calls=%async_computation.1 | async-start | bytes 2113536 | tf_op jit(solution)/shard_map/all_to_all | solution.py:179
  119.8 5.4 %fusion.3 = f32[624,1024]{1,0:T(8,128)} fusion(bf16[2048,1024]{1,0:T(8,128)(2,1)} %param.26, s32[]{:T(128)S(6)} %select_n.234, bf16[624,512]{1,0:T(8,128)(2,1)} %collective-permute-done.8, bf16[624,512]{1,0:T(8,128)(2,1)} %collective-permute-done.6, pred[]{:T(512)S(6)} %eq.27), kind=kOutput, calls=%fused_computation.13 | convolution fusion | flops 1314373632 | bytes 5931013 | tf_op jit(solution)/shard_map/dot_general | solution.py:85
  125.2 12.6 %fusion.11 = f32[624,2048]{1,0:T(8,128)} fusion(bf16[1024,2048]{1,0:T(8,128)(2,1)} %param.27, f32[624,1024]{1,0:T(8,128)} %fusion.7, f32[624,1024]{1,0:T(8,128)} %fusion.3, f32[624,1024]{1,0:T(8,128)} %fusion.9, bf16[2048,1024]{1,0:T(8,128)(2,1)} %param.25, s32[]{:T(128)S(6)} %select_n.234, bf16[624,512]{1,0:T(8,128)(2,1)} %collective-permute-done.8, ...), kind=kOutput, calls=%fused_computation.22 | convolution fusion | flops 3936731136 | bytes 20348932 | tf_op jit(solution)/shard_map/dot_general | solution.py:97
  137.8 4.8 %select_bitcast_fusion.3 = (f32[1,624,512]{2,1,0:T(8,128)}, f32[1,624,512]{2,1,0:T(8,128)}, f32[1,624,512]{2,1,0:T(8,128)S(1)}, f32[1,624,512]{2,1,0:T(8,128)S(1)}) fusion(f32[624,2048]{1,0:T(8,128)} %fusion.11, pred[]{:T(512)S(6)} %eq.27), kind=kLoop, calls=%fused_computation.36 | loop fusion | flops 1277952 | bytes 10223617 | tf_op jit(solution)/shard_map/stack | solution.py:104
  142.5 1.8 %pad_maximum_fusion.2 = f32[2,624,512]{2,1,0:T(8,128)} fusion(f32[1,624,512]{2,1,0:T(8,128)S(1)} %get-tuple-element.13, f32[1,624,512]{2,1,0:T(8,128)S(1)} %get-tuple-element.14), kind=kLoop, calls=%fused_computation.11 | loop fusion | flops 638976 | bytes 5111808 | tf_op jit(solution)/shard_map/stack | solution.py:105
  144.7 1.7 %all-to-all-done.1 = bf16[8,2,129,256]{3,1,2,0:T(2,128)(2,1)} async-done(((bf16[8,2,129,256]{3,1,2,0:T(2,128)(2,1)}), bf16[8,2,129,256]{3,1,2,0:T(2,128)(2,1)}, u32[]{:S(2)}, u32[]{:S(2)}) %all-to-all-start.1) | async-done | bytes 1056800 | tf_op jit(solution)/shard_map/all_to_all | solution.py:179
  149.3 2.8 %gather_fusion.1 = bf16[13,129,256]{2,1,0:T(8,128)(2,1)} fusion(bf16[16,129,256]{2,1,0:T(8,128)(2,1)} %bitcast.117, s32[1024]{0:T(1024)S(1)} %pad_clamp_fusion), kind=kCustom, calls=%fused_computation.1 | custom fusion | bytes 1717300 | tf_op jit(solution)/shard_map/jit(_take)/gather | solution.py:187
  152.1 2.7 %maximum_add_fusion.1 = f32[2,624,512]{2,1,0:T(8,128)S(1)} fusion(f32[2,624,512]{2,1,0:T(8,128)} %collective-permute-done.9, f32[1,624,512]{2,1,0:T(8,128)} %get-tuple-element.12, f32[1,624,512]{2,1,0:T(8,128)S(1)} %copy-done.2), kind=kLoop, calls=%fused_computation.10 | loop fusion | flops 1277952 | bytes 7667712 | tf_op jit(solution)/shard_map/add | solution.py:106
  154.9 1.6 collective-permute-start.10
  157.7 13.0 %collective-permute-done.10 = bf16[624,512]{1,0:T(8,128)(2,1)S(1)} collective-permute-done((bf16[624,512]{1,0:T(8,128)(2,1)S(1)}, bf16[624,512]{1,0:T(8,128)(2,1)S(1)}, u32[]{:S(2)}, u32[]{:S(2)}) %collective-permute-start.10) | collective-permute-done | bytes 639008 | tf_op jit(solution)/shard_map/ppermute | solution.py:41
  (121 shorter events, 28.5 us)
Async XLA Ops:
  0.6 49.3 %copy-start = (bf16[512,2048]{1,0:T(8,128)(2,1)S(1)}, bf16[512,2048]{1,0:T(8,128)(2,1)}, u32[]{:S(2)}) copy-start(bf16[512,2048]{1,0:T(8,128)(2,1)} %param.23) | copy-start | bytes 6291460
  0.6 18.6 %collective-permute-start = (bf16[624,512]{1,0:T(8,128)(2,1)}, bf16[624,512]{1,0:T(8,128)(2,1)}, u32[]{:S(2)}, u32[]{:S(2)}) collective-permute-start(bf16[624,512]{1,0:T(8,128)(2,1)} %param.15), channel_id=1, source_target_pairs={{0,2},{2,0},{1,3},{3,1},{4,6},{6,4},{5,7},{7,5},{8,10},{10,8},{9,1... | collective-permute-start | bytes 1916936 | tf_op jit(solution)/shard_map/ppermute | solution.py:41
  6.9 5.4 %copy-start.21 = (s32[13]{0:T(128)S(1)}, s32[13]{0:T(128)}, u32[]{:S(2)}) copy-start(s32[13]{0:T(128)} %param.17) | copy-start | bytes 160
  8.0 13.4 %copy-start.15 = (s32[13]{0:T(128)S(1)}, s32[13]{0:T(128)}, u32[]{:S(2)}) copy-start(s32[13]{0:T(128)} %param.16) | copy-start | bytes 160
  8.0 19.5 %all-to-all-start = ((bf16[2,4,13,16,256]{4,3,2,0,1:T(8,128)(2,1)}), bf16[2,4,13,16,256]{4,3,2,0,1:T(8,128)(2,1)}, u32[]{:S(2)}, u32[]{:S(2)}) async-start(bf16[2,4,13,16,256]{4,3,2,0,1:T(8,128)(2,1)} %copy.70), calls=%async_computation | async-start | bytes 1703936 | tf_op jit(solution)/shard_map/all_to_all | solution.py:155
  21.2 8.5 %collective-permute-start.1 = (bf16[2,624,512]{2,1,0:T(8,128)(2,1)S(1)}, bf16[2,624,512]{2,1,0:T(8,128)(2,1)}, u32[]{:S(2)}, u32[]{:S(2)}) collective-permute-start(bf16[2,624,512]{2,1,0:T(8,128)(2,1)S(1)} %maximum_select_fusion), channel_id=1, source_target_pairs={{0,1},{1,0},{2,3},{3,2},{4,5},{5,4},{6,7},{7,6},{8,9},{9,8},{10,11... | collective-permute-start | bytes 3833864 | tf_op jit(solution)/shard_map/ppermute | solution.py:41
  31.2 2.1 %copy-start.14 = (f32[2048]{0:T(1024)S(1)}, f32[2048]{0:T(1024)}, u32[]{:S(2)}) copy-start(f32[2048]{0:T(1024)} %param.19) | copy-start | bytes 24580
  33.3 2.4 %copy-start.18 = (bf16[2048,512]{1,0:T(8,128)(2,1)S(1)}, bf16[2048,512]{1,0:T(8,128)(2,1)}, u32[]{:S(2)}) copy-start(bf16[2048,512]{1,0:T(8,128)(2,1)} %param.20) | copy-start | bytes 6291460
  34.2 1.5 copy-start.6
  40.3 1.7 %copy-start.7 = (bf16[624,2048]{1,0:T(8,128)(2,1)S(1)}, bf16[624,2048]{1,0:T(8,128)(2,1)}, u32[]{:S(2)}) copy-start(bf16[624,2048]{1,0:T(8,128)(2,1)} %copy-done.6) | copy-start | bytes 7667716
  42.0 3.7 %copy-start.19 = (bf16[2048,256]{1,0:T(8,128)(2,1)S(1)}, bf16[2048,256]{1,0:T(8,128)(2,1)}, u32[]{:S(2)}) copy-start(bf16[2048,256]{1,0:T(8,128)(2,1)} %param.22) | copy-start | bytes 3145732
  45.8 1.1 copy-start.13
  46.7 1.1 copy-start.8
  52.4 4.9 %collective-permute-start.2 = (f32[2,624,512]{2,1,0:T(8,128)S(1)}, f32[2,624,512]{2,1,0:T(8,128)S(1)}, u32[]{:S(2)}, u32[]{:S(2)}) collective-permute-start(f32[2,624,512]{2,1,0:T(8,128)S(1)} %pad_maximum_fusion.1), channel_id=1, source_target_pairs={{0,1},{1,0},{2,3},{3,2},{4,5},{5,4},{6,7},{7,6},{8,9},{9,8},{10,11... | collective-permute-start | bytes 7667720 | tf_op jit(solution)/shard_map/ppermute | solution.py:41
  57.9 2.1 %copy-start.16 = (s32[13]{0:T(128)S(1)}, s32[13]{0:T(128)}, u32[]{:S(2)}) copy-start(s32[13]{0:T(128)} %param.18) | copy-start | bytes 160
  57.9 30.5 %copy-start.5 = (bf16[624,512]{1,0:T(8,128)(2,1)S(1)}, bf16[624,512]{1,0:T(8,128)(2,1)}, u32[]{:S(2)}) copy-start(bf16[624,512]{1,0:T(8,128)(2,1)} %param.15) | copy-start | bytes 1916932
  58.2 30.2 %collective-permute-start.3 = (f32[624,512]{1,0:T(8,128)S(1)}, f32[624,512]{1,0:T(8,128)S(1)}, u32[]{:S(2)}, u32[]{:S(2)}) collective-permute-start(f32[624,512]{1,0:T(8,128)S(1)} %select_bitcast_fusion.4), channel_id=1, source_target_pairs={{0,2},{2,0},{1,3},{3,1},{4,6},{6,4},{5,7},{7,5},{8,10},{10,8},{9,1... | collective-permute-start | bytes 3833864 | tf_op jit(solution)/shard_map/ppermute | solution.py:41
  88.7 1.2 collective-permute-start.4
  90.0 3.6 %collective-permute-start.5 = (f32[624,1]{0,1:T(1,128)S(1)}, f32[624,1]{0,1:T(1,128)S(1)}, u32[]{:S(2)}, u32[]{:S(2)}) collective-permute-start(f32[624,1]{0,1:T(1,128)S(1)} %reshape_add_fusion), channel_id=1, source_target_pairs={{0,2},{2,0},{1,3},{3,1},{4,6},{6,4},{5,7},{7,5},{8,10},{10,8},{9,1... | collective-permute-start | bytes 7496 | tf_op jit(solution)/shard_map/ppermute | solution.py:41
  93.8 2.5 %collective-permute-start.7 = (bf16[624,512]{1,0:T(8,128)(2,1)S(1)}, bf16[624,512]{1,0:T(8,128)(2,1)S(1)}, u32[]{:S(2)}, u32[]{:S(2)}) collective-permute-start(bf16[624,512]{1,0:T(8,128)(2,1)S(1)} %multiply_convert_fusion.2), channel_id=1, source_target_pairs={{0,1},{1,0},{2,3},{3,2},{4,5},{5,4},{6,7},{7,6},{8,9},{9,8},{10,11... | collective-permute-start | bytes 1916936 | tf_op jit(solution)/shard_map/ppermute | solution.py:41
  94.0 17.0 %collective-permute-start.6 = (bf16[624,512]{1,0:T(8,128)(2,1)S(1)}, bf16[624,512]{1,0:T(8,128)(2,1)}, u32[]{:S(2)}, u32[]{:S(2)}) collective-permute-start(bf16[624,512]{1,0:T(8,128)(2,1)S(1)} %multiply_convert_fusion.2), channel_id=1, source_target_pairs={{0,2},{2,0},{1,3},{3,1},{4,6},{6,4},{5,7},{7,5},{8,10},{10,8},{9,1... | collective-permute-start | bytes 1916936 | tf_op jit(solution)/shard_map/ppermute | solution.py:41
  96.2 6.0 %copy-start.17 = (bf16[2048,1024]{1,0:T(8,128)(2,1)S(1)}, bf16[2048,1024]{1,0:T(8,128)(2,1)}, u32[]{:S(2)}) copy-start(bf16[2048,1024]{1,0:T(8,128)(2,1)} %param.25) | copy-start | bytes 12582916
  102.2 8.7 %copy-start.9 = (bf16[1,13,4,16,256]{4,3,2,1,0:T(8,128)(2,1)S(1)}, bf16[1,13,4,16,256]{4,3,2,1,0:T(8,128)(2,1)}, u32[]{:S(2)}) copy-start(bf16[1,13,4,16,256]{4,3,2,1,0:T(8,128)(2,1)} %get-tuple-element.29) | copy-start | bytes 1277956
  102.3 8.7 %copy-start.11 = (bf16[1,13,4,16,256]{4,3,2,1,0:T(8,128)(2,1)S(1)}, bf16[1,13,4,16,256]{4,3,2,1,0:T(8,128)(2,1)}, u32[]{:S(2)}) copy-start(bf16[1,13,4,16,256]{4,3,2,1,0:T(8,128)(2,1)} %get-tuple-element.30) | copy-start | bytes 1277956
  110.9 8.8 %collective-permute-start.8 = (bf16[624,512]{1,0:T(8,128)(2,1)}, bf16[624,512]{1,0:T(8,128)(2,1)}, u32[]{:S(2)}, u32[]{:S(2)}) collective-permute-start(bf16[624,512]{1,0:T(8,128)(2,1)} %collective-permute-done.6), channel_id=1, source_target_pairs={{0,1},{1,0},{2,3},{3,2},{4,5},{5,4},{6,7},{7,6},{8,9},{9,8},{10,11... | collective-permute-start | bytes 1916936 | tf_op jit(solution)/shard_map/ppermute | solution.py:41
  113.7 32.7 %all-to-all-start.1 = ((bf16[8,2,129,256]{3,1,2,0:T(2,128)(2,1)}), bf16[8,2,129,256]{3,1,2,0:T(2,128)(2,1)}, u32[]{:S(2)}, u32[]{:S(2)}) async-start(bf16[8,2,129,256]{3,1,2,0:T(2,128)(2,1)} %copy.77), calls=%async_computation.1 | async-start | bytes 2113536 | tf_op jit(solution)/shard_map/all_to_all | solution.py:179
  144.3 7.7 %copy-start.2 = (f32[1,624,512]{2,1,0:T(8,128)S(1)}, f32[1,624,512]{2,1,0:T(8,128)}, u32[]{:S(2)}) copy-start(f32[1,624,512]{2,1,0:T(8,128)} %get-tuple-element.11) | copy-start | bytes 3833860
  144.3 7.7 %collective-permute-start.9 = (f32[2,624,512]{2,1,0:T(8,128)}, f32[2,624,512]{2,1,0:T(8,128)}, u32[]{:S(2)}, u32[]{:S(2)}) collective-permute-start(f32[2,624,512]{2,1,0:T(8,128)} %pad_maximum_fusion.2), channel_id=1, source_target_pairs={{0,1},{1,0},{2,3},{3,2},{4,5},{5,4},{6,7},{7,6},{8,9},{9,8},{10,11... | collective-permute-start | bytes 7667720 | tf_op jit(solution)/shard_map/ppermute | solution.py:41
  147.8 1.1 copy-start.3
  154.7 1.7 %copy-start.4 = (bf16[13,129,256]{2,1,0:T(8,128)(2,1)S(1)}, bf16[13,129,256]{2,1,0:T(8,128)(2,1)}, u32[]{:S(2)}) copy-start(bf16[13,129,256]{2,1,0:T(8,128)(2,1)} %gather_fusion.1) | copy-start | bytes 2575876
  154.9 15.8 %collective-permute-start.10 = (bf16[624,512]{1,0:T(8,128)(2,1)S(1)}, bf16[624,512]{1,0:T(8,128)(2,1)S(1)}, u32[]{:S(2)}, u32[]{:S(2)}) collective-permute-start(bf16[624,512]{1,0:T(8,128)(2,1)S(1)} %fusion.30), channel_id=1, source_target_pairs={{0,2},{2,0},{1,3},{3,1},{4,6},{6,4},{5,7},{7,5},{8,10},{10,8},{9,1... | collective-permute-start | bytes 1916936 | tf_op jit(solution)/shard_map/ppermute | solution.py:41
  156.6 15.2 %copy-start.1 = (bf16[512,2048]{1,0:T(8,128)(2,1)S(1)}, bf16[512,2048]{1,0:T(8,128)(2,1)}, u32[]{:S(2)}) copy-start(bf16[512,2048]{1,0:T(8,128)(2,1)} %param.23) | copy-start | bytes 6291460
  (3 other events, 2.8 us)

commit v9 on v8

--- a/solution.py
+++ b/solution.py
@@ -109,6 +109,27 @@
     if link_type is not None:
         theirs = theirs.astype(link_type)
     return mine + swap(theirs, "kvy").astype(jnp.float32)
+
+
+def scatter_pipelined(matrix_in, weight, link_type):
+    chip = lax.axis_index("kvy")
+    core = lax.axis_index("core")
+    width = weight.shape[1] // (2 * CORES)
+
+    def product(chip_block, core_block, left):
+        start = (chip_block * CORES + core_block) * width
+        columns = lax.dynamic_slice_in_dim(weight, start, width, 1)
+        return jnp.dot(left, columns, preferred_element_type=jnp.float32)
+
+    for_partner = product(1 - chip, 1 - core, matrix_in)
+    theirs = product(1 - chip, core, matrix_in) + swap(for_partner, "core")
+    theirs = theirs.astype(link_type)
+    theirs, later_in = lax.optimization_barrier((theirs, matrix_in))
+    arrived = swap(theirs, "kvy")
+    from_partner = swap(product(chip, 1 - core, later_in), "core")
+    own = product(chip, core, later_in)
+    own, from_partner = lax.optimization_barrier((own, from_partner))
+    return own + from_partner + arrived.astype(jnp.float32)
 
 
 def row_scale(values, gain_share):
@@ -235,7 +256,7 @@
     normed_share = row_scale(residual_share, gain_share).astype(jnp.bfloat16)
     gate_proj, upward = gather_project(normed_share, (gate_weight, up_weight))
     hidden = (jax.nn.silu(gate_proj) * upward).astype(jnp.bfloat16)
-    mlp_share = scatter_features(hidden, down_weight, jnp.bfloat16)
+    mlp_share = scatter_pipelined(hidden, down_weight, jnp.bfloat16)
     live_rows = (jnp.arange(span_size, dtype=jnp.int32)[None, :] < span_length[:, None]).reshape(
         total_rows
     )

time: 173 us -> 176 us (1.017)
  waiting for transfers between devices: 64.9 us -> 76.4 us
  other arithmetic: 25.6 us -> 18.9 us
  local copies, waits for them, and re-layouts: 23.5 us -> 20 us
  matrix products: 35.7 us -> 38.5 us
    dot_general x0 -> x4, matrix products: none -> 12.8 us  [product(): return jnp.dot(left, columns, preferred_element_type=jnp.float32)]
    dot_general x2 -> x1, matrix products: 14.1 us -> 1.52 us  [scatter_features(): product = jnp.dot(matrix_in, weight, preferred_element_type=jnp.float32)]
    all_to_all x1, waiting for transfers between devices: 1.72 us -> 13.8 us  [local(): lax.all_to_all(packed, 'req', split_axis=0, concat_axis=0, tiled=True)]
    another operation x2 -> x1, other arithmetic: 5.46 us -> 0.69 us  [scatter_features(): jnp.stack([jnp.where(core == 0, block(k, 0), block(k, 1)) for k in range(...]
    add x2 -> x1, other arithmetic: 3.27 us -> 0.6 us  [scatter_features(): chip_sum = keep + swap(give, 'core')]
    gather x1, local copies, waits for them, and re-layouts: 2.81 us -> 0.61 us  [local(): decode_rows = jnp.take(landed, slot_position, axis=0)]
    dot_general x1 -> x2, matrix products: 5.41 us -> 7.35 us  [gather_project(): jnp.dot(remote_pair, lax.dynamic_slice_in_dim(weight, (1 - chip) * half,...]
    another operation x2 -> x1, other arithmetic: 2.02 us -> 0.23 us  [scatter_features(): jnp.stack([jnp.where(core == 0, block(k, 1), block(k, 0)) for k in range(...]
  transfers between devices with their start and end apart: 13 -> 14, of which waited for: 9 -> 9; matrix products, arithmetic and copies ran while one was open for 32% -> 24% of each run, Pallas kernels for 0% -> 0%
where the time goes in v9:
time: 176 us
  waiting for transfers between devices  76.4 us (43%)
  matrix products  38.5 us (22%)
  starting transfers between devices  20.7 us (12%)
  local copies, waits for them, and re-layouts  20 us (11%)
  other arithmetic  18.9 us (11%)
    ppermute x12, waiting for transfers between devices, swap(): return lax.ppermute(values, axis_name, [(0, 1), (1, 0)])  58.6 us
    all_to_all x1, waiting for transfers between devices, local(): lax.all_to_all(packed, 'req', split_axis=0, concat_axis=0, tiled=True)  13.8 us
    dot_general x4, matrix products, product(): return jnp.dot(left, columns, preferred_element_type=jnp.float32)  12.8 us
    ppermute x12, starting transfers between devices, swap(): return lax.ppermute(values, axis_name, [(0, 1), (1, 0)])  10.4 us
    dot_general x2, matrix products, gather_project(): jnp.dot(local_pair, lax.dynamic_slice_in_dim(weight, chip * half, half, 0...  9.61 us
    dot_general x2, matrix products, gather_project(): jnp.dot(remote_pair, lax.dynamic_slice_in_dim(weight, (1 - chip) * half,...  7.35 us
    all_to_all x1, starting transfers between devices, local(): lax.all_to_all(packed, 'req', split_axis=0, concat_axis=0, tiled=True)  6.02 us
    unnamed x58, local copies, waits for them, and re-layouts  5.46 us
  transfers between devices with their start and end apart: 14, of which 9 were waited for; matrix products, arithmetic and copies ran while one was open for 24% of the time, Pallas kernels for 0%

profile of v9, /device:TPU:0, one launch (start us, length us, event | category | flops | bytes accessed | tf_op | source)
XLA Modules:
  0.0 175.6 jit_solution(18336902580872472782)
XLA Ops:
  0.6 3.0 %collective-permute-start = (bf16[624,512]{1,0:T(8,128)(2,1)}, bf16[624,512]{1,0:T(8,128)(2,1)}, u32[]{:S(2)}, u32[]{:S(2)}) collective-permute-start(bf16[624,512]{1,0:T(8,128)(2,1)} %param.15), channel_id=1, source_target_pairs={{0,2},{2,0},{1,3},{3,1},{4,6},{6,4},{5,7},{7,5},{8,10},{10,8},{9,1... | collective-permute-start | bytes 1916936 | tf_op jit(solution)/shard_map/ppermute | solution.py:41
  8.0 4.2 %all-to-all-start = ((bf16[2,4,13,16,256]{4,3,2,0,1:T(8,128)(2,1)}), bf16[2,4,13,16,256]{4,3,2,0,1:T(8,128)(2,1)}, u32[]{:S(2)}, u32[]{:S(2)}) async-start(bf16[2,4,13,16,256]{4,3,2,0,1:T(8,128)(2,1)} %copy.70), calls=%async_computation | async-start | bytes 1703936 | tf_op jit(solution)/shard_map/all_to_all | solution.py:176
  12.3 6.9 %collective-permute-done = bf16[624,512]{1,0:T(8,128)(2,1)} collective-permute-done((bf16[624,512]{1,0:T(8,128)(2,1)}, bf16[624,512]{1,0:T(8,128)(2,1)}, u32[]{:S(2)}, u32[]{:S(2)}) %collective-permute-start) | collective-permute-done | bytes 639008 | tf_op jit(solution)/shard_map/ppermute | solution.py:41
  19.2 1.9 %maximum_select_fusion = bf16[2,624,512]{2,1,0:T(8,128)(2,1)S(1)} fusion(bf16[1,624,512]{2,1,0:T(8,128)(2,1)} %bitcast.4, bf16[1,624,512]{2,1,0:T(8,128)(2,1)} %bitcast.105, pred[]{:T(512)S(6)} %eq.26), kind=kLoop, calls=%fused_computation.22 | loop fusion | flops 1916928 | bytes 2555905 | tf_op jit(solution)/shard_map/jit(_where)/select_n | solution.py:48
  21.5 2.1 %multiply_cosine_fusion = (f32[13,48,128]{2,1,0:T(8,128)}, f32[13,48,128]{2,1,0:T(8,128)}) fusion(f32[128]{0:T(128)S(1)} %multiply_exponential_fusion, f32[13,48]{1,0:T(8,128)S(1)} %iota_add_fusion), kind=kLoop, calls=%fused_computation.73 | loop fusion | flops 79872 | bytes 641984 | tf_op jit(solution)/shard_map/cos | solution.py:22
  23.5 4.0 %all-to-all-done = bf16[2,4,13,16,256]{4,3,2,0,1:T(8,128)(2,1)} async-done(((bf16[2,4,13,16,256]{4,3,2,0,1:T(8,128)(2,1)}), bf16[2,4,13,16,256]{4,3,2,0,1:T(8,128)(2,1)}, u32[]{:S(2)}, u32[]{:S(2)}) %all-to-all-start) | async-done | bytes 852000 | tf_op jit(solution)/shard_map/all_to_all | solution.py:176
  31.2 2.0 %fusion = f32[624]{0:T(1024)S(1)} fusion(bf16[624,512]{1,0:T(8,128)(2,1)S(1)} %get-tuple-element.25, bf16[624,512]{1,0:T(8,128)(2,1)S(1)} %get-tuple-element.26, bf16[624,512]{1,0:T(8,128)(2,1)S(1)} %get-tuple-element.24, bf16[624,512]{1,0:T(8,128)(2,1)S(1)} %get-tuple-element.23), kind=kLoop, calls=%fused_computation.4 | loop fusion | flops 12778896 | bytes 2558400 | tf_op jit(solution)/shard_map/reduce_sum | solution.py:213
  34.5 1.6 convolution_convert_fusion.1
  37.1 2.6 %fusion.73 = f32[624,512]{1,0:T(8,128)} fusion(bf16[624,2048]{1,0:T(8,128)(2,1)S(1)} %fusion.2, bf16[2048,512]{1,0:T(8,128)(2,1)S(1)} %copy-done.23), kind=kOutput, calls=%fused_computation.150 | convolution fusion | flops 1308622848 | bytes 5931008 | tf_op jit(solution)/shard_map/dot_general | solution.py:220
  39.7 2.1 %reshape.300 = f32[13,48,2,256]{3,2,1,0:T(2,128)S(1)} reshape(f32[624,512]{1,0:T(8,128)} %fusion.73) | data formatting | bytes 2555904 | tf_op jit(solution)/shard_map/reshape | solution.py:222
  43.5 2.1 %fusion.72 = f32[624,256]{1,0:T(8,128)S(1)} fusion(bf16[624,2048]{1,0:T(8,128)(2,1)S(1)} %copy-done.8, bf16[2048,256]{1,0:T(8,128)(2,1)} %param.21), kind=kOutput, calls=%fused_computation.149 | convolution fusion | flops 654311424 | bytes 4243456 | tf_op jit(solution)/shard_map/dot_general | solution.py:224
  45.6 1.6 fusion.38
  53.1 4.8 %collective-permute-done.2 = f32[2,624,512]{2,1,0:T(8,128)S(1)} collective-permute-done((f32[2,624,512]{2,1,0:T(8,128)S(1)}, f32[2,624,512]{2,1,0:T(8,128)S(1)}, u32[]{:S(2)}, u32[]{:S(2)}) %collective-permute-start.2) | collective-permute-done | bytes 2555936 | tf_op jit(solution)/shard_map/ppermute | solution.py:41
  58.8 1.8 %collective-permute-start.3 = (f32[624,512]{1,0:T(8,128)S(1)}, f32[624,512]{1,0:T(8,128)S(1)}, u32[]{:S(2)}, u32[]{:S(2)}) collective-permute-start(f32[624,512]{1,0:T(8,128)S(1)} %select_bitcast_fusion), channel_id=1, source_target_pairs={{0,2},{2,0},{1,3},{3,1},{4,6},{6,4},{5,7},{7,5},{8,10},{10,8},{9,1... | collective-permute-start | bytes 3833864 | tf_op jit(solution)/shard_map/ppermute | solution.py:41
  60.6 28.4 %collective-permute-done.3 = f32[624,512]{1,0:T(8,128)S(1)} collective-permute-done((f32[624,512]{1,0:T(8,128)S(1)}, f32[624,512]{1,0:T(8,128)S(1)}, u32[]{:S(2)}, u32[]{:S(2)}) %collective-permute-start.3) | collective-permute-done | bytes 1277984 | tf_op jit(solution)/shard_map/ppermute | solution.py:41
  90.6 1.7 collective-permute-start.5
  94.6 1.8 %collective-permute-start.6 = (bf16[624,512]{1,0:T(8,128)(2,1)S(1)}, bf16[624,512]{1,0:T(8,128)(2,1)}, u32[]{:S(2)}, u32[]{:S(2)}) collective-permute-start(bf16[624,512]{1,0:T(8,128)(2,1)S(1)} %multiply_convert_fusion.1), channel_id=1, source_target_pairs={{0,2},{2,0},{1,3},{3,1},{4,6},{6,4},{5,7},{7,5},{8,10},{10,8},{9,1... | collective-permute-start | bytes 1916936 | tf_op jit(solution)/shard_map/ppermute | solution.py:41
  97.7 5.2 %fusion.9 = f32[624,1024]{1,0:T(8,128)} fusion(bf16[2048,1024]{1,0:T(8,128)(2,1)} %param.25, s32[]{:T(128)S(6)} %select_n.214, bf16[624,512]{1,0:T(8,128)(2,1)S(1)} %collective-permute-done.7, bf16[624,512]{1,0:T(8,128)(2,1)S(1)} %multiply_convert_fusion.1, pred[]{:T(512)S(6)} %eq.27), kind=kOutput, calls=%fused_computation.17 | convolution fusion | flops 1314373632 | bytes 5931013 | tf_op jit(solution)/shard_map/dot_general | solution.py:69
  102.9 4.4 %fusion.7 = f32[624,1024]{1,0:T(8,128)} fusion(bf16[2048,1024]{1,0:T(8,128)(2,1)S(1)} %copy-done.21, s32[]{:T(128)S(6)} %select_n.214, bf16[624,512]{1,0:T(8,128)(2,1)} %copy-done.25, bf16[624,512]{1,0:T(8,128)(2,1)S(1)} %multiply_convert_fusion.1, pred[]{:T(512)S(6)} %eq.27), kind=kOutput, calls=%fused_computation.15 | convolution fusion | flops 1314373632 | bytes 5931013 | tf_op jit(solution)/shard_map/dot_general | solution.py:69
  107.3 4.3 %collective-permute-done.6 = bf16[624,512]{1,0:T(8,128)(2,1)} collective-permute-done((bf16[624,512]{1,0:T(8,128)(2,1)S(1)}, bf16[624,512]{1,0:T(8,128)(2,1)}, u32[]{:S(2)}, u32[]{:S(2)}) %collective-permute-start.6) | collective-permute-done | bytes 639008 | tf_op jit(solution)/shard_map/ppermute | solution.py:41
  112.5 1.8 %copy.77 = bf16[8,2,129,256]{3,1,2,0:T(2,128)(2,1)} copy(bf16[8,2,129,256]{3,2,1,0:T(8,128)(2,1)S(1)} %select_select_fusion) | data formatting | bytes 2113536 | tf_op jit(solution)/shard_map/jit(_where)/select_n | solution.py:198
  114.4 6.0 %all-to-all-start.1 = ((bf16[8,2,129,256]{3,1,2,0:T(2,128)(2,1)}), bf16[8,2,129,256]{3,1,2,0:T(2,128)(2,1)S(1)}, u32[]{:S(2)}, u32[]{:S(2)}) async-start(bf16[8,2,129,256]{3,1,2,0:T(2,128)(2,1)} %copy.77), calls=%async_computation.1 | async-start | bytes 2113536 | tf_op jit(solution)/shard_map/all_to_all | solution.py:200
  120.4 4.0 %fusion.3 = f32[624,1024]{1,0:T(8,128)S(1)} fusion(bf16[2048,1024]{1,0:T(8,128)(2,1)} %param.26, s32[]{:T(128)S(6)} %select_n.216, bf16[624,512]{1,0:T(8,128)(2,1)} %collective-permute-done.8, bf16[624,512]{1,0:T(8,128)(2,1)} %collective-permute-done.6, pred[]{:T(512)S(6)} %eq.27), kind=kOutput, calls=%fused_computation.11 | convolution fusion | flops 1314373632 | bytes 5931013 | tf_op jit(solution)/shard_map/dot_general | solution.py:85
  124.4 3.3 %fusion.5 = f32[624,1024]{1,0:T(8,128)S(1)} fusion(bf16[2048,1024]{1,0:T(8,128)(2,1)S(1)} %copy-done.22, s32[]{:T(128)S(6)} %select_n.216, bf16[624,512]{1,0:T(8,128)(2,1)} %collective-permute-done.8, bf16[624,512]{1,0:T(8,128)(2,1)} %collective-permute-done.6, pred[]{:T(512)S(6)} %eq.27), kind=kOutput, calls=%fused_computation.13 | convolution fusion | flops 1314373632 | bytes 5931013 | tf_op jit(solution)/shard_map/dot_general | solution.py:85
  129.2 3.6 %fusion.20 = f32[624,512]{1,0:T(8,128)} fusion(bf16[624,1024]{1,0:T(8,128)(2,1)S(1)} %multiply_convert_fusion, bf16[1024,2048]{1,0:T(8,128)(2,1)} %param.27, s32[]{:T(128)S(6)} %select_n.218), kind=kOutput, calls=%fused_computation.45 | convolution fusion | flops 654311424 | bytes 3604484 | tf_op jit(solution)/shard_map/dot_general | solution.py:122
  133.2 13.8 %all-to-all-done.1 = bf16[8,2,129,256]{3,1,2,0:T(2,128)(2,1)S(1)} async-done(((bf16[8,2,129,256]{3,1,2,0:T(2,128)(2,1)}), bf16[8,2,129,256]{3,1,2,0:T(2,128)(2,1)S(1)}, u32[]{:S(2)}, u32[]{:S(2)}) %all-to-all-start.1) | async-done | bytes 1056800 | tf_op jit(solution)/shard_map/all_to_all | solution.py:200
  148.5 3.8 %fusion.11 = bf16[624,512]{1,0:T(8,128)(2,1)} fusion(f32[624,512]{1,0:T(8,128)} %collective-permute-done.9, bf16[624,1024]{1,0:T(8,128)(2,1)} %copy-done.15, bf16[1024,2048]{1,0:T(8,128)(2,1)} %param.27, s32[]{:T(128)S(6)} %select_n.217), kind=kOutput, calls=%fused_computation.20 | convolution fusion | flops 654950400 | bytes 4243460 | tf_op jit(solution)/shard_map/dot_general | solution.py:122
  152.2 3.2 %fusion.16 = f32[624,512]{1,0:T(8,128)} fusion(bf16[624,1024]{1,0:T(8,128)(2,1)S(1)} %copy-done.16, bf16[1024,2048]{1,0:T(8,128)(2,1)} %param.27, s32[]{:T(128)S(6)} %select_n.219), kind=kOutput, calls=%fused_computation.41 | convolution fusion | flops 654311424 | bytes 3604484 | tf_op jit(solution)/shard_map/dot_general | solution.py:122
  156.1 1.6 collective-permute-start.11
  158.8 2.2 %fusion.18 = f32[624,512]{1,0:T(8,128)S(1)} fusion(bf16[624,1024]{1,0:T(8,128)(2,1)S(1)} %copy-done.17, bf16[1024,2048]{1,0:T(8,128)(2,1)} %param.27, s32[]{:T(128)S(6)} %select_n.211), kind=kOutput, calls=%fused_computation.43 | convolution fusion | flops 654311424 | bytes 3604484 | tf_op jit(solution)/shard_map/dot_general | solution.py:122
  161.0 12.1 %collective-permute-done.11 = bf16[624,512]{1,0:T(8,128)(2,1)S(1)} collective-permute-done((bf16[624,512]{1,0:T(8,128)(2,1)}, bf16[624,512]{1,0:T(8,128)(2,1)S(1)}, u32[]{:S(2)}, u32[]{:S(2)}) %collective-permute-start.11) | collective-permute-done | bytes 639008 | tf_op jit(solution)/shard_map/ppermute | solution.py:41
  173.2 2.5 %select_convert_fusion = bf16[624,512]{1,0:T(8,128)(2,1)} fusion(f32[624,512]{1,0:T(8,128)S(1)} %get-tuple-element.18, bf16[624,512]{1,0:T(8,128)(2,1)S(1)} %collective-permute-done.11, f32[624,512]{1,0:T(8,128)S(1)} %fusion.18, f32[624,512]{1,0:T(8,128)} %collective-permute-done.10, pred[624]{0:T(1024)(128)(4,1)S(1)} %lt.123), kind=kLoop, calls=%fused_computation.27 | loop fusion | flops 1916928 | bytes 5112432 | tf_op jit(solution)/shard_map/convert_element_type | solution.py:263
  (136 shorter events, 30.0 us)
Async XLA Ops:
  0.6 49.9 %copy-start = (bf16[512,2048]{1,0:T(8,128)(2,1)S(1)}, bf16[512,2048]{1,0:T(8,128)(2,1)}, u32[]{:S(2)}) copy-start(bf16[512,2048]{1,0:T(8,128)(2,1)} %param.23) | copy-start | bytes 6291460
  0.6 18.6 %collective-permute-start = (bf16[624,512]{1,0:T(8,128)(2,1)}, bf16[624,512]{1,0:T(8,128)(2,1)}, u32[]{:S(2)}, u32[]{:S(2)}) collective-permute-start(bf16[624,512]{1,0:T(8,128)(2,1)} %param.15), channel_id=1, source_target_pairs={{0,2},{2,0},{1,3},{3,1},{4,6},{6,4},{5,7},{7,5},{8,10},{10,8},{9,1... | collective-permute-start | bytes 1916936 | tf_op jit(solution)/shard_map/ppermute | solution.py:41
  6.9 5.3 %copy-start.26 = (s32[13]{0:T(128)S(1)}, s32[13]{0:T(128)}, u32[]{:S(2)}) copy-start(s32[13]{0:T(128)} %param.17) | copy-start | bytes 160
  8.0 19.5 %all-to-all-start = ((bf16[2,4,13,16,256]{4,3,2,0,1:T(8,128)(2,1)}), bf16[2,4,13,16,256]{4,3,2,0,1:T(8,128)(2,1)}, u32[]{:S(2)}, u32[]{:S(2)}) async-start(bf16[2,4,13,16,256]{4,3,2,0,1:T(8,128)(2,1)} %copy.70), calls=%async_computation | async-start | bytes 1703936 | tf_op jit(solution)/shard_map/all_to_all | solution.py:176
  12.2 9.1 %copy-start.19 = (s32[13]{0:T(128)S(1)}, s32[13]{0:T(128)}, u32[]{:S(2)}) copy-start(s32[13]{0:T(128)} %param.16) | copy-start | bytes 160
  21.2 8.6 %collective-permute-start.1 = (bf16[2,624,512]{2,1,0:T(8,128)(2,1)S(1)}, bf16[2,624,512]{2,1,0:T(8,128)(2,1)}, u32[]{:S(2)}, u32[]{:S(2)}) collective-permute-start(bf16[2,624,512]{2,1,0:T(8,128)(2,1)S(1)} %maximum_select_fusion), channel_id=1, source_target_pairs={{0,1},{1,0},{2,3},{3,2},{4,5},{5,4},{6,7},{7,6},{8,9},{9,8},{10,11... | collective-permute-start | bytes 3833864 | tf_op jit(solution)/shard_map/ppermute | solution.py:41
  34.5 2.6 %copy-start.23 = (bf16[2048,512]{1,0:T(8,128)(2,1)S(1)}, bf16[2048,512]{1,0:T(8,128)(2,1)}, u32[]{:S(2)}) copy-start(bf16[2048,512]{1,0:T(8,128)(2,1)} %param.20) | copy-start | bytes 6291460
  43.5 3.7 %copy-start.13 = (f32[13,48,128]{2,1,0:T(8,128)S(1)}, f32[13,48,128]{2,1,0:T(8,128)}, u32[]{:S(2)}) copy-start(f32[13,48,128]{2,1,0:T(8,128)} %get-tuple-element.37) | copy-start | bytes 958468
  43.5 3.7 %copy-start.14 = (f32[13,48,128]{2,1,0:T(8,128)S(1)}, f32[13,48,128]{2,1,0:T(8,128)}, u32[]{:S(2)}) copy-start(f32[13,48,128]{2,1,0:T(8,128)} %get-tuple-element.38) | copy-start | bytes 958468
  53.0 4.9 %collective-permute-start.2 = (f32[2,624,512]{2,1,0:T(8,128)S(1)}, f32[2,624,512]{2,1,0:T(8,128)S(1)}, u32[]{:S(2)}, u32[]{:S(2)}) collective-permute-start(f32[2,624,512]{2,1,0:T(8,128)S(1)} %pad_maximum_fusion.1), channel_id=1, source_target_pairs={{0,1},{1,0},{2,3},{3,2},{4,5},{5,4},{6,7},{7,6},{8,9},{9,8},{10,11... | collective-permute-start | bytes 7667720 | tf_op jit(solution)/shard_map/ppermute | solution.py:41
  58.5 30.5 %copy-start.6 = (bf16[624,512]{1,0:T(8,128)(2,1)S(1)}, bf16[624,512]{1,0:T(8,128)(2,1)}, u32[]{:S(2)}) copy-start(bf16[624,512]{1,0:T(8,128)(2,1)} %param.15) | copy-start | bytes 1916932
  58.8 30.2 %collective-permute-start.3 = (f32[624,512]{1,0:T(8,128)S(1)}, f32[624,512]{1,0:T(8,128)S(1)}, u32[]{:S(2)}, u32[]{:S(2)}) collective-permute-start(f32[624,512]{1,0:T(8,128)S(1)} %select_bitcast_fusion), channel_id=1, source_target_pairs={{0,2},{2,0},{1,3},{3,1},{4,6},{6,4},{5,7},{7,5},{8,10},{10,8},{9,1... | collective-permute-start | bytes 3833864 | tf_op jit(solution)/shard_map/ppermute | solution.py:41
  89.3 1.2 collective-permute-start.4
  90.6 3.6 %collective-permute-start.5 = (f32[624,1]{0,1:T(1,128)S(1)}, f32[624,1]{0,1:T(1,128)S(1)}, u32[]{:S(2)}, u32[]{:S(2)}) collective-permute-start(f32[624,1]{0,1:T(1,128)S(1)} %reshape_add_fusion), channel_id=1, source_target_pairs={{0,2},{2,0},{1,3},{3,1},{4,6},{6,4},{5,7},{7,5},{8,10},{10,8},{9,1... | collective-permute-start | bytes 7496 | tf_op jit(solution)/shard_map/ppermute | solution.py:41
  94.4 2.4 %collective-permute-start.7 = (bf16[624,512]{1,0:T(8,128)(2,1)S(1)}, bf16[624,512]{1,0:T(8,128)(2,1)S(1)}, u32[]{:S(2)}, u32[]{:S(2)}) collective-permute-start(bf16[624,512]{1,0:T(8,128)(2,1)S(1)} %multiply_convert_fusion.1), channel_id=1, source_target_pairs={{0,1},{1,0},{2,3},{3,2},{4,5},{5,4},{6,7},{7,6},{8,9},{9,8},{10,11... | collective-permute-start | bytes 1916936 | tf_op jit(solution)/shard_map/ppermute | solution.py:41
  94.6 17.0 %collective-permute-start.6 = (bf16[624,512]{1,0:T(8,128)(2,1)S(1)}, bf16[624,512]{1,0:T(8,128)(2,1)}, u32[]{:S(2)}, u32[]{:S(2)}) collective-permute-start(bf16[624,512]{1,0:T(8,128)(2,1)S(1)} %multiply_convert_fusion.1), channel_id=1, source_target_pairs={{0,2},{2,0},{1,3},{3,1},{4,6},{6,4},{5,7},{7,5},{8,10},{10,8},{9,1... | collective-permute-start | bytes 1916936 | tf_op jit(solution)/shard_map/ppermute | solution.py:41
  96.8 6.1 %copy-start.21 = (bf16[2048,1024]{1,0:T(8,128)(2,1)S(1)}, bf16[2048,1024]{1,0:T(8,128)(2,1)}, u32[]{:S(2)}) copy-start(bf16[2048,1024]{1,0:T(8,128)(2,1)} %param.26) | copy-start | bytes 12582916
  102.9 8.7 %copy-start.10 = (bf16[1,13,4,16,256]{4,3,2,1,0:T(8,128)(2,1)S(1)}, bf16[1,13,4,16,256]{4,3,2,1,0:T(8,128)(2,1)}, u32[]{:S(2)}) copy-start(bf16[1,13,4,16,256]{4,3,2,1,0:T(8,128)(2,1)} %get-tuple-element.33) | copy-start | bytes 1277956
  102.9 8.7 %copy-start.12 = (bf16[1,13,4,16,256]{4,3,2,1,0:T(8,128)(2,1)S(1)}, bf16[1,13,4,16,256]{4,3,2,1,0:T(8,128)(2,1)}, u32[]{:S(2)}) copy-start(bf16[1,13,4,16,256]{4,3,2,1,0:T(8,128)(2,1)} %get-tuple-element.34) | copy-start | bytes 1277956
  111.5 8.9 %collective-permute-start.8 = (bf16[624,512]{1,0:T(8,128)(2,1)}, bf16[624,512]{1,0:T(8,128)(2,1)}, u32[]{:S(2)}, u32[]{:S(2)}) collective-permute-start(bf16[624,512]{1,0:T(8,128)(2,1)} %collective-permute-done.6), channel_id=1, source_target_pairs={{0,1},{1,0},{2,3},{3,2},{4,5},{5,4},{6,7},{7,6},{8,9},{9,8},{10,11... | collective-permute-start | bytes 1916936 | tf_op jit(solution)/shard_map/ppermute | solution.py:41
  114.4 32.6 %all-to-all-start.1 = ((bf16[8,2,129,256]{3,1,2,0:T(2,128)(2,1)}), bf16[8,2,129,256]{3,1,2,0:T(2,128)(2,1)S(1)}, u32[]{:S(2)}, u32[]{:S(2)}) async-start(bf16[8,2,129,256]{3,1,2,0:T(2,128)(2,1)} %copy.77), calls=%async_computation.1 | async-start | bytes 2113536 | tf_op jit(solution)/shard_map/all_to_all | solution.py:200
  120.4 4.0 %copy-start.22 = (bf16[2048,1024]{1,0:T(8,128)(2,1)S(1)}, bf16[2048,1024]{1,0:T(8,128)(2,1)}, u32[]{:S(2)}) copy-start(bf16[2048,1024]{1,0:T(8,128)(2,1)} %param.25) | copy-start | bytes 12582916
  124.4 3.4 %copy-start.4 = (f32[624,1024]{1,0:T(8,128)S(1)}, f32[624,1024]{1,0:T(8,128)}, u32[]{:S(2)}) copy-start(f32[624,1024]{1,0:T(8,128)} %fusion.9) | copy-start | bytes 7667716
  124.4 3.4 %copy-start.5 = (f32[624,1024]{1,0:T(8,128)S(1)}, f32[624,1024]{1,0:T(8,128)}, u32[]{:S(2)}) copy-start(f32[624,1024]{1,0:T(8,128)} %fusion.7) | copy-start | bytes 7667716
  129.2 3.6 %copy-start.15 = (bf16[624,1024]{1,0:T(8,128)(2,1)}, bf16[624,1024]{1,0:T(8,128)(2,1)S(1)}, u32[]{:S(2)}) copy-start(bf16[624,1024]{1,0:T(8,128)(2,1)S(1)} %multiply_convert_fusion) | copy-start | bytes 3833860
  132.8 15.7 %collective-permute-start.9 = (f32[624,512]{1,0:T(8,128)}, f32[624,512]{1,0:T(8,128)}, u32[]{:S(2)}, u32[]{:S(2)}) collective-permute-start(f32[624,512]{1,0:T(8,128)} %fusion.20), channel_id=1, source_target_pairs={{0,1},{1,0},{2,3},{3,2},{4,5},{5,4},{6,7},{7,6},{8,9},{9,8},{10,11... | collective-permute-start | bytes 3833864 | tf_op jit(solution)/shard_map/ppermute | solution.py:41
  148.4 3.8 %copy-start.16 = (bf16[624,1024]{1,0:T(8,128)(2,1)S(1)}, bf16[624,1024]{1,0:T(8,128)(2,1)}, u32[]{:S(2)}) copy-start(bf16[624,1024]{1,0:T(8,128)(2,1)} %copy-done.15) | copy-start | bytes 3833860
  152.2 3.2 %copy-start.3 = (bf16[8,2,129,256]{3,2,1,0:T(8,128)(2,1)S(1)}, bf16[8,2,129,256]{3,2,1,0:T(8,128)(2,1)}, u32[]{:S(2)}) copy-start(bf16[8,2,129,256]{3,2,1,0:T(8,128)(2,1)} %copy-done.2) | copy-start | bytes 3170308
  155.4 5.6 %collective-permute-start.10 = (f32[624,512]{1,0:T(8,128)}, f32[624,512]{1,0:T(8,128)}, u32[]{:S(2)}, u32[]{:S(2)}) collective-permute-start(f32[624,512]{1,0:T(8,128)} %fusion.16), channel_id=1, source_target_pairs={{0,1},{1,0},{2,3},{3,2},{4,5},{5,4},{6,7},{7,6},{8,9},{9,8},{10,11... | collective-permute-start | bytes 3833864 | tf_op jit(solution)/shard_map/ppermute | solution.py:41
  156.1 2.7 %copy-start.17 = (bf16[624,1024]{1,0:T(8,128)(2,1)S(1)}, bf16[624,1024]{1,0:T(8,128)(2,1)}, u32[]{:S(2)}) copy-start(bf16[624,1024]{1,0:T(8,128)(2,1)} %copy-done.15) | copy-start | bytes 3833860
  156.1 17.1 %collective-permute-start.11 = (bf16[624,512]{1,0:T(8,128)(2,1)}, bf16[624,512]{1,0:T(8,128)(2,1)S(1)}, u32[]{:S(2)}, u32[]{:S(2)}) collective-permute-start(bf16[624,512]{1,0:T(8,128)(2,1)} %fusion.11), channel_id=1, source_target_pairs={{0,2},{2,0},{1,3},{3,1},{4,6},{6,4},{5,7},{7,5},{8,10},{10,8},{9,1... | collective-permute-start | bytes 1916936 | tf_op jit(solution)/shard_map/ppermute | solution.py:41
  158.8 16.8 %copy-start.1 = (bf16[512,2048]{1,0:T(8,128)(2,1)S(1)}, bf16[512,2048]{1,0:T(8,128)(2,1)}, u32[]{:S(2)}) copy-start(bf16[512,2048]{1,0:T(8,128)(2,1)} %param.23) | copy-start | bytes 6291460
  (10 other events, 13.6 us)

commit v10 on v8

--- a/solution.py
+++ b/solution.py
@@ -109,6 +109,28 @@
     if link_type is not None:
         theirs = theirs.astype(link_type)
     return mine + swap(theirs, "kvy").astype(jnp.float32)
+
+
+def scatter_halves(matrix_in, weight, link_type):
+    chip = lax.axis_index("kvy")
+    core = lax.axis_index("core")
+    width = weight.shape[1] // (2 * CORES)
+
+    def columns(core_block):
+        return jnp.concatenate(
+            [
+                lax.dynamic_slice_in_dim(weight, (chip_block * CORES + core_block) * width, width, 1)
+                for chip_block in range(2)
+            ],
+            axis=1,
+        )
+
+    keep = jnp.dot(matrix_in, columns(core), preferred_element_type=jnp.float32)
+    give = jnp.dot(matrix_in, columns(1 - core), preferred_element_type=jnp.float32)
+    chip_sum = keep + swap(give, "core")
+    mine = lax.dynamic_slice_in_dim(chip_sum, chip * width, width, 1)
+    theirs = lax.dynamic_slice_in_dim(chip_sum, (1 - chip) * width, width, 1)
+    return mine + swap(theirs.astype(link_type), "kvy").astype(jnp.float32)
 
 
 def row_scale(values, gain_share):
@@ -235,7 +257,7 @@
     normed_share = row_scale(residual_share, gain_share).astype(jnp.bfloat16)
     gate_proj, upward = gather_project(normed_share, (gate_weight, up_weight))
     hidden = (jax.nn.silu(gate_proj) * upward).astype(jnp.bfloat16)
-    mlp_share = scatter_features(hidden, down_weight, jnp.bfloat16)
+    mlp_share = scatter_halves(hidden, down_weight, jnp.bfloat16)
     live_rows = (jnp.arange(span_size, dtype=jnp.int32)[None, :] < span_length[:, None]).reshape(
         total_rows
     )

time: 173 us -> 176 us (1.017)
  waiting for transfers between devices: 64.9 us -> 75.6 us
  other arithmetic: 25.6 us -> 18.5 us
  matrix products: 35.7 us -> 32.8 us
  local copies, waits for them, and re-layouts: 23.5 us -> 25.6 us
    dot_general x2 -> x1, matrix products: 14.1 us -> 1.49 us  [scatter_features(): product = jnp.dot(matrix_in, weight, preferred_element_type=jnp.float32)]
    all_to_all x1, waiting for transfers between devices: 1.72 us -> 14.3 us  [local(): lax.all_to_all(packed, 'req', split_axis=0, concat_axis=0, tiled=True)]
    dot_general x0 -> x2, matrix products: none -> 7.18 us  [the longest x1 4.24 us: scatter_halves(): keep = jnp.dot(matrix_in, columns(core), preferred_element_type=jnp.float32)]
    another operation x2 -> x1, other arithmetic: 5.46 us -> 0.62 us  [scatter_features(): jnp.stack([jnp.where(core == 0, block(k, 0), block(k, 1)) for k in range(...]
    dynamic_slice x0 -> x1, local copies, waits for them, and re-layouts: none -> 4.21 us  [columns(): lax.dynamic_slice_in_dim(weight, (chip_block * CORES + core_block) * widt...]
    add x2 -> x1, other arithmetic: 3.27 us -> 0.6 us  [scatter_features(): chip_sum = keep + swap(give, 'core')]
    dot_general x1 -> x2, matrix products: 5.41 us -> 7.35 us  [gather_project(): jnp.dot(remote_pair, lax.dynamic_slice_in_dim(weight, (1 - chip) * half,...]
    ppermute x11, waiting for transfers between devices: 59.3 us -> 57.3 us  [swap(): return lax.ppermute(values, axis_name, [(0, 1), (1, 0)])]
  transfers between devices with their start and end apart: 13 -> 13, of which waited for: 9 -> 9; matrix products, arithmetic and copies ran while one was open for 32% -> 26% of each run, Pallas kernels for 0% -> 0%
where the time goes in v10:
time: 176 us; the launch traced here: 175 us
  waiting for transfers between devices  75.6 us (43%)
  matrix products  32.8 us (19%)
  local copies, waits for them, and re-layouts  25.6 us (15%)
  starting transfers between devices  20.8 us (12%)
  other arithmetic  18.5 us (11%)
    ppermute x11, waiting for transfers between devices, swap(): return lax.ppermute(values, axis_name, [(0, 1), (1, 0)])  57.3 us
    all_to_all x1, waiting for transfers between devices, local(): lax.all_to_all(packed, 'req', split_axis=0, concat_axis=0, tiled=True)  14.3 us
    ppermute x11, starting transfers between devices, swap(): return lax.ppermute(values, axis_name, [(0, 1), (1, 0)])  10.4 us
    dot_general x2, matrix products, gather_project(): jnp.dot(local_pair, lax.dynamic_slice_in_dim(weight, chip * half, half, 0...  9.58 us
    dot_general x2, matrix products, gather_project(): jnp.dot(remote_pair, lax.dynamic_slice_in_dim(weight, (1 - chip) * half,...  7.35 us
    all_to_all x1, starting transfers between devices, local(): lax.all_to_all(packed, 'req', split_axis=0, concat_axis=0, tiled=True)  6.02 us
    unnamed x56, local copies, waits for them, and re-layouts  4.78 us
    all_to_all x1, starting transfers between devices, local(): lax.all_to_all(stacked, ('kvy', 'core'), split_axis=1, concat_axis=1, til...  4.34 us
  transfers between devices with their start and end apart: 13, of which 9 were waited for; matrix products, arithmetic and copies ran while one was open for 26% of the time, Pallas kernels for 0%

profile of v10, /device:TPU:0, one launch (start us, length us, event | category | flops | bytes accessed | tf_op | source)
XLA Modules:
  0.0 174.7 jit_solution(10931191023290044216)
XLA Ops:
  0.6 3.0 %collective-permute-start = (bf16[624,512]{1,0:T(8,128)(2,1)}, bf16[624,512]{1,0:T(8,128)(2,1)}, u32[]{:S(2)}, u32[]{:S(2)}) collective-permute-start(bf16[624,512]{1,0:T(8,128)(2,1)} %param.15), channel_id=1, source_target_pairs={{0,2},{2,0},{1,3},{3,1},{4,6},{6,4},{5,7},{7,5},{8,10},{10,8},{9,1... | collective-permute-start | bytes 1916936 | tf_op jit(solution)/shard_map/ppermute | solution.py:41
  5.0 2.1 %stack.53 = bf16[1,13,16,4,256]{4,3,2,1,0:T(4,128)(2,1)} reshape(bf16[13,16,1024]{2,1,0:T(8,128)(2,1)} %param.28) | data formatting | bytes 851968 | tf_op jit(solution)/shard_map/stack | solution.py:174
  7.1 1.6 maximum_bitcast_fusion
  9.8 4.3 %all-to-all-start = ((bf16[2,4,13,16,256]{4,3,2,0,1:T(8,128)(2,1)}), bf16[2,4,13,16,256]{4,3,2,0,1:T(8,128)(2,1)}, u32[]{:S(2)}, u32[]{:S(2)}) async-start(bf16[2,4,13,16,256]{4,3,2,0,1:T(8,128)(2,1)} %copy.70), calls=%async_computation | async-start | bytes 1703936 | tf_op jit(solution)/shard_map/all_to_all | solution.py:177
  14.2 5.0 %collective-permute-done = bf16[624,512]{1,0:T(8,128)(2,1)} collective-permute-done((bf16[624,512]{1,0:T(8,128)(2,1)}, bf16[624,512]{1,0:T(8,128)(2,1)}, u32[]{:S(2)}, u32[]{:S(2)}) %collective-permute-start) | collective-permute-done | bytes 639008 | tf_op jit(solution)/shard_map/ppermute | solution.py:41
  19.2 1.9 %maximum_select_fusion = bf16[2,624,512]{2,1,0:T(8,128)(2,1)S(1)} fusion(bf16[1,624,512]{2,1,0:T(8,128)(2,1)} %bitcast.4, bf16[1,624,512]{2,1,0:T(8,128)(2,1)} %bitcast.103, pred[]{:T(512)S(6)} %eq.26), kind=kLoop, calls=%fused_computation.29 | loop fusion | flops 1916928 | bytes 2555905 | tf_op jit(solution)/shard_map/jit(_where)/select_n | solution.py:48
  21.4 2.1 %multiply_cosine_fusion = (f32[13,48,128]{2,1,0:T(8,128)}, f32[13,48,128]{2,1,0:T(8,128)}) fusion(f32[128]{0:T(128)S(1)} %multiply_exponential_fusion, f32[13,48]{1,0:T(8,128)S(1)} %iota_add_fusion), kind=kLoop, calls=%fused_computation.74 | loop fusion | flops 79872 | bytes 641984 | tf_op jit(solution)/shard_map/cos | solution.py:22
  23.5 4.0 %all-to-all-done = bf16[2,4,13,16,256]{4,3,2,0,1:T(8,128)(2,1)} async-done(((bf16[2,4,13,16,256]{4,3,2,0,1:T(8,128)(2,1)}), bf16[2,4,13,16,256]{4,3,2,0,1:T(8,128)(2,1)}, u32[]{:S(2)}, u32[]{:S(2)}) %all-to-all-start) | async-done | bytes 852000 | tf_op jit(solution)/shard_map/all_to_all | solution.py:177
  31.2 2.0 %fusion = f32[624]{0:T(1024)S(1)} fusion(bf16[624,512]{1,0:T(8,128)(2,1)S(1)} %get-tuple-element.21, bf16[624,512]{1,0:T(8,128)(2,1)S(1)} %get-tuple-element.22, bf16[624,512]{1,0:T(8,128)(2,1)S(1)} %get-tuple-element.20, bf16[624,512]{1,0:T(8,128)(2,1)S(1)} %get-tuple-element.19), kind=kLoop, calls=%fused_computation.4 | loop fusion | flops 12778896 | bytes 2558400 | tf_op jit(solution)/shard_map/reduce_sum | solution.py:214
  34.5 1.6 convolution_convert_fusion.1
  37.1 2.6 %fusion.74 = f32[624,512]{1,0:T(8,128)} fusion(bf16[624,2048]{1,0:T(8,128)(2,1)S(1)} %fusion.2, bf16[2048,512]{1,0:T(8,128)(2,1)S(1)} %copy-done.22), kind=kOutput, calls=%fused_computation.153 | convolution fusion | flops 1308622848 | bytes 5931008 | tf_op jit(solution)/shard_map/dot_general | solution.py:221
  39.7 2.1 %reshape.300 = f32[13,48,2,256]{3,2,1,0:T(2,128)S(1)} reshape(f32[624,512]{1,0:T(8,128)} %fusion.74) | data formatting | bytes 2555904 | tf_op jit(solution)/shard_map/reshape | solution.py:223
  43.5 2.1 %fusion.73 = f32[624,256]{1,0:T(8,128)S(1)} fusion(bf16[624,2048]{1,0:T(8,128)(2,1)S(1)} %copy-done.7, bf16[2048,256]{1,0:T(8,128)(2,1)} %param.21), kind=kOutput, calls=%fused_computation.152 | convolution fusion | flops 654311424 | bytes 4243456 | tf_op jit(solution)/shard_map/dot_general | solution.py:225
  52.2 4.8 %collective-permute-done.2 = f32[2,624,512]{2,1,0:T(8,128)S(1)} collective-permute-done((f32[2,624,512]{2,1,0:T(8,128)S(1)}, f32[2,624,512]{2,1,0:T(8,128)S(1)}, u32[]{:S(2)}, u32[]{:S(2)}) %collective-permute-start.2) | collective-permute-done | bytes 2555936 | tf_op jit(solution)/shard_map/ppermute | solution.py:41
  57.9 1.8 %collective-permute-start.3 = (f32[624,512]{1,0:T(8,128)S(1)}, f32[624,512]{1,0:T(8,128)S(1)}, u32[]{:S(2)}, u32[]{:S(2)}) collective-permute-start(f32[624,512]{1,0:T(8,128)S(1)} %select_bitcast_fusion), channel_id=1, source_target_pairs={{0,2},{2,0},{1,3},{3,1},{4,6},{6,4},{5,7},{7,5},{8,10},{10,8},{9,1... | collective-permute-start | bytes 3833864 | tf_op jit(solution)/shard_map/ppermute | solution.py:41
  59.9 28.2 %collective-permute-done.3 = f32[624,512]{1,0:T(8,128)S(1)} collective-permute-done((f32[624,512]{1,0:T(8,128)S(1)}, f32[624,512]{1,0:T(8,128)S(1)}, u32[]{:S(2)}, u32[]{:S(2)}) %collective-permute-start.3) | collective-permute-done | bytes 1277984 | tf_op jit(solution)/shard_map/ppermute | solution.py:41
  89.7 1.7 collective-permute-start.5
  93.6 4.2 %constant_dynamic-slice_fusion.3 = (bf16[1024,512]{1,0:T(8,128)(2,1)}, bf16[1024,512]{1,0:T(8,128)(2,1)}, bf16[1024,512]{1,0:T(8,128)(2,1)}, bf16[1024,512]{1,0:T(8,128)(2,1)}) fusion(bf16[1024,2048]{1,0:T(8,128)(2,1)} %param.27, s32[]{:T(128)S(6)} %select_n.225, s32[]{:T(128)S(6)} %select_n.226, s32[]{:T(128)S(6)} %select_n.228, s32[]{:T(128)S(6)} %select_n.227), kind=kLoop, calls=%fused_computation.116 | loop fusion | bytes 8388624 | tf_op jit(solution)/shard_map/dynamic_slice | solution.py:122
  97.8 1.7 collective-permute-start.6
  100.8 5.2 %fusion.17 = f32[624,1024]{1,0:T(8,128)} fusion(bf16[2048,1024]{1,0:T(8,128)(2,1)} %param.25, s32[]{:T(128)S(6)} %select_n.222, bf16[624,512]{1,0:T(8,128)(2,1)S(1)} %collective-permute-done.7, bf16[624,512]{1,0:T(8,128)(2,1)S(1)} %multiply_convert_fusion.1, pred[]{:T(512)S(6)} %eq.27), kind=kOutput, calls=%fused_computation.25 | convolution fusion | flops 1314373632 | bytes 5931013 | tf_op jit(solution)/shard_map/dot_general | solution.py:69
  106.0 4.4 %fusion.15 = f32[624,1024]{1,0:T(8,128)} fusion(bf16[2048,1024]{1,0:T(8,128)(2,1)S(1)} %copy-done.20, s32[]{:T(128)S(6)} %select_n.222, bf16[624,512]{1,0:T(8,128)(2,1)} %copy-done.24, bf16[624,512]{1,0:T(8,128)(2,1)S(1)} %multiply_convert_fusion.1, pred[]{:T(512)S(6)} %eq.27), kind=kOutput, calls=%fused_computation.23 | convolution fusion | flops 1314373632 | bytes 5931013 | tf_op jit(solution)/shard_map/dot_general | solution.py:69
  110.4 4.3 %collective-permute-done.6 = bf16[624,512]{1,0:T(8,128)(2,1)} collective-permute-done((bf16[624,512]{1,0:T(8,128)(2,1)S(1)}, bf16[624,512]{1,0:T(8,128)(2,1)}, u32[]{:S(2)}, u32[]{:S(2)}) %collective-permute-start.6) | collective-permute-done | bytes 639008 | tf_op jit(solution)/shard_map/ppermute | solution.py:41
  115.7 1.8 %copy.77 = bf16[8,2,129,256]{3,1,2,0:T(2,128)(2,1)} copy(bf16[8,2,129,256]{3,2,1,0:T(8,128)(2,1)S(1)} %select_select_fusion) | data formatting | bytes 2113536 | tf_op jit(solution)/shard_map/jit(_where)/select_n | solution.py:199
  117.5 6.0 %all-to-all-start.1 = ((bf16[8,2,129,256]{3,1,2,0:T(2,128)(2,1)}), bf16[8,2,129,256]{3,1,2,0:T(2,128)(2,1)S(1)}, u32[]{:S(2)}, u32[]{:S(2)}) async-start(bf16[8,2,129,256]{3,1,2,0:T(2,128)(2,1)} %copy.77), calls=%async_computation.1 | async-start | bytes 2113536 | tf_op jit(solution)/shard_map/all_to_all | solution.py:201
  123.5 4.0 %fusion.11 = f32[624,1024]{1,0:T(8,128)S(1)} fusion(bf16[2048,1024]{1,0:T(8,128)(2,1)} %param.26, s32[]{:T(128)S(6)} %select_n.224, bf16[624,512]{1,0:T(8,128)(2,1)} %collective-permute-done.8, bf16[624,512]{1,0:T(8,128)(2,1)} %collective-permute-done.6, pred[]{:T(512)S(6)} %eq.27), kind=kOutput, calls=%fused_computation.19 | convolution fusion | flops 1314373632 | bytes 5931013 | tf_op jit(solution)/shard_map/dot_general | solution.py:85
  127.6 3.3 %fusion.13 = f32[624,1024]{1,0:T(8,128)S(1)} fusion(bf16[2048,1024]{1,0:T(8,128)(2,1)S(1)} %copy-done.21, s32[]{:T(128)S(6)} %select_n.224, bf16[624,512]{1,0:T(8,128)(2,1)} %collective-permute-done.8, bf16[624,512]{1,0:T(8,128)(2,1)} %collective-permute-done.6, pred[]{:T(512)S(6)} %eq.27), kind=kOutput, calls=%fused_computation.21 | convolution fusion | flops 1314373632 | bytes 5931013 | tf_op jit(solution)/shard_map/dot_general | solution.py:85
  132.5 2.9 %fusion.7 = f32[624,1024]{1,0:T(8,128)} fusion(bf16[624,1024]{1,0:T(8,128)(2,1)S(1)} %multiply_convert_fusion, bf16[1024,512]{1,0:T(8,128)(2,1)S(1)} %copy-done.15, bf16[1024,512]{1,0:T(8,128)(2,1)S(1)} %copy-done.16), kind=kOutput, calls=%fused_computation.15 | convolution fusion | flops 1312817152 | bytes 5931008 | tf_op jit(solution)/shard_map/dot_general | solution.py:129
  135.8 14.3 %all-to-all-done.1 = bf16[8,2,129,256]{3,1,2,0:T(2,128)(2,1)S(1)} async-done(((bf16[8,2,129,256]{3,1,2,0:T(2,128)(2,1)}), bf16[8,2,129,256]{3,1,2,0:T(2,128)(2,1)S(1)}, u32[]{:S(2)}, u32[]{:S(2)}) %all-to-all-start.1) | async-done | bytes 1056800 | tf_op jit(solution)/shard_map/all_to_all | solution.py:201
  151.6 1.9 %gather_fusion.1 = bf16[13,129,256]{2,1,0:T(8,128)(2,1)S(1)} fusion(bf16[16,129,256]{2,1,0:T(8,128)(2,1)} %bitcast.100, s32[1024]{0:T(1024)S(1)} %pad_clamp_fusion), kind=kCustom, calls=%fused_computation.1 | custom fusion | bytes 1717300 | tf_op jit(solution)/shard_map/jit(_take)/gather | solution.py:209
  153.5 4.2 %fusion.19 = f32[624,1024]{1,0:T(8,128)S(1)} fusion(f32[624,1024]{1,0:T(8,128)} %collective-permute-done.9, bf16[624,1024]{1,0:T(8,128)(2,1)} %copy-done.14, bf16[1024,512]{1,0:T(8,128)(2,1)} %get-tuple-element.16, bf16[1024,512]{1,0:T(8,128)(2,1)} %get-tuple-element.15), kind=kOutput, calls=%fused_computation.27 | convolution fusion | flops 1313456128 | bytes 8486912 | tf_op jit(solution)/shard_map/dot_general | solution.py:128
  157.8 1.6 collective-permute-start.10
  160.6 13.0 %collective-permute-done.10 = bf16[624,512]{1,0:T(8,128)(2,1)S(1)} collective-permute-done((bf16[624,512]{1,0:T(8,128)(2,1)S(1)}, bf16[624,512]{1,0:T(8,128)(2,1)S(1)}, u32[]{:S(2)}, u32[]{:S(2)}) %collective-permute-start.10) | collective-permute-done | bytes 639008 | tf_op jit(solution)/shard_map/ppermute | solution.py:41
  (132 shorter events, 29.5 us)
Async XLA Ops:
  0.6 49.1 %copy-start = (bf16[512,2048]{1,0:T(8,128)(2,1)S(1)}, bf16[512,2048]{1,0:T(8,128)(2,1)}, u32[]{:S(2)}) copy-start(bf16[512,2048]{1,0:T(8,128)(2,1)} %param.23) | copy-start | bytes 6291460
  0.6 18.6 %collective-permute-start = (bf16[624,512]{1,0:T(8,128)(2,1)}, bf16[624,512]{1,0:T(8,128)(2,1)}, u32[]{:S(2)}, u32[]{:S(2)}) collective-permute-start(bf16[624,512]{1,0:T(8,128)(2,1)} %param.15), channel_id=1, source_target_pairs={{0,2},{2,0},{1,3},{3,1},{4,6},{6,4},{5,7},{7,5},{8,10},{10,8},{9,1... | collective-permute-start | bytes 1916936 | tf_op jit(solution)/shard_map/ppermute | solution.py:41
  8.7 5.4 %copy-start.25 = (s32[13]{0:T(128)S(1)}, s32[13]{0:T(128)}, u32[]{:S(2)}) copy-start(s32[13]{0:T(128)} %param.17) | copy-start | bytes 160
  9.8 11.5 %copy-start.18 = (s32[13]{0:T(128)S(1)}, s32[13]{0:T(128)}, u32[]{:S(2)}) copy-start(s32[13]{0:T(128)} %param.16) | copy-start | bytes 160
  9.8 17.7 %all-to-all-start = ((bf16[2,4,13,16,256]{4,3,2,0,1:T(8,128)(2,1)}), bf16[2,4,13,16,256]{4,3,2,0,1:T(8,128)(2,1)}, u32[]{:S(2)}, u32[]{:S(2)}) async-start(bf16[2,4,13,16,256]{4,3,2,0,1:T(8,128)(2,1)} %copy.70), calls=%async_computation | async-start | bytes 1703936 | tf_op jit(solution)/shard_map/all_to_all | solution.py:177
  21.1 8.6 %collective-permute-start.1 = (bf16[2,624,512]{2,1,0:T(8,128)(2,1)S(1)}, bf16[2,624,512]{2,1,0:T(8,128)(2,1)}, u32[]{:S(2)}, u32[]{:S(2)}) collective-permute-start(bf16[2,624,512]{2,1,0:T(8,128)(2,1)S(1)} %maximum_select_fusion), channel_id=1, source_target_pairs={{0,1},{1,0},{2,3},{3,2},{4,5},{5,4},{6,7},{7,6},{8,9},{9,8},{10,11... | collective-permute-start | bytes 3833864 | tf_op jit(solution)/shard_map/ppermute | solution.py:41
  31.2 2.1 %copy-start.17 = (f32[2048]{0:T(1024)S(1)}, f32[2048]{0:T(1024)}, u32[]{:S(2)}) copy-start(f32[2048]{0:T(1024)} %param.19) | copy-start | bytes 24580
  34.5 2.6 %copy-start.22 = (bf16[2048,512]{1,0:T(8,128)(2,1)S(1)}, bf16[2048,512]{1,0:T(8,128)(2,1)}, u32[]{:S(2)}) copy-start(bf16[2048,512]{1,0:T(8,128)(2,1)} %param.20) | copy-start | bytes 6291460
  41.8 1.7 copy-start.7
  43.5 3.7 %copy-start.12 = (f32[13,48,128]{2,1,0:T(8,128)S(1)}, f32[13,48,128]{2,1,0:T(8,128)}, u32[]{:S(2)}) copy-start(f32[13,48,128]{2,1,0:T(8,128)} %get-tuple-element.33) | copy-start | bytes 958468
  43.5 3.7 %copy-start.13 = (f32[13,48,128]{2,1,0:T(8,128)S(1)}, f32[13,48,128]{2,1,0:T(8,128)}, u32[]{:S(2)}) copy-start(f32[13,48,128]{2,1,0:T(8,128)} %get-tuple-element.34) | copy-start | bytes 958468
  45.6 1.8 %copy-start.8 = (bf16[1,13,4,16,256]{4,3,2,1,0:T(8,128)(2,1)S(1)}, bf16[1,13,4,16,256]{4,3,2,1,0:T(8,128)(2,1)}, u32[]{:S(2)}) copy-start(bf16[1,13,4,16,256]{4,3,2,1,0:T(8,128)(2,1)} %get-tuple-element.29) | copy-start | bytes 1277956
  52.1 4.9 %collective-permute-start.2 = (f32[2,624,512]{2,1,0:T(8,128)S(1)}, f32[2,624,512]{2,1,0:T(8,128)S(1)}, u32[]{:S(2)}, u32[]{:S(2)}) collective-permute-start(f32[2,624,512]{2,1,0:T(8,128)S(1)} %pad_maximum_fusion.1), channel_id=1, source_target_pairs={{0,1},{1,0},{2,3},{3,2},{4,5},{5,4},{6,7},{7,6},{8,9},{9,8},{10,11... | collective-permute-start | bytes 7667720 | tf_op jit(solution)/shard_map/ppermute | solution.py:41
  57.6 2.1 %copy-start.19 = (s32[13]{0:T(128)S(1)}, s32[13]{0:T(128)}, u32[]{:S(2)}) copy-start(s32[13]{0:T(128)} %param.18) | copy-start | bytes 160
  57.6 30.5 %copy-start.5 = (bf16[624,512]{1,0:T(8,128)(2,1)S(1)}, bf16[624,512]{1,0:T(8,128)(2,1)}, u32[]{:S(2)}) copy-start(bf16[624,512]{1,0:T(8,128)(2,1)} %param.15) | copy-start | bytes 1916932
  57.9 30.2 %collective-permute-start.3 = (f32[624,512]{1,0:T(8,128)S(1)}, f32[624,512]{1,0:T(8,128)S(1)}, u32[]{:S(2)}, u32[]{:S(2)}) collective-permute-start(f32[624,512]{1,0:T(8,128)S(1)} %select_bitcast_fusion), channel_id=1, source_target_pairs={{0,2},{2,0},{1,3},{3,1},{4,6},{6,4},{5,7},{7,5},{8,10},{10,8},{9,1... | collective-permute-start | bytes 3833864 | tf_op jit(solution)/shard_map/ppermute | solution.py:41
  88.5 1.2 collective-permute-start.4
  89.7 3.6 %collective-permute-start.5 = (f32[624,1]{0,1:T(1,128)S(1)}, f32[624,1]{0,1:T(1,128)S(1)}, u32[]{:S(2)}, u32[]{:S(2)}) collective-permute-start(f32[624,1]{0,1:T(1,128)S(1)} %reshape_add_fusion), channel_id=1, source_target_pairs={{0,2},{2,0},{1,3},{3,1},{4,6},{6,4},{5,7},{7,5},{8,10},{10,8},{9,1... | collective-permute-start | bytes 7496 | tf_op jit(solution)/shard_map/ppermute | solution.py:41
  93.5 6.5 %collective-permute-start.7 = (bf16[624,512]{1,0:T(8,128)(2,1)S(1)}, bf16[624,512]{1,0:T(8,128)(2,1)S(1)}, u32[]{:S(2)}, u32[]{:S(2)}) collective-permute-start(bf16[624,512]{1,0:T(8,128)(2,1)S(1)} %multiply_convert_fusion.1), channel_id=1, source_target_pairs={{0,1},{1,0},{2,3},{3,2},{4,5},{5,4},{6,7},{7,6},{8,9},{9,8},{10,11... | collective-permute-start | bytes 1916936 | tf_op jit(solution)/shard_map/ppermute | solution.py:41
  97.8 16.9 %collective-permute-start.6 = (bf16[624,512]{1,0:T(8,128)(2,1)S(1)}, bf16[624,512]{1,0:T(8,128)(2,1)}, u32[]{:S(2)}, u32[]{:S(2)}) collective-permute-start(bf16[624,512]{1,0:T(8,128)(2,1)S(1)} %multiply_convert_fusion.1), channel_id=1, source_target_pairs={{0,2},{2,0},{1,3},{3,1},{4,6},{6,4},{5,7},{7,5},{8,10},{10,8},{9,1... | collective-permute-start | bytes 1916936 | tf_op jit(solution)/shard_map/ppermute | solution.py:41
  99.9 6.0 %copy-start.20 = (bf16[2048,1024]{1,0:T(8,128)(2,1)S(1)}, bf16[2048,1024]{1,0:T(8,128)(2,1)}, u32[]{:S(2)}) copy-start(bf16[2048,1024]{1,0:T(8,128)(2,1)} %param.26) | copy-start | bytes 12582916
  106.0 8.7 %copy-start.9 = (bf16[1,13,4,16,256]{4,3,2,1,0:T(8,128)(2,1)S(1)}, bf16[1,13,4,16,256]{4,3,2,1,0:T(8,128)(2,1)}, u32[]{:S(2)}) copy-start(bf16[1,13,4,16,256]{4,3,2,1,0:T(8,128)(2,1)} %get-tuple-element.29) | copy-start | bytes 1277956
  106.0 8.7 %copy-start.11 = (bf16[1,13,4,16,256]{4,3,2,1,0:T(8,128)(2,1)S(1)}, bf16[1,13,4,16,256]{4,3,2,1,0:T(8,128)(2,1)}, u32[]{:S(2)}) copy-start(bf16[1,13,4,16,256]{4,3,2,1,0:T(8,128)(2,1)} %get-tuple-element.30) | copy-start | bytes 1277956
  114.7 8.9 %collective-permute-start.8 = (bf16[624,512]{1,0:T(8,128)(2,1)}, bf16[624,512]{1,0:T(8,128)(2,1)}, u32[]{:S(2)}, u32[]{:S(2)}) collective-permute-start(bf16[624,512]{1,0:T(8,128)(2,1)} %collective-permute-done.6), channel_id=1, source_target_pairs={{0,1},{1,0},{2,3},{3,2},{4,5},{5,4},{6,7},{7,6},{8,9},{9,8},{10,11... | collective-permute-start | bytes 1916936 | tf_op jit(solution)/shard_map/ppermute | solution.py:41
  117.5 32.6 %all-to-all-start.1 = ((bf16[8,2,129,256]{3,1,2,0:T(2,128)(2,1)}), bf16[8,2,129,256]{3,1,2,0:T(2,128)(2,1)S(1)}, u32[]{:S(2)}, u32[]{:S(2)}) async-start(bf16[8,2,129,256]{3,1,2,0:T(2,128)(2,1)} %copy.77), calls=%async_computation.1 | async-start | bytes 2113536 | tf_op jit(solution)/shard_map/all_to_all | solution.py:201
  123.5 4.0 %copy-start.21 = (bf16[2048,1024]{1,0:T(8,128)(2,1)S(1)}, bf16[2048,1024]{1,0:T(8,128)(2,1)}, u32[]{:S(2)}) copy-start(bf16[2048,1024]{1,0:T(8,128)(2,1)} %param.25) | copy-start | bytes 12582916
  127.5 3.4 %copy-start.3 = (f32[624,1024]{1,0:T(8,128)S(1)}, f32[624,1024]{1,0:T(8,128)}, u32[]{:S(2)}) copy-start(f32[624,1024]{1,0:T(8,128)} %fusion.17) | copy-start | bytes 7667716
  127.5 3.4 %copy-start.4 = (f32[624,1024]{1,0:T(8,128)S(1)}, f32[624,1024]{1,0:T(8,128)}, u32[]{:S(2)}) copy-start(f32[624,1024]{1,0:T(8,128)} %fusion.15) | copy-start | bytes 7667716
  132.4 3.1 %copy-start.14 = (bf16[624,1024]{1,0:T(8,128)(2,1)}, bf16[624,1024]{1,0:T(8,128)(2,1)S(1)}, u32[]{:S(2)}) copy-start(bf16[624,1024]{1,0:T(8,128)(2,1)S(1)} %multiply_convert_fusion) | copy-start | bytes 3833860
  135.4 18.1 %collective-permute-start.9 = (f32[624,1024]{1,0:T(8,128)}, f32[624,1024]{1,0:T(8,128)}, u32[]{:S(2)}, u32[]{:S(2)}) collective-permute-start(f32[624,1024]{1,0:T(8,128)} %fusion.7), channel_id=1, source_target_pairs={{0,1},{1,0},{2,3},{3,2},{4,5},{5,4},{6,7},{7,6},{8,9},{9,8},{10,11... | collective-permute-start | bytes 7667720 | tf_op jit(solution)/shard_map/ppermute | solution.py:41
  157.8 15.8 %collective-permute-start.10 = (bf16[624,512]{1,0:T(8,128)(2,1)S(1)}, bf16[624,512]{1,0:T(8,128)(2,1)S(1)}, u32[]{:S(2)}, u32[]{:S(2)}) collective-permute-start(bf16[624,512]{1,0:T(8,128)(2,1)S(1)} %dynamic-slice_convert_fusion), channel_id=1, source_target_pairs={{0,2},{2,0},{1,3},{3,1},{4,6},{6,4},{5,7},{7,5},{8,10},{10,8},{9,1... | collective-permute-start | bytes 1916936 | tf_op jit(solution)/shard_map/ppermute | solution.py:41
  159.6 15.1 %copy-start.1 = (bf16[512,2048]{1,0:T(8,128)(2,1)S(1)}, bf16[512,2048]{1,0:T(8,128)(2,1)}, u32[]{:S(2)}) copy-start(bf16[512,2048]{1,0:T(8,128)(2,1)} %param.23) | copy-start | bytes 6291460
  (8 other events, 9.7 us)

commit v11 on v8

--- a/solution.py
+++ b/solution.py
@@ -109,6 +109,21 @@
     if link_type is not None:
         theirs = theirs.astype(link_type)
     return mine + swap(theirs, "kvy").astype(jnp.float32)
+
+
+def project_heads(mixed, weight, weight_far):
+    chip = lax.axis_index("kvy")
+    core = lax.axis_index("core")
+    half = weight_far.shape[1]
+    width = half // CORES
+    mixed_far = swap(mixed, "kvy")
+    weight_near = lax.dynamic_slice_in_dim(weight, chip * half, half, 1)
+    chip_sum = jnp.dot(mixed, weight_near, preferred_element_type=jnp.float32) + jnp.dot(
+        mixed_far, weight_far, preferred_element_type=jnp.float32
+    )
+    keep = lax.dynamic_slice_in_dim(chip_sum, core * width, width, 1)
+    give = lax.dynamic_slice_in_dim(chip_sum, (1 - core) * width, width, 1)
+    return keep + swap(give, "core")
 
 
 def row_scale(values, gain_share):
@@ -188,6 +203,12 @@
     decode_kv = (decode_rows[:, :past_size], decode_rows[:, past_size:2 * past_size])
 
     x_whole = gather_features(activations)
+    chip_cols = output_weight.shape[1] // chips
+    far_cols = lax.dynamic_slice_in_dim(
+        output_weight, (1 - lax.axis_index("kvy")) * chip_cols, chip_cols, 1
+    )
+    far_cols, x_whole = lax.optimization_barrier((far_cols, x_whole))
+    weight_far = swap(far_cols, "kvy")
     x_float = x_whole.astype(jnp.float32)
     square_sum = jnp.sum(x_float * x_float, axis=-1, keepdims=True)
     normalized_input = (
@@ -228,7 +249,7 @@
         "rkgcs,rskd->rckgd", weights, combined_values, preferred_element_type=jnp.float32
     )
     mixed_heads = mixed_heads.astype(jnp.bfloat16).reshape(total_rows, local_q * HEAD_WIDTH)
-    head_share = scatter_features(mixed_heads, output_weight)
+    head_share = project_heads(mixed_heads, output_weight, weight_far)
     residual_share = activations.astype(jnp.float32) + head_share
 
     gain_share = lax.dynamic_slice_in_dim(feedforward_gain, kv_index * width_share, width_share)

time: 173 us -> 176 us (1.017)
  local copies, waits for them, and re-layouts: 23.5 us -> 25.9 us
    dot_general x0 -> x2, matrix products: none -> 2.92 us  [the longest x1 2.09 us: project_heads(): jnp.dot(mixed_far, weight_far, preferred_element_type=jnp.float32)]
    ppermute x11 -> x12, waiting for transfers between devices: 59.3 us -> 61.8 us  [swap(): return lax.ppermute(values, axis_name, [(0, 1), (1, 0)])]
    dot_general x2 -> x1, matrix products: 14.1 us -> 12.6 us  [scatter_features(): product = jnp.dot(matrix_in, weight, preferred_element_type=jnp.float32)]
    unnamed x46 -> x54, local copies, waits for them, and re-layouts: 5.61 us -> 6.58 us
    another operation x2 -> x1, other arithmetic: 5.46 us -> 4.75 us  [scatter_features(): jnp.stack([jnp.where(core == 0, block(k, 0), block(k, 1)) for k in range(...]
    ppermute x11 -> x12, starting transfers between devices: 10.5 us -> 10.8 us  [swap(): return lax.ppermute(values, axis_name, [(0, 1), (1, 0)])]
  transfers between devices with their start and end apart: 13 -> 14, of which waited for: 9 -> 9; matrix products, arithmetic and copies ran while one was open for 32% -> 34% of each run, Pallas kernels for 0% -> 0%
where the time goes in v11:
time: 176 us; the launch traced here: 175 us
  waiting for transfers between devices  66 us (38%)
  matrix products  37.1 us (21%)
  local copies, waits for them, and re-layouts  25.9 us (15%)
  other arithmetic  24.5 us (14%)
  starting transfers between devices  20.7 us (12%)
    ppermute x12, waiting for transfers between devices, swap(): return lax.ppermute(values, axis_name, [(0, 1), (1, 0)])  61.8 us
    dot_general x1, matrix products, scatter_features(): product = jnp.dot(matrix_in, weight, preferred_element_type=jnp.float32)  12.6 us
    ppermute x12, starting transfers between devices, swap(): return lax.ppermute(values, axis_name, [(0, 1), (1, 0)])  10.8 us
    dot_general x2, matrix products, gather_project(): jnp.dot(local_pair, lax.dynamic_slice_in_dim(weight, chip * half, half, 0...  9.58 us
    unnamed x54, local copies, waits for them, and re-layouts  6.58 us
    all_to_all x1, starting transfers between devices, local(): lax.all_to_all(packed, 'req', split_axis=0, concat_axis=0, tiled=True)  5.7 us
    dot_general x1, matrix products, gather_project(): jnp.dot(remote_pair, lax.dynamic_slice_in_dim(weight, (1 - chip) * half,...  5.38 us
    another operation x1, other arithmetic, scatter_features(): jnp.stack([jnp.where(core == 0, block(k, 0), block(k, 1)) for k in range(...  4.75 us
  transfers between devices with their start and end apart: 14, of which 9 were waited for; matrix products, arithmetic and copies ran while one was open for 34% of the time, Pallas kernels for 0%

profile of v11, /device:TPU:0, one launch (start us, length us, event | category | flops | bytes accessed | tf_op | source)
XLA Modules:
  0.0 175.3 jit_solution(2206434420135187366)
XLA Ops:
  0.6 3.0 %collective-permute-start = (bf16[624,512]{1,0:T(8,128)(2,1)}, bf16[624,512]{1,0:T(8,128)(2,1)}, u32[]{:S(2)}, u32[]{:S(2)}) collective-permute-start(bf16[624,512]{1,0:T(8,128)(2,1)} %param.15), channel_id=1, source_target_pairs={{0,2},{2,0},{1,3},{3,1},{4,6},{6,4},{5,7},{7,5},{8,10},{10,8},{9,1... | collective-permute-start | bytes 1916936 | tf_op jit(solution)/shard_map/ppermute | solution.py:41
  8.0 4.2 %all-to-all-start = ((bf16[2,4,13,16,256]{4,3,2,0,1:T(8,128)(2,1)}), bf16[2,4,13,16,256]{4,3,2,0,1:T(8,128)(2,1)}, u32[]{:S(2)}, u32[]{:S(2)}) async-start(bf16[2,4,13,16,256]{4,3,2,0,1:T(8,128)(2,1)} %copy.70), calls=%async_computation | async-start | bytes 1703936 | tf_op jit(solution)/shard_map/all_to_all | solution.py:170
  12.4 6.9 %collective-permute-done = bf16[624,512]{1,0:T(8,128)(2,1)} collective-permute-done((bf16[624,512]{1,0:T(8,128)(2,1)}, bf16[624,512]{1,0:T(8,128)(2,1)}, u32[]{:S(2)}, u32[]{:S(2)}) %collective-permute-start) | collective-permute-done | bytes 639008 | tf_op jit(solution)/shard_map/ppermute | solution.py:41
  19.2 2.0 %maximum_select_fusion = bf16[2,624,512]{2,1,0:T(8,128)(2,1)S(1)} fusion(bf16[1,624,512]{2,1,0:T(8,128)(2,1)} %bitcast.4, bf16[1,624,512]{2,1,0:T(8,128)(2,1)} %bitcast.105, pred[]{:T(512)S(6)} %eq.27), kind=kLoop, calls=%fused_computation.22 | loop fusion | flops 1916928 | bytes 2555905 | tf_op jit(solution)/shard_map/jit(_where)/select_n | solution.py:48
  23.1 2.0 %multiply_cosine_fusion = (f32[13,48,128]{2,1,0:T(8,128)}, f32[13,48,128]{2,1,0:T(8,128)}) fusion(f32[128]{0:T(128)S(1)} %multiply_exponential_fusion, f32[13,48]{1,0:T(8,128)S(1)} %iota_add_fusion), kind=kLoop, calls=%fused_computation.72 | loop fusion | flops 79872 | bytes 641984 | tf_op jit(solution)/shard_map/cos | solution.py:22
  25.1 2.4 %all-to-all-done = bf16[2,4,13,16,256]{4,3,2,0,1:T(8,128)(2,1)} async-done(((bf16[2,4,13,16,256]{4,3,2,0,1:T(8,128)(2,1)}), bf16[2,4,13,16,256]{4,3,2,0,1:T(8,128)(2,1)}, u32[]{:S(2)}, u32[]{:S(2)}) %all-to-all-start) | async-done | bytes 852000 | tf_op jit(solution)/shard_map/all_to_all | solution.py:170
  29.7 1.4 select_bitcast_fusion.7
  34.5 2.1 %fusion.41 = (bf16[13,48,1,128]{3,1,0,2:T(8,128)(2,1)S(1)}, bf16[13,48,1,128]{3,1,0,2:T(8,128)(2,1)}) fusion(f32[13,48,1,256]{3,1,0,2:T(8,128)S(1)} %bitcast.110, f32[128]{0:T(128)S(1)} %multiply_exponential_fusion, f32[13,48]{1,0:T(8,128)S(1)} %iota_add_fusion), kind=kLoop, calls=%fused_computation.80 | loop fusion | flops 718848 | bytes 961472 | tf_op jit(solution)/shard_map/convert.7
  36.5 2.6 %fusion.70 = f32[624,512]{1,0:T(8,128)} fusion(bf16[2048,512]{1,0:T(8,128)(2,1)S(1)} %copy-done.20, bf16[624,2048]{1,0:T(8,128)(2,1)S(1)} %pad_maximum_fusion, f32[2048]{0:T(1024)S(1)} %copy-done.23, f32[624]{0:T(1024)S(1)} %add_rsqrt_fusion), kind=kOutput, calls=%fused_computation.144 | convolution fusion | flops 1313734656 | bytes 5941696 | tf_op jit(solution)/shard_map/dot_general | solution.py:220
  39.1 2.3 %reshape.301 = f32[13,48,2,256]{3,2,1,0:T(2,128)S(1)} reshape(f32[624,512]{1,0:T(8,128)} %fusion.70) | data formatting | bytes 2555904 | tf_op jit(solution)/shard_map/reshape | solution.py:222
  43.1 2.2 %convolution_convert_fusion.1 = bf16[624,256]{1,0:T(8,128)(2,1)S(1)} fusion(bf16[2048,256]{1,0:T(8,128)(2,1)} %param.22, bf16[624,2048]{1,0:T(8,128)(2,1)S(1)} %copy-done.4, f32[2048]{0:T(1024)S(1)} %copy-done.24, f32[624]{0:T(1024)S(1)} %add_rsqrt_fusion), kind=kOutput, calls=%fused_computation.41 | convolution fusion | flops 659582976 | bytes 3934656 | tf_op jit(solution)/shard_map/dot_general | solution.py:229
  45.4 1.8 %collective-permute-start.3 = (bf16[512,1024]{1,0:T(8,128)(2,1)}, bf16[512,1024]{1,0:T(8,128)(2,1)}, u32[]{:S(2)}, u32[]{:S(2)}) collective-permute-start(bf16[512,1024]{1,0:T(8,128)(2,1)} %constant_dynamic-slice_fusion.1), channel_id=1, source_target_pairs={{0,2},{2,0},{1,3},{3,1},{4,6},{6,4},{5,7},{7,5},{8,10},{10,8},{9,1... | collective-permute-start | bytes 3145736 | tf_op jit(solution)/shard_map/ppermute | solution.py:41
  51.3 32.4 %collective-permute-done.2 = bf16[624,512]{1,0:T(8,128)(2,1)S(1)} collective-permute-done((bf16[624,512]{1,0:T(8,128)(2,1)S(1)}, bf16[624,512]{1,0:T(8,128)(2,1)S(1)}, u32[]{:S(2)}, u32[]{:S(2)}) %collective-permute-start.2) | collective-permute-done | bytes 639008 | tf_op jit(solution)/shard_map/ppermute | solution.py:41
  83.7 2.1 %convolution_add_fusion = f32[624,1024]{1,0:T(8,128)S(1)} fusion(f32[624,1024]{1,0:T(8,128)S(1)} %fusion.19, bf16[624,512]{1,0:T(8,128)(2,1)S(1)} %collective-permute-done.2, bf16[512,1024]{1,0:T(8,128)(2,1)} %collective-permute-done.3), kind=kOutput, calls=%fused_computation.19 | convolution fusion | flops 654950400 | bytes 6799360 | tf_op jit(solution)/shard_map/dot_general | solution.py:121
  85.8 1.5 copy-done.2
  87.9 2.6 %collective-permute-done.4 = f32[624,512]{1,0:T(8,128)} collective-permute-done((f32[624,512]{1,0:T(8,128)S(1)}, f32[624,512]{1,0:T(8,128)}, u32[]{:S(2)}, u32[]{:S(2)}) %collective-permute-start.4) | collective-permute-done | bytes 1277984 | tf_op jit(solution)/shard_map/ppermute | solution.py:41
  90.6 2.0 %multiply_reduce_fusion = (f32[624]{0:T(1024)S(1)}, f32[624,512]{1,0:T(8,128)S(1)}) fusion(f32[624,512]{1,0:T(8,128)} %collective-permute-done.4, f32[624,1024]{1,0:T(8,128)} %copy-done.2, s32[]{:T(128)S(6)} %select_n.199, bf16[624,512]{1,0:T(8,128)(2,1)S(1)} %copy-done.8), kind=kLoop, calls=%fused_computation.36 | loop fusion | flops 1596816 | bytes 4475332 | tf_op jit(solution)/shard_map/reduce_sum | solution.py:130
  97.8 1.5 collective-permute-start.7
  100.6 5.2 %fusion.7 = f32[624,1024]{1,0:T(8,128)} fusion(bf16[2048,1024]{1,0:T(8,128)(2,1)} %param.26, s32[]{:T(128)S(6)} %select_n.198, bf16[624,512]{1,0:T(8,128)(2,1)S(1)} %collective-permute-done.8, bf16[624,512]{1,0:T(8,128)(2,1)S(1)} %multiply_convert_fusion.2, pred[]{:T(512)S(6)} %eq.26), kind=kOutput, calls=%fused_computation.15 | convolution fusion | flops 1314373632 | bytes 5931013 | tf_op jit(solution)/shard_map/dot_general | solution.py:69
  105.8 4.4 %fusion.9 = f32[624,1024]{1,0:T(8,128)} fusion(bf16[2048,1024]{1,0:T(8,128)(2,1)S(1)} %copy-done.19, s32[]{:T(128)S(6)} %select_n.198, bf16[624,512]{1,0:T(8,128)(2,1)} %copy-done.22, bf16[624,512]{1,0:T(8,128)(2,1)S(1)} %multiply_convert_fusion.2, pred[]{:T(512)S(6)} %eq.26), kind=kOutput, calls=%fused_computation.17 | convolution fusion | flops 1314373632 | bytes 5931013 | tf_op jit(solution)/shard_map/dot_general | solution.py:69
  110.2 4.6 %collective-permute-done.7 = bf16[624,512]{1,0:T(8,128)(2,1)} collective-permute-done((bf16[624,512]{1,0:T(8,128)(2,1)S(1)}, bf16[624,512]{1,0:T(8,128)(2,1)}, u32[]{:S(2)}, u32[]{:S(2)}) %collective-permute-start.7) | collective-permute-done | bytes 639008 | tf_op jit(solution)/shard_map/ppermute | solution.py:41
  115.8 1.8 %copy.77 = bf16[8,2,129,256]{3,1,2,0:T(2,128)(2,1)} copy(bf16[8,2,129,256]{3,2,1,0:T(8,128)(2,1)S(1)} %select_select_fusion) | data formatting | bytes 2113536 | tf_op jit(solution)/shard_map/jit(_where)/select_n | solution.py:192
  117.6 5.7 %all-to-all-start.1 = ((bf16[8,2,129,256]{3,1,2,0:T(2,128)(2,1)}), bf16[8,2,129,256]{3,1,2,0:T(2,128)(2,1)}, u32[]{:S(2)}, u32[]{:S(2)}) async-start(bf16[8,2,129,256]{3,1,2,0:T(2,128)(2,1)} %copy.77), calls=%async_computation.1 | async-start | bytes 2113536 | tf_op jit(solution)/shard_map/all_to_all | solution.py:194
  123.3 5.4 %fusion.3 = f32[624,1024]{1,0:T(8,128)} fusion(bf16[2048,1024]{1,0:T(8,128)(2,1)} %param.26, s32[]{:T(128)S(6)} %select_n.184, bf16[624,512]{1,0:T(8,128)(2,1)} %collective-permute-done.9, bf16[624,512]{1,0:T(8,128)(2,1)} %collective-permute-done.7, pred[]{:T(512)S(6)} %eq.26), kind=kOutput, calls=%fused_computation.11 | convolution fusion | flops 1314373632 | bytes 5931013 | tf_op jit(solution)/shard_map/dot_general | solution.py:85
  128.7 12.6 %fusion.11 = f32[624,2048]{1,0:T(8,128)} fusion(bf16[1024,2048]{1,0:T(8,128)(2,1)} %param.27, f32[624,1024]{1,0:T(8,128)} %fusion.7, f32[624,1024]{1,0:T(8,128)} %fusion.3, f32[624,1024]{1,0:T(8,128)} %fusion.9, bf16[2048,1024]{1,0:T(8,128)(2,1)} %param.25, s32[]{:T(128)S(6)} %select_n.184, bf16[624,512]{1,0:T(8,128)(2,1)} %collective-permute-done.9, ...), kind=kOutput, calls=%fused_computation.21 | convolution fusion | flops 3936731136 | bytes 20348932 | tf_op jit(solution)/shard_map/dot_general | solution.py:97
  141.3 4.8 %select_bitcast_fusion.3 = (f32[1,624,512]{2,1,0:T(8,128)}, f32[1,624,512]{2,1,0:T(8,128)}, f32[1,624,512]{2,1,0:T(8,128)S(1)}, f32[1,624,512]{2,1,0:T(8,128)S(1)}) fusion(f32[624,2048]{1,0:T(8,128)} %fusion.11, pred[]{:T(512)S(6)} %eq.26), kind=kLoop, calls=%fused_computation.33 | loop fusion | flops 1277952 | bytes 10223617 | tf_op jit(solution)/shard_map/stack | solution.py:104
  146.0 1.8 %pad_maximum_fusion.1 = f32[2,624,512]{2,1,0:T(8,128)} fusion(f32[1,624,512]{2,1,0:T(8,128)S(1)} %get-tuple-element.17, f32[1,624,512]{2,1,0:T(8,128)S(1)} %get-tuple-element.18), kind=kLoop, calls=%fused_computation.9 | loop fusion | flops 638976 | bytes 5111808 | tf_op jit(solution)/shard_map/stack | solution.py:105
  148.2 1.8 %all-to-all-done.1 = bf16[8,2,129,256]{3,1,2,0:T(2,128)(2,1)} async-done(((bf16[8,2,129,256]{3,1,2,0:T(2,128)(2,1)}), bf16[8,2,129,256]{3,1,2,0:T(2,128)(2,1)}, u32[]{:S(2)}, u32[]{:S(2)}) %all-to-all-start.1) | async-done | bytes 1056800 | tf_op jit(solution)/shard_map/all_to_all | solution.py:194
  152.8 2.8 %gather_fusion.1 = bf16[13,129,256]{2,1,0:T(8,128)(2,1)} fusion(bf16[16,129,256]{2,1,0:T(8,128)(2,1)} %bitcast.100, s32[1024]{0:T(1024)S(1)} %pad_clamp_fusion), kind=kCustom, calls=%fused_computation.1 | custom fusion | bytes 1717300 | tf_op jit(solution)/shard_map/jit(_take)/gather | solution.py:202
  155.6 2.7 %maximum_add_fusion = f32[2,624,512]{2,1,0:T(8,128)S(1)} fusion(f32[2,624,512]{2,1,0:T(8,128)} %collective-permute-done.10, f32[1,624,512]{2,1,0:T(8,128)} %get-tuple-element.16, f32[1,624,512]{2,1,0:T(8,128)S(1)} %copy-done.5), kind=kLoop, calls=%fused_computation.8 | loop fusion | flops 1277952 | bytes 7667712 | tf_op jit(solution)/shard_map/add | solution.py:106
  158.4 1.6 collective-permute-start.11
  161.1 13.0 %collective-permute-done.11 = bf16[624,512]{1,0:T(8,128)(2,1)S(1)} collective-permute-done((bf16[624,512]{1,0:T(8,128)(2,1)S(1)}, bf16[624,512]{1,0:T(8,128)(2,1)S(1)}, u32[]{:S(2)}, u32[]{:S(2)}) %collective-permute-start.11) | collective-permute-done | bytes 639008 | tf_op jit(solution)/shard_map/ppermute | solution.py:41
  (130 shorter events, 31.2 us)
Async XLA Ops:
  0.6 20.7 %copy-start = (bf16[512,2048]{1,0:T(8,128)(2,1)S(1)}, bf16[512,2048]{1,0:T(8,128)(2,1)}, u32[]{:S(2)}) copy-start(bf16[512,2048]{1,0:T(8,128)(2,1)} %param.23) | copy-start | bytes 6291460
  0.6 18.6 %collective-permute-start = (bf16[624,512]{1,0:T(8,128)(2,1)}, bf16[624,512]{1,0:T(8,128)(2,1)}, u32[]{:S(2)}, u32[]{:S(2)}) collective-permute-start(bf16[624,512]{1,0:T(8,128)(2,1)} %param.15), channel_id=1, source_target_pairs={{0,2},{2,0},{1,3},{3,1},{4,6},{6,4},{5,7},{7,5},{8,10},{10,8},{9,1... | collective-permute-start | bytes 1916936 | tf_op jit(solution)/shard_map/ppermute | solution.py:41
  6.9 5.3 %copy-start.25 = (s32[13]{0:T(128)S(1)}, s32[13]{0:T(128)}, u32[]{:S(2)}) copy-start(s32[13]{0:T(128)} %param.17) | copy-start | bytes 160
  7.0 5.3 %copy-start.17 = (s32[13]{0:T(128)S(1)}, s32[13]{0:T(128)}, u32[]{:S(2)}) copy-start(s32[13]{0:T(128)} %param.16) | copy-start | bytes 160
  8.0 19.5 %all-to-all-start = ((bf16[2,4,13,16,256]{4,3,2,0,1:T(8,128)(2,1)}), bf16[2,4,13,16,256]{4,3,2,0,1:T(8,128)(2,1)}, u32[]{:S(2)}, u32[]{:S(2)}) async-start(bf16[2,4,13,16,256]{4,3,2,0,1:T(8,128)(2,1)} %copy.70), calls=%async_computation | async-start | bytes 1703936 | tf_op jit(solution)/shard_map/all_to_all | solution.py:170
  21.2 8.6 %collective-permute-start.1 = (bf16[2,624,512]{2,1,0:T(8,128)(2,1)S(1)}, bf16[2,624,512]{2,1,0:T(8,128)(2,1)}, u32[]{:S(2)}, u32[]{:S(2)}) collective-permute-start(bf16[2,624,512]{2,1,0:T(8,128)(2,1)S(1)} %maximum_select_fusion), channel_id=1, source_target_pairs={{0,1},{1,0},{2,3},{3,2},{4,5},{5,4},{6,7},{7,6},{8,9},{9,8},{10,11... | collective-permute-start | bytes 3833864 | tf_op jit(solution)/shard_map/ppermute | solution.py:41
  31.6 5.0 %copy-start.3 = (bf16[624,2048]{1,0:T(8,128)(2,1)}, bf16[624,2048]{1,0:T(8,128)(2,1)S(1)}, u32[]{:S(2)}) copy-start(bf16[624,2048]{1,0:T(8,128)(2,1)S(1)} %pad_maximum_fusion) | copy-start | bytes 7667716
  31.6 2.0 %copy-start.21 = (bf16[2048,256]{1,0:T(8,128)(2,1)S(1)}, bf16[2048,256]{1,0:T(8,128)(2,1)}, u32[]{:S(2)}) copy-start(bf16[2048,256]{1,0:T(8,128)(2,1)} %param.21) | copy-start | bytes 3145732
  33.6 3.0 %copy-start.20 = (bf16[2048,512]{1,0:T(8,128)(2,1)S(1)}, bf16[2048,512]{1,0:T(8,128)(2,1)}, u32[]{:S(2)}) copy-start(bf16[2048,512]{1,0:T(8,128)(2,1)} %param.20) | copy-start | bytes 6291460
  39.1 3.0 %copy-start.24 = (f32[2048]{0:T(1024)S(1)}, f32[2048]{0:T(1024)}, u32[]{:S(2)}) copy-start(f32[2048]{0:T(1024)} %param.19) | copy-start | bytes 24580
  43.1 4.0 %copy-start.13 = (f32[13,48,128]{2,1,0:T(8,128)S(1)}, f32[13,48,128]{2,1,0:T(8,128)}, u32[]{:S(2)}) copy-start(f32[13,48,128]{2,1,0:T(8,128)} %get-tuple-element.33) | copy-start | bytes 958468
  43.1 4.0 %copy-start.14 = (f32[13,48,128]{2,1,0:T(8,128)S(1)}, f32[13,48,128]{2,1,0:T(8,128)}, u32[]{:S(2)}) copy-start(f32[13,48,128]{2,1,0:T(8,128)} %get-tuple-element.34) | copy-start | bytes 958468
  45.3 2.0 %copy-start.9 = (bf16[1,13,4,16,256]{4,3,2,1,0:T(8,128)(2,1)S(1)}, bf16[1,13,4,16,256]{4,3,2,1,0:T(8,128)(2,1)}, u32[]{:S(2)}) copy-start(bf16[1,13,4,16,256]{4,3,2,1,0:T(8,128)(2,1)} %get-tuple-element.29) | copy-start | bytes 1277956
  45.3 2.0 %copy-start.15 = (bf16[13,48,1,128]{3,1,0,2:T(8,128)(2,1)S(1)}, bf16[13,48,1,128]{3,1,0,2:T(8,128)(2,1)}, u32[]{:S(2)}) copy-start(bf16[13,48,1,128]{3,1,0,2:T(8,128)(2,1)} %get-tuple-element.32) | copy-start | bytes 479236
  45.4 2.0 %copy-start.16 = (pred[13,48,112]{2,1,0:T(8,128)(4,1)S(1)}, pred[13,48,112]{2,1,0:T(8,128)(4,1)}, u32[]{:S(2)}) copy-start(pred[13,48,112]{2,1,0:T(8,128)(4,1)} %and_or_fusion) | copy-start | bytes 209668
  45.4 38.3 %collective-permute-start.3 = (bf16[512,1024]{1,0:T(8,128)(2,1)}, bf16[512,1024]{1,0:T(8,128)(2,1)}, u32[]{:S(2)}, u32[]{:S(2)}) collective-permute-start(bf16[512,1024]{1,0:T(8,128)(2,1)} %constant_dynamic-slice_fusion.1), channel_id=1, source_target_pairs={{0,2},{2,0},{1,3},{3,1},{4,6},{6,4},{5,7},{7,5},{8,10},{10,8},{9,1... | collective-permute-start | bytes 3145736 | tf_op jit(solution)/shard_map/ppermute | solution.py:41
  49.6 34.1 %collective-permute-start.2 = (bf16[624,512]{1,0:T(8,128)(2,1)S(1)}, bf16[624,512]{1,0:T(8,128)(2,1)S(1)}, u32[]{:S(2)}, u32[]{:S(2)}) collective-permute-start(bf16[624,512]{1,0:T(8,128)(2,1)S(1)} %bitcast.102), channel_id=1, source_target_pairs={{0,2},{2,0},{1,3},{3,1},{4,6},{6,4},{5,7},{7,5},{8,10},{10,8},{9,1... | collective-permute-start | bytes 1916936 | tf_op jit(solution)/shard_map/ppermute | solution.py:41
  87.3 3.3 %copy-start.8 = (bf16[624,512]{1,0:T(8,128)(2,1)S(1)}, bf16[624,512]{1,0:T(8,128)(2,1)}, u32[]{:S(2)}) copy-start(bf16[624,512]{1,0:T(8,128)(2,1)} %param.15) | copy-start | bytes 1916932
  87.4 3.2 %collective-permute-start.4 = (f32[624,512]{1,0:T(8,128)S(1)}, f32[624,512]{1,0:T(8,128)}, u32[]{:S(2)}, u32[]{:S(2)}) collective-permute-start(f32[624,512]{1,0:T(8,128)S(1)} %constant_dynamic-slice_fusion), channel_id=1, source_target_pairs={{0,1},{1,0},{2,3},{3,2},{4,5},{5,4},{6,7},{7,6},{8,9},{9,8},{10,11... | collective-permute-start | bytes 3833864 | tf_op jit(solution)/shard_map/ppermute | solution.py:41
  92.6 1.2 collective-permute-start.5
  93.8 3.6 %collective-permute-start.6 = (f32[624,1]{0,1:T(1,128)S(1)}, f32[624,1]{0,1:T(1,128)S(1)}, u32[]{:S(2)}, u32[]{:S(2)}) collective-permute-start(f32[624,1]{0,1:T(1,128)S(1)} %reshape_add_fusion), channel_id=1, source_target_pairs={{0,2},{2,0},{1,3},{3,1},{4,6},{6,4},{5,7},{7,5},{8,10},{10,8},{9,1... | collective-permute-start | bytes 7496 | tf_op jit(solution)/shard_map/ppermute | solution.py:41
  97.6 2.1 %collective-permute-start.8 = (bf16[624,512]{1,0:T(8,128)(2,1)S(1)}, bf16[624,512]{1,0:T(8,128)(2,1)S(1)}, u32[]{:S(2)}, u32[]{:S(2)}) collective-permute-start(bf16[624,512]{1,0:T(8,128)(2,1)S(1)} %multiply_convert_fusion.2), channel_id=1, source_target_pairs={{0,1},{1,0},{2,3},{3,2},{4,5},{5,4},{6,7},{7,6},{8,9},{9,8},{10,11... | collective-permute-start | bytes 1916936 | tf_op jit(solution)/shard_map/ppermute | solution.py:41
  97.8 17.0 %collective-permute-start.7 = (bf16[624,512]{1,0:T(8,128)(2,1)S(1)}, bf16[624,512]{1,0:T(8,128)(2,1)}, u32[]{:S(2)}, u32[]{:S(2)}) collective-permute-start(bf16[624,512]{1,0:T(8,128)(2,1)S(1)} %multiply_convert_fusion.2), channel_id=1, source_target_pairs={{0,2},{2,0},{1,3},{3,1},{4,6},{6,4},{5,7},{7,5},{8,10},{10,8},{9,1... | collective-permute-start | bytes 1916936 | tf_op jit(solution)/shard_map/ppermute | solution.py:41
  99.7 6.0 %copy-start.19 = (bf16[2048,1024]{1,0:T(8,128)(2,1)S(1)}, bf16[2048,1024]{1,0:T(8,128)(2,1)}, u32[]{:S(2)}) copy-start(bf16[2048,1024]{1,0:T(8,128)(2,1)} %param.25) | copy-start | bytes 12582916
  105.7 9.0 %copy-start.10 = (bf16[1,13,4,16,256]{4,3,2,1,0:T(8,128)(2,1)S(1)}, bf16[1,13,4,16,256]{4,3,2,1,0:T(8,128)(2,1)}, u32[]{:S(2)}) copy-start(bf16[1,13,4,16,256]{4,3,2,1,0:T(8,128)(2,1)} %get-tuple-element.29) | copy-start | bytes 1277956
  105.8 9.1 %copy-start.12 = (bf16[1,13,4,16,256]{4,3,2,1,0:T(8,128)(2,1)S(1)}, bf16[1,13,4,16,256]{4,3,2,1,0:T(8,128)(2,1)}, u32[]{:S(2)}) copy-start(bf16[1,13,4,16,256]{4,3,2,1,0:T(8,128)(2,1)} %get-tuple-element.30) | copy-start | bytes 1277956
  114.8 8.5 %collective-permute-start.9 = (bf16[624,512]{1,0:T(8,128)(2,1)}, bf16[624,512]{1,0:T(8,128)(2,1)}, u32[]{:S(2)}, u32[]{:S(2)}) collective-permute-start(bf16[624,512]{1,0:T(8,128)(2,1)} %collective-permute-done.7), channel_id=1, source_target_pairs={{0,1},{1,0},{2,3},{3,2},{4,5},{5,4},{6,7},{7,6},{8,9},{9,8},{10,11... | collective-permute-start | bytes 1916936 | tf_op jit(solution)/shard_map/ppermute | solution.py:41
  117.6 32.4 %all-to-all-start.1 = ((bf16[8,2,129,256]{3,1,2,0:T(2,128)(2,1)}), bf16[8,2,129,256]{3,1,2,0:T(2,128)(2,1)}, u32[]{:S(2)}, u32[]{:S(2)}) async-start(bf16[8,2,129,256]{3,1,2,0:T(2,128)(2,1)} %copy.77), calls=%async_computation.1 | async-start | bytes 2113536 | tf_op jit(solution)/shard_map/all_to_all | solution.py:194
  147.8 7.8 %copy-start.5 = (f32[1,624,512]{2,1,0:T(8,128)S(1)}, f32[1,624,512]{2,1,0:T(8,128)}, u32[]{:S(2)}) copy-start(f32[1,624,512]{2,1,0:T(8,128)} %get-tuple-element.15) | copy-start | bytes 3833860
  147.8 7.7 %collective-permute-start.10 = (f32[2,624,512]{2,1,0:T(8,128)}, f32[2,624,512]{2,1,0:T(8,128)}, u32[]{:S(2)}, u32[]{:S(2)}) collective-permute-start(f32[2,624,512]{2,1,0:T(8,128)} %pad_maximum_fusion.1), channel_id=1, source_target_pairs={{0,1},{1,0},{2,3},{3,2},{4,5},{5,4},{6,7},{7,6},{8,9},{9,8},{10,11... | collective-permute-start | bytes 7667720 | tf_op jit(solution)/shard_map/ppermute | solution.py:41
  158.4 15.8 %collective-permute-start.11 = (bf16[624,512]{1,0:T(8,128)(2,1)S(1)}, bf16[624,512]{1,0:T(8,128)(2,1)S(1)}, u32[]{:S(2)}, u32[]{:S(2)}) collective-permute-start(bf16[624,512]{1,0:T(8,128)(2,1)S(1)} %fusion.31), channel_id=1, source_target_pairs={{0,2},{2,0},{1,3},{3,1},{4,6},{6,4},{5,7},{7,5},{8,10},{10,8},{9,1... | collective-permute-start | bytes 1916936 | tf_op jit(solution)/shard_map/ppermute | solution.py:41
  160.1 15.2 %copy-start.1 = (bf16[512,2048]{1,0:T(8,128)(2,1)S(1)}, bf16[512,2048]{1,0:T(8,128)(2,1)}, u32[]{:S(2)}) copy-start(bf16[512,2048]{1,0:T(8,128)(2,1)} %param.23) | copy-start | bytes 6291460
  (8 other events, 10.5 us)

commit v12 on v11

--- a/solution.py
+++ b/solution.py
@@ -207,7 +207,6 @@
     far_cols = lax.dynamic_slice_in_dim(
         output_weight, (1 - lax.axis_index("kvy")) * chip_cols, chip_cols, 1
     )
-    far_cols, x_whole = lax.optimization_barrier((far_cols, x_whole))
     weight_far = swap(far_cols, "kvy")
     x_float = x_whole.astype(jnp.float32)
     square_sum = jnp.sum(x_float * x_float, axis=-1, keepdims=True)

time: 176 us -> 158 us (0.90)
  waiting for transfers between devices: 66 us -> 44.8 us
    ppermute x12, waiting for transfers between devices: 61.8 us -> 38.1 us  [swap(): return lax.ppermute(values, axis_name, [(0, 1), (1, 0)])]
    all_to_all x1, waiting for transfers between devices: 2.38 us -> 4.89 us  [local(): lax.all_to_all(stacked, ('kvy', 'core'), split_axis=1, concat_axis=1, til...]
    unnamed x54 -> x48, local copies, waits for them, and re-layouts: 6.58 us -> 7.51 us
  transfers between devices with their start and end apart: 14 -> 14, of which waited for: 9 -> 9; matrix products, arithmetic and copies ran while one was open for 34% -> 47% of each run, Pallas kernels for 0% -> 0%
where the time goes in v12:
time: 158 us; the launch traced here: 157 us
  waiting for transfers between devices  44.8 us (28%)
  matrix products  37 us (23%)
  local copies, waits for them, and re-layouts  26.6 us (17%)
  other arithmetic  25.3 us (16%)
  starting transfers between devices  22.3 us (14%)
    ppermute x12, waiting for transfers between devices, swap(): return lax.ppermute(values, axis_name, [(0, 1), (1, 0)])  38.1 us
    dot_general x1, matrix products, scatter_features(): product = jnp.dot(matrix_in, weight, preferred_element_type=jnp.float32)  12.6 us
    ppermute x12, starting transfers between devices, swap(): return lax.ppermute(values, axis_name, [(0, 1), (1, 0)])  12.2 us
    dot_general x2, matrix products, gather_project(): jnp.dot(local_pair, lax.dynamic_slice_in_dim(weight, chip * half, half, 0...  9.6 us
    unnamed x48, local copies, waits for them, and re-layouts  7.51 us
    all_to_all x1, starting transfers between devices, local(): lax.all_to_all(packed, 'req', split_axis=0, concat_axis=0, tiled=True)  5.7 us
    dot_general x1, matrix products, gather_project(): jnp.dot(remote_pair, lax.dynamic_slice_in_dim(weight, (1 - chip) * half,...  5.39 us
    all_to_all x1, waiting for transfers between devices, local(): lax.all_to_all(stacked, ('kvy', 'core'), split_axis=1, concat_axis=1, til...  4.89 us
  transfers between devices with their start and end apart: 14, of which 9 were waited for; matrix products, arithmetic and copies ran while one was open for 47% of the time, Pallas kernels for 0%

profile of v12, /device:TPU:0, one launch (start us, length us, event | category | flops | bytes accessed | tf_op | source)
XLA Modules:
  0.0 157.2 jit_solution(12621369377901018442)
XLA Ops:
  0.6 3.0 %collective-permute-start = (bf16[624,512]{1,0:T(8,128)(2,1)}, bf16[624,512]{1,0:T(8,128)(2,1)}, u32[]{:S(2)}, u32[]{:S(2)}) collective-permute-start(bf16[624,512]{1,0:T(8,128)(2,1)} %param.15), channel_id=1, source_target_pairs={{0,2},{2,0},{1,3},{3,1},{4,6},{6,4},{5,7},{7,5},{8,10},{10,8},{9,1... | collective-permute-start | bytes 1916936 | tf_op jit(solution)/shard_map/ppermute | solution.py:41
  8.0 4.3 %all-to-all-start = ((bf16[2,4,13,16,256]{4,3,2,0,1:T(8,128)(2,1)}), bf16[2,4,13,16,256]{4,3,2,0,1:T(8,128)(2,1)}, u32[]{:S(2)}, u32[]{:S(2)}) async-start(bf16[2,4,13,16,256]{4,3,2,0,1:T(8,128)(2,1)} %copy.70), calls=%async_computation | async-start | bytes 1703936 | tf_op jit(solution)/shard_map/all_to_all | solution.py:170
  13.4 1.9 %collective-permute-start.3 = (bf16[512,1024]{1,0:T(8,128)(2,1)}, bf16[512,1024]{1,0:T(8,128)(2,1)}, u32[]{:S(2)}, u32[]{:S(2)}) collective-permute-start(bf16[512,1024]{1,0:T(8,128)(2,1)} %constant_dynamic-slice_fusion.1), channel_id=1, source_target_pairs={{0,2},{2,0},{1,3},{3,1},{4,6},{6,4},{5,7},{7,5},{8,10},{10,8},{9,1... | collective-permute-start | bytes 3145736 | tf_op jit(solution)/shard_map/ppermute | solution.py:41
  15.4 3.8 %collective-permute-done = bf16[624,512]{1,0:T(8,128)(2,1)} collective-permute-done((bf16[624,512]{1,0:T(8,128)(2,1)}, bf16[624,512]{1,0:T(8,128)(2,1)}, u32[]{:S(2)}, u32[]{:S(2)}) %collective-permute-start) | collective-permute-done | bytes 639008 | tf_op jit(solution)/shard_map/ppermute | solution.py:41
  19.2 1.9 %maximum_select_fusion = bf16[2,624,512]{2,1,0:T(8,128)(2,1)S(1)} fusion(bf16[1,624,512]{2,1,0:T(8,128)(2,1)} %bitcast.4, bf16[1,624,512]{2,1,0:T(8,128)(2,1)} %bitcast.108, pred[]{:T(512)S(6)} %eq.27), kind=kLoop, calls=%fused_computation.22 | loop fusion | flops 1916928 | bytes 2555905 | tf_op jit(solution)/shard_map/jit(_where)/select_n | solution.py:48
  21.4 2.0 %multiply_cosine_fusion = (f32[13,48,128]{2,1,0:T(8,128)}, f32[13,48,128]{2,1,0:T(8,128)}) fusion(f32[128]{0:T(128)S(1)} %multiply_exponential_fusion, f32[13,48]{1,0:T(8,128)S(1)} %iota_add_fusion), kind=kLoop, calls=%fused_computation.72 | loop fusion | flops 79872 | bytes 641984 | tf_op jit(solution)/shard_map/cos | solution.py:22
  23.4 4.9 %all-to-all-done = bf16[2,4,13,16,256]{4,3,2,0,1:T(8,128)(2,1)} async-done(((bf16[2,4,13,16,256]{4,3,2,0,1:T(8,128)(2,1)}), bf16[2,4,13,16,256]{4,3,2,0,1:T(8,128)(2,1)}, u32[]{:S(2)}, u32[]{:S(2)}) %all-to-all-start) | async-done | bytes 852000 | tf_op jit(solution)/shard_map/all_to_all | solution.py:170
  32.0 2.0 %fusion = f32[624]{0:T(1024)S(1)} fusion(bf16[624,512]{1,0:T(8,128)(2,1)S(1)} %get-tuple-element.17, bf16[624,512]{1,0:T(8,128)(2,1)S(1)} %get-tuple-element.18, bf16[624,512]{1,0:T(8,128)(2,1)S(1)} %get-tuple-element.16, bf16[624,512]{1,0:T(8,128)(2,1)S(1)} %get-tuple-element.15), kind=kLoop, calls=%fused_computation.4 | loop fusion | flops 12778896 | bytes 2558400 | tf_op jit(solution)/shard_map/reduce_sum | solution.py:212
  36.5 2.6 %fusion.75 = f32[624,512]{1,0:T(8,128)} fusion(bf16[624,2048]{1,0:T(8,128)(2,1)S(1)} %fusion.2, bf16[2048,512]{1,0:T(8,128)(2,1)S(1)} %copy-done.19), kind=kOutput, calls=%fused_computation.149 | convolution fusion | flops 1308622848 | bytes 5931008 | tf_op jit(solution)/shard_map/dot_general | solution.py:219
  39.0 2.1 %reshape.301 = f32[13,48,2,256]{3,2,1,0:T(2,128)S(1)} reshape(f32[624,512]{1,0:T(8,128)} %fusion.75) | data formatting | bytes 2555904 | tf_op jit(solution)/shard_map/reshape | solution.py:221
  42.8 2.1 %fusion.74 = f32[624,256]{1,0:T(8,128)S(1)} fusion(bf16[624,2048]{1,0:T(8,128)(2,1)S(1)} %copy-done.7, bf16[2048,256]{1,0:T(8,128)(2,1)} %param.21), kind=kOutput, calls=%fused_computation.148 | convolution fusion | flops 654311424 | bytes 4243456 | tf_op jit(solution)/shard_map/dot_general | solution.py:223
  45.0 1.6 %fusion.41 = (bf16[13,48,1,128]{3,1,0,2:T(8,128)(2,1)S(1)}, bf16[13,48,1,128]{3,1,0,2:T(8,128)(2,1)S(1)}) fusion(f32[13,48,1,256]{3,1,0,2:T(8,128)S(1)} %bitcast.113, f32[128]{0:T(128)S(1)} %multiply_exponential_fusion, f32[13,48]{1,0:T(8,128)S(1)} %iota_add_fusion), kind=kLoop, calls=%fused_computation.80 | loop fusion | flops 718848 | bytes 961472 | tf_op jit(solution)/shard_map/convert.7
  50.7 2.1 %collective-permute-start.2 = (bf16[624,512]{1,0:T(8,128)(2,1)S(1)}, bf16[624,512]{1,0:T(8,128)(2,1)S(1)}, u32[]{:S(2)}, u32[]{:S(2)}) collective-permute-start(bf16[624,512]{1,0:T(8,128)(2,1)S(1)} %bitcast.105), channel_id=1, source_target_pairs={{0,2},{2,0},{1,3},{3,1},{4,6},{6,4},{5,7},{7,5},{8,10},{10,8},{9,1... | collective-permute-start | bytes 1916936 | tf_op jit(solution)/shard_map/ppermute | solution.py:41
  53.7 11.8 %collective-permute-done.2 = bf16[624,512]{1,0:T(8,128)(2,1)S(1)} collective-permute-done((bf16[624,512]{1,0:T(8,128)(2,1)S(1)}, bf16[624,512]{1,0:T(8,128)(2,1)S(1)}, u32[]{:S(2)}, u32[]{:S(2)}) %collective-permute-start.2) | collective-permute-done | bytes 639008 | tf_op jit(solution)/shard_map/ppermute | solution.py:41
  65.5 2.1 %convolution_add_fusion = f32[624,1024]{1,0:T(8,128)S(1)} fusion(f32[624,1024]{1,0:T(8,128)S(1)} %fusion.19, bf16[624,512]{1,0:T(8,128)(2,1)S(1)} %collective-permute-done.2, bf16[512,1024]{1,0:T(8,128)(2,1)} %collective-permute-done.3), kind=kOutput, calls=%fused_computation.19 | convolution fusion | flops 654950400 | bytes 6799360 | tf_op jit(solution)/shard_map/dot_general | solution.py:121
  69.8 2.6 %collective-permute-done.4 = f32[624,512]{1,0:T(8,128)} collective-permute-done((f32[624,512]{1,0:T(8,128)S(1)}, f32[624,512]{1,0:T(8,128)}, u32[]{:S(2)}, u32[]{:S(2)}) %collective-permute-start.4) | collective-permute-done | bytes 1277984 | tf_op jit(solution)/shard_map/ppermute | solution.py:41
  72.4 2.0 %multiply_reduce_fusion = (f32[624]{0:T(1024)S(1)}, f32[624,512]{1,0:T(8,128)S(1)}) fusion(f32[624,512]{1,0:T(8,128)} %collective-permute-done.4, f32[624,1024]{1,0:T(8,128)} %copy-done.2, s32[]{:T(128)S(6)} %select_n.199, bf16[624,512]{1,0:T(8,128)(2,1)S(1)} %copy-done.8), kind=kLoop, calls=%fused_computation.36 | loop fusion | flops 1596816 | bytes 4475332 | tf_op jit(solution)/shard_map/reduce_sum | solution.py:130
  79.7 1.5 collective-permute-start.7
  82.4 5.2 %fusion.7 = f32[624,1024]{1,0:T(8,128)} fusion(bf16[2048,1024]{1,0:T(8,128)(2,1)} %param.26, s32[]{:T(128)S(6)} %select_n.197, bf16[624,512]{1,0:T(8,128)(2,1)S(1)} %collective-permute-done.8, bf16[624,512]{1,0:T(8,128)(2,1)S(1)} %multiply_convert_fusion.2, pred[]{:T(512)S(6)} %eq.26), kind=kOutput, calls=%fused_computation.15 | convolution fusion | flops 1314373632 | bytes 5931013 | tf_op jit(solution)/shard_map/dot_general | solution.py:69
  87.6 4.4 %fusion.9 = f32[624,1024]{1,0:T(8,128)} fusion(bf16[2048,1024]{1,0:T(8,128)(2,1)S(1)} %copy-done.18, s32[]{:T(128)S(6)} %select_n.197, bf16[624,512]{1,0:T(8,128)(2,1)} %copy-done.21, bf16[624,512]{1,0:T(8,128)(2,1)S(1)} %multiply_convert_fusion.2, pred[]{:T(512)S(6)} %eq.26), kind=kOutput, calls=%fused_computation.17 | convolution fusion | flops 1314373632 | bytes 5931013 | tf_op jit(solution)/shard_map/dot_general | solution.py:69
  92.0 4.6 %collective-permute-done.7 = bf16[624,512]{1,0:T(8,128)(2,1)} collective-permute-done((bf16[624,512]{1,0:T(8,128)(2,1)S(1)}, bf16[624,512]{1,0:T(8,128)(2,1)}, u32[]{:S(2)}, u32[]{:S(2)}) %collective-permute-start.7) | collective-permute-done | bytes 639008 | tf_op jit(solution)/shard_map/ppermute | solution.py:41
  97.6 1.8 %copy.77 = bf16[8,2,129,256]{3,1,2,0:T(2,128)(2,1)} copy(bf16[8,2,129,256]{3,2,1,0:T(8,128)(2,1)S(1)} %select_select_fusion) | data formatting | bytes 2113536 | tf_op jit(solution)/shard_map/jit(_where)/select_n | solution.py:192
  99.4 5.7 %all-to-all-start.1 = ((bf16[8,2,129,256]{3,1,2,0:T(2,128)(2,1)}), bf16[8,2,129,256]{3,1,2,0:T(2,128)(2,1)}, u32[]{:S(2)}, u32[]{:S(2)}) async-start(bf16[8,2,129,256]{3,1,2,0:T(2,128)(2,1)} %copy.77), calls=%async_computation.1 | async-start | bytes 2113536 | tf_op jit(solution)/shard_map/all_to_all | solution.py:194
  105.1 5.4 %fusion.3 = f32[624,1024]{1,0:T(8,128)} fusion(bf16[2048,1024]{1,0:T(8,128)(2,1)} %param.26, s32[]{:T(128)S(6)} %select_n.198, bf16[624,512]{1,0:T(8,128)(2,1)} %collective-permute-done.9, bf16[624,512]{1,0:T(8,128)(2,1)} %collective-permute-done.7, pred[]{:T(512)S(6)} %eq.26), kind=kOutput, calls=%fused_computation.11 | convolution fusion | flops 1314373632 | bytes 5931013 | tf_op jit(solution)/shard_map/dot_general | solution.py:85
  110.5 12.6 %fusion.11 = f32[624,2048]{1,0:T(8,128)} fusion(bf16[1024,2048]{1,0:T(8,128)(2,1)} %param.27, f32[624,1024]{1,0:T(8,128)} %fusion.7, f32[624,1024]{1,0:T(8,128)} %fusion.3, f32[624,1024]{1,0:T(8,128)} %fusion.9, bf16[2048,1024]{1,0:T(8,128)(2,1)} %param.25, s32[]{:T(128)S(6)} %select_n.198, bf16[624,512]{1,0:T(8,128)(2,1)} %collective-permute-done.9, ...), kind=kOutput, calls=%fused_computation.21 | convolution fusion | flops 3936731136 | bytes 20348932 | tf_op jit(solution)/shard_map/dot_general | solution.py:97
  123.1 4.8 %select_bitcast_fusion.3 = (f32[1,624,512]{2,1,0:T(8,128)}, f32[1,624,512]{2,1,0:T(8,128)}, f32[1,624,512]{2,1,0:T(8,128)S(1)}, f32[1,624,512]{2,1,0:T(8,128)S(1)}) fusion(f32[624,2048]{1,0:T(8,128)} %fusion.11, pred[]{:T(512)S(6)} %eq.26), kind=kLoop, calls=%fused_computation.33 | loop fusion | flops 1277952 | bytes 10223617 | tf_op jit(solution)/shard_map/stack | solution.py:104
  127.9 1.8 %pad_maximum_fusion.1 = f32[2,624,512]{2,1,0:T(8,128)} fusion(f32[1,624,512]{2,1,0:T(8,128)S(1)} %get-tuple-element.13, f32[1,624,512]{2,1,0:T(8,128)S(1)} %get-tuple-element.14), kind=kLoop, calls=%fused_computation.9 | loop fusion | flops 638976 | bytes 5111808 | tf_op jit(solution)/shard_map/stack | solution.py:105
  130.1 1.8 %all-to-all-done.1 = bf16[8,2,129,256]{3,1,2,0:T(2,128)(2,1)} async-done(((bf16[8,2,129,256]{3,1,2,0:T(2,128)(2,1)}), bf16[8,2,129,256]{3,1,2,0:T(2,128)(2,1)}, u32[]{:S(2)}, u32[]{:S(2)}) %all-to-all-start.1) | async-done | bytes 1056800 | tf_op jit(solution)/shard_map/all_to_all | solution.py:194
  134.7 2.8 %gather_fusion.1 = bf16[13,129,256]{2,1,0:T(8,128)(2,1)} fusion(bf16[16,129,256]{2,1,0:T(8,128)(2,1)} %bitcast.103, s32[1024]{0:T(1024)S(1)} %pad_clamp_fusion), kind=kCustom, calls=%fused_computation.1 | custom fusion | bytes 1717300 | tf_op jit(solution)/shard_map/jit(_take)/gather | solution.py:202
  137.5 2.7 %maximum_add_fusion = f32[2,624,512]{2,1,0:T(8,128)S(1)} fusion(f32[2,624,512]{2,1,0:T(8,128)} %collective-permute-done.10, f32[1,624,512]{2,1,0:T(8,128)} %get-tuple-element.12, f32[1,624,512]{2,1,0:T(8,128)S(1)} %copy-done.3), kind=kLoop, calls=%fused_computation.8 | loop fusion | flops 1277952 | bytes 7667712 | tf_op jit(solution)/shard_map/add | solution.py:106
  140.3 1.6 %collective-permute-start.11 = (bf16[624,512]{1,0:T(8,128)(2,1)S(1)}, bf16[624,512]{1,0:T(8,128)(2,1)S(1)}, u32[]{:S(2)}, u32[]{:S(2)}) collective-permute-start(bf16[624,512]{1,0:T(8,128)(2,1)S(1)} %fusion.31), channel_id=1, source_target_pairs={{0,2},{2,0},{1,3},{3,1},{4,6},{6,4},{5,7},{7,5},{8,10},{10,8},{9,1... | collective-permute-start | bytes 1916936 | tf_op jit(solution)/shard_map/ppermute | solution.py:41
  143.0 13.0 %collective-permute-done.11 = bf16[624,512]{1,0:T(8,128)(2,1)S(1)} collective-permute-done((bf16[624,512]{1,0:T(8,128)(2,1)S(1)}, bf16[624,512]{1,0:T(8,128)(2,1)S(1)}, u32[]{:S(2)}, u32[]{:S(2)}) %collective-permute-start.11) | collective-permute-done | bytes 639008 | tf_op jit(solution)/shard_map/ppermute | solution.py:41
  (124 shorter events, 33.5 us)
Async XLA Ops:
  0.6 11.7 %copy-start = (bf16[512,2048]{1,0:T(8,128)(2,1)S(1)}, bf16[512,2048]{1,0:T(8,128)(2,1)}, u32[]{:S(2)}) copy-start(bf16[512,2048]{1,0:T(8,128)(2,1)} %param.23) | copy-start | bytes 6291460
  0.6 18.6 %collective-permute-start = (bf16[624,512]{1,0:T(8,128)(2,1)}, bf16[624,512]{1,0:T(8,128)(2,1)}, u32[]{:S(2)}, u32[]{:S(2)}) collective-permute-start(bf16[624,512]{1,0:T(8,128)(2,1)} %param.15), channel_id=1, source_target_pairs={{0,2},{2,0},{1,3},{3,1},{4,6},{6,4},{5,7},{7,5},{8,10},{10,8},{9,1... | collective-permute-start | bytes 1916936 | tf_op jit(solution)/shard_map/ppermute | solution.py:41
  8.0 7.4 %copy-start.22 = (s32[13]{0:T(128)S(1)}, s32[13]{0:T(128)}, u32[]{:S(2)}) copy-start(s32[13]{0:T(128)} %param.17) | copy-start | bytes 160
  8.0 20.4 %all-to-all-start = ((bf16[2,4,13,16,256]{4,3,2,0,1:T(8,128)(2,1)}), bf16[2,4,13,16,256]{4,3,2,0,1:T(8,128)(2,1)}, u32[]{:S(2)}, u32[]{:S(2)}) async-start(bf16[2,4,13,16,256]{4,3,2,0,1:T(8,128)(2,1)} %copy.70), calls=%async_computation | async-start | bytes 1703936 | tf_op jit(solution)/shard_map/all_to_all | solution.py:170
  12.3 8.9 %copy-start.16 = (s32[13]{0:T(128)S(1)}, s32[13]{0:T(128)}, u32[]{:S(2)}) copy-start(s32[13]{0:T(128)} %param.16) | copy-start | bytes 160
  13.4 40.3 %collective-permute-start.3 = (bf16[512,1024]{1,0:T(8,128)(2,1)}, bf16[512,1024]{1,0:T(8,128)(2,1)}, u32[]{:S(2)}, u32[]{:S(2)}) collective-permute-start(bf16[512,1024]{1,0:T(8,128)(2,1)} %constant_dynamic-slice_fusion.1), channel_id=1, source_target_pairs={{0,2},{2,0},{1,3},{3,1},{4,6},{6,4},{5,7},{7,5},{8,10},{10,8},{9,1... | collective-permute-start | bytes 3145736 | tf_op jit(solution)/shard_map/ppermute | solution.py:41
  21.1 9.5 %collective-permute-start.1 = (bf16[2,624,512]{2,1,0:T(8,128)(2,1)S(1)}, bf16[2,624,512]{2,1,0:T(8,128)(2,1)}, u32[]{:S(2)}, u32[]{:S(2)}) collective-permute-start(bf16[2,624,512]{2,1,0:T(8,128)(2,1)S(1)} %maximum_select_fusion), channel_id=1, source_target_pairs={{0,1},{1,0},{2,3},{3,2},{4,5},{5,4},{6,7},{7,6},{8,9},{9,8},{10,11... | collective-permute-start | bytes 3833864 | tf_op jit(solution)/shard_map/ppermute | solution.py:41
  32.0 2.1 %copy-start.15 = (f32[2048]{0:T(1024)S(1)}, f32[2048]{0:T(1024)}, u32[]{:S(2)}) copy-start(f32[2048]{0:T(1024)} %param.19) | copy-start | bytes 24580
  34.1 2.4 %copy-start.19 = (bf16[2048,512]{1,0:T(8,128)(2,1)S(1)}, bf16[2048,512]{1,0:T(8,128)(2,1)}, u32[]{:S(2)}) copy-start(bf16[2048,512]{1,0:T(8,128)(2,1)} %param.20) | copy-start | bytes 6291460
  35.0 1.5 copy-start.6
  41.1 1.7 %copy-start.7 = (bf16[624,2048]{1,0:T(8,128)(2,1)S(1)}, bf16[624,2048]{1,0:T(8,128)(2,1)}, u32[]{:S(2)}) copy-start(bf16[624,2048]{1,0:T(8,128)(2,1)} %copy-done.6) | copy-start | bytes 7667716
  42.8 3.7 %copy-start.20 = (bf16[2048,256]{1,0:T(8,128)(2,1)S(1)}, bf16[2048,256]{1,0:T(8,128)(2,1)}, u32[]{:S(2)}) copy-start(bf16[2048,256]{1,0:T(8,128)(2,1)} %param.22) | copy-start | bytes 3145732
  46.6 1.1 copy-start.14
  50.7 14.8 %collective-permute-start.2 = (bf16[624,512]{1,0:T(8,128)(2,1)S(1)}, bf16[624,512]{1,0:T(8,128)(2,1)S(1)}, u32[]{:S(2)}, u32[]{:S(2)}) collective-permute-start(bf16[624,512]{1,0:T(8,128)(2,1)S(1)} %bitcast.105), channel_id=1, source_target_pairs={{0,2},{2,0},{1,3},{3,1},{4,6},{6,4},{5,7},{7,5},{8,10},{10,8},{9,1... | collective-permute-start | bytes 1916936 | tf_op jit(solution)/shard_map/ppermute | solution.py:41
  67.6 1.5 copy-start.2
  69.1 3.3 %copy-start.8 = (bf16[624,512]{1,0:T(8,128)(2,1)S(1)}, bf16[624,512]{1,0:T(8,128)(2,1)}, u32[]{:S(2)}) copy-start(bf16[624,512]{1,0:T(8,128)(2,1)} %param.15) | copy-start | bytes 1916932
  69.3 3.2 %collective-permute-start.4 = (f32[624,512]{1,0:T(8,128)S(1)}, f32[624,512]{1,0:T(8,128)}, u32[]{:S(2)}, u32[]{:S(2)}) collective-permute-start(f32[624,512]{1,0:T(8,128)S(1)} %constant_dynamic-slice_fusion), channel_id=1, source_target_pairs={{0,1},{1,0},{2,3},{3,2},{4,5},{5,4},{6,7},{7,6},{8,9},{9,8},{10,11... | collective-permute-start | bytes 3833864 | tf_op jit(solution)/shard_map/ppermute | solution.py:41
  74.4 1.2 collective-permute-start.5
  75.7 3.6 %collective-permute-start.6 = (f32[624,1]{0,1:T(1,128)S(1)}, f32[624,1]{0,1:T(1,128)S(1)}, u32[]{:S(2)}, u32[]{:S(2)}) collective-permute-start(f32[624,1]{0,1:T(1,128)S(1)} %reshape_add_fusion), channel_id=1, source_target_pairs={{0,2},{2,0},{1,3},{3,1},{4,6},{6,4},{5,7},{7,5},{8,10},{10,8},{9,1... | collective-permute-start | bytes 7496 | tf_op jit(solution)/shard_map/ppermute | solution.py:41
  79.5 2.1 %collective-permute-start.8 = (bf16[624,512]{1,0:T(8,128)(2,1)S(1)}, bf16[624,512]{1,0:T(8,128)(2,1)S(1)}, u32[]{:S(2)}, u32[]{:S(2)}) collective-permute-start(bf16[624,512]{1,0:T(8,128)(2,1)S(1)} %multiply_convert_fusion.2), channel_id=1, source_target_pairs={{0,1},{1,0},{2,3},{3,2},{4,5},{5,4},{6,7},{7,6},{8,9},{9,8},{10,11... | collective-permute-start | bytes 1916936 | tf_op jit(solution)/shard_map/ppermute | solution.py:41
  79.7 17.0 %collective-permute-start.7 = (bf16[624,512]{1,0:T(8,128)(2,1)S(1)}, bf16[624,512]{1,0:T(8,128)(2,1)}, u32[]{:S(2)}, u32[]{:S(2)}) collective-permute-start(bf16[624,512]{1,0:T(8,128)(2,1)S(1)} %multiply_convert_fusion.2), channel_id=1, source_target_pairs={{0,2},{2,0},{1,3},{3,1},{4,6},{6,4},{5,7},{7,5},{8,10},{10,8},{9,1... | collective-permute-start | bytes 1916936 | tf_op jit(solution)/shard_map/ppermute | solution.py:41
  81.6 6.0 %copy-start.18 = (bf16[2048,1024]{1,0:T(8,128)(2,1)S(1)}, bf16[2048,1024]{1,0:T(8,128)(2,1)}, u32[]{:S(2)}) copy-start(bf16[2048,1024]{1,0:T(8,128)(2,1)} %param.25) | copy-start | bytes 12582916
  87.6 9.0 %copy-start.10 = (bf16[1,13,4,16,256]{4,3,2,1,0:T(8,128)(2,1)S(1)}, bf16[1,13,4,16,256]{4,3,2,1,0:T(8,128)(2,1)}, u32[]{:S(2)}) copy-start(bf16[1,13,4,16,256]{4,3,2,1,0:T(8,128)(2,1)} %get-tuple-element.25) | copy-start | bytes 1277956
  87.6 9.0 %copy-start.12 = (bf16[1,13,4,16,256]{4,3,2,1,0:T(8,128)(2,1)S(1)}, bf16[1,13,4,16,256]{4,3,2,1,0:T(8,128)(2,1)}, u32[]{:S(2)}) copy-start(bf16[1,13,4,16,256]{4,3,2,1,0:T(8,128)(2,1)} %get-tuple-element.26) | copy-start | bytes 1277956
  96.6 8.5 %collective-permute-start.9 = (bf16[624,512]{1,0:T(8,128)(2,1)}, bf16[624,512]{1,0:T(8,128)(2,1)}, u32[]{:S(2)}, u32[]{:S(2)}) collective-permute-start(bf16[624,512]{1,0:T(8,128)(2,1)} %collective-permute-done.7), channel_id=1, source_target_pairs={{0,1},{1,0},{2,3},{3,2},{4,5},{5,4},{6,7},{7,6},{8,9},{9,8},{10,11... | collective-permute-start | bytes 1916936 | tf_op jit(solution)/shard_map/ppermute | solution.py:41
  99.4 32.4 %all-to-all-start.1 = ((bf16[8,2,129,256]{3,1,2,0:T(2,128)(2,1)}), bf16[8,2,129,256]{3,1,2,0:T(2,128)(2,1)}, u32[]{:S(2)}, u32[]{:S(2)}) async-start(bf16[8,2,129,256]{3,1,2,0:T(2,128)(2,1)} %copy.77), calls=%async_computation.1 | async-start | bytes 2113536 | tf_op jit(solution)/shard_map/all_to_all | solution.py:194
  129.7 7.8 %copy-start.3 = (f32[1,624,512]{2,1,0:T(8,128)S(1)}, f32[1,624,512]{2,1,0:T(8,128)}, u32[]{:S(2)}) copy-start(f32[1,624,512]{2,1,0:T(8,128)} %get-tuple-element.11) | copy-start | bytes 3833860
  129.7 7.8 %collective-permute-start.10 = (f32[2,624,512]{2,1,0:T(8,128)}, f32[2,624,512]{2,1,0:T(8,128)}, u32[]{:S(2)}, u32[]{:S(2)}) collective-permute-start(f32[2,624,512]{2,1,0:T(8,128)} %pad_maximum_fusion.1), channel_id=1, source_target_pairs={{0,1},{1,0},{2,3},{3,2},{4,5},{5,4},{6,7},{7,6},{8,9},{9,8},{10,11... | collective-permute-start | bytes 7667720 | tf_op jit(solution)/shard_map/ppermute | solution.py:41
  133.2 1.1 copy-start.4
  140.1 1.7 %copy-start.5 = (bf16[13,129,256]{2,1,0:T(8,128)(2,1)S(1)}, bf16[13,129,256]{2,1,0:T(8,128)(2,1)}, u32[]{:S(2)}) copy-start(bf16[13,129,256]{2,1,0:T(8,128)(2,1)} %gather_fusion.1) | copy-start | bytes 2575876
  140.3 15.8 %collective-permute-start.11 = (bf16[624,512]{1,0:T(8,128)(2,1)S(1)}, bf16[624,512]{1,0:T(8,128)(2,1)S(1)}, u32[]{:S(2)}, u32[]{:S(2)}) collective-permute-start(bf16[624,512]{1,0:T(8,128)(2,1)S(1)} %fusion.31), channel_id=1, source_target_pairs={{0,2},{2,0},{1,3},{3,1},{4,6},{6,4},{5,7},{7,5},{8,10},{10,8},{9,1... | collective-permute-start | bytes 1916936 | tf_op jit(solution)/shard_map/ppermute | solution.py:41
  142.0 15.2 %copy-start.1 = (bf16[512,2048]{1,0:T(8,128)(2,1)S(1)}, bf16[512,2048]{1,0:T(8,128)(2,1)}, u32[]{:S(2)}) copy-start(bf16[512,2048]{1,0:T(8,128)(2,1)} %param.23) | copy-start | bytes 6291460
  (5 other events, 4.5 us)

commit v13 on v12

--- a/solution.py
+++ b/solution.py
@@ -166,11 +166,25 @@
     past_share = earlier_rotated_keys.shape[1]
     stacked = jnp.stack([earlier_rotated_keys, earlier_values])
     stacked = stacked.reshape(2, request_list, past_share, kv_count, local_kv * HEAD_WIDTH)
-    stacked = stacked.transpose(0, 3, 1, 2, 4)
-    arrived = lax.all_to_all(stacked, ("kvy", "core"), split_axis=1, concat_axis=1, tiled=True)
-    head_kv = arrived.transpose(0, 2, 1, 3, 4).reshape(
-        2, request_list, kv_count * past_share, local_kv * HEAD_WIDTH
-    )
+
+    def chunk_for(target):
+        return lax.dynamic_index_in_dim(stacked, target, 3, keepdims=False)
+
+    diagonal = [(source, kv_count - 1 - source) for source in range(kv_count)]
+    pieces = {
+        0: chunk_for(kv_index),
+        1: swap(chunk_for(kv_index ^ 1), "core"),
+        2: swap(chunk_for(kv_index ^ 2), "kvy"),
+        3: lax.ppermute(chunk_for(kv_index ^ 3), ("kvy", "core"), diagonal),
+    }
+    blocks = []
+    for source in range(kv_count):
+        relation = source ^ kv_index
+        block = pieces[3]
+        for known in (2, 1, 0):
+            block = jnp.where(relation == known, pieces[known], block)
+        blocks.append(block)
+    head_kv = jnp.concatenate(blocks, axis=2)
     past_size = head_kv.shape[2]
 
     capacity = max(2, (request_list + req_count - 1) // req_count)

time: 158 us -> 173 us (1.095)
  waiting for transfers between devices: 44.8 us -> 61.8 us
  starting transfers between devices: 22.3 us -> 19 us
  other arithmetic: 25.3 us -> 28.2 us
  matrix products: 37 us -> 35.2 us
    ppermute x12 -> x14, waiting for transfers between devices: 38.1 us -> 60 us  [swap(): return lax.ppermute(values, axis_name, [(0, 1), (1, 0)])]
    all_to_all x1 -> x0, waiting for transfers between devices: 4.89 us -> none  [local(): lax.all_to_all(stacked, ('kvy', 'core'), split_axis=1, concat_axis=1, til...]
    all_to_all x1 -> x0, starting transfers between devices: 4.33 us -> none  [local(): lax.all_to_all(stacked, ('kvy', 'core'), split_axis=1, concat_axis=1, til...]
    squeeze x0 -> x2, local copies, waits for them, and re-layouts: none -> 3.25 us  [the longest x1 1.97 us: chunk_for(): return lax.dynamic_index_in_dim(stacked, target, 3, keepdims=False)]
    select_n x1, other arithmetic: 0.26 us -> 2.28 us  [local(): jnp.where(filled[:, None, None], packed, -jnp.ones((), packed.dtype))]
    select_n x1 -> x0, local copies, waits for them, and re-layouts: 1.81 us -> none  [local(): jnp.where(filled[:, None, None], packed, -jnp.ones((), packed.dtype))]
    dot_general x2, matrix products: 9.6 us -> 7.8 us  [gather_project(): jnp.dot(local_pair, lax.dynamic_slice_in_dim(weight, chip * half, half, 0...]
    another operation x2 -> x3, local copies, waits for them, and re-layouts: 2.65 us -> 3.61 us  [local(): stacked = jnp.stack([earlier_rotated_keys, earlier_values])]
  transfers between devices with their start and end apart: 14 -> 16, of which waited for: 9 -> 9; matrix products, arithmetic and copies ran while one was open for 47% -> 40% of each run, Pallas kernels for 0% -> 0%
where the time goes in v13:
time: 173 us; the launch traced here: 172 us
  waiting for transfers between devices  61.8 us (36%)
  matrix products  35.2 us (20%)
  other arithmetic  28.2 us (16%)
  local copies, waits for them, and re-layouts  26.6 us (15%)
  starting transfers between devices  19 us (11%)
    ppermute x14, waiting for transfers between devices, swap(): return lax.ppermute(values, axis_name, [(0, 1), (1, 0)])  60 us
    ppermute x14, starting transfers between devices, swap(): return lax.ppermute(values, axis_name, [(0, 1), (1, 0)])  12.8 us
    dot_general x1, matrix products, scatter_features(): product = jnp.dot(matrix_in, weight, preferred_element_type=jnp.float32)  12.6 us
    unnamed x51, local copies, waits for them, and re-layouts  8.32 us
    dot_general x2, matrix products, gather_project(): jnp.dot(local_pair, lax.dynamic_slice_in_dim(weight, chip * half, half, 0...  7.8 us
    all_to_all x1, starting transfers between devices, local(): lax.all_to_all(packed, 'req', split_axis=0, concat_axis=0, tiled=True)  6.04 us
    dot_general x1, matrix products, gather_project(): jnp.dot(remote_pair, lax.dynamic_slice_in_dim(weight, (1 - chip) * half,...  5.38 us
    another operation x1, other arithmetic, scatter_features(): jnp.stack([jnp.where(core == 0, block(k, 0), block(k, 1)) for k in range(...  4.75 us
  transfers between devices with their start and end apart: 16, of which 9 were waited for; matrix products, arithmetic and copies ran while one was open for 40% of the time, Pallas kernels for 0%

profile of v13, /device:TPU:0, one launch (start us, length us, event | category | flops | bytes accessed | tf_op | source)
XLA Modules:
  0.0 172.0 jit_solution(3832843864959228535)
XLA Ops:
  5.2 2.0 %dynamic-slice_bitcast_fusion = (bf16[2,13,16,256]{3,2,1,0:T(8,128)(2,1)}, bf16[2,13,16,256]{3,2,1,0:T(8,128)(2,1)}, bf16[2,13,16,256]{3,2,1,0:T(8,128)(2,1)}) fusion(bf16[2,13,16,4,256]{4,2,1,0,3:T(8,128)(2,1)} %copy_dynamic-update-slice_fusion, s32[]{:T(128)S(6)} %select_n.277, s32[]{:T(128)S(6)} %select_n.276, s32[]{:T(128)S(6)} %select_n.274), kind=kLoop, calls=%fused_computation.96 | loop fusion | bytes 1277964 | tf_op jit(solution)/shard_map/jit(dynamic_index_in_dim)/squeeze | solution.py:171
  7.6 2.5 %collective-permute-start.1 = (bf16[2,13,16,256]{3,2,1,0:T(8,128)(2,1)}, bf16[2,13,16,256]{3,2,1,0:T(8,128)(2,1)}, u32[]{:S(2)}, u32[]{:S(2)}) collective-permute-start(bf16[2,13,16,256]{3,2,1,0:T(8,128)(2,1)} %get-tuple-element.34), channel_id=1, source_target_pairs={{0,2},{2,0},{1,3},{3,1},{4,6},{6,4},{5,7},{7,5},{8,10},{10,8},{9,1... | collective-permute-start | bytes 638984 | tf_op jit(solution)/shard_map/ppermute | solution.py:41
  10.3 1.7 collective-permute-start.3
  13.5 21.1 %collective-permute-done.3 = bf16[624,512]{1,0:T(8,128)(2,1)S(1)} collective-permute-done((bf16[624,512]{1,0:T(8,128)(2,1)S(1)}, bf16[624,512]{1,0:T(8,128)(2,1)S(1)}, u32[]{:S(2)}, u32[]{:S(2)}) %collective-permute-start.3) | collective-permute-done | bytes 639008 | tf_op jit(solution)/shard_map/ppermute | solution.py:41
  35.5 2.0 %maximum_select_fusion = bf16[2,624,512]{2,1,0:T(8,128)(2,1)S(1)} fusion(bf16[1,624,512]{2,1,0:T(8,128)(2,1)} %bitcast.118, bf16[1,624,512]{2,1,0:T(8,128)(2,1)} %bitcast.117, pred[]{:T(512)S(6)} %eq.109), kind=kLoop, calls=%fused_computation.24 | loop fusion | flops 1916928 | bytes 2555905 | tf_op jit(solution)/shard_map/jit(_where)/select_n | solution.py:48
  37.6 2.1 %multiply_cosine_fusion = (f32[13,48,128]{2,1,0:T(8,128)}, f32[13,48,128]{2,1,0:T(8,128)}) fusion(f32[128]{0:T(128)S(1)} %multiply_exponential_fusion, f32[13,48]{1,0:T(8,128)S(1)} %iota_add_fusion), kind=kLoop, calls=%fused_computation.72 | loop fusion | flops 79872 | bytes 641984 | tf_op jit(solution)/shard_map/cos | solution.py:22
  44.0 2.0 %fusion = f32[624]{0:T(1024)S(1)} fusion(bf16[624,512]{1,0:T(8,128)(2,1)S(1)} %get-tuple-element.17, bf16[624,512]{1,0:T(8,128)(2,1)S(1)} %get-tuple-element.18, bf16[624,512]{1,0:T(8,128)(2,1)S(1)} %get-tuple-element.16, bf16[624,512]{1,0:T(8,128)(2,1)S(1)} %get-tuple-element.15), kind=kLoop, calls=%fused_computation.4 | loop fusion | flops 12778896 | bytes 2558400 | tf_op jit(solution)/shard_map/reduce_sum | solution.py:226
  48.4 2.6 %fusion.74 = f32[624,512]{1,0:T(8,128)} fusion(bf16[624,2048]{1,0:T(8,128)(2,1)S(1)} %fusion.2, bf16[2048,512]{1,0:T(8,128)(2,1)S(1)} %copy-done.21), kind=kOutput, calls=%fused_computation.161 | convolution fusion | flops 1308622848 | bytes 5931008 | tf_op jit(solution)/shard_map/dot_general | solution.py:233
  51.0 2.1 %reshape.294 = f32[13,48,2,256]{3,2,1,0:T(2,128)S(1)} reshape(f32[624,512]{1,0:T(8,128)} %fusion.74) | data formatting | bytes 2555904 | tf_op jit(solution)/shard_map/reshape | solution.py:235
  54.8 2.2 %fusion.73 = f32[624,256]{1,0:T(8,128)S(1)} fusion(bf16[624,2048]{1,0:T(8,128)(2,1)S(1)} %copy-done.7, bf16[2048,256]{1,0:T(8,128)(2,1)} %param.21), kind=kOutput, calls=%fused_computation.160 | convolution fusion | flops 654311424 | bytes 4243456 | tf_op jit(solution)/shard_map/dot_general | solution.py:237
  57.0 1.6 fusion.41
  62.7 2.0 %collective-permute-start.5 = (bf16[624,512]{1,0:T(8,128)(2,1)S(1)}, bf16[624,512]{1,0:T(8,128)(2,1)S(1)}, u32[]{:S(2)}, u32[]{:S(2)}) collective-permute-start(bf16[624,512]{1,0:T(8,128)(2,1)S(1)} %bitcast.114), channel_id=1, source_target_pairs={{0,2},{2,0},{1,3},{3,1},{4,6},{6,4},{5,7},{7,5},{8,10},{10,8},{9,1... | collective-permute-start | bytes 1916936 | tf_op jit(solution)/shard_map/ppermute | solution.py:41
  65.5 14.1 %collective-permute-done.5 = bf16[624,512]{1,0:T(8,128)(2,1)S(1)} collective-permute-done((bf16[624,512]{1,0:T(8,128)(2,1)S(1)}, bf16[624,512]{1,0:T(8,128)(2,1)S(1)}, u32[]{:S(2)}, u32[]{:S(2)}) %collective-permute-start.5) | collective-permute-done | bytes 639008 | tf_op jit(solution)/shard_map/ppermute | solution.py:41
  79.7 2.1 %convolution_add_fusion = f32[624,1024]{1,0:T(8,128)S(1)} fusion(f32[624,1024]{1,0:T(8,128)S(1)} %fusion.19, bf16[624,512]{1,0:T(8,128)(2,1)S(1)} %collective-permute-done.5, bf16[512,1024]{1,0:T(8,128)(2,1)} %collective-permute-done.6), kind=kOutput, calls=%fused_computation.21 | convolution fusion | flops 654950400 | bytes 6799360 | tf_op jit(solution)/shard_map/dot_general | solution.py:121
  84.1 2.5 %collective-permute-done.7 = f32[624,512]{1,0:T(8,128)} collective-permute-done((f32[624,512]{1,0:T(8,128)S(1)}, f32[624,512]{1,0:T(8,128)}, u32[]{:S(2)}, u32[]{:S(2)}) %collective-permute-start.7) | collective-permute-done | bytes 1277984 | tf_op jit(solution)/shard_map/ppermute | solution.py:41
  86.6 2.0 %multiply_reduce_fusion = (f32[624]{0:T(1024)S(1)}, f32[624,512]{1,0:T(8,128)S(1)}) fusion(f32[624,512]{1,0:T(8,128)} %collective-permute-done.7, f32[624,1024]{1,0:T(8,128)} %copy-done.2, s32[]{:T(128)S(6)} %select_n.314, bf16[624,512]{1,0:T(8,128)(2,1)S(1)} %copy-done.9), kind=kLoop, calls=%fused_computation.38 | loop fusion | flops 1596816 | bytes 4475332 | tf_op jit(solution)/shard_map/reduce_sum | solution.py:130
  89.8 1.7 %collective-permute-start.9 = (f32[624,1]{0,1:T(1,128)S(1)}, f32[624,1]{0,1:T(1,128)S(1)}, u32[]{:S(2)}, u32[]{:S(2)}) collective-permute-start(f32[624,1]{0,1:T(1,128)S(1)} %reshape_add_fusion), channel_id=1, source_target_pairs={{0,2},{2,0},{1,3},{3,1},{4,6},{6,4},{5,7},{7,5},{8,10},{10,8},{9,1... | collective-permute-start | bytes 7496 | tf_op jit(solution)/shard_map/ppermute | solution.py:41
  93.8 1.8 %collective-permute-start.10 = (bf16[624,512]{1,0:T(8,128)(2,1)S(1)}, bf16[624,512]{1,0:T(8,128)(2,1)}, u32[]{:S(2)}, u32[]{:S(2)}) collective-permute-start(bf16[624,512]{1,0:T(8,128)(2,1)S(1)} %multiply_convert_fusion.2), channel_id=1, source_target_pairs={{0,2},{2,0},{1,3},{3,1},{4,6},{6,4},{5,7},{7,5},{8,10},{10,8},{9,1... | collective-permute-start | bytes 1916936 | tf_op jit(solution)/shard_map/ppermute | solution.py:41
  95.7 4.7 %fusion.7 = f32[624,1024]{1,0:T(8,128)} fusion(bf16[2048,1024]{1,0:T(8,128)(2,1)} %param.26, s32[]{:T(128)S(6)} %select_n.312, bf16[624,512]{1,0:T(8,128)(2,1)S(1)} %collective-permute-done.11, bf16[624,512]{1,0:T(8,128)(2,1)S(1)} %multiply_convert_fusion.2, pred[]{:T(512)S(6)} %eq.108), kind=kOutput, calls=%fused_computation.17 | convolution fusion | flops 1314373632 | bytes 5931013 | tf_op jit(solution)/shard_map/dot_general | solution.py:69
  100.5 3.1 %fusion.9 = f32[624,1024]{1,0:T(8,128)} fusion(bf16[2048,1024]{1,0:T(8,128)(2,1)S(1)} %copy-done.20, s32[]{:T(128)S(6)} %select_n.312, bf16[624,512]{1,0:T(8,128)(2,1)S(1)} %collective-permute-done.11, bf16[624,512]{1,0:T(8,128)(2,1)S(1)} %multiply_convert_fusion.2, pred[]{:T(512)S(6)} %eq.108), kind=kOutput, calls=%fused_computation.19 | convolution fusion | flops 1314373632 | bytes 5931013 | tf_op jit(solution)/shard_map/dot_general | solution.py:69
  103.5 7.2 %collective-permute-done.10 = bf16[624,512]{1,0:T(8,128)(2,1)} collective-permute-done((bf16[624,512]{1,0:T(8,128)(2,1)S(1)}, bf16[624,512]{1,0:T(8,128)(2,1)}, u32[]{:S(2)}, u32[]{:S(2)}) %collective-permute-start.10) | collective-permute-done | bytes 639008 | tf_op jit(solution)/shard_map/ppermute | solution.py:41
  111.7 2.3 %broadcast_select_fusion.1 = bf16[8,2,129,256]{3,1,2,0:T(2,128)(2,1)} fusion(pred[8,2]{1,0:T(8,128)(4,1)S(1)} %broadcast_in_dim.128, pred[8,2]{1,0:T(8,128)(4,1)S(1)} %compare_and_fusion, bf16[8,2,129,256]{3,2,1,0:T(8,128)(2,1)S(1)} %bitcast.111), kind=kLoop, calls=%fused_computation.12 | loop fusion | flops 1056768 | bytes 2113568 | tf_op jit(solution)/shard_map/jit(_where)/select_n | solution.py:206
  114.0 6.0 %all-to-all-start = ((bf16[8,2,129,256]{3,1,2,0:T(2,128)(2,1)}), bf16[8,2,129,256]{3,1,2,0:T(2,128)(2,1)}, u32[]{:S(2)}, u32[]{:S(2)}) async-start(bf16[8,2,129,256]{3,1,2,0:T(2,128)(2,1)} %broadcast_select_fusion.1), calls=%async_computation | async-start | bytes 2113536 | tf_op jit(solution)/shard_map/all_to_all | solution.py:208
  120.0 5.4 %fusion.3 = f32[624,1024]{1,0:T(8,128)} fusion(bf16[2048,1024]{1,0:T(8,128)(2,1)} %param.26, s32[]{:T(128)S(6)} %select_n.313, bf16[624,512]{1,0:T(8,128)(2,1)} %collective-permute-done.12, bf16[624,512]{1,0:T(8,128)(2,1)} %collective-permute-done.10, pred[]{:T(512)S(6)} %eq.108), kind=kOutput, calls=%fused_computation.13 | convolution fusion | flops 1314373632 | bytes 5931013 | tf_op jit(solution)/shard_map/dot_general | solution.py:85
  125.4 12.6 %fusion.11 = f32[624,2048]{1,0:T(8,128)} fusion(bf16[1024,2048]{1,0:T(8,128)(2,1)} %param.27, f32[624,1024]{1,0:T(8,128)} %fusion.7, f32[624,1024]{1,0:T(8,128)} %fusion.3, f32[624,1024]{1,0:T(8,128)} %fusion.9, bf16[2048,1024]{1,0:T(8,128)(2,1)} %param.25, s32[]{:T(128)S(6)} %select_n.313, bf16[624,512]{1,0:T(8,128)(2,1)} %collective-permute-done.12, ...), kind=kOutput, calls=%fused_computation.23 | convolution fusion | flops 3936731136 | bytes 20348932 | tf_op jit(solution)/shard_map/dot_general | solution.py:97
  138.0 4.7 %select_bitcast_fusion.3 = (f32[1,624,512]{2,1,0:T(8,128)}, f32[1,624,512]{2,1,0:T(8,128)}, f32[1,624,512]{2,1,0:T(8,128)S(1)}, f32[1,624,512]{2,1,0:T(8,128)S(1)}) fusion(f32[624,2048]{1,0:T(8,128)} %fusion.11, pred[]{:T(512)S(6)} %eq.108), kind=kLoop, calls=%fused_computation.35 | loop fusion | flops 1277952 | bytes 10223617 | tf_op jit(solution)/shard_map/stack | solution.py:104
  142.8 1.8 %pad_maximum_fusion.1 = f32[2,624,512]{2,1,0:T(8,128)} fusion(f32[1,624,512]{2,1,0:T(8,128)S(1)} %get-tuple-element.13, f32[1,624,512]{2,1,0:T(8,128)S(1)} %get-tuple-element.14), kind=kLoop, calls=%fused_computation.9 | loop fusion | flops 638976 | bytes 5111808 | tf_op jit(solution)/shard_map/stack | solution.py:105
  144.9 1.8 %all-to-all-done = bf16[8,2,129,256]{3,1,2,0:T(2,128)(2,1)} async-done(((bf16[8,2,129,256]{3,1,2,0:T(2,128)(2,1)}), bf16[8,2,129,256]{3,1,2,0:T(2,128)(2,1)}, u32[]{:S(2)}, u32[]{:S(2)}) %all-to-all-start) | async-done | bytes 1056800 | tf_op jit(solution)/shard_map/all_to_all | solution.py:208
  149.5 2.8 %gather_fusion.1 = bf16[13,129,256]{2,1,0:T(8,128)(2,1)} fusion(bf16[16,129,256]{2,1,0:T(8,128)(2,1)} %bitcast.113, s32[1024]{0:T(1024)S(1)} %pad_clamp_fusion), kind=kCustom, calls=%fused_computation.1 | custom fusion | bytes 1717300 | tf_op jit(solution)/shard_map/jit(_take)/gather | solution.py:216
  152.3 2.7 %maximum_add_fusion = f32[2,624,512]{2,1,0:T(8,128)S(1)} fusion(f32[2,624,512]{2,1,0:T(8,128)} %collective-permute-done.13, f32[1,624,512]{2,1,0:T(8,128)} %get-tuple-element.12, f32[1,624,512]{2,1,0:T(8,128)S(1)} %copy-done.3), kind=kLoop, calls=%fused_computation.8 | loop fusion | flops 1277952 | bytes 7667712 | tf_op jit(solution)/shard_map/add | solution.py:106
  155.1 1.6 collective-permute-start.14
  157.9 13.0 %collective-permute-done.14 = bf16[624,512]{1,0:T(8,128)(2,1)S(1)} collective-permute-done((bf16[624,512]{1,0:T(8,128)(2,1)S(1)}, bf16[624,512]{1,0:T(8,128)(2,1)S(1)}, u32[]{:S(2)}, u32[]{:S(2)}) %collective-permute-start.14) | collective-permute-done | bytes 639008 | tf_op jit(solution)/shard_map/ppermute | solution.py:41
  (131 shorter events, 33.2 us)
Async XLA Ops:
  0.6 11.3 %copy-start = (bf16[512,2048]{1,0:T(8,128)(2,1)S(1)}, bf16[512,2048]{1,0:T(8,128)(2,1)}, u32[]{:S(2)}) copy-start(bf16[512,2048]{1,0:T(8,128)(2,1)} %param.23) | copy-start | bytes 6291460
  2.1 8.1 %copy-start.8 = (bf16[624,512]{1,0:T(8,128)(2,1)S(1)}, bf16[624,512]{1,0:T(8,128)(2,1)}, u32[]{:S(2)}) copy-start(bf16[624,512]{1,0:T(8,128)(2,1)} %param.15) | copy-start | bytes 1916932
  4.3 9.0 %copy-start.23 = (s32[13]{0:T(128)S(1)}, s32[13]{0:T(128)}, u32[]{:S(2)}) copy-start(s32[13]{0:T(128)} %param.17) | copy-start | bytes 160
  4.3 9.0 %copy-start.18 = (s32[13]{0:T(128)S(1)}, s32[13]{0:T(128)}, u32[]{:S(2)}) copy-start(s32[13]{0:T(128)} %param.16) | copy-start | bytes 160
  7.1 32.6 %collective-permute-start = (bf16[2,13,16,256]{3,2,1,0:T(8,128)(2,1)}, bf16[2,13,16,256]{3,2,1,0:T(8,128)(2,1)}, u32[]{:S(2)}, u32[]{:S(2)}) collective-permute-start(bf16[2,13,16,256]{3,2,1,0:T(8,128)(2,1)} %get-tuple-element.35), channel_id=1, source_target_pairs={{0,1},{1,0},{2,3},{3,2},{4,5},{5,4},{6,7},{7,6},{8,9},{9,8},{10,11... | collective-permute-start | bytes 638984 | tf_op jit(solution)/shard_map/ppermute | solution.py:41
  7.6 32.2 %collective-permute-start.1 = (bf16[2,13,16,256]{3,2,1,0:T(8,128)(2,1)}, bf16[2,13,16,256]{3,2,1,0:T(8,128)(2,1)}, u32[]{:S(2)}, u32[]{:S(2)}) collective-permute-start(bf16[2,13,16,256]{3,2,1,0:T(8,128)(2,1)} %get-tuple-element.34), channel_id=1, source_target_pairs={{0,2},{2,0},{1,3},{3,1},{4,6},{6,4},{5,7},{7,5},{8,10},{10,8},{9,1... | collective-permute-start | bytes 638984 | tf_op jit(solution)/shard_map/ppermute | solution.py:41
  10.1 29.7 %collective-permute-start.2 = (bf16[2,13,16,256]{3,2,1,0:T(8,128)(2,1)}, bf16[2,13,16,256]{3,2,1,0:T(8,128)(2,1)}, u32[]{:S(2)}, u32[]{:S(2)}) collective-permute-start(bf16[2,13,16,256]{3,2,1,0:T(8,128)(2,1)} %get-tuple-element.33), channel_id=1, source_target_pairs={{0,3},{1,2},{2,1},{3,0},{4,7},{5,6},{6,5},{7,4},{8,11},{9,10},{10,... | collective-permute-start | bytes 638984 | tf_op jit(solution)/shard_map/ppermute | solution.py:178
  10.3 24.4 %collective-permute-start.3 = (bf16[624,512]{1,0:T(8,128)(2,1)S(1)}, bf16[624,512]{1,0:T(8,128)(2,1)S(1)}, u32[]{:S(2)}, u32[]{:S(2)}) collective-permute-start(bf16[624,512]{1,0:T(8,128)(2,1)S(1)} %copy-done.8), channel_id=1, source_target_pairs={{0,2},{2,0},{1,3},{3,1},{4,6},{6,4},{5,7},{7,5},{8,10},{10,8},{9,1... | collective-permute-start | bytes 1916936 | tf_op jit(solution)/shard_map/ppermute | solution.py:41
  13.0 52.5 %collective-permute-start.6 = (bf16[512,1024]{1,0:T(8,128)(2,1)}, bf16[512,1024]{1,0:T(8,128)(2,1)}, u32[]{:S(2)}, u32[]{:S(2)}) collective-permute-start(bf16[512,1024]{1,0:T(8,128)(2,1)} %constant_dynamic-slice_fusion.1), channel_id=1, source_target_pairs={{0,2},{2,0},{1,3},{3,1},{4,6},{6,4},{5,7},{7,5},{8,10},{10,8},{9,1... | collective-permute-start | bytes 3145736 | tf_op jit(solution)/shard_map/ppermute | solution.py:41
  37.5 5.0 %collective-permute-start.4 = (bf16[2,624,512]{2,1,0:T(8,128)(2,1)S(1)}, bf16[2,624,512]{2,1,0:T(8,128)(2,1)}, u32[]{:S(2)}, u32[]{:S(2)}) collective-permute-start(bf16[2,624,512]{2,1,0:T(8,128)(2,1)S(1)} %maximum_select_fusion), channel_id=1, source_target_pairs={{0,1},{1,0},{2,3},{3,2},{4,5},{5,4},{6,7},{7,6},{8,9},{9,8},{10,11... | collective-permute-start | bytes 3833864 | tf_op jit(solution)/shard_map/ppermute | solution.py:41
  44.0 2.1 %copy-start.17 = (f32[2048]{0:T(1024)S(1)}, f32[2048]{0:T(1024)}, u32[]{:S(2)}) copy-start(f32[2048]{0:T(1024)} %param.19) | copy-start | bytes 24580
  46.0 2.4 %copy-start.21 = (bf16[2048,512]{1,0:T(8,128)(2,1)S(1)}, bf16[2048,512]{1,0:T(8,128)(2,1)}, u32[]{:S(2)}) copy-start(bf16[2048,512]{1,0:T(8,128)(2,1)} %param.20) | copy-start | bytes 6291460
  46.9 1.5 copy-start.6
  53.1 1.7 %copy-start.7 = (bf16[624,2048]{1,0:T(8,128)(2,1)S(1)}, bf16[624,2048]{1,0:T(8,128)(2,1)}, u32[]{:S(2)}) copy-start(bf16[624,2048]{1,0:T(8,128)(2,1)} %copy-done.6) | copy-start | bytes 7667716
  54.8 3.7 %copy-start.22 = (bf16[2048,256]{1,0:T(8,128)(2,1)S(1)}, bf16[2048,256]{1,0:T(8,128)(2,1)}, u32[]{:S(2)}) copy-start(bf16[2048,256]{1,0:T(8,128)(2,1)} %param.22) | copy-start | bytes 3145732
  62.7 17.0 %collective-permute-start.5 = (bf16[624,512]{1,0:T(8,128)(2,1)S(1)}, bf16[624,512]{1,0:T(8,128)(2,1)S(1)}, u32[]{:S(2)}, u32[]{:S(2)}) collective-permute-start(bf16[624,512]{1,0:T(8,128)(2,1)S(1)} %bitcast.114), channel_id=1, source_target_pairs={{0,2},{2,0},{1,3},{3,1},{4,6},{6,4},{5,7},{7,5},{8,10},{10,8},{9,1... | collective-permute-start | bytes 1916936 | tf_op jit(solution)/shard_map/ppermute | solution.py:41
  83.3 3.3 %copy-start.9 = (bf16[624,512]{1,0:T(8,128)(2,1)S(1)}, bf16[624,512]{1,0:T(8,128)(2,1)}, u32[]{:S(2)}) copy-start(bf16[624,512]{1,0:T(8,128)(2,1)} %param.15) | copy-start | bytes 1916932
  83.4 3.2 %collective-permute-start.7 = (f32[624,512]{1,0:T(8,128)S(1)}, f32[624,512]{1,0:T(8,128)}, u32[]{:S(2)}, u32[]{:S(2)}) collective-permute-start(f32[624,512]{1,0:T(8,128)S(1)} %constant_dynamic-slice_fusion), channel_id=1, source_target_pairs={{0,1},{1,0},{2,3},{3,2},{4,5},{5,4},{6,7},{7,6},{8,9},{9,8},{10,11... | collective-permute-start | bytes 3833864 | tf_op jit(solution)/shard_map/ppermute | solution.py:41
  88.6 1.2 collective-permute-start.8
  89.8 3.6 %collective-permute-start.9 = (f32[624,1]{0,1:T(1,128)S(1)}, f32[624,1]{0,1:T(1,128)S(1)}, u32[]{:S(2)}, u32[]{:S(2)}) collective-permute-start(f32[624,1]{0,1:T(1,128)S(1)} %reshape_add_fusion), channel_id=1, source_target_pairs={{0,2},{2,0},{1,3},{3,1},{4,6},{6,4},{5,7},{7,5},{8,10},{10,8},{9,1... | collective-permute-start | bytes 7496 | tf_op jit(solution)/shard_map/ppermute | solution.py:41
  93.6 2.1 %collective-permute-start.11 = (bf16[624,512]{1,0:T(8,128)(2,1)S(1)}, bf16[624,512]{1,0:T(8,128)(2,1)S(1)}, u32[]{:S(2)}, u32[]{:S(2)}) collective-permute-start(bf16[624,512]{1,0:T(8,128)(2,1)S(1)} %multiply_convert_fusion.2), channel_id=1, source_target_pairs={{0,1},{1,0},{2,3},{3,2},{4,5},{5,4},{6,7},{7,6},{8,9},{9,8},{10,11... | collective-permute-start | bytes 1916936 | tf_op jit(solution)/shard_map/ppermute | solution.py:41
  93.8 17.0 %collective-permute-start.10 = (bf16[624,512]{1,0:T(8,128)(2,1)S(1)}, bf16[624,512]{1,0:T(8,128)(2,1)}, u32[]{:S(2)}, u32[]{:S(2)}) collective-permute-start(bf16[624,512]{1,0:T(8,128)(2,1)S(1)} %multiply_convert_fusion.2), channel_id=1, source_target_pairs={{0,2},{2,0},{1,3},{3,1},{4,6},{6,4},{5,7},{7,5},{8,10},{10,8},{9,1... | collective-permute-start | bytes 1916936 | tf_op jit(solution)/shard_map/ppermute | solution.py:41
  95.6 4.8 %copy-start.20 = (bf16[2048,1024]{1,0:T(8,128)(2,1)S(1)}, bf16[2048,1024]{1,0:T(8,128)(2,1)}, u32[]{:S(2)}) copy-start(bf16[2048,1024]{1,0:T(8,128)(2,1)} %param.25) | copy-start | bytes 12582916
  100.5 10.5 %copy-start.10 = (bf16[13,64,256]{2,1,0:T(8,128)(2,1)S(1)}, bf16[13,64,256]{2,1,0:T(8,128)(2,1)}, u32[]{:S(2)}) copy-start(bf16[13,64,256]{2,1,0:T(8,128)(2,1)} %get-tuple-element.29) | copy-start | bytes 1277956
  100.5 10.5 %copy-start.11 = (bf16[13,64,256]{2,1,0:T(8,128)(2,1)S(1)}, bf16[13,64,256]{2,1,0:T(8,128)(2,1)}, u32[]{:S(2)}) copy-start(bf16[13,64,256]{2,1,0:T(8,128)(2,1)} %get-tuple-element.30) | copy-start | bytes 1277956
  110.8 9.3 %collective-permute-start.12 = (bf16[624,512]{1,0:T(8,128)(2,1)}, bf16[624,512]{1,0:T(8,128)(2,1)}, u32[]{:S(2)}, u32[]{:S(2)}) collective-permute-start(bf16[624,512]{1,0:T(8,128)(2,1)} %collective-permute-done.10), channel_id=1, source_target_pairs={{0,1},{1,0},{2,3},{3,2},{4,5},{5,4},{6,7},{7,6},{8,9},{9,8},{10,11... | collective-permute-start | bytes 1916936 | tf_op jit(solution)/shard_map/ppermute | solution.py:41
  114.0 32.8 %all-to-all-start = ((bf16[8,2,129,256]{3,1,2,0:T(2,128)(2,1)}), bf16[8,2,129,256]{3,1,2,0:T(2,128)(2,1)}, u32[]{:S(2)}, u32[]{:S(2)}) async-start(bf16[8,2,129,256]{3,1,2,0:T(2,128)(2,1)} %broadcast_select_fusion.1), calls=%async_computation | async-start | bytes 2113536 | tf_op jit(solution)/shard_map/all_to_all | solution.py:208
  144.5 7.8 %copy-start.3 = (f32[1,624,512]{2,1,0:T(8,128)S(1)}, f32[1,624,512]{2,1,0:T(8,128)}, u32[]{:S(2)}) copy-start(f32[1,624,512]{2,1,0:T(8,128)} %get-tuple-element.11) | copy-start | bytes 3833860
  144.5 7.8 %collective-permute-start.13 = (f32[2,624,512]{2,1,0:T(8,128)}, f32[2,624,512]{2,1,0:T(8,128)}, u32[]{:S(2)}, u32[]{:S(2)}) collective-permute-start(f32[2,624,512]{2,1,0:T(8,128)} %pad_maximum_fusion.1), channel_id=1, source_target_pairs={{0,1},{1,0},{2,3},{3,2},{4,5},{5,4},{6,7},{7,6},{8,9},{9,8},{10,11... | collective-permute-start | bytes 7667720 | tf_op jit(solution)/shard_map/ppermute | solution.py:41
  155.0 1.7 copy-start.5
  155.1 15.8 %collective-permute-start.14 = (bf16[624,512]{1,0:T(8,128)(2,1)S(1)}, bf16[624,512]{1,0:T(8,128)(2,1)S(1)}, u32[]{:S(2)}, u32[]{:S(2)}) collective-permute-start(bf16[624,512]{1,0:T(8,128)(2,1)S(1)} %fusion.31), channel_id=1, source_target_pairs={{0,2},{2,0},{1,3},{3,1},{4,6},{6,4},{5,7},{7,5},{8,10},{10,8},{9,1... | collective-permute-start | bytes 1916936 | tf_op jit(solution)/shard_map/ppermute | solution.py:41
  156.8 15.2 %copy-start.1 = (bf16[512,2048]{1,0:T(8,128)(2,1)S(1)}, bf16[512,2048]{1,0:T(8,128)(2,1)}, u32[]{:S(2)}) copy-start(bf16[512,2048]{1,0:T(8,128)(2,1)} %param.23) | copy-start | bytes 6291460
  (8 other events, 8.1 us)

commit v14 on v12

--- a/solution.py
+++ b/solution.py
@@ -186,7 +186,7 @@
     filled = jnp.any(matches, axis=1)
     lanes = local_kv * HEAD_WIDTH
     slot_code = jnp.stack([decode_slot // 16, decode_slot % 16], axis=1).astype(jnp.bfloat16)
-    trailer = jnp.pad(slot_code, ((0, 0), (0, lanes - 2)))[:, None, :]
+    trailer = jnp.pad(slot_code[:, None, :], ((0, 0), (0, 7), (0, lanes - 2)))
     payload = jnp.concatenate([head_kv[0], head_kv[1], trailer], axis=1)
     packed = jnp.take(payload, picked, axis=0)
     packed = jnp.where(filled[:, None, None], packed, -jnp.ones((), packed.dtype))

time: 158 us -> 157 us (level)
  local copies, waits for them, and re-layouts: 26.6 us -> 23.3 us
    select_n x1 -> x0, local copies, waits for them, and re-layouts: 1.81 us -> none  [local(): jnp.where(filled[:, None, None], packed, -jnp.ones((), packed.dtype))]
    unnamed x48 -> x46, local copies, waits for them, and re-layouts: 7.51 us -> 6.45 us
  transfers between devices with their start and end apart: 14 -> 14, of which waited for: 9 -> 9; matrix products, arithmetic and copies ran while one was open for 47% -> 46% of each run, Pallas kernels for 0% -> 0%
where the time goes in v14:
time: 157 us; the launch traced here: 156 us
  waiting for transfers between devices  46.2 us (29%)
  matrix products  37 us (24%)
  other arithmetic  26.3 us (17%)
  local copies, waits for them, and re-layouts  23.3 us (15%)
  starting transfers between devices  22.3 us (14%)
    ppermute x12, waiting for transfers between devices, swap(): return lax.ppermute(values, axis_name, [(0, 1), (1, 0)])  38.3 us
    dot_general x1, matrix products, scatter_features(): product = jnp.dot(matrix_in, weight, preferred_element_type=jnp.float32)  12.6 us
    ppermute x12, starting transfers between devices, swap(): return lax.ppermute(values, axis_name, [(0, 1), (1, 0)])  12.2 us
    dot_general x2, matrix products, gather_project(): jnp.dot(local_pair, lax.dynamic_slice_in_dim(weight, chip * half, half, 0...  9.58 us
    unnamed x46, local copies, waits for them, and re-layouts  6.45 us
    all_to_all x1, starting transfers between devices, local(): lax.all_to_all(packed, 'req', split_axis=0, concat_axis=0, tiled=True)  5.7 us
    dot_general x1, matrix products, gather_project(): jnp.dot(remote_pair, lax.dynamic_slice_in_dim(weight, (1 - chip) * half,...  5.38 us
    all_to_all x1, waiting for transfers between devices, local(): lax.all_to_all(stacked, ('kvy', 'core'), split_axis=1, concat_axis=1, til...  4.89 us
  transfers between devices with their start and end apart: 14, of which 9 were waited for; matrix products, arithmetic and copies ran while one was open for 46% of the time, Pallas kernels for 0%

profile of v14, /device:TPU:0, one launch (start us, length us, event | category | flops | bytes accessed | tf_op | source)
XLA Modules:
  0.0 156.1 jit_solution(14982067117817899582)
XLA Ops:
  0.6 3.0 %collective-permute-start = (bf16[624,512]{1,0:T(8,128)(2,1)}, bf16[624,512]{1,0:T(8,128)(2,1)}, u32[]{:S(2)}, u32[]{:S(2)}) collective-permute-start(bf16[624,512]{1,0:T(8,128)(2,1)} %param.15), channel_id=1, source_target_pairs={{0,2},{2,0},{1,3},{3,1},{4,6},{6,4},{5,7},{7,5},{8,10},{10,8},{9,1... | collective-permute-start | bytes 1916936 | tf_op jit(solution)/shard_map/ppermute | solution.py:41
  8.0 4.3 %all-to-all-start = ((bf16[2,4,13,16,256]{4,3,2,0,1:T(8,128)(2,1)}), bf16[2,4,13,16,256]{4,3,2,0,1:T(8,128)(2,1)}, u32[]{:S(2)}, u32[]{:S(2)}) async-start(bf16[2,4,13,16,256]{4,3,2,0,1:T(8,128)(2,1)} %copy.60), calls=%async_computation | async-start | bytes 1703936 | tf_op jit(solution)/shard_map/all_to_all | solution.py:170
  13.4 1.9 %collective-permute-start.3 = (bf16[512,1024]{1,0:T(8,128)(2,1)}, bf16[512,1024]{1,0:T(8,128)(2,1)}, u32[]{:S(2)}, u32[]{:S(2)}) collective-permute-start(bf16[512,1024]{1,0:T(8,128)(2,1)} %constant_dynamic-slice_fusion.1), channel_id=1, source_target_pairs={{0,2},{2,0},{1,3},{3,1},{4,6},{6,4},{5,7},{7,5},{8,10},{10,8},{9,1... | collective-permute-start | bytes 3145736 | tf_op jit(solution)/shard_map/ppermute | solution.py:41
  15.4 3.8 %collective-permute-done = bf16[624,512]{1,0:T(8,128)(2,1)} collective-permute-done((bf16[624,512]{1,0:T(8,128)(2,1)}, bf16[624,512]{1,0:T(8,128)(2,1)}, u32[]{:S(2)}, u32[]{:S(2)}) %collective-permute-start) | collective-permute-done | bytes 639008 | tf_op jit(solution)/shard_map/ppermute | solution.py:41
  19.2 1.9 %maximum_select_fusion = bf16[2,624,512]{2,1,0:T(8,128)(2,1)S(1)} fusion(bf16[1,624,512]{2,1,0:T(8,128)(2,1)} %bitcast.4, bf16[1,624,512]{2,1,0:T(8,128)(2,1)} %bitcast.104, pred[]{:T(512)S(6)} %eq.27), kind=kLoop, calls=%fused_computation.24 | loop fusion | flops 1916928 | bytes 2555905 | tf_op jit(solution)/shard_map/jit(_where)/select_n | solution.py:48
  21.4 2.0 %multiply_cosine_fusion = (f32[13,48,128]{2,1,0:T(8,128)}, f32[13,48,128]{2,1,0:T(8,128)}) fusion(f32[128]{0:T(128)S(1)} %multiply_exponential_fusion, f32[13,48]{1,0:T(8,128)S(1)} %iota_add_fusion), kind=kLoop, calls=%fused_computation.74 | loop fusion | flops 79872 | bytes 641984 | tf_op jit(solution)/shard_map/cos | solution.py:22
  23.4 4.9 %all-to-all-done = bf16[2,4,13,16,256]{4,3,2,0,1:T(8,128)(2,1)} async-done(((bf16[2,4,13,16,256]{4,3,2,0,1:T(8,128)(2,1)}), bf16[2,4,13,16,256]{4,3,2,0,1:T(8,128)(2,1)}, u32[]{:S(2)}, u32[]{:S(2)}) %all-to-all-start) | async-done | bytes 852000 | tf_op jit(solution)/shard_map/all_to_all | solution.py:170
  32.0 2.0 %fusion = f32[624]{0:T(1024)S(1)} fusion(bf16[624,512]{1,0:T(8,128)(2,1)S(1)} %get-tuple-element.17, bf16[624,512]{1,0:T(8,128)(2,1)S(1)} %get-tuple-element.18, bf16[624,512]{1,0:T(8,128)(2,1)S(1)} %get-tuple-element.16, bf16[624,512]{1,0:T(8,128)(2,1)S(1)} %get-tuple-element.15), kind=kLoop, calls=%fused_computation.4 | loop fusion | flops 12778896 | bytes 2558400 | tf_op jit(solution)/shard_map/reduce_sum | solution.py:212
  35.0 1.5 copy-done.5
  36.5 2.6 %fusion.73 = f32[624,512]{1,0:T(8,128)} fusion(bf16[624,2048]{1,0:T(8,128)(2,1)S(1)} %fusion.2, bf16[2048,512]{1,0:T(8,128)(2,1)S(1)} %copy-done.18), kind=kOutput, calls=%fused_computation.147 | convolution fusion | flops 1308622848 | bytes 5931008 | tf_op jit(solution)/shard_map/dot_general | solution.py:219
  39.0 2.1 %reshape.334 = f32[13,48,2,256]{3,2,1,0:T(2,128)S(1)} reshape(f32[624,512]{1,0:T(8,128)} %fusion.73) | data formatting | bytes 2555904 | tf_op jit(solution)/shard_map/reshape | solution.py:221
  42.8 2.1 %fusion.72 = f32[624,256]{1,0:T(8,128)S(1)} fusion(bf16[624,2048]{1,0:T(8,128)(2,1)S(1)} %copy-done.6, bf16[2048,256]{1,0:T(8,128)(2,1)} %param.21), kind=kOutput, calls=%fused_computation.146 | convolution fusion | flops 654311424 | bytes 4243456 | tf_op jit(solution)/shard_map/dot_general | solution.py:223
  45.0 1.6 %fusion.43 = (bf16[13,48,1,128]{3,1,0,2:T(8,128)(2,1)S(1)}, bf16[13,48,1,128]{3,1,0,2:T(8,128)(2,1)S(1)}) fusion(f32[13,48,1,256]{3,1,0,2:T(8,128)S(1)} %bitcast.109, f32[128]{0:T(128)S(1)} %multiply_exponential_fusion, f32[13,48]{1,0:T(8,128)S(1)} %iota_add_fusion), kind=kLoop, calls=%fused_computation.82 | loop fusion | flops 718848 | bytes 961472 | tf_op jit(solution)/shard_map/convert.7
  50.7 2.1 %collective-permute-start.2 = (bf16[624,512]{1,0:T(8,128)(2,1)S(1)}, bf16[624,512]{1,0:T(8,128)(2,1)S(1)}, u32[]{:S(2)}, u32[]{:S(2)}) collective-permute-start(bf16[624,512]{1,0:T(8,128)(2,1)S(1)} %bitcast.101), channel_id=1, source_target_pairs={{0,2},{2,0},{1,3},{3,1},{4,6},{6,4},{5,7},{7,5},{8,10},{10,8},{9,1... | collective-permute-start | bytes 1916936 | tf_op jit(solution)/shard_map/ppermute | solution.py:41
  53.7 11.8 %collective-permute-done.2 = bf16[624,512]{1,0:T(8,128)(2,1)S(1)} collective-permute-done((bf16[624,512]{1,0:T(8,128)(2,1)S(1)}, bf16[624,512]{1,0:T(8,128)(2,1)S(1)}, u32[]{:S(2)}, u32[]{:S(2)}) %collective-permute-start.2) | collective-permute-done | bytes 639008 | tf_op jit(solution)/shard_map/ppermute | solution.py:41
  65.6 2.1 %convolution_add_fusion = f32[624,1024]{1,0:T(8,128)S(1)} fusion(f32[624,1024]{1,0:T(8,128)S(1)} %fusion.20, bf16[624,512]{1,0:T(8,128)(2,1)S(1)} %collective-permute-done.2, bf16[512,1024]{1,0:T(8,128)(2,1)} %collective-permute-done.3), kind=kOutput, calls=%fused_computation.21 | convolution fusion | flops 654950400 | bytes 6799360 | tf_op jit(solution)/shard_map/dot_general | solution.py:121
  69.8 2.6 %collective-permute-done.4 = f32[624,512]{1,0:T(8,128)} collective-permute-done((f32[624,512]{1,0:T(8,128)S(1)}, f32[624,512]{1,0:T(8,128)}, u32[]{:S(2)}, u32[]{:S(2)}) %collective-permute-start.4) | collective-permute-done | bytes 1277984 | tf_op jit(solution)/shard_map/ppermute | solution.py:41
  72.5 2.0 %multiply_reduce_fusion = (f32[624]{0:T(1024)S(1)}, f32[624,512]{1,0:T(8,128)S(1)}) fusion(f32[624,512]{1,0:T(8,128)} %collective-permute-done.4, f32[624,1024]{1,0:T(8,128)} %copy-done.2, s32[]{:T(128)S(6)} %select_n.199, bf16[624,512]{1,0:T(8,128)(2,1)S(1)} %copy-done.7), kind=kLoop, calls=%fused_computation.38 | loop fusion | flops 1596816 | bytes 4475332 | tf_op jit(solution)/shard_map/reduce_sum | solution.py:130
  79.8 1.5 collective-permute-start.7
  82.4 5.2 %fusion.7 = f32[624,1024]{1,0:T(8,128)} fusion(bf16[2048,1024]{1,0:T(8,128)(2,1)} %param.26, s32[]{:T(128)S(6)} %select_n.197, bf16[624,512]{1,0:T(8,128)(2,1)S(1)} %collective-permute-done.8, bf16[624,512]{1,0:T(8,128)(2,1)S(1)} %multiply_convert_fusion.2, pred[]{:T(512)S(6)} %eq.26), kind=kOutput, calls=%fused_computation.15 | convolution fusion | flops 1314373632 | bytes 5931013 | tf_op jit(solution)/shard_map/dot_general | solution.py:69
  87.6 4.4 %fusion.9 = f32[624,1024]{1,0:T(8,128)} fusion(bf16[2048,1024]{1,0:T(8,128)(2,1)S(1)} %copy-done.17, s32[]{:T(128)S(6)} %select_n.197, bf16[624,512]{1,0:T(8,128)(2,1)} %copy-done.20, bf16[624,512]{1,0:T(8,128)(2,1)S(1)} %multiply_convert_fusion.2, pred[]{:T(512)S(6)} %eq.26), kind=kOutput, calls=%fused_computation.17 | convolution fusion | flops 1314373632 | bytes 5931013 | tf_op jit(solution)/shard_map/dot_general | solution.py:69
  92.0 4.7 %collective-permute-done.7 = bf16[624,512]{1,0:T(8,128)(2,1)} collective-permute-done((bf16[624,512]{1,0:T(8,128)(2,1)S(1)}, bf16[624,512]{1,0:T(8,128)(2,1)}, u32[]{:S(2)}, u32[]{:S(2)}) %collective-permute-start.7) | collective-permute-done | bytes 639008 | tf_op jit(solution)/shard_map/ppermute | solution.py:41
  98.8 5.7 %all-to-all-start.1 = ((bf16[8,2,136,256]{3,2,1,0:T(8,128)(2,1)}), bf16[8,2,136,256]{3,2,1,0:T(8,128)(2,1)}, u32[]{:S(2)}, u32[]{:S(2)}) async-start(bf16[8,2,136,256]{3,2,1,0:T(8,128)(2,1)} %select_select_fusion), calls=%async_computation.1 | async-start | bytes 2228224 | tf_op jit(solution)/shard_map/all_to_all | solution.py:194
  104.5 5.4 %fusion.3 = f32[624,1024]{1,0:T(8,128)} fusion(bf16[2048,1024]{1,0:T(8,128)(2,1)} %param.26, s32[]{:T(128)S(6)} %select_n.198, bf16[624,512]{1,0:T(8,128)(2,1)} %collective-permute-done.9, bf16[624,512]{1,0:T(8,128)(2,1)} %collective-permute-done.7, pred[]{:T(512)S(6)} %eq.26), kind=kOutput, calls=%fused_computation.11 | convolution fusion | flops 1314373632 | bytes 5931013 | tf_op jit(solution)/shard_map/dot_general | solution.py:85
  109.8 12.6 %fusion.12 = f32[624,2048]{1,0:T(8,128)} fusion(bf16[1024,2048]{1,0:T(8,128)(2,1)} %param.27, f32[624,1024]{1,0:T(8,128)} %fusion.7, f32[624,1024]{1,0:T(8,128)} %fusion.3, f32[624,1024]{1,0:T(8,128)} %fusion.9, bf16[2048,1024]{1,0:T(8,128)(2,1)} %param.25, s32[]{:T(128)S(6)} %select_n.198, bf16[624,512]{1,0:T(8,128)(2,1)} %collective-permute-done.9, ...), kind=kOutput, calls=%fused_computation.23 | convolution fusion | flops 3936731136 | bytes 20348932 | tf_op jit(solution)/shard_map/dot_general | solution.py:97
  122.5 4.8 %select_bitcast_fusion.3 = (f32[1,624,512]{2,1,0:T(8,128)}, f32[1,624,512]{2,1,0:T(8,128)}, f32[1,624,512]{2,1,0:T(8,128)S(1)}, f32[1,624,512]{2,1,0:T(8,128)S(1)}) fusion(f32[624,2048]{1,0:T(8,128)} %fusion.12, pred[]{:T(512)S(6)} %eq.26), kind=kLoop, calls=%fused_computation.35 | loop fusion | flops 1277952 | bytes 10223617 | tf_op jit(solution)/shard_map/stack | solution.py:104
  127.2 1.8 %pad_maximum_fusion.1 = f32[2,624,512]{2,1,0:T(8,128)} fusion(f32[1,624,512]{2,1,0:T(8,128)S(1)} %get-tuple-element.13, f32[1,624,512]{2,1,0:T(8,128)S(1)} %get-tuple-element.14), kind=kLoop, calls=%fused_computation.9 | loop fusion | flops 638976 | bytes 5111808 | tf_op jit(solution)/shard_map/stack | solution.py:105
  129.4 3.0 %all-to-all-done.1 = bf16[8,2,136,256]{3,2,1,0:T(8,128)(2,1)} async-done(((bf16[8,2,136,256]{3,2,1,0:T(8,128)(2,1)}), bf16[8,2,136,256]{3,2,1,0:T(8,128)(2,1)}, u32[]{:S(2)}, u32[]{:S(2)}) %all-to-all-start.1) | async-done | bytes 1114144 | tf_op jit(solution)/shard_map/all_to_all | solution.py:194
  133.5 2.9 %gather_fusion.1 = bf16[13,136,256]{2,1,0:T(8,128)(2,1)} fusion(bf16[16,136,256]{2,1,0:T(8,128)(2,1)} %bitcast.36, s32[1024]{0:T(1024)S(1)} %pad_clamp_fusion), kind=kCustom, calls=%fused_computation.1 | custom fusion | bytes 1810484 | tf_op jit(solution)/shard_map/jit(_take)/gather | solution.py:202
  136.4 2.7 %maximum_add_fusion = f32[2,624,512]{2,1,0:T(8,128)S(1)} fusion(f32[2,624,512]{2,1,0:T(8,128)} %collective-permute-done.10, f32[1,624,512]{2,1,0:T(8,128)} %get-tuple-element.12, f32[1,624,512]{2,1,0:T(8,128)S(1)} %copy-done.3), kind=kLoop, calls=%fused_computation.8 | loop fusion | flops 1277952 | bytes 7667712 | tf_op jit(solution)/shard_map/add | solution.py:106
  139.2 1.6 %collective-permute-start.11 = (bf16[624,512]{1,0:T(8,128)(2,1)S(1)}, bf16[624,512]{1,0:T(8,128)(2,1)S(1)}, u32[]{:S(2)}, u32[]{:S(2)}) collective-permute-start(bf16[624,512]{1,0:T(8,128)(2,1)S(1)} %fusion.33), channel_id=1, source_target_pairs={{0,2},{2,0},{1,3},{3,1},{4,6},{6,4},{5,7},{7,5},{8,10},{10,8},{9,1... | collective-permute-start | bytes 1916936 | tf_op jit(solution)/shard_map/ppermute | solution.py:41
  142.0 13.0 %collective-permute-done.11 = bf16[624,512]{1,0:T(8,128)(2,1)S(1)} collective-permute-done((bf16[624,512]{1,0:T(8,128)(2,1)S(1)}, bf16[624,512]{1,0:T(8,128)(2,1)S(1)}, u32[]{:S(2)}, u32[]{:S(2)}) %collective-permute-start.11) | collective-permute-done | bytes 639008 | tf_op jit(solution)/shard_map/ppermute | solution.py:41
  (120 shorter events, 31.4 us)
Async XLA Ops:
  0.6 11.7 %copy-start = (bf16[512,2048]{1,0:T(8,128)(2,1)S(1)}, bf16[512,2048]{1,0:T(8,128)(2,1)}, u32[]{:S(2)}) copy-start(bf16[512,2048]{1,0:T(8,128)(2,1)} %param.23) | copy-start | bytes 6291460
  0.6 18.6 %collective-permute-start = (bf16[624,512]{1,0:T(8,128)(2,1)}, bf16[624,512]{1,0:T(8,128)(2,1)}, u32[]{:S(2)}, u32[]{:S(2)}) collective-permute-start(bf16[624,512]{1,0:T(8,128)(2,1)} %param.15), channel_id=1, source_target_pairs={{0,2},{2,0},{1,3},{3,1},{4,6},{6,4},{5,7},{7,5},{8,10},{10,8},{9,1... | collective-permute-start | bytes 1916936 | tf_op jit(solution)/shard_map/ppermute | solution.py:41
  8.0 7.4 %copy-start.21 = (s32[13]{0:T(128)S(1)}, s32[13]{0:T(128)}, u32[]{:S(2)}) copy-start(s32[13]{0:T(128)} %param.17) | copy-start | bytes 160
  8.0 20.4 %all-to-all-start = ((bf16[2,4,13,16,256]{4,3,2,0,1:T(8,128)(2,1)}), bf16[2,4,13,16,256]{4,3,2,0,1:T(8,128)(2,1)}, u32[]{:S(2)}, u32[]{:S(2)}) async-start(bf16[2,4,13,16,256]{4,3,2,0,1:T(8,128)(2,1)} %copy.60), calls=%async_computation | async-start | bytes 1703936 | tf_op jit(solution)/shard_map/all_to_all | solution.py:170
  12.3 8.9 %copy-start.15 = (s32[13]{0:T(128)S(1)}, s32[13]{0:T(128)}, u32[]{:S(2)}) copy-start(s32[13]{0:T(128)} %param.16) | copy-start | bytes 160
  13.4 40.3 %collective-permute-start.3 = (bf16[512,1024]{1,0:T(8,128)(2,1)}, bf16[512,1024]{1,0:T(8,128)(2,1)}, u32[]{:S(2)}, u32[]{:S(2)}) collective-permute-start(bf16[512,1024]{1,0:T(8,128)(2,1)} %constant_dynamic-slice_fusion.1), channel_id=1, source_target_pairs={{0,2},{2,0},{1,3},{3,1},{4,6},{6,4},{5,7},{7,5},{8,10},{10,8},{9,1... | collective-permute-start | bytes 3145736 | tf_op jit(solution)/shard_map/ppermute | solution.py:41
  21.1 9.5 %collective-permute-start.1 = (bf16[2,624,512]{2,1,0:T(8,128)(2,1)S(1)}, bf16[2,624,512]{2,1,0:T(8,128)(2,1)}, u32[]{:S(2)}, u32[]{:S(2)}) collective-permute-start(bf16[2,624,512]{2,1,0:T(8,128)(2,1)S(1)} %maximum_select_fusion), channel_id=1, source_target_pairs={{0,1},{1,0},{2,3},{3,2},{4,5},{5,4},{6,7},{7,6},{8,9},{9,8},{10,11... | collective-permute-start | bytes 3833864 | tf_op jit(solution)/shard_map/ppermute | solution.py:41
  32.0 2.1 %copy-start.14 = (f32[2048]{0:T(1024)S(1)}, f32[2048]{0:T(1024)}, u32[]{:S(2)}) copy-start(f32[2048]{0:T(1024)} %param.19) | copy-start | bytes 24580
  34.1 2.4 %copy-start.18 = (bf16[2048,512]{1,0:T(8,128)(2,1)S(1)}, bf16[2048,512]{1,0:T(8,128)(2,1)}, u32[]{:S(2)}) copy-start(bf16[2048,512]{1,0:T(8,128)(2,1)} %param.20) | copy-start | bytes 6291460
  35.0 1.5 copy-start.5
  41.1 1.7 %copy-start.6 = (bf16[624,2048]{1,0:T(8,128)(2,1)S(1)}, bf16[624,2048]{1,0:T(8,128)(2,1)}, u32[]{:S(2)}) copy-start(bf16[624,2048]{1,0:T(8,128)(2,1)} %copy-done.5) | copy-start | bytes 7667716
  42.8 3.7 %copy-start.19 = (bf16[2048,256]{1,0:T(8,128)(2,1)S(1)}, bf16[2048,256]{1,0:T(8,128)(2,1)}, u32[]{:S(2)}) copy-start(bf16[2048,256]{1,0:T(8,128)(2,1)} %param.22) | copy-start | bytes 3145732
  46.6 1.1 copy-start.13
  47.5 1.1 copy-start.8
  50.7 14.8 %collective-permute-start.2 = (bf16[624,512]{1,0:T(8,128)(2,1)S(1)}, bf16[624,512]{1,0:T(8,128)(2,1)S(1)}, u32[]{:S(2)}, u32[]{:S(2)}) collective-permute-start(bf16[624,512]{1,0:T(8,128)(2,1)S(1)} %bitcast.101), channel_id=1, source_target_pairs={{0,2},{2,0},{1,3},{3,1},{4,6},{6,4},{5,7},{7,5},{8,10},{10,8},{9,1... | collective-permute-start | bytes 1916936 | tf_op jit(solution)/shard_map/ppermute | solution.py:41
  67.7 1.5 copy-start.2
  69.1 3.3 %copy-start.7 = (bf16[624,512]{1,0:T(8,128)(2,1)S(1)}, bf16[624,512]{1,0:T(8,128)(2,1)}, u32[]{:S(2)}) copy-start(bf16[624,512]{1,0:T(8,128)(2,1)} %param.15) | copy-start | bytes 1916932
  69.3 3.2 %collective-permute-start.4 = (f32[624,512]{1,0:T(8,128)S(1)}, f32[624,512]{1,0:T(8,128)}, u32[]{:S(2)}, u32[]{:S(2)}) collective-permute-start(f32[624,512]{1,0:T(8,128)S(1)} %constant_dynamic-slice_fusion), channel_id=1, source_target_pairs={{0,1},{1,0},{2,3},{3,2},{4,5},{5,4},{6,7},{7,6},{8,9},{9,8},{10,11... | collective-permute-start | bytes 3833864 | tf_op jit(solution)/shard_map/ppermute | solution.py:41
  74.4 1.2 collective-permute-start.5
  75.7 3.6 %collective-permute-start.6 = (f32[624,1]{0,1:T(1,128)S(1)}, f32[624,1]{0,1:T(1,128)S(1)}, u32[]{:S(2)}, u32[]{:S(2)}) collective-permute-start(f32[624,1]{0,1:T(1,128)S(1)} %reshape_add_fusion), channel_id=1, source_target_pairs={{0,2},{2,0},{1,3},{3,1},{4,6},{6,4},{5,7},{7,5},{8,10},{10,8},{9,1... | collective-permute-start | bytes 7496 | tf_op jit(solution)/shard_map/ppermute | solution.py:41
  79.5 2.1 %collective-permute-start.8 = (bf16[624,512]{1,0:T(8,128)(2,1)S(1)}, bf16[624,512]{1,0:T(8,128)(2,1)S(1)}, u32[]{:S(2)}, u32[]{:S(2)}) collective-permute-start(bf16[624,512]{1,0:T(8,128)(2,1)S(1)} %multiply_convert_fusion.2), channel_id=1, source_target_pairs={{0,1},{1,0},{2,3},{3,2},{4,5},{5,4},{6,7},{7,6},{8,9},{9,8},{10,11... | collective-permute-start | bytes 1916936 | tf_op jit(solution)/shard_map/ppermute | solution.py:41
  79.8 17.0 %collective-permute-start.7 = (bf16[624,512]{1,0:T(8,128)(2,1)S(1)}, bf16[624,512]{1,0:T(8,128)(2,1)}, u32[]{:S(2)}, u32[]{:S(2)}) collective-permute-start(bf16[624,512]{1,0:T(8,128)(2,1)S(1)} %multiply_convert_fusion.2), channel_id=1, source_target_pairs={{0,2},{2,0},{1,3},{3,1},{4,6},{6,4},{5,7},{7,5},{8,10},{10,8},{9,1... | collective-permute-start | bytes 1916936 | tf_op jit(solution)/shard_map/ppermute | solution.py:41
  81.6 6.0 %copy-start.17 = (bf16[2048,1024]{1,0:T(8,128)(2,1)S(1)}, bf16[2048,1024]{1,0:T(8,128)(2,1)}, u32[]{:S(2)}) copy-start(bf16[2048,1024]{1,0:T(8,128)(2,1)} %param.25) | copy-start | bytes 12582916
  87.6 9.1 %copy-start.9 = (bf16[1,13,4,16,256]{4,3,2,1,0:T(8,128)(2,1)S(1)}, bf16[1,13,4,16,256]{4,3,2,1,0:T(8,128)(2,1)}, u32[]{:S(2)}) copy-start(bf16[1,13,4,16,256]{4,3,2,1,0:T(8,128)(2,1)} %get-tuple-element.25) | copy-start | bytes 1277956
  87.6 9.2 %copy-start.11 = (bf16[1,13,4,16,256]{4,3,2,1,0:T(8,128)(2,1)S(1)}, bf16[1,13,4,16,256]{4,3,2,1,0:T(8,128)(2,1)}, u32[]{:S(2)}) copy-start(bf16[1,13,4,16,256]{4,3,2,1,0:T(8,128)(2,1)} %get-tuple-element.26) | copy-start | bytes 1277956
  96.7 7.7 %collective-permute-start.9 = (bf16[624,512]{1,0:T(8,128)(2,1)}, bf16[624,512]{1,0:T(8,128)(2,1)}, u32[]{:S(2)}, u32[]{:S(2)}) collective-permute-start(bf16[624,512]{1,0:T(8,128)(2,1)} %collective-permute-done.7), channel_id=1, source_target_pairs={{0,1},{1,0},{2,3},{3,2},{4,5},{5,4},{6,7},{7,6},{8,9},{9,8},{10,11... | collective-permute-start | bytes 1916936 | tf_op jit(solution)/shard_map/ppermute | solution.py:41
  98.8 33.6 %all-to-all-start.1 = ((bf16[8,2,136,256]{3,2,1,0:T(8,128)(2,1)}), bf16[8,2,136,256]{3,2,1,0:T(8,128)(2,1)}, u32[]{:S(2)}, u32[]{:S(2)}) async-start(bf16[8,2,136,256]{3,2,1,0:T(8,128)(2,1)} %select_select_fusion), calls=%async_computation.1 | async-start | bytes 2228224 | tf_op jit(solution)/shard_map/all_to_all | solution.py:194
  129.0 7.4 %copy-start.3 = (f32[1,624,512]{2,1,0:T(8,128)S(1)}, f32[1,624,512]{2,1,0:T(8,128)}, u32[]{:S(2)}) copy-start(f32[1,624,512]{2,1,0:T(8,128)} %get-tuple-element.11) | copy-start | bytes 3833860
  129.0 7.4 %collective-permute-start.10 = (f32[2,624,512]{2,1,0:T(8,128)}, f32[2,624,512]{2,1,0:T(8,128)}, u32[]{:S(2)}, u32[]{:S(2)}) collective-permute-start(f32[2,624,512]{2,1,0:T(8,128)} %pad_maximum_fusion.1), channel_id=1, source_target_pairs={{0,1},{1,0},{2,3},{3,2},{4,5},{5,4},{6,7},{7,6},{8,9},{9,8},{10,11... | collective-permute-start | bytes 7667720 | tf_op jit(solution)/shard_map/ppermute | solution.py:41
  139.1 1.7 %copy-start.4 = (bf16[13,136,256]{2,1,0:T(8,128)(2,1)S(1)}, bf16[13,136,256]{2,1,0:T(8,128)(2,1)}, u32[]{:S(2)}) copy-start(bf16[13,136,256]{2,1,0:T(8,128)(2,1)} %gather_fusion.1) | copy-start | bytes 2715652
  139.2 15.8 %collective-permute-start.11 = (bf16[624,512]{1,0:T(8,128)(2,1)S(1)}, bf16[624,512]{1,0:T(8,128)(2,1)S(1)}, u32[]{:S(2)}, u32[]{:S(2)}) collective-permute-start(bf16[624,512]{1,0:T(8,128)(2,1)S(1)} %fusion.33), channel_id=1, source_target_pairs={{0,2},{2,0},{1,3},{3,1},{4,6},{6,4},{5,7},{7,5},{8,10},{10,8},{9,1... | collective-permute-start | bytes 1916936 | tf_op jit(solution)/shard_map/ppermute | solution.py:41
  141.0 15.2 %copy-start.1 = (bf16[512,2048]{1,0:T(8,128)(2,1)S(1)}, bf16[512,2048]{1,0:T(8,128)(2,1)}, u32[]{:S(2)}) copy-start(bf16[512,2048]{1,0:T(8,128)(2,1)} %param.23) | copy-start | bytes 6291460
  (4 other events, 3.5 us)

commit v15 on v14

--- a/solution.py
+++ b/solution.py
@@ -164,12 +164,16 @@
     query_groups = local_q // local_kv
 
     past_share = earlier_rotated_keys.shape[1]
-    stacked = jnp.stack([earlier_rotated_keys, earlier_values])
-    stacked = stacked.reshape(2, request_list, past_share, kv_count, local_kv * HEAD_WIDTH)
-    stacked = stacked.transpose(0, 3, 1, 2, 4)
-    arrived = lax.all_to_all(stacked, ("kvy", "core"), split_axis=1, concat_axis=1, tiled=True)
-    head_kv = arrived.transpose(0, 2, 1, 3, 4).reshape(
-        2, request_list, kv_count * past_share, local_kv * HEAD_WIDTH
+    lanes_share = local_kv * HEAD_WIDTH
+    stacked = jnp.stack(
+        [
+            jnp.stack([past[..., j * lanes_share:(j + 1) * lanes_share] for past in (earlier_rotated_keys, earlier_values)])
+            for j in range(kv_count)
+        ]
+    )
+    arrived = lax.all_to_all(stacked, ("kvy", "core"), split_axis=0, concat_axis=0, tiled=True)
+    head_kv = arrived.transpose(1, 2, 0, 3, 4).reshape(
+        2, request_list, kv_count * past_share, lanes_share
     )
     past_size = head_kv.shape[2]
 

time: 157 us -> 157 us (level)
    unnamed x46 -> x48, local copies, waits for them, and re-layouts: 6.45 us -> 7.26 us
where the time goes in v15:
time: 157 us; the launch traced here: 156 us
  waiting for transfers between devices  46.3 us (29%)
  matrix products  37 us (24%)
  other arithmetic  26.8 us (17%)
  local copies, waits for them, and re-layouts  22.5 us (14%)
  starting transfers between devices  22.2 us (14%)
    ppermute x12, waiting for transfers between devices, swap(): return lax.ppermute(values, axis_name, [(0, 1), (1, 0)])  39.1 us
    dot_general x1, matrix products, scatter_features(): product = jnp.dot(matrix_in, weight, preferred_element_type=jnp.float32)  12.6 us
    ppermute x12, starting transfers between devices, swap(): return lax.ppermute(values, axis_name, [(0, 1), (1, 0)])  12.2 us
    dot_general x2, matrix products, gather_project(): jnp.dot(local_pair, lax.dynamic_slice_in_dim(weight, chip * half, half, 0...  9.59 us
    unnamed x48, local copies, waits for them, and re-layouts  7.26 us
    all_to_all x1, starting transfers between devices, local(): lax.all_to_all(packed, 'req', split_axis=0, concat_axis=0, tiled=True)  5.71 us
    dot_general x1, matrix products, gather_project(): jnp.dot(remote_pair, lax.dynamic_slice_in_dim(weight, (1 - chip) * half,...  5.38 us
    another operation x1, other arithmetic, scatter_features(): jnp.stack([jnp.where(core == 0, block(k, 0), block(k, 1)) for k in range(...  4.75 us
  transfers between devices with their start and end apart: 14, of which 9 were waited for; matrix products, arithmetic and copies ran while one was open for 46% of the time, Pallas kernels for 0%

profile of v15, /device:TPU:0, one launch (start us, length us, event | category | flops | bytes accessed | tf_op | source)
XLA Modules:
  0.0 156.0 jit_solution(6617455126110966990)
XLA Ops:
  0.6 3.0 %collective-permute-start = (bf16[624,512]{1,0:T(8,128)(2,1)}, bf16[624,512]{1,0:T(8,128)(2,1)S(1)}, u32[]{:S(2)}, u32[]{:S(2)}) collective-permute-start(bf16[624,512]{1,0:T(8,128)(2,1)} %param.15), channel_id=1, source_target_pairs={{0,2},{2,0},{1,3},{3,1},{4,6},{6,4},{5,7},{7,5},{8,10},{10,8},{9,1... | collective-permute-start | bytes 1916936 | tf_op jit(solution)/shard_map/ppermute | solution.py:41
  7.0 4.3 %all-to-all-start = ((bf16[4,2,13,16,256]{4,3,2,1,0:T(8,128)(2,1)}), bf16[4,2,13,16,256]{4,3,2,1,0:T(8,128)(2,1)}, u32[]{:S(2)}, u32[]{:S(2)}) async-start(bf16[4,2,13,16,256]{4,3,2,1,0:T(8,128)(2,1)} %pad_maximum_fusion.2), calls=%async_computation | async-start | bytes 1703936 | tf_op jit(solution)/shard_map/all_to_all | solution.py:174
  12.4 1.9 %collective-permute-start.3 = (bf16[512,1024]{1,0:T(8,128)(2,1)}, bf16[512,1024]{1,0:T(8,128)(2,1)}, u32[]{:S(2)}, u32[]{:S(2)}) collective-permute-start(bf16[512,1024]{1,0:T(8,128)(2,1)} %constant_dynamic-slice_fusion.1), channel_id=1, source_target_pairs={{0,2},{2,0},{1,3},{3,1},{4,6},{6,4},{5,7},{7,5},{8,10},{10,8},{9,1... | collective-permute-start | bytes 3145736 | tf_op jit(solution)/shard_map/ppermute | solution.py:41
  14.4 4.7 %collective-permute-done = bf16[624,512]{1,0:T(8,128)(2,1)S(1)} collective-permute-done((bf16[624,512]{1,0:T(8,128)(2,1)}, bf16[624,512]{1,0:T(8,128)(2,1)S(1)}, u32[]{:S(2)}, u32[]{:S(2)}) %collective-permute-start) | collective-permute-done | bytes 639008 | tf_op jit(solution)/shard_map/ppermute | solution.py:41
  19.9 2.0 %maximum_select_fusion = bf16[2,624,512]{2,1,0:T(8,128)(2,1)S(1)} fusion(bf16[1,624,512]{2,1,0:T(8,128)(2,1)} %bitcast.131, bf16[1,624,512]{2,1,0:T(8,128)(2,1)} %bitcast.126, pred[]{:T(512)S(6)} %eq.27), kind=kLoop, calls=%fused_computation.24 | loop fusion | flops 1916928 | bytes 2555905 | tf_op jit(solution)/shard_map/jit(_where)/select_n | solution.py:48
  22.2 2.0 %multiply_cosine_fusion = (f32[13,48,128]{2,1,0:T(8,128)}, f32[13,48,128]{2,1,0:T(8,128)}) fusion(f32[128]{0:T(128)S(1)} %multiply_exponential_fusion, f32[13,48]{1,0:T(8,128)S(1)} %iota_add_fusion), kind=kLoop, calls=%fused_computation.74 | loop fusion | flops 79872 | bytes 641984 | tf_op jit(solution)/shard_map/cos | solution.py:22
  24.2 4.1 %all-to-all-done = bf16[4,2,13,16,256]{4,3,2,1,0:T(8,128)(2,1)} async-done(((bf16[4,2,13,16,256]{4,3,2,1,0:T(8,128)(2,1)}), bf16[4,2,13,16,256]{4,3,2,1,0:T(8,128)(2,1)}, u32[]{:S(2)}, u32[]{:S(2)}) %all-to-all-start) | async-done | bytes 852000 | tf_op jit(solution)/shard_map/all_to_all | solution.py:174
  32.0 2.0 %fusion = f32[624]{0:T(1024)S(1)} fusion(bf16[624,512]{1,0:T(8,128)(2,1)S(1)} %get-tuple-element.17, bf16[624,512]{1,0:T(8,128)(2,1)S(1)} %get-tuple-element.18, bf16[624,512]{1,0:T(8,128)(2,1)S(1)} %get-tuple-element.16, bf16[624,512]{1,0:T(8,128)(2,1)S(1)} %get-tuple-element.15), kind=kLoop, calls=%fused_computation.4 | loop fusion | flops 12778896 | bytes 2558400 | tf_op jit(solution)/shard_map/reduce_sum | solution.py:216
  35.0 1.5 copy-done.5
  36.5 2.6 %fusion.73 = f32[624,512]{1,0:T(8,128)} fusion(bf16[624,2048]{1,0:T(8,128)(2,1)S(1)} %fusion.2, bf16[2048,512]{1,0:T(8,128)(2,1)S(1)} %copy-done.19), kind=kOutput, calls=%fused_computation.159 | convolution fusion | flops 1308622848 | bytes 5931008 | tf_op jit(solution)/shard_map/dot_general | solution.py:223
  39.0 2.1 %reshape.329 = f32[13,48,2,256]{3,2,1,0:T(2,128)S(1)} reshape(f32[624,512]{1,0:T(8,128)} %fusion.73) | data formatting | bytes 2555904 | tf_op jit(solution)/shard_map/reshape | solution.py:225
  42.8 2.2 %fusion.72 = f32[624,256]{1,0:T(8,128)S(1)} fusion(bf16[624,2048]{1,0:T(8,128)(2,1)S(1)} %copy-done.6, bf16[2048,256]{1,0:T(8,128)(2,1)} %param.21), kind=kOutput, calls=%fused_computation.158 | convolution fusion | flops 654311424 | bytes 4243456 | tf_op jit(solution)/shard_map/dot_general | solution.py:227
  45.0 1.6 %fusion.43 = (bf16[13,48,1,128]{3,1,0,2:T(8,128)(2,1)S(1)}, bf16[13,48,1,128]{3,1,0,2:T(8,128)(2,1)S(1)}) fusion(f32[13,48,1,256]{3,1,0,2:T(8,128)S(1)} %bitcast.132, f32[128]{0:T(128)S(1)} %multiply_exponential_fusion, f32[13,48]{1,0:T(8,128)S(1)} %iota_add_fusion), kind=kLoop, calls=%fused_computation.82 | loop fusion | flops 718848 | bytes 961472 | tf_op jit(solution)/shard_map/convert.7
  50.7 2.1 %collective-permute-start.2 = (bf16[624,512]{1,0:T(8,128)(2,1)S(1)}, bf16[624,512]{1,0:T(8,128)(2,1)S(1)}, u32[]{:S(2)}, u32[]{:S(2)}) collective-permute-start(bf16[624,512]{1,0:T(8,128)(2,1)S(1)} %bitcast.123), channel_id=1, source_target_pairs={{0,2},{2,0},{1,3},{3,1},{4,6},{6,4},{5,7},{7,5},{8,10},{10,8},{9,1... | collective-permute-start | bytes 1916936 | tf_op jit(solution)/shard_map/ppermute | solution.py:41
  53.7 11.8 %collective-permute-done.2 = bf16[624,512]{1,0:T(8,128)(2,1)S(1)} collective-permute-done((bf16[624,512]{1,0:T(8,128)(2,1)S(1)}, bf16[624,512]{1,0:T(8,128)(2,1)S(1)}, u32[]{:S(2)}, u32[]{:S(2)}) %collective-permute-start.2) | collective-permute-done | bytes 639008 | tf_op jit(solution)/shard_map/ppermute | solution.py:41
  65.5 2.1 %convolution_add_fusion = f32[624,1024]{1,0:T(8,128)S(1)} fusion(f32[624,1024]{1,0:T(8,128)S(1)} %fusion.20, bf16[624,512]{1,0:T(8,128)(2,1)S(1)} %collective-permute-done.2, bf16[512,1024]{1,0:T(8,128)(2,1)} %collective-permute-done.3), kind=kOutput, calls=%fused_computation.21 | convolution fusion | flops 654950400 | bytes 6799360 | tf_op jit(solution)/shard_map/dot_general | solution.py:121
  69.8 2.6 %collective-permute-done.4 = f32[624,512]{1,0:T(8,128)} collective-permute-done((f32[624,512]{1,0:T(8,128)S(1)}, f32[624,512]{1,0:T(8,128)}, u32[]{:S(2)}, u32[]{:S(2)}) %collective-permute-start.4) | collective-permute-done | bytes 1277984 | tf_op jit(solution)/shard_map/ppermute | solution.py:41
  72.4 2.0 %multiply_reduce_fusion = (f32[624]{0:T(1024)S(1)}, f32[624,512]{1,0:T(8,128)S(1)}) fusion(f32[624,512]{1,0:T(8,128)} %collective-permute-done.4, f32[624,1024]{1,0:T(8,128)} %copy-done.2, s32[]{:T(128)S(6)} %select_n.199, bf16[624,512]{1,0:T(8,128)(2,1)S(1)} %copy-done.7), kind=kLoop, calls=%fused_computation.38 | loop fusion | flops 1596816 | bytes 4475332 | tf_op jit(solution)/shard_map/reduce_sum | solution.py:130
  79.8 1.5 collective-permute-start.7
  82.4 5.2 %fusion.7 = f32[624,1024]{1,0:T(8,128)} fusion(bf16[2048,1024]{1,0:T(8,128)(2,1)} %param.26, s32[]{:T(128)S(6)} %select_n.197, bf16[624,512]{1,0:T(8,128)(2,1)S(1)} %collective-permute-done.8, bf16[624,512]{1,0:T(8,128)(2,1)S(1)} %multiply_convert_fusion.2, pred[]{:T(512)S(6)} %eq.26), kind=kOutput, calls=%fused_computation.15 | convolution fusion | flops 1314373632 | bytes 5931013 | tf_op jit(solution)/shard_map/dot_general | solution.py:69
  87.6 4.4 %fusion.9 = f32[624,1024]{1,0:T(8,128)} fusion(bf16[2048,1024]{1,0:T(8,128)(2,1)S(1)} %copy-done.18, s32[]{:T(128)S(6)} %select_n.197, bf16[624,512]{1,0:T(8,128)(2,1)} %copy-done.21, bf16[624,512]{1,0:T(8,128)(2,1)S(1)} %multiply_convert_fusion.2, pred[]{:T(512)S(6)} %eq.26), kind=kOutput, calls=%fused_computation.17 | convolution fusion | flops 1314373632 | bytes 5931013 | tf_op jit(solution)/shard_map/dot_general | solution.py:69
  92.0 4.7 %collective-permute-done.7 = bf16[624,512]{1,0:T(8,128)(2,1)} collective-permute-done((bf16[624,512]{1,0:T(8,128)(2,1)S(1)}, bf16[624,512]{1,0:T(8,128)(2,1)}, u32[]{:S(2)}, u32[]{:S(2)}) %collective-permute-start.7) | collective-permute-done | bytes 639008 | tf_op jit(solution)/shard_map/ppermute | solution.py:41
  98.7 5.7 %all-to-all-start.1 = ((bf16[8,2,136,256]{3,2,1,0:T(8,128)(2,1)}), bf16[8,2,136,256]{3,2,1,0:T(8,128)(2,1)}, u32[]{:S(2)}, u32[]{:S(2)}) async-start(bf16[8,2,136,256]{3,2,1,0:T(8,128)(2,1)} %select_select_fusion), calls=%async_computation.1 | async-start | bytes 2228224 | tf_op jit(solution)/shard_map/all_to_all | solution.py:198
  104.4 5.4 %fusion.3 = f32[624,1024]{1,0:T(8,128)} fusion(bf16[2048,1024]{1,0:T(8,128)(2,1)} %param.26, s32[]{:T(128)S(6)} %select_n.198, bf16[624,512]{1,0:T(8,128)(2,1)} %collective-permute-done.9, bf16[624,512]{1,0:T(8,128)(2,1)} %collective-permute-done.7, pred[]{:T(512)S(6)} %eq.26), kind=kOutput, calls=%fused_computation.11 | convolution fusion | flops 1314373632 | bytes 5931013 | tf_op jit(solution)/shard_map/dot_general | solution.py:85
  109.8 12.6 %fusion.12 = f32[624,2048]{1,0:T(8,128)} fusion(bf16[1024,2048]{1,0:T(8,128)(2,1)} %param.27, f32[624,1024]{1,0:T(8,128)} %fusion.7, f32[624,1024]{1,0:T(8,128)} %fusion.3, f32[624,1024]{1,0:T(8,128)} %fusion.9, bf16[2048,1024]{1,0:T(8,128)(2,1)} %param.25, s32[]{:T(128)S(6)} %select_n.198, bf16[624,512]{1,0:T(8,128)(2,1)} %collective-permute-done.9, ...), kind=kOutput, calls=%fused_computation.23 | convolution fusion | flops 3936731136 | bytes 20348932 | tf_op jit(solution)/shard_map/dot_general | solution.py:97
  122.4 4.7 %select_bitcast_fusion.3 = (f32[1,624,512]{2,1,0:T(8,128)}, f32[1,624,512]{2,1,0:T(8,128)}, f32[1,624,512]{2,1,0:T(8,128)S(1)}, f32[1,624,512]{2,1,0:T(8,128)S(1)}) fusion(f32[624,2048]{1,0:T(8,128)} %fusion.12, pred[]{:T(512)S(6)} %eq.26), kind=kLoop, calls=%fused_computation.35 | loop fusion | flops 1277952 | bytes 10223617 | tf_op jit(solution)/shard_map/stack | solution.py:104
  127.2 1.8 %pad_maximum_fusion.1 = f32[2,624,512]{2,1,0:T(8,128)} fusion(f32[1,624,512]{2,1,0:T(8,128)S(1)} %get-tuple-element.13, f32[1,624,512]{2,1,0:T(8,128)S(1)} %get-tuple-element.14), kind=kLoop, calls=%fused_computation.9 | loop fusion | flops 638976 | bytes 5111808 | tf_op jit(solution)/shard_map/stack | solution.py:105
  129.3 3.0 %all-to-all-done.1 = bf16[8,2,136,256]{3,2,1,0:T(8,128)(2,1)} async-done(((bf16[8,2,136,256]{3,2,1,0:T(8,128)(2,1)}), bf16[8,2,136,256]{3,2,1,0:T(8,128)(2,1)}, u32[]{:S(2)}, u32[]{:S(2)}) %all-to-all-start.1) | async-done | bytes 1114144 | tf_op jit(solution)/shard_map/all_to_all | solution.py:198
  133.4 2.9 %gather_fusion.1 = bf16[13,136,256]{2,1,0:T(8,128)(2,1)} fusion(bf16[16,136,256]{2,1,0:T(8,128)(2,1)} %bitcast.47, s32[1024]{0:T(1024)S(1)} %pad_clamp_fusion), kind=kCustom, calls=%fused_computation.1 | custom fusion | bytes 1810484 | tf_op jit(solution)/shard_map/jit(_take)/gather | solution.py:206
  136.3 2.7 %maximum_add_fusion = f32[2,624,512]{2,1,0:T(8,128)S(1)} fusion(f32[2,624,512]{2,1,0:T(8,128)} %collective-permute-done.10, f32[1,624,512]{2,1,0:T(8,128)} %get-tuple-element.12, f32[1,624,512]{2,1,0:T(8,128)S(1)} %copy-done.3), kind=kLoop, calls=%fused_computation.8 | loop fusion | flops 1277952 | bytes 7667712 | tf_op jit(solution)/shard_map/add | solution.py:106
  139.1 1.6 %collective-permute-start.11 = (bf16[624,512]{1,0:T(8,128)(2,1)S(1)}, bf16[624,512]{1,0:T(8,128)(2,1)S(1)}, u32[]{:S(2)}, u32[]{:S(2)}) collective-permute-start(bf16[624,512]{1,0:T(8,128)(2,1)S(1)} %fusion.33), channel_id=1, source_target_pairs={{0,2},{2,0},{1,3},{3,1},{4,6},{6,4},{5,7},{7,5},{8,10},{10,8},{9,1... | collective-permute-start | bytes 1916936 | tf_op jit(solution)/shard_map/ppermute | solution.py:41
  141.9 13.0 %collective-permute-done.11 = bf16[624,512]{1,0:T(8,128)(2,1)S(1)} collective-permute-done((bf16[624,512]{1,0:T(8,128)(2,1)S(1)}, bf16[624,512]{1,0:T(8,128)(2,1)S(1)}, u32[]{:S(2)}, u32[]{:S(2)}) %collective-permute-start.11) | collective-permute-done | bytes 639008 | tf_op jit(solution)/shard_map/ppermute | solution.py:41
  (123 shorter events, 31.1 us)
Async XLA Ops:
  0.6 10.7 %copy-start = (bf16[512,2048]{1,0:T(8,128)(2,1)S(1)}, bf16[512,2048]{1,0:T(8,128)(2,1)}, u32[]{:S(2)}) copy-start(bf16[512,2048]{1,0:T(8,128)(2,1)} %param.23) | copy-start | bytes 6291460
  0.6 18.5 %collective-permute-start = (bf16[624,512]{1,0:T(8,128)(2,1)}, bf16[624,512]{1,0:T(8,128)(2,1)S(1)}, u32[]{:S(2)}, u32[]{:S(2)}) collective-permute-start(bf16[624,512]{1,0:T(8,128)(2,1)} %param.15), channel_id=1, source_target_pairs={{0,2},{2,0},{1,3},{3,1},{4,6},{6,4},{5,7},{7,5},{8,10},{10,8},{9,1... | collective-permute-start | bytes 1916936 | tf_op jit(solution)/shard_map/ppermute | solution.py:41
  7.0 7.4 %copy-start.22 = (s32[13]{0:T(128)S(1)}, s32[13]{0:T(128)}, u32[]{:S(2)}) copy-start(s32[13]{0:T(128)} %param.17) | copy-start | bytes 160
  7.0 21.4 %all-to-all-start = ((bf16[4,2,13,16,256]{4,3,2,1,0:T(8,128)(2,1)}), bf16[4,2,13,16,256]{4,3,2,1,0:T(8,128)(2,1)}, u32[]{:S(2)}, u32[]{:S(2)}) async-start(bf16[4,2,13,16,256]{4,3,2,1,0:T(8,128)(2,1)} %pad_maximum_fusion.2), calls=%async_computation | async-start | bytes 1703936 | tf_op jit(solution)/shard_map/all_to_all | solution.py:174
  11.3 10.7 %copy-start.16 = (s32[13]{0:T(128)S(1)}, s32[13]{0:T(128)}, u32[]{:S(2)}) copy-start(s32[13]{0:T(128)} %param.16) | copy-start | bytes 160
  12.4 41.3 %collective-permute-start.3 = (bf16[512,1024]{1,0:T(8,128)(2,1)}, bf16[512,1024]{1,0:T(8,128)(2,1)}, u32[]{:S(2)}, u32[]{:S(2)}) collective-permute-start(bf16[512,1024]{1,0:T(8,128)(2,1)} %constant_dynamic-slice_fusion.1), channel_id=1, source_target_pairs={{0,2},{2,0},{1,3},{3,1},{4,6},{6,4},{5,7},{7,5},{8,10},{10,8},{9,1... | collective-permute-start | bytes 3145736 | tf_op jit(solution)/shard_map/ppermute | solution.py:41
  21.9 8.7 %collective-permute-start.1 = (bf16[2,624,512]{2,1,0:T(8,128)(2,1)S(1)}, bf16[2,624,512]{2,1,0:T(8,128)(2,1)}, u32[]{:S(2)}, u32[]{:S(2)}) collective-permute-start(bf16[2,624,512]{2,1,0:T(8,128)(2,1)S(1)} %maximum_select_fusion), channel_id=1, source_target_pairs={{0,1},{1,0},{2,3},{3,2},{4,5},{5,4},{6,7},{7,6},{8,9},{9,8},{10,11... | collective-permute-start | bytes 3833864 | tf_op jit(solution)/shard_map/ppermute | solution.py:41
  32.0 2.1 %copy-start.15 = (f32[2048]{0:T(1024)S(1)}, f32[2048]{0:T(1024)}, u32[]{:S(2)}) copy-start(f32[2048]{0:T(1024)} %param.19) | copy-start | bytes 24580
  34.1 2.4 %copy-start.19 = (bf16[2048,512]{1,0:T(8,128)(2,1)S(1)}, bf16[2048,512]{1,0:T(8,128)(2,1)}, u32[]{:S(2)}) copy-start(bf16[2048,512]{1,0:T(8,128)(2,1)} %param.20) | copy-start | bytes 6291460
  35.0 1.5 copy-start.5
  41.1 1.7 %copy-start.6 = (bf16[624,2048]{1,0:T(8,128)(2,1)S(1)}, bf16[624,2048]{1,0:T(8,128)(2,1)}, u32[]{:S(2)}) copy-start(bf16[624,2048]{1,0:T(8,128)(2,1)} %copy-done.5) | copy-start | bytes 7667716
  42.8 3.7 %copy-start.20 = (bf16[2048,256]{1,0:T(8,128)(2,1)S(1)}, bf16[2048,256]{1,0:T(8,128)(2,1)}, u32[]{:S(2)}) copy-start(bf16[2048,256]{1,0:T(8,128)(2,1)} %param.22) | copy-start | bytes 3145732
  46.6 1.1 copy-start.13
  47.5 1.1 copy-start.8
  50.7 14.8 %collective-permute-start.2 = (bf16[624,512]{1,0:T(8,128)(2,1)S(1)}, bf16[624,512]{1,0:T(8,128)(2,1)S(1)}, u32[]{:S(2)}, u32[]{:S(2)}) collective-permute-start(bf16[624,512]{1,0:T(8,128)(2,1)S(1)} %bitcast.123), channel_id=1, source_target_pairs={{0,2},{2,0},{1,3},{3,1},{4,6},{6,4},{5,7},{7,5},{8,10},{10,8},{9,1... | collective-permute-start | bytes 1916936 | tf_op jit(solution)/shard_map/ppermute | solution.py:41
  67.6 1.5 copy-start.2
  69.1 3.3 %copy-start.7 = (bf16[624,512]{1,0:T(8,128)(2,1)S(1)}, bf16[624,512]{1,0:T(8,128)(2,1)}, u32[]{:S(2)}) copy-start(bf16[624,512]{1,0:T(8,128)(2,1)} %param.15) | copy-start | bytes 1916932
  69.2 3.2 %collective-permute-start.4 = (f32[624,512]{1,0:T(8,128)S(1)}, f32[624,512]{1,0:T(8,128)}, u32[]{:S(2)}, u32[]{:S(2)}) collective-permute-start(f32[624,512]{1,0:T(8,128)S(1)} %constant_dynamic-slice_fusion), channel_id=1, source_target_pairs={{0,1},{1,0},{2,3},{3,2},{4,5},{5,4},{6,7},{7,6},{8,9},{9,8},{10,11... | collective-permute-start | bytes 3833864 | tf_op jit(solution)/shard_map/ppermute | solution.py:41
  74.4 1.2 collective-permute-start.5
  75.6 3.6 %collective-permute-start.6 = (f32[624,1]{0,1:T(1,128)S(1)}, f32[624,1]{0,1:T(1,128)S(1)}, u32[]{:S(2)}, u32[]{:S(2)}) collective-permute-start(f32[624,1]{0,1:T(1,128)S(1)} %reshape_add_fusion), channel_id=1, source_target_pairs={{0,2},{2,0},{1,3},{3,1},{4,6},{6,4},{5,7},{7,5},{8,10},{10,8},{9,1... | collective-permute-start | bytes 7496 | tf_op jit(solution)/shard_map/ppermute | solution.py:41
  79.4 2.1 %collective-permute-start.8 = (bf16[624,512]{1,0:T(8,128)(2,1)S(1)}, bf16[624,512]{1,0:T(8,128)(2,1)S(1)}, u32[]{:S(2)}, u32[]{:S(2)}) collective-permute-start(bf16[624,512]{1,0:T(8,128)(2,1)S(1)} %multiply_convert_fusion.2), channel_id=1, source_target_pairs={{0,1},{1,0},{2,3},{3,2},{4,5},{5,4},{6,7},{7,6},{8,9},{9,8},{10,11... | collective-permute-start | bytes 1916936 | tf_op jit(solution)/shard_map/ppermute | solution.py:41
  79.8 17.0 %collective-permute-start.7 = (bf16[624,512]{1,0:T(8,128)(2,1)S(1)}, bf16[624,512]{1,0:T(8,128)(2,1)}, u32[]{:S(2)}, u32[]{:S(2)}) collective-permute-start(bf16[624,512]{1,0:T(8,128)(2,1)S(1)} %multiply_convert_fusion.2), channel_id=1, source_target_pairs={{0,2},{2,0},{1,3},{3,1},{4,6},{6,4},{5,7},{7,5},{8,10},{10,8},{9,1... | collective-permute-start | bytes 1916936 | tf_op jit(solution)/shard_map/ppermute | solution.py:41
  81.6 6.0 %copy-start.18 = (bf16[2048,1024]{1,0:T(8,128)(2,1)S(1)}, bf16[2048,1024]{1,0:T(8,128)(2,1)}, u32[]{:S(2)}) copy-start(bf16[2048,1024]{1,0:T(8,128)(2,1)} %param.25) | copy-start | bytes 12582916
  87.6 9.1 %copy-start.9 = (bf16[1,13,4,16,256]{4,3,2,1,0:T(8,128)(2,1)S(1)}, bf16[1,13,4,16,256]{4,3,2,1,0:T(8,128)(2,1)}, u32[]{:S(2)}) copy-start(bf16[1,13,4,16,256]{4,3,2,1,0:T(8,128)(2,1)} %get-tuple-element.25) | copy-start | bytes 1277956
  87.6 9.2 %copy-start.11 = (bf16[1,13,4,16,256]{4,3,2,1,0:T(8,128)(2,1)S(1)}, bf16[1,13,4,16,256]{4,3,2,1,0:T(8,128)(2,1)}, u32[]{:S(2)}) copy-start(bf16[1,13,4,16,256]{4,3,2,1,0:T(8,128)(2,1)} %get-tuple-element.26) | copy-start | bytes 1277956
  96.7 7.7 %collective-permute-start.9 = (bf16[624,512]{1,0:T(8,128)(2,1)}, bf16[624,512]{1,0:T(8,128)(2,1)}, u32[]{:S(2)}, u32[]{:S(2)}) collective-permute-start(bf16[624,512]{1,0:T(8,128)(2,1)} %collective-permute-done.7), channel_id=1, source_target_pairs={{0,1},{1,0},{2,3},{3,2},{4,5},{5,4},{6,7},{7,6},{8,9},{9,8},{10,11... | collective-permute-start | bytes 1916936 | tf_op jit(solution)/shard_map/ppermute | solution.py:41
  98.7 33.6 %all-to-all-start.1 = ((bf16[8,2,136,256]{3,2,1,0:T(8,128)(2,1)}), bf16[8,2,136,256]{3,2,1,0:T(8,128)(2,1)}, u32[]{:S(2)}, u32[]{:S(2)}) async-start(bf16[8,2,136,256]{3,2,1,0:T(8,128)(2,1)} %select_select_fusion), calls=%async_computation.1 | async-start | bytes 2228224 | tf_op jit(solution)/shard_map/all_to_all | solution.py:198
  128.9 7.4 %copy-start.3 = (f32[1,624,512]{2,1,0:T(8,128)S(1)}, f32[1,624,512]{2,1,0:T(8,128)}, u32[]{:S(2)}) copy-start(f32[1,624,512]{2,1,0:T(8,128)} %get-tuple-element.11) | copy-start | bytes 3833860
  128.9 7.4 %collective-permute-start.10 = (f32[2,624,512]{2,1,0:T(8,128)}, f32[2,624,512]{2,1,0:T(8,128)}, u32[]{:S(2)}, u32[]{:S(2)}) collective-permute-start(f32[2,624,512]{2,1,0:T(8,128)} %pad_maximum_fusion.1), channel_id=1, source_target_pairs={{0,1},{1,0},{2,3},{3,2},{4,5},{5,4},{6,7},{7,6},{8,9},{9,8},{10,11... | collective-permute-start | bytes 7667720 | tf_op jit(solution)/shard_map/ppermute | solution.py:41
  139.0 1.7 %copy-start.4 = (bf16[13,136,256]{2,1,0:T(8,128)(2,1)S(1)}, bf16[13,136,256]{2,1,0:T(8,128)(2,1)}, u32[]{:S(2)}) copy-start(bf16[13,136,256]{2,1,0:T(8,128)(2,1)} %gather_fusion.1) | copy-start | bytes 2715652
  139.1 15.8 %collective-permute-start.11 = (bf16[624,512]{1,0:T(8,128)(2,1)S(1)}, bf16[624,512]{1,0:T(8,128)(2,1)S(1)}, u32[]{:S(2)}, u32[]{:S(2)}) collective-permute-start(bf16[624,512]{1,0:T(8,128)(2,1)S(1)} %fusion.33), channel_id=1, source_target_pairs={{0,2},{2,0},{1,3},{3,1},{4,6},{6,4},{5,7},{7,5},{8,10},{10,8},{9,1... | collective-permute-start | bytes 1916936 | tf_op jit(solution)/shard_map/ppermute | solution.py:41
  140.9 15.2 %copy-start.1 = (bf16[512,2048]{1,0:T(8,128)(2,1)S(1)}, bf16[512,2048]{1,0:T(8,128)(2,1)}, u32[]{:S(2)}) copy-start(bf16[512,2048]{1,0:T(8,128)(2,1)} %param.23) | copy-start | bytes 6291460
  (5 other events, 4.3 us)

commit v16 on v14

--- a/solution.py
+++ b/solution.py
@@ -255,6 +255,7 @@
     normed_share = row_scale(residual_share, gain_share).astype(jnp.bfloat16)
     gate_proj, upward = gather_project(normed_share, (gate_weight, up_weight))
     hidden = (jax.nn.silu(gate_proj) * upward).astype(jnp.bfloat16)
+    hidden = lax.optimization_barrier(hidden)
     mlp_share = scatter_features(hidden, down_weight, jnp.bfloat16)
     live_rows = (jnp.arange(span_size, dtype=jnp.int32)[None, :] < span_length[:, None]).reshape(
         total_rows

time: 157 us -> 157 us (level)
  waiting for transfers between devices: 46.2 us -> 54.3 us
  matrix products: 37 us -> 29.9 us
    dot_general x1, matrix products: 12.6 us -> 2.85 us  [scatter_features(): product = jnp.dot(matrix_in, weight, preferred_element_type=jnp.float32)]
    all_to_all x1, waiting for transfers between devices: 2.99 us -> 11.2 us  [local(): lax.all_to_all(packed, 'req', split_axis=0, concat_axis=0, tiled=True)]
    another operation x1, other arithmetic: 4.77 us -> 2.09 us  [scatter_features(): jnp.stack([jnp.where(core == 0, block(k, 0), block(k, 1)) for k in range(...]
    dot_general x1 -> x2, matrix products: 5.38 us -> 7.35 us  [gather_project(): jnp.dot(remote_pair, lax.dynamic_slice_in_dim(weight, (1 - chip) * half,...]
    unnamed x46 -> x56, local copies, waits for them, and re-layouts: 6.45 us -> 6.37 us
  transfers between devices with their start and end apart: 14 -> 14, of which waited for: 9 -> 9; matrix products, arithmetic and copies ran while one was open for 46% -> 41% of each run, Pallas kernels for 0% -> 0%
where the time goes in v16:
time: 157 us; the launch traced here: 156 us
  waiting for transfers between devices  54.3 us (35%)
  matrix products  29.9 us (19%)
  other arithmetic  25.1 us (16%)
  local copies, waits for them, and re-layouts  23.1 us (15%)
  starting transfers between devices  22.2 us (14%)
    ppermute x12, waiting for transfers between devices, swap(): return lax.ppermute(values, axis_name, [(0, 1), (1, 0)])  38.3 us
    ppermute x12, starting transfers between devices, swap(): return lax.ppermute(values, axis_name, [(0, 1), (1, 0)])  12.2 us
    all_to_all x1, waiting for transfers between devices, local(): lax.all_to_all(packed, 'req', split_axis=0, concat_axis=0, tiled=True)  11.2 us
    dot_general x2, matrix products, gather_project(): jnp.dot(local_pair, lax.dynamic_slice_in_dim(weight, chip * half, half, 0...  9.57 us
    dot_general x2, matrix products, gather_project(): jnp.dot(remote_pair, lax.dynamic_slice_in_dim(weight, (1 - chip) * half,...  7.35 us
    unnamed x56, local copies, waits for them, and re-layouts  6.37 us
    all_to_all x1, starting transfers between devices, local(): lax.all_to_all(packed, 'req', split_axis=0, concat_axis=0, tiled=True)  5.71 us
    all_to_all x1, waiting for transfers between devices, local(): lax.all_to_all(stacked, ('kvy', 'core'), split_axis=1, concat_axis=1, til...  4.79 us
  transfers between devices with their start and end apart: 14, of which 9 were waited for; matrix products, arithmetic and copies ran while one was open for 41% of the time, Pallas kernels for 0%

profile of v16, /device:TPU:0, one launch (start us, length us, event | category | flops | bytes accessed | tf_op | source)
XLA Modules:
  0.0 155.8 jit_solution(12988933166340208278)
XLA Ops:
  0.6 3.0 %collective-permute-start = (bf16[624,512]{1,0:T(8,128)(2,1)}, bf16[624,512]{1,0:T(8,128)(2,1)}, u32[]{:S(2)}, u32[]{:S(2)}) collective-permute-start(bf16[624,512]{1,0:T(8,128)(2,1)} %param.15), channel_id=1, source_target_pairs={{0,2},{2,0},{1,3},{3,1},{4,6},{6,4},{5,7},{7,5},{8,10},{10,8},{9,1... | collective-permute-start | bytes 1916936 | tf_op jit(solution)/shard_map/ppermute | solution.py:41
  8.0 4.3 %all-to-all-start = ((bf16[2,4,13,16,256]{4,3,2,0,1:T(8,128)(2,1)}), bf16[2,4,13,16,256]{4,3,2,0,1:T(8,128)(2,1)}, u32[]{:S(2)}, u32[]{:S(2)}) async-start(bf16[2,4,13,16,256]{4,3,2,0,1:T(8,128)(2,1)} %copy.60), calls=%async_computation | async-start | bytes 1703936 | tf_op jit(solution)/shard_map/all_to_all | solution.py:170
  13.4 1.9 %collective-permute-start.3 = (bf16[512,1024]{1,0:T(8,128)(2,1)}, bf16[512,1024]{1,0:T(8,128)(2,1)}, u32[]{:S(2)}, u32[]{:S(2)}) collective-permute-start(bf16[512,1024]{1,0:T(8,128)(2,1)} %constant_dynamic-slice_fusion.1), channel_id=1, source_target_pairs={{0,2},{2,0},{1,3},{3,1},{4,6},{6,4},{5,7},{7,5},{8,10},{10,8},{9,1... | collective-permute-start | bytes 3145736 | tf_op jit(solution)/shard_map/ppermute | solution.py:41
  15.4 3.8 %collective-permute-done = bf16[624,512]{1,0:T(8,128)(2,1)} collective-permute-done((bf16[624,512]{1,0:T(8,128)(2,1)}, bf16[624,512]{1,0:T(8,128)(2,1)}, u32[]{:S(2)}, u32[]{:S(2)}) %collective-permute-start) | collective-permute-done | bytes 639008 | tf_op jit(solution)/shard_map/ppermute | solution.py:41
  19.2 2.0 %maximum_select_fusion = bf16[2,624,512]{2,1,0:T(8,128)(2,1)S(1)} fusion(bf16[1,624,512]{2,1,0:T(8,128)(2,1)} %bitcast.4, bf16[1,624,512]{2,1,0:T(8,128)(2,1)} %bitcast.105, pred[]{:T(512)S(6)} %eq.27), kind=kLoop, calls=%fused_computation.23 | loop fusion | flops 1916928 | bytes 2555905 | tf_op jit(solution)/shard_map/jit(_where)/select_n | solution.py:48
  21.5 2.0 %multiply_cosine_fusion = (f32[13,48,128]{2,1,0:T(8,128)}, f32[13,48,128]{2,1,0:T(8,128)}) fusion(f32[128]{0:T(128)S(1)} %multiply_exponential_fusion, f32[13,48]{1,0:T(8,128)S(1)} %iota_add_fusion), kind=kLoop, calls=%fused_computation.72 | loop fusion | flops 79872 | bytes 641984 | tf_op jit(solution)/shard_map/cos | solution.py:22
  23.5 4.8 %all-to-all-done = bf16[2,4,13,16,256]{4,3,2,0,1:T(8,128)(2,1)} async-done(((bf16[2,4,13,16,256]{4,3,2,0,1:T(8,128)(2,1)}), bf16[2,4,13,16,256]{4,3,2,0,1:T(8,128)(2,1)}, u32[]{:S(2)}, u32[]{:S(2)}) %all-to-all-start) | async-done | bytes 852000 | tf_op jit(solution)/shard_map/all_to_all | solution.py:170
  32.0 2.0 %fusion = f32[624]{0:T(1024)S(1)} fusion(bf16[624,512]{1,0:T(8,128)(2,1)S(1)} %get-tuple-element.17, bf16[624,512]{1,0:T(8,128)(2,1)S(1)} %get-tuple-element.18, bf16[624,512]{1,0:T(8,128)(2,1)S(1)} %get-tuple-element.16, bf16[624,512]{1,0:T(8,128)(2,1)S(1)} %get-tuple-element.15), kind=kLoop, calls=%fused_computation.4 | loop fusion | flops 12778896 | bytes 2558400 | tf_op jit(solution)/shard_map/reduce_sum | solution.py:212
  35.3 1.6 %convolution_convert_fusion.1 = bf16[624,256]{1,0:T(8,128)(2,1)} fusion(bf16[624,2048]{1,0:T(8,128)(2,1)S(1)} %fusion.2, bf16[2048,256]{1,0:T(8,128)(2,1)S(1)} %copy-done.23), kind=kOutput, calls=%fused_computation.41 | convolution fusion | flops 654471168 | bytes 3923968 | tf_op jit(solution)/shard_map/dot_general | solution.py:228
  37.9 2.6 %fusion.64 = f32[624,512]{1,0:T(8,128)} fusion(bf16[624,2048]{1,0:T(8,128)(2,1)S(1)} %fusion.2, bf16[2048,512]{1,0:T(8,128)(2,1)S(1)} %copy-done.22), kind=kOutput, calls=%fused_computation.144 | convolution fusion | flops 1308622848 | bytes 5931008 | tf_op jit(solution)/shard_map/dot_general | solution.py:219
  40.5 2.1 %reshape.334 = f32[13,48,2,256]{3,2,1,0:T(2,128)S(1)} reshape(f32[624,512]{1,0:T(8,128)} %fusion.64) | data formatting | bytes 2555904 | tf_op jit(solution)/shard_map/reshape | solution.py:221
  44.3 2.1 %fusion.63 = f32[624,256]{1,0:T(8,128)S(1)} fusion(bf16[624,2048]{1,0:T(8,128)(2,1)S(1)} %copy-done.8, bf16[2048,256]{1,0:T(8,128)(2,1)} %param.21), kind=kOutput, calls=%fused_computation.143 | convolution fusion | flops 654311424 | bytes 4243456 | tf_op jit(solution)/shard_map/dot_general | solution.py:223
  46.5 1.6 %fusion.37 = (bf16[13,48,1,128]{3,1,0,2:T(8,128)(2,1)S(1)}, bf16[13,48,1,128]{3,1,0,2:T(8,128)(2,1)S(1)}) fusion(f32[13,48,1,256]{3,1,0,2:T(8,128)S(1)} %bitcast.110, f32[128]{0:T(128)S(1)} %multiply_exponential_fusion, f32[13,48]{1,0:T(8,128)S(1)} %iota_add_fusion), kind=kLoop, calls=%fused_computation.80 | loop fusion | flops 718848 | bytes 961472 | tf_op jit(solution)/shard_map/convert.7
  50.6 2.1 %collective-permute-start.2 = (bf16[624,512]{1,0:T(8,128)(2,1)S(1)}, bf16[624,512]{1,0:T(8,128)(2,1)S(1)}, u32[]{:S(2)}, u32[]{:S(2)}) collective-permute-start(bf16[624,512]{1,0:T(8,128)(2,1)S(1)} %bitcast.102), channel_id=1, source_target_pairs={{0,2},{2,0},{1,3},{3,1},{4,6},{6,4},{5,7},{7,5},{8,10},{10,8},{9,1... | collective-permute-start | bytes 1916936 | tf_op jit(solution)/shard_map/ppermute | solution.py:41
  53.5 11.8 %collective-permute-done.2 = bf16[624,512]{1,0:T(8,128)(2,1)S(1)} collective-permute-done((bf16[624,512]{1,0:T(8,128)(2,1)S(1)}, bf16[624,512]{1,0:T(8,128)(2,1)S(1)}, u32[]{:S(2)}, u32[]{:S(2)}) %collective-permute-start.2) | collective-permute-done | bytes 639008 | tf_op jit(solution)/shard_map/ppermute | solution.py:41
  65.4 2.1 %convolution_add_fusion = f32[624,1024]{1,0:T(8,128)S(1)} fusion(f32[624,1024]{1,0:T(8,128)S(1)} %fusion.18, bf16[624,512]{1,0:T(8,128)(2,1)S(1)} %collective-permute-done.2, bf16[512,1024]{1,0:T(8,128)(2,1)} %collective-permute-done.3), kind=kOutput, calls=%fused_computation.21 | convolution fusion | flops 654950400 | bytes 6799360 | tf_op jit(solution)/shard_map/dot_general | solution.py:121
  69.6 2.6 %collective-permute-done.4 = f32[624,512]{1,0:T(8,128)} collective-permute-done((f32[624,512]{1,0:T(8,128)S(1)}, f32[624,512]{1,0:T(8,128)}, u32[]{:S(2)}, u32[]{:S(2)}) %collective-permute-start.4) | collective-permute-done | bytes 1277984 | tf_op jit(solution)/shard_map/ppermute | solution.py:41
  72.3 2.0 %multiply_reduce_fusion = (f32[624]{0:T(1024)S(1)}, f32[624,512]{1,0:T(8,128)S(1)}) fusion(f32[624,512]{1,0:T(8,128)} %collective-permute-done.4, f32[624,1024]{1,0:T(8,128)} %copy-done.2, s32[]{:T(128)S(6)} %select_n.199, bf16[624,512]{1,0:T(8,128)(2,1)S(1)} %copy-done.9), kind=kLoop, calls=%fused_computation.36 | loop fusion | flops 1596816 | bytes 4475332 | tf_op jit(solution)/shard_map/reduce_sum | solution.py:130
  82.3 5.2 %fusion.9 = f32[624,1024]{1,0:T(8,128)} fusion(bf16[2048,1024]{1,0:T(8,128)(2,1)} %param.25, s32[]{:T(128)S(6)} %select_n.197, bf16[624,512]{1,0:T(8,128)(2,1)S(1)} %collective-permute-done.8, bf16[624,512]{1,0:T(8,128)(2,1)S(1)} %multiply_convert_fusion.1, pred[]{:T(512)S(6)} %eq.26), kind=kOutput, calls=%fused_computation.17 | convolution fusion | flops 1314373632 | bytes 5931013 | tf_op jit(solution)/shard_map/dot_general | solution.py:69
  87.5 4.4 %fusion.7 = f32[624,1024]{1,0:T(8,128)} fusion(bf16[2048,1024]{1,0:T(8,128)(2,1)S(1)} %copy-done.19, s32[]{:T(128)S(6)} %select_n.197, bf16[624,512]{1,0:T(8,128)(2,1)} %copy-done.24, bf16[624,512]{1,0:T(8,128)(2,1)S(1)} %multiply_convert_fusion.1, pred[]{:T(512)S(6)} %eq.26), kind=kOutput, calls=%fused_computation.15 | convolution fusion | flops 1314373632 | bytes 5931013 | tf_op jit(solution)/shard_map/dot_general | solution.py:69
  91.8 4.7 %collective-permute-done.7 = bf16[624,512]{1,0:T(8,128)(2,1)} collective-permute-done((bf16[624,512]{1,0:T(8,128)(2,1)S(1)}, bf16[624,512]{1,0:T(8,128)(2,1)}, u32[]{:S(2)}, u32[]{:S(2)}) %collective-permute-start.7) | collective-permute-done | bytes 639008 | tf_op jit(solution)/shard_map/ppermute | solution.py:41
  98.5 5.7 %all-to-all-start.1 = ((bf16[8,2,136,256]{3,2,1,0:T(8,128)(2,1)}), bf16[8,2,136,256]{3,2,1,0:T(8,128)(2,1)}, u32[]{:S(2)}, u32[]{:S(2)}) async-start(bf16[8,2,136,256]{3,2,1,0:T(8,128)(2,1)} %select_select_fusion), calls=%async_computation.1 | async-start | bytes 2228224 | tf_op jit(solution)/shard_map/all_to_all | solution.py:194
  104.3 4.0 %fusion.3 = f32[624,1024]{1,0:T(8,128)S(1)} fusion(bf16[2048,1024]{1,0:T(8,128)(2,1)} %param.26, s32[]{:T(128)S(6)} %select_n.198, bf16[624,512]{1,0:T(8,128)(2,1)} %collective-permute-done.9, bf16[624,512]{1,0:T(8,128)(2,1)} %collective-permute-done.7, pred[]{:T(512)S(6)} %eq.26), kind=kOutput, calls=%fused_computation.11 | convolution fusion | flops 1314373632 | bytes 5931013 | tf_op jit(solution)/shard_map/dot_general | solution.py:85
  108.3 3.3 %fusion.5 = f32[624,1024]{1,0:T(8,128)S(1)} fusion(bf16[2048,1024]{1,0:T(8,128)(2,1)S(1)} %copy-done.20, s32[]{:T(128)S(6)} %select_n.198, bf16[624,512]{1,0:T(8,128)(2,1)} %collective-permute-done.9, bf16[624,512]{1,0:T(8,128)(2,1)} %collective-permute-done.7, pred[]{:T(512)S(6)} %eq.26), kind=kOutput, calls=%fused_computation.13 | convolution fusion | flops 1314373632 | bytes 5931013 | tf_op jit(solution)/shard_map/dot_general | solution.py:85
  113.9 2.9 %fusion.65 = f32[624,2048]{1,0:T(8,128)S(1)} fusion(bf16[624,1024]{1,0:T(8,128)(2,1)S(1)} %multiply_convert_fusion, bf16[1024,2048]{1,0:T(8,128)(2,1)S(1)} %copy-done.21), kind=kOutput, calls=%fused_computation.145 | convolution fusion | flops 2617245696 | bytes 10584064 | tf_op jit(solution)/shard_map/dot_general | solution.py:97
  116.7 2.1 %select_bitcast_fusion.3 = (f32[1,624,512]{2,1,0:T(8,128)}, f32[1,624,512]{2,1,0:T(8,128)}, f32[1,624,512]{2,1,0:T(8,128)S(1)}, f32[1,624,512]{2,1,0:T(8,128)S(1)}) fusion(f32[624,2048]{1,0:T(8,128)S(1)} %fusion.65, pred[]{:T(512)S(6)} %eq.26), kind=kLoop, calls=%fused_computation.34 | loop fusion | flops 1277952 | bytes 10223617 | tf_op jit(solution)/shard_map/stack | solution.py:104
  118.8 1.8 %pad_maximum_fusion.1 = f32[2,624,512]{2,1,0:T(8,128)} fusion(f32[1,624,512]{2,1,0:T(8,128)S(1)} %get-tuple-element.13, f32[1,624,512]{2,1,0:T(8,128)S(1)} %get-tuple-element.14), kind=kLoop, calls=%fused_computation.9 | loop fusion | flops 638976 | bytes 5111808 | tf_op jit(solution)/shard_map/stack | solution.py:105
  121.0 11.2 %all-to-all-done.1 = bf16[8,2,136,256]{3,2,1,0:T(8,128)(2,1)} async-done(((bf16[8,2,136,256]{3,2,1,0:T(8,128)(2,1)}), bf16[8,2,136,256]{3,2,1,0:T(8,128)(2,1)}, u32[]{:S(2)}, u32[]{:S(2)}) %all-to-all-start.1) | async-done | bytes 1114144 | tf_op jit(solution)/shard_map/all_to_all | solution.py:194
  133.3 2.8 %gather_fusion.1 = bf16[13,136,256]{2,1,0:T(8,128)(2,1)} fusion(bf16[16,136,256]{2,1,0:T(8,128)(2,1)} %bitcast.36, s32[1024]{0:T(1024)S(1)} %pad_clamp_fusion), kind=kCustom, calls=%fused_computation.1 | custom fusion | bytes 1810484 | tf_op jit(solution)/shard_map/jit(_take)/gather | solution.py:202
  136.1 2.7 %maximum_add_fusion = f32[2,624,512]{2,1,0:T(8,128)S(1)} fusion(f32[2,624,512]{2,1,0:T(8,128)} %collective-permute-done.10, f32[1,624,512]{2,1,0:T(8,128)} %get-tuple-element.12, f32[1,624,512]{2,1,0:T(8,128)S(1)} %copy-done.3), kind=kLoop, calls=%fused_computation.8 | loop fusion | flops 1277952 | bytes 7667712 | tf_op jit(solution)/shard_map/add | solution.py:106
  138.9 1.6 %collective-permute-start.11 = (bf16[624,512]{1,0:T(8,128)(2,1)S(1)}, bf16[624,512]{1,0:T(8,128)(2,1)S(1)}, u32[]{:S(2)}, u32[]{:S(2)}) collective-permute-start(bf16[624,512]{1,0:T(8,128)(2,1)S(1)} %fusion.27), channel_id=1, source_target_pairs={{0,2},{2,0},{1,3},{3,1},{4,6},{6,4},{5,7},{7,5},{8,10},{10,8},{9,1... | collective-permute-start | bytes 1916936 | tf_op jit(solution)/shard_map/ppermute | solution.py:41
  141.7 13.0 %collective-permute-done.11 = bf16[624,512]{1,0:T(8,128)(2,1)S(1)} collective-permute-done((bf16[624,512]{1,0:T(8,128)(2,1)S(1)}, bf16[624,512]{1,0:T(8,128)(2,1)S(1)}, u32[]{:S(2)}, u32[]{:S(2)}) %collective-permute-start.11) | collective-permute-done | bytes 639008 | tf_op jit(solution)/shard_map/ppermute | solution.py:41
  (132 shorter events, 34.8 us)
Async XLA Ops:
  0.6 11.7 %copy-start = (bf16[512,2048]{1,0:T(8,128)(2,1)S(1)}, bf16[512,2048]{1,0:T(8,128)(2,1)}, u32[]{:S(2)}) copy-start(bf16[512,2048]{1,0:T(8,128)(2,1)} %param.23) | copy-start | bytes 6291460
  0.6 18.6 %collective-permute-start = (bf16[624,512]{1,0:T(8,128)(2,1)}, bf16[624,512]{1,0:T(8,128)(2,1)}, u32[]{:S(2)}, u32[]{:S(2)}) collective-permute-start(bf16[624,512]{1,0:T(8,128)(2,1)} %param.15), channel_id=1, source_target_pairs={{0,2},{2,0},{1,3},{3,1},{4,6},{6,4},{5,7},{7,5},{8,10},{10,8},{9,1... | collective-permute-start | bytes 1916936 | tf_op jit(solution)/shard_map/ppermute | solution.py:41
  8.0 7.4 %copy-start.25 = (s32[13]{0:T(128)S(1)}, s32[13]{0:T(128)}, u32[]{:S(2)}) copy-start(s32[13]{0:T(128)} %param.17) | copy-start | bytes 160
  8.0 20.4 %all-to-all-start = ((bf16[2,4,13,16,256]{4,3,2,0,1:T(8,128)(2,1)}), bf16[2,4,13,16,256]{4,3,2,0,1:T(8,128)(2,1)}, u32[]{:S(2)}, u32[]{:S(2)}) async-start(bf16[2,4,13,16,256]{4,3,2,0,1:T(8,128)(2,1)} %copy.60), calls=%async_computation | async-start | bytes 1703936 | tf_op jit(solution)/shard_map/all_to_all | solution.py:170
  12.3 9.0 %copy-start.17 = (s32[13]{0:T(128)S(1)}, s32[13]{0:T(128)}, u32[]{:S(2)}) copy-start(s32[13]{0:T(128)} %param.16) | copy-start | bytes 160
  13.4 40.1 %collective-permute-start.3 = (bf16[512,1024]{1,0:T(8,128)(2,1)}, bf16[512,1024]{1,0:T(8,128)(2,1)}, u32[]{:S(2)}, u32[]{:S(2)}) collective-permute-start(bf16[512,1024]{1,0:T(8,128)(2,1)} %constant_dynamic-slice_fusion.1), channel_id=1, source_target_pairs={{0,2},{2,0},{1,3},{3,1},{4,6},{6,4},{5,7},{7,5},{8,10},{10,8},{9,1... | collective-permute-start | bytes 3145736 | tf_op jit(solution)/shard_map/ppermute | solution.py:41
  21.2 9.4 %collective-permute-start.1 = (bf16[2,624,512]{2,1,0:T(8,128)(2,1)S(1)}, bf16[2,624,512]{2,1,0:T(8,128)(2,1)}, u32[]{:S(2)}, u32[]{:S(2)}) collective-permute-start(bf16[2,624,512]{2,1,0:T(8,128)(2,1)S(1)} %maximum_select_fusion), channel_id=1, source_target_pairs={{0,1},{1,0},{2,3},{3,2},{4,5},{5,4},{6,7},{7,6},{8,9},{9,8},{10,11... | collective-permute-start | bytes 3833864 | tf_op jit(solution)/shard_map/ppermute | solution.py:41
  32.0 2.1 %copy-start.16 = (f32[2048]{0:T(1024)S(1)}, f32[2048]{0:T(1024)}, u32[]{:S(2)}) copy-start(f32[2048]{0:T(1024)} %param.19) | copy-start | bytes 24580
  35.3 2.6 %copy-start.22 = (bf16[2048,512]{1,0:T(8,128)(2,1)S(1)}, bf16[2048,512]{1,0:T(8,128)(2,1)}, u32[]{:S(2)}) copy-start(bf16[2048,512]{1,0:T(8,128)(2,1)} %param.20) | copy-start | bytes 6291460
  44.3 3.7 %copy-start.14 = (f32[13,48,128]{2,1,0:T(8,128)S(1)}, f32[13,48,128]{2,1,0:T(8,128)}, u32[]{:S(2)}) copy-start(f32[13,48,128]{2,1,0:T(8,128)} %get-tuple-element.29) | copy-start | bytes 958468
  44.3 3.7 %copy-start.15 = (f32[13,48,128]{2,1,0:T(8,128)S(1)}, f32[13,48,128]{2,1,0:T(8,128)}, u32[]{:S(2)}) copy-start(f32[13,48,128]{2,1,0:T(8,128)} %get-tuple-element.30) | copy-start | bytes 958468
  46.5 1.8 %copy-start.10 = (bf16[1,13,4,16,256]{4,3,2,1,0:T(8,128)(2,1)S(1)}, bf16[1,13,4,16,256]{4,3,2,1,0:T(8,128)(2,1)}, u32[]{:S(2)}) copy-start(bf16[1,13,4,16,256]{4,3,2,1,0:T(8,128)(2,1)} %get-tuple-element.25) | copy-start | bytes 1277956
  50.6 14.8 %collective-permute-start.2 = (bf16[624,512]{1,0:T(8,128)(2,1)S(1)}, bf16[624,512]{1,0:T(8,128)(2,1)S(1)}, u32[]{:S(2)}, u32[]{:S(2)}) collective-permute-start(bf16[624,512]{1,0:T(8,128)(2,1)S(1)} %bitcast.102), channel_id=1, source_target_pairs={{0,2},{2,0},{1,3},{3,1},{4,6},{6,4},{5,7},{7,5},{8,10},{10,8},{9,1... | collective-permute-start | bytes 1916936 | tf_op jit(solution)/shard_map/ppermute | solution.py:41
  69.0 3.3 %copy-start.9 = (bf16[624,512]{1,0:T(8,128)(2,1)S(1)}, bf16[624,512]{1,0:T(8,128)(2,1)}, u32[]{:S(2)}) copy-start(bf16[624,512]{1,0:T(8,128)(2,1)} %param.15) | copy-start | bytes 1916932
  69.1 3.2 %collective-permute-start.4 = (f32[624,512]{1,0:T(8,128)S(1)}, f32[624,512]{1,0:T(8,128)}, u32[]{:S(2)}, u32[]{:S(2)}) collective-permute-start(f32[624,512]{1,0:T(8,128)S(1)} %constant_dynamic-slice_fusion), channel_id=1, source_target_pairs={{0,1},{1,0},{2,3},{3,2},{4,5},{5,4},{6,7},{7,6},{8,9},{9,8},{10,11... | collective-permute-start | bytes 3833864 | tf_op jit(solution)/shard_map/ppermute | solution.py:41
  74.3 1.2 collective-permute-start.5
  75.5 3.6 %collective-permute-start.6 = (f32[624,1]{0,1:T(1,128)S(1)}, f32[624,1]{0,1:T(1,128)S(1)}, u32[]{:S(2)}, u32[]{:S(2)}) collective-permute-start(f32[624,1]{0,1:T(1,128)S(1)} %reshape_add_fusion), channel_id=1, source_target_pairs={{0,2},{2,0},{1,3},{3,1},{4,6},{6,4},{5,7},{7,5},{8,10},{10,8},{9,1... | collective-permute-start | bytes 7496 | tf_op jit(solution)/shard_map/ppermute | solution.py:41
  79.3 2.1 %collective-permute-start.8 = (bf16[624,512]{1,0:T(8,128)(2,1)S(1)}, bf16[624,512]{1,0:T(8,128)(2,1)S(1)}, u32[]{:S(2)}, u32[]{:S(2)}) collective-permute-start(bf16[624,512]{1,0:T(8,128)(2,1)S(1)} %multiply_convert_fusion.1), channel_id=1, source_target_pairs={{0,1},{1,0},{2,3},{3,2},{4,5},{5,4},{6,7},{7,6},{8,9},{9,8},{10,11... | collective-permute-start | bytes 1916936 | tf_op jit(solution)/shard_map/ppermute | solution.py:41
  79.6 17.0 %collective-permute-start.7 = (bf16[624,512]{1,0:T(8,128)(2,1)S(1)}, bf16[624,512]{1,0:T(8,128)(2,1)}, u32[]{:S(2)}, u32[]{:S(2)}) collective-permute-start(bf16[624,512]{1,0:T(8,128)(2,1)S(1)} %multiply_convert_fusion.1), channel_id=1, source_target_pairs={{0,2},{2,0},{1,3},{3,1},{4,6},{6,4},{5,7},{7,5},{8,10},{10,8},{9,1... | collective-permute-start | bytes 1916936 | tf_op jit(solution)/shard_map/ppermute | solution.py:41
  81.4 6.1 %copy-start.19 = (bf16[2048,1024]{1,0:T(8,128)(2,1)S(1)}, bf16[2048,1024]{1,0:T(8,128)(2,1)}, u32[]{:S(2)}) copy-start(bf16[2048,1024]{1,0:T(8,128)(2,1)} %param.26) | copy-start | bytes 12582916
  87.5 9.1 %copy-start.11 = (bf16[1,13,4,16,256]{4,3,2,1,0:T(8,128)(2,1)S(1)}, bf16[1,13,4,16,256]{4,3,2,1,0:T(8,128)(2,1)}, u32[]{:S(2)}) copy-start(bf16[1,13,4,16,256]{4,3,2,1,0:T(8,128)(2,1)} %get-tuple-element.25) | copy-start | bytes 1277956
  87.5 9.1 %copy-start.13 = (bf16[1,13,4,16,256]{4,3,2,1,0:T(8,128)(2,1)S(1)}, bf16[1,13,4,16,256]{4,3,2,1,0:T(8,128)(2,1)}, u32[]{:S(2)}) copy-start(bf16[1,13,4,16,256]{4,3,2,1,0:T(8,128)(2,1)} %get-tuple-element.26) | copy-start | bytes 1277956
  96.6 7.7 %collective-permute-start.9 = (bf16[624,512]{1,0:T(8,128)(2,1)}, bf16[624,512]{1,0:T(8,128)(2,1)}, u32[]{:S(2)}, u32[]{:S(2)}) collective-permute-start(bf16[624,512]{1,0:T(8,128)(2,1)} %collective-permute-done.7), channel_id=1, source_target_pairs={{0,1},{1,0},{2,3},{3,2},{4,5},{5,4},{6,7},{7,6},{8,9},{9,8},{10,11... | collective-permute-start | bytes 1916936 | tf_op jit(solution)/shard_map/ppermute | solution.py:41
  98.5 33.6 %all-to-all-start.1 = ((bf16[8,2,136,256]{3,2,1,0:T(8,128)(2,1)}), bf16[8,2,136,256]{3,2,1,0:T(8,128)(2,1)}, u32[]{:S(2)}, u32[]{:S(2)}) async-start(bf16[8,2,136,256]{3,2,1,0:T(8,128)(2,1)} %select_select_fusion), calls=%async_computation.1 | async-start | bytes 2228224 | tf_op jit(solution)/shard_map/all_to_all | solution.py:194
  104.3 4.0 %copy-start.20 = (bf16[2048,1024]{1,0:T(8,128)(2,1)S(1)}, bf16[2048,1024]{1,0:T(8,128)(2,1)}, u32[]{:S(2)}) copy-start(bf16[2048,1024]{1,0:T(8,128)(2,1)} %param.25) | copy-start | bytes 12582916
  108.3 3.4 %copy-start.5 = (f32[624,1024]{1,0:T(8,128)S(1)}, f32[624,1024]{1,0:T(8,128)}, u32[]{:S(2)}) copy-start(f32[624,1024]{1,0:T(8,128)} %fusion.9) | copy-start | bytes 7667716
  108.3 3.4 %copy-start.6 = (f32[624,1024]{1,0:T(8,128)S(1)}, f32[624,1024]{1,0:T(8,128)}, u32[]{:S(2)}) copy-start(f32[624,1024]{1,0:T(8,128)} %fusion.7) | copy-start | bytes 7667716
  111.7 2.2 %copy-start.21 = (bf16[1024,2048]{1,0:T(8,128)(2,1)S(1)}, bf16[1024,2048]{1,0:T(8,128)(2,1)}, u32[]{:S(2)}) copy-start(bf16[1024,2048]{1,0:T(8,128)(2,1)} %param.27) | copy-start | bytes 12582916
  120.6 15.5 %copy-start.3 = (f32[1,624,512]{2,1,0:T(8,128)S(1)}, f32[1,624,512]{2,1,0:T(8,128)}, u32[]{:S(2)}) copy-start(f32[1,624,512]{2,1,0:T(8,128)} %get-tuple-element.11) | copy-start | bytes 3833860
  120.6 15.5 %collective-permute-start.10 = (f32[2,624,512]{2,1,0:T(8,128)}, f32[2,624,512]{2,1,0:T(8,128)}, u32[]{:S(2)}, u32[]{:S(2)}) collective-permute-start(f32[2,624,512]{2,1,0:T(8,128)} %pad_maximum_fusion.1), channel_id=1, source_target_pairs={{0,1},{1,0},{2,3},{3,2},{4,5},{5,4},{6,7},{7,6},{8,9},{9,8},{10,11... | collective-permute-start | bytes 7667720 | tf_op jit(solution)/shard_map/ppermute | solution.py:41
  138.9 15.8 %collective-permute-start.11 = (bf16[624,512]{1,0:T(8,128)(2,1)S(1)}, bf16[624,512]{1,0:T(8,128)(2,1)S(1)}, u32[]{:S(2)}, u32[]{:S(2)}) collective-permute-start(bf16[624,512]{1,0:T(8,128)(2,1)S(1)} %fusion.27), channel_id=1, source_target_pairs={{0,2},{2,0},{1,3},{3,1},{4,6},{6,4},{5,7},{7,5},{8,10},{10,8},{9,1... | collective-permute-start | bytes 1916936 | tf_op jit(solution)/shard_map/ppermute | solution.py:41
  140.6 15.2 %copy-start.1 = (bf16[512,2048]{1,0:T(8,128)(2,1)S(1)}, bf16[512,2048]{1,0:T(8,128)(2,1)}, u32[]{:S(2)}) copy-start(bf16[512,2048]{1,0:T(8,128)(2,1)} %param.23) | copy-start | bytes 6291460
  (9 other events, 11.3 us)

commit v17 on v16

--- a/solution.py
+++ b/solution.py
@@ -192,16 +192,6 @@
     packed = jnp.where(filled[:, None, None], packed, -jnp.ones((), packed.dtype))
     packed = packed.reshape((req_count, capacity) + payload.shape[1:])
     landed = lax.all_to_all(packed, "req", split_axis=0, concat_axis=0, tiled=True)
-    landed = landed.reshape((req_count * capacity,) + payload.shape[1:])
-    code = landed[:, 2 * past_size, :2].astype(jnp.int32)
-    landed_slots = code[:, 0] * 16 + code[:, 1]
-    wanted = req_index * request_list + order_ids
-    slot_hits = landed_slots[None, :] == wanted[:, None]
-    entry_ids = jnp.arange(req_count * capacity, dtype=jnp.int32)
-    slot_position = jnp.sum(jnp.where(slot_hits, entry_ids[None, :], 0), axis=1)
-    decode_rows = jnp.take(landed, slot_position, axis=0)
-    decode_kv = (decode_rows[:, :past_size], decode_rows[:, past_size:2 * past_size])
-
     x_whole = gather_features(activations)
     chip_cols = output_weight.shape[1] // chips
     far_cols = lax.dynamic_slice_in_dim(
@@ -257,6 +247,17 @@
     hidden = (jax.nn.silu(gate_proj) * upward).astype(jnp.bfloat16)
     hidden = lax.optimization_barrier(hidden)
     mlp_share = scatter_features(hidden, down_weight, jnp.bfloat16)
+    landed, mlp_share = lax.optimization_barrier((landed, mlp_share))
+    landed = landed.reshape((req_count * capacity,) + payload.shape[1:])
+    code = landed[:, 2 * past_size, :2].astype(jnp.int32)
+    landed_slots = code[:, 0] * 16 + code[:, 1]
+    wanted = req_index * request_list + order_ids
+    slot_hits = landed_slots[None, :] == wanted[:, None]
+    entry_ids = jnp.arange(req_count * capacity, dtype=jnp.int32)
+    slot_position = jnp.sum(jnp.where(slot_hits, entry_ids[None, :], 0), axis=1)
+    decode_rows = jnp.take(landed, slot_position, axis=0)
+    decode_kv = (decode_rows[:, :past_size], decode_rows[:, past_size:2 * past_size])
+
     live_rows = (jnp.arange(span_size, dtype=jnp.int32)[None, :] < span_length[:, None]).reshape(
         total_rows
     )

time: 157 us -> 156 us (level)
  matrix products: 29.9 us -> 21.9 us
  waiting for transfers between devices: 54.3 us -> 59.5 us
  other arithmetic: 25.1 us -> 27.5 us
    ppermute x12, waiting for transfers between devices: 38.3 us -> 48.8 us  [swap(): return lax.ppermute(values, axis_name, [(0, 1), (1, 0)])]
    all_to_all x1, waiting for transfers between devices: 11.2 us -> 5.8 us  [local(): lax.all_to_all(packed, 'req', split_axis=0, concat_axis=0, tiled=True)]
    dot_general x2, matrix products: 9.57 us -> 4.66 us  [gather_project(): jnp.dot(local_pair, lax.dynamic_slice_in_dim(weight, chip * half, half, 0...]
    dot_general x2, matrix products: 7.35 us -> 3.07 us  [gather_project(): jnp.dot(remote_pair, lax.dynamic_slice_in_dim(weight, (1 - chip) * half,...]
    dot_general x1, matrix products: 2.09 us -> 3.78 us  [project_heads(): jnp.dot(mixed_far, weight_far, preferred_element_type=jnp.float32)]
    unnamed x56 -> x46, local copies, waits for them, and re-layouts: 6.37 us -> 5.28 us
  transfers between devices with their start and end apart: 14 -> 14, of which waited for: 9 -> 11; matrix products, arithmetic and copies ran while one was open for 41% -> 28% of each run, Pallas kernels for 0% -> 0%
where the time goes in v17:
time: 156 us; the launch traced here: 155 us
  waiting for transfers between devices  59.5 us (38%)
  other arithmetic  27.5 us (18%)
  local copies, waits for them, and re-layouts  22.4 us (14%)
  starting transfers between devices  22.1 us (14%)
  matrix products  21.9 us (14%)
    ppermute x12, waiting for transfers between devices, swap(): return lax.ppermute(values, axis_name, [(0, 1), (1, 0)])  48.8 us
    ppermute x12, starting transfers between devices, swap(): return lax.ppermute(values, axis_name, [(0, 1), (1, 0)])  12.1 us
    all_to_all x1, waiting for transfers between devices, local(): lax.all_to_all(packed, 'req', split_axis=0, concat_axis=0, tiled=True)  5.8 us
    all_to_all x1, starting transfers between devices, local(): lax.all_to_all(packed, 'req', split_axis=0, concat_axis=0, tiled=True)  5.72 us
    unnamed x46, local copies, waits for them, and re-layouts  5.28 us
    all_to_all x1, waiting for transfers between devices, local(): lax.all_to_all(stacked, ('kvy', 'core'), split_axis=1, concat_axis=1, til...  4.87 us
    dot_general x2, matrix products, gather_project(): jnp.dot(local_pair, lax.dynamic_slice_in_dim(weight, chip * half, half, 0...  4.66 us
    all_to_all x1, starting transfers between devices, local(): lax.all_to_all(stacked, ('kvy', 'core'), split_axis=1, concat_axis=1, til...  4.34 us
  transfers between devices with their start and end apart: 14, of which 11 were waited for; matrix products, arithmetic and copies ran while one was open for 28% of the time, Pallas kernels for 0%

profile of v17, /device:TPU:0, one launch (start us, length us, event | category | flops | bytes accessed | tf_op | source)
XLA Modules:
  0.0 154.7 jit_solution(1988099521444607593)
XLA Ops:
  0.6 3.0 %collective-permute-start = (bf16[624,512]{1,0:T(8,128)(2,1)}, bf16[624,512]{1,0:T(8,128)(2,1)}, u32[]{:S(2)}, u32[]{:S(2)}) collective-permute-start(bf16[624,512]{1,0:T(8,128)(2,1)} %param.15), channel_id=1, source_target_pairs={{0,2},{2,0},{1,3},{3,1},{4,6},{6,4},{5,7},{7,5},{8,10},{10,8},{9,1... | collective-permute-start | bytes 1916936 | tf_op jit(solution)/shard_map/ppermute | solution.py:41
  8.0 4.3 %all-to-all-start = ((bf16[2,4,13,16,256]{4,3,2,0,1:T(8,128)(2,1)}), bf16[2,4,13,16,256]{4,3,2,0,1:T(8,128)(2,1)}, u32[]{:S(2)}, u32[]{:S(2)}) async-start(bf16[2,4,13,16,256]{4,3,2,0,1:T(8,128)(2,1)} %copy.60), calls=%async_computation | async-start | bytes 1703936 | tf_op jit(solution)/shard_map/all_to_all | solution.py:170
  13.5 1.9 %collective-permute-start.3 = (bf16[512,1024]{1,0:T(8,128)(2,1)}, bf16[512,1024]{1,0:T(8,128)(2,1)}, u32[]{:S(2)}, u32[]{:S(2)}) collective-permute-start(bf16[512,1024]{1,0:T(8,128)(2,1)} %constant_dynamic-slice_fusion.1), channel_id=1, source_target_pairs={{0,2},{2,0},{1,3},{3,1},{4,6},{6,4},{5,7},{7,5},{8,10},{10,8},{9,1... | collective-permute-start | bytes 3145736 | tf_op jit(solution)/shard_map/ppermute | solution.py:41
  15.5 3.7 %collective-permute-done = bf16[624,512]{1,0:T(8,128)(2,1)} collective-permute-done((bf16[624,512]{1,0:T(8,128)(2,1)}, bf16[624,512]{1,0:T(8,128)(2,1)}, u32[]{:S(2)}, u32[]{:S(2)}) %collective-permute-start) | collective-permute-done | bytes 639008 | tf_op jit(solution)/shard_map/ppermute | solution.py:41
  19.2 1.9 %maximum_select_fusion = bf16[2,624,512]{2,1,0:T(8,128)(2,1)S(1)} fusion(bf16[1,624,512]{2,1,0:T(8,128)(2,1)} %bitcast.4, bf16[1,624,512]{2,1,0:T(8,128)(2,1)} %bitcast.99, pred[]{:T(512)S(6)} %eq.27), kind=kLoop, calls=%fused_computation.23 | loop fusion | flops 1916928 | bytes 2555905 | tf_op jit(solution)/shard_map/jit(_where)/select_n | solution.py:48
  21.4 2.0 %multiply_cosine_fusion = (f32[13,48,128]{2,1,0:T(8,128)}, f32[13,48,128]{2,1,0:T(8,128)}) fusion(f32[128]{0:T(128)S(1)} %multiply_exponential_fusion, f32[13,48]{1,0:T(8,128)S(1)} %iota_add_fusion), kind=kLoop, calls=%fused_computation.70 | loop fusion | flops 79872 | bytes 641984 | tf_op jit(solution)/shard_map/cos | solution.py:22
  23.5 4.9 %all-to-all-done = bf16[2,4,13,16,256]{4,3,2,0,1:T(8,128)(2,1)} async-done(((bf16[2,4,13,16,256]{4,3,2,0,1:T(8,128)(2,1)}), bf16[2,4,13,16,256]{4,3,2,0,1:T(8,128)(2,1)}, u32[]{:S(2)}, u32[]{:S(2)}) %all-to-all-start) | async-done | bytes 852000 | tf_op jit(solution)/shard_map/all_to_all | solution.py:170
  32.0 2.0 %fusion = f32[624]{0:T(1024)S(1)} fusion(bf16[624,512]{1,0:T(8,128)(2,1)S(1)} %get-tuple-element.21, bf16[624,512]{1,0:T(8,128)(2,1)S(1)} %get-tuple-element.22, bf16[624,512]{1,0:T(8,128)(2,1)S(1)} %get-tuple-element.20, bf16[624,512]{1,0:T(8,128)(2,1)S(1)} %get-tuple-element.19), kind=kLoop, calls=%fused_computation.4 | loop fusion | flops 12778896 | bytes 2558400 | tf_op jit(solution)/shard_map/reduce_sum | solution.py:202
  36.5 2.5 %fusion.61 = f32[624,512]{1,0:T(8,128)} fusion(bf16[624,2048]{1,0:T(8,128)(2,1)S(1)} %fusion.2, bf16[2048,512]{1,0:T(8,128)(2,1)S(1)} %copy-done.19), kind=kOutput, calls=%fused_computation.142 | convolution fusion | flops 1308622848 | bytes 5931008 | tf_op jit(solution)/shard_map/dot_general | solution.py:209
  39.0 2.1 %reshape.334 = f32[13,48,2,256]{3,2,1,0:T(2,128)S(1)} reshape(f32[624,512]{1,0:T(8,128)} %fusion.61) | data formatting | bytes 2555904 | tf_op jit(solution)/shard_map/reshape | solution.py:211
  42.8 2.2 %fusion.60 = f32[624,256]{1,0:T(8,128)S(1)} fusion(bf16[624,2048]{1,0:T(8,128)(2,1)S(1)} %copy-done.6, bf16[2048,256]{1,0:T(8,128)(2,1)} %param.21), kind=kOutput, calls=%fused_computation.141 | convolution fusion | flops 654311424 | bytes 4243456 | tf_op jit(solution)/shard_map/dot_general | solution.py:213
  45.0 1.6 %fusion.34 = (bf16[13,48,1,128]{3,1,0,2:T(8,128)(2,1)S(1)}, bf16[13,48,1,128]{3,1,0,2:T(8,128)(2,1)S(1)}) fusion(f32[13,48,1,256]{3,1,0,2:T(8,128)S(1)} %bitcast.104, f32[128]{0:T(128)S(1)} %multiply_exponential_fusion, f32[13,48]{1,0:T(8,128)S(1)} %iota_add_fusion), kind=kLoop, calls=%fused_computation.78 | loop fusion | flops 718848 | bytes 961472 | tf_op jit(solution)/shard_map/convert.7
  50.7 2.1 %collective-permute-start.2 = (bf16[624,512]{1,0:T(8,128)(2,1)S(1)}, bf16[624,512]{1,0:T(8,128)(2,1)}, u32[]{:S(2)}, u32[]{:S(2)}) collective-permute-start(bf16[624,512]{1,0:T(8,128)(2,1)S(1)} %bitcast.96), channel_id=1, source_target_pairs={{0,2},{2,0},{1,3},{3,1},{4,6},{6,4},{5,7},{7,5},{8,10},{10,8},{9,1... | collective-permute-start | bytes 1916936 | tf_op jit(solution)/shard_map/ppermute | solution.py:41
  53.7 11.9 %collective-permute-done.2 = bf16[624,512]{1,0:T(8,128)(2,1)} collective-permute-done((bf16[624,512]{1,0:T(8,128)(2,1)S(1)}, bf16[624,512]{1,0:T(8,128)(2,1)}, u32[]{:S(2)}, u32[]{:S(2)}) %collective-permute-start.2) | collective-permute-done | bytes 639008 | tf_op jit(solution)/shard_map/ppermute | solution.py:41
  65.6 3.8 %convolution_add_fusion = f32[624,1024]{1,0:T(8,128)} fusion(f32[624,1024]{1,0:T(8,128)S(1)} %fusion.15, bf16[624,512]{1,0:T(8,128)(2,1)} %collective-permute-done.2, bf16[512,1024]{1,0:T(8,128)(2,1)} %collective-permute-done.3), kind=kOutput, calls=%fused_computation.21 | convolution fusion | flops 654950400 | bytes 6799360 | tf_op jit(solution)/shard_map/dot_general | solution.py:121
  71.0 3.1 %collective-permute-done.4 = f32[624,512]{1,0:T(8,128)} collective-permute-done((f32[624,512]{1,0:T(8,128)S(1)}, f32[624,512]{1,0:T(8,128)}, u32[]{:S(2)}, u32[]{:S(2)}) %collective-permute-start.4) | collective-permute-done | bytes 1277984 | tf_op jit(solution)/shard_map/ppermute | solution.py:41
  74.1 2.0 %multiply_reduce_fusion = (f32[624]{0:T(1024)S(1)}, f32[624,512]{1,0:T(8,128)S(1)}) fusion(f32[624,512]{1,0:T(8,128)} %collective-permute-done.4, f32[624,1024]{1,0:T(8,128)} %convolution_add_fusion, s32[]{:T(128)S(6)} %select_n.199, bf16[624,512]{1,0:T(8,128)(2,1)S(1)} %copy-done.7), kind=kLoop, calls=%fused_computation.34 | loop fusion | flops 1596816 | bytes 4475332 | tf_op jit(solution)/shard_map/reduce_sum | solution.py:130
  83.2 3.1 %fusion.7 = f32[624,1024]{1,0:T(8,128)S(1)} fusion(bf16[2048,1024]{1,0:T(8,128)(2,1)} %param.26, s32[]{:T(128)S(6)} %select_n.197, bf16[624,512]{1,0:T(8,128)(2,1)S(1)} %collective-permute-done.8, bf16[624,512]{1,0:T(8,128)(2,1)S(1)} %multiply_convert_fusion.1, pred[]{:T(512)S(6)} %eq.26), kind=kOutput, calls=%fused_computation.15 | convolution fusion | flops 1314373632 | bytes 5931013 | tf_op jit(solution)/shard_map/dot_general | solution.py:69
  86.4 1.5 fusion.9
  87.9 10.0 %collective-permute-done.7 = bf16[624,512]{1,0:T(8,128)(2,1)S(1)} collective-permute-done((bf16[624,512]{1,0:T(8,128)(2,1)S(1)}, bf16[624,512]{1,0:T(8,128)(2,1)S(1)}, u32[]{:S(2)}, u32[]{:S(2)}) %collective-permute-start.7) | collective-permute-done | bytes 639008 | tf_op jit(solution)/shard_map/ppermute | solution.py:41
  98.0 2.1 %collective-permute-done.9 = bf16[624,512]{1,0:T(8,128)(2,1)S(1)} collective-permute-done((bf16[624,512]{1,0:T(8,128)(2,1)S(1)}, bf16[624,512]{1,0:T(8,128)(2,1)S(1)}, u32[]{:S(2)}, u32[]{:S(2)}) %collective-permute-start.9) | collective-permute-done | bytes 639008 | tf_op jit(solution)/shard_map/ppermute | solution.py:41
  100.0 1.5 fusion.5
  101.6 1.5 fusion.3
  105.3 3.1 %fusion.62 = f32[624,2048]{1,0:T(8,128)S(1)} fusion(bf16[624,1024]{1,0:T(8,128)(2,1)S(1)} %multiply_convert_fusion, bf16[1024,2048]{1,0:T(8,128)(2,1)S(1)} %copy-done.18), kind=kOutput, calls=%fused_computation.143 | convolution fusion | flops 2617245696 | bytes 10584064 | tf_op jit(solution)/shard_map/dot_general | solution.py:97
  108.4 2.1 %select_bitcast_fusion.3 = (f32[1,624,512]{2,1,0:T(8,128)}, f32[1,624,512]{2,1,0:T(8,128)}, f32[1,624,512]{2,1,0:T(8,128)S(1)}, f32[1,624,512]{2,1,0:T(8,128)S(1)}) fusion(f32[624,2048]{1,0:T(8,128)S(1)} %fusion.62, pred[]{:T(512)S(6)} %eq.26), kind=kLoop, calls=%fused_computation.32 | loop fusion | flops 1277952 | bytes 10223617 | tf_op jit(solution)/shard_map/stack | solution.py:104
  110.5 1.7 %pad_maximum_fusion.1 = f32[2,624,512]{2,1,0:T(8,128)} fusion(f32[1,624,512]{2,1,0:T(8,128)S(1)} %get-tuple-element.17, f32[1,624,512]{2,1,0:T(8,128)S(1)} %get-tuple-element.18), kind=kLoop, calls=%fused_computation.9 | loop fusion | flops 638976 | bytes 5111808 | tf_op jit(solution)/shard_map/stack | solution.py:105
  115.2 5.7 %all-to-all-start.1 = ((bf16[8,2,136,256]{3,2,1,0:T(8,128)(2,1)}), bf16[8,2,136,256]{3,2,1,0:T(8,128)(2,1)}, u32[]{:S(2)}, u32[]{:S(2)}) async-start(bf16[8,2,136,256]{3,2,1,0:T(8,128)(2,1)} %select_select_fusion), calls=%async_computation.1 | async-start | bytes 2228224 | tf_op jit(solution)/shard_map/all_to_all | solution.py:194
  120.9 3.1 %maximum_add_fusion = f32[2,624,512]{2,1,0:T(8,128)S(1)} fusion(f32[2,624,512]{2,1,0:T(8,128)} %collective-permute-done.10, f32[1,624,512]{2,1,0:T(8,128)} %get-tuple-element.16, f32[1,624,512]{2,1,0:T(8,128)} %get-tuple-element.15), kind=kLoop, calls=%fused_computation.8 | loop fusion | flops 1277952 | bytes 7667712 | tf_op jit(solution)/shard_map/add | solution.py:106
  124.9 1.5 collective-permute-start.11
  126.6 14.9 %collective-permute-done.11 = bf16[624,512]{1,0:T(8,128)(2,1)S(1)} collective-permute-done((bf16[624,512]{1,0:T(8,128)(2,1)}, bf16[624,512]{1,0:T(8,128)(2,1)S(1)}, u32[]{:S(2)}, u32[]{:S(2)}) %collective-permute-start.11) | collective-permute-done | bytes 639008 | tf_op jit(solution)/shard_map/ppermute | solution.py:41
  142.9 5.8 %all-to-all-done.1 = bf16[8,2,136,256]{3,2,1,0:T(8,128)(2,1)} async-done(((bf16[8,2,136,256]{3,2,1,0:T(8,128)(2,1)}), bf16[8,2,136,256]{3,2,1,0:T(8,128)(2,1)}, u32[]{:S(2)}, u32[]{:S(2)}) %all-to-all-start.1) | async-done | bytes 1114144 | tf_op jit(solution)/shard_map/all_to_all | solution.py:194
  149.8 1.9 %gather_fusion.1 = bf16[13,136,256]{2,1,0:T(8,128)(2,1)S(1)} fusion(bf16[16,136,256]{2,1,0:T(8,128)(2,1)} %bitcast.36, s32[1024]{0:T(1024)S(1)} %pad_clamp_fusion), kind=kCustom, calls=%fused_computation.1 | custom fusion | bytes 1810484 | tf_op jit(solution)/shard_map/jit(_take)/gather | solution.py:258
  (123 shorter events, 38.7 us)
Async XLA Ops:
  0.6 11.7 %copy-start = (bf16[512,2048]{1,0:T(8,128)(2,1)S(1)}, bf16[512,2048]{1,0:T(8,128)(2,1)}, u32[]{:S(2)}) copy-start(bf16[512,2048]{1,0:T(8,128)(2,1)} %param.23) | copy-start | bytes 6291460
  0.6 18.6 %collective-permute-start = (bf16[624,512]{1,0:T(8,128)(2,1)}, bf16[624,512]{1,0:T(8,128)(2,1)}, u32[]{:S(2)}, u32[]{:S(2)}) collective-permute-start(bf16[624,512]{1,0:T(8,128)(2,1)} %param.15), channel_id=1, source_target_pairs={{0,2},{2,0},{1,3},{3,1},{4,6},{6,4},{5,7},{7,5},{8,10},{10,8},{9,1... | collective-permute-start | bytes 1916936 | tf_op jit(solution)/shard_map/ppermute | solution.py:41
  8.0 7.4 %copy-start.21 = (s32[13]{0:T(128)S(1)}, s32[13]{0:T(128)}, u32[]{:S(2)}) copy-start(s32[13]{0:T(128)} %param.17) | copy-start | bytes 160
  8.0 20.4 %all-to-all-start = ((bf16[2,4,13,16,256]{4,3,2,0,1:T(8,128)(2,1)}), bf16[2,4,13,16,256]{4,3,2,0,1:T(8,128)(2,1)}, u32[]{:S(2)}, u32[]{:S(2)}) async-start(bf16[2,4,13,16,256]{4,3,2,0,1:T(8,128)(2,1)} %copy.60), calls=%async_computation | async-start | bytes 1703936 | tf_op jit(solution)/shard_map/all_to_all | solution.py:170
  12.3 8.9 %copy-start.14 = (s32[13]{0:T(128)S(1)}, s32[13]{0:T(128)}, u32[]{:S(2)}) copy-start(s32[13]{0:T(128)} %param.16) | copy-start | bytes 160
  13.5 40.2 %collective-permute-start.3 = (bf16[512,1024]{1,0:T(8,128)(2,1)}, bf16[512,1024]{1,0:T(8,128)(2,1)}, u32[]{:S(2)}, u32[]{:S(2)}) collective-permute-start(bf16[512,1024]{1,0:T(8,128)(2,1)} %constant_dynamic-slice_fusion.1), channel_id=1, source_target_pairs={{0,2},{2,0},{1,3},{3,1},{4,6},{6,4},{5,7},{7,5},{8,10},{10,8},{9,1... | collective-permute-start | bytes 3145736 | tf_op jit(solution)/shard_map/ppermute | solution.py:41
  21.1 9.4 %collective-permute-start.1 = (bf16[2,624,512]{2,1,0:T(8,128)(2,1)S(1)}, bf16[2,624,512]{2,1,0:T(8,128)(2,1)}, u32[]{:S(2)}, u32[]{:S(2)}) collective-permute-start(bf16[2,624,512]{2,1,0:T(8,128)(2,1)S(1)} %maximum_select_fusion), channel_id=1, source_target_pairs={{0,1},{1,0},{2,3},{3,2},{4,5},{5,4},{6,7},{7,6},{8,9},{9,8},{10,11... | collective-permute-start | bytes 3833864 | tf_op jit(solution)/shard_map/ppermute | solution.py:41
  32.0 2.1 %copy-start.13 = (f32[2048]{0:T(1024)S(1)}, f32[2048]{0:T(1024)}, u32[]{:S(2)}) copy-start(f32[2048]{0:T(1024)} %param.19) | copy-start | bytes 24580
  34.1 2.4 %copy-start.19 = (bf16[2048,512]{1,0:T(8,128)(2,1)S(1)}, bf16[2048,512]{1,0:T(8,128)(2,1)}, u32[]{:S(2)}) copy-start(bf16[2048,512]{1,0:T(8,128)(2,1)} %param.20) | copy-start | bytes 6291460
  35.0 1.5 copy-start.5
  41.1 1.7 %copy-start.6 = (bf16[624,2048]{1,0:T(8,128)(2,1)S(1)}, bf16[624,2048]{1,0:T(8,128)(2,1)}, u32[]{:S(2)}) copy-start(bf16[624,2048]{1,0:T(8,128)(2,1)} %copy-done.5) | copy-start | bytes 7667716
  42.8 3.7 %copy-start.20 = (bf16[2048,256]{1,0:T(8,128)(2,1)S(1)}, bf16[2048,256]{1,0:T(8,128)(2,1)}, u32[]{:S(2)}) copy-start(bf16[2048,256]{1,0:T(8,128)(2,1)} %param.22) | copy-start | bytes 3145732
  50.7 14.9 %collective-permute-start.2 = (bf16[624,512]{1,0:T(8,128)(2,1)S(1)}, bf16[624,512]{1,0:T(8,128)(2,1)}, u32[]{:S(2)}, u32[]{:S(2)}) collective-permute-start(bf16[624,512]{1,0:T(8,128)(2,1)S(1)} %bitcast.96), channel_id=1, source_target_pairs={{0,2},{2,0},{1,3},{3,1},{4,6},{6,4},{5,7},{7,5},{8,10},{10,8},{9,1... | collective-permute-start | bytes 1916936 | tf_op jit(solution)/shard_map/ppermute | solution.py:41
  69.4 4.7 %copy-start.7 = (bf16[624,512]{1,0:T(8,128)(2,1)S(1)}, bf16[624,512]{1,0:T(8,128)(2,1)}, u32[]{:S(2)}) copy-start(bf16[624,512]{1,0:T(8,128)(2,1)} %param.15) | copy-start | bytes 1916932
  70.9 3.2 %collective-permute-start.4 = (f32[624,512]{1,0:T(8,128)S(1)}, f32[624,512]{1,0:T(8,128)}, u32[]{:S(2)}, u32[]{:S(2)}) collective-permute-start(f32[624,512]{1,0:T(8,128)S(1)} %constant_dynamic-slice_fusion), channel_id=1, source_target_pairs={{0,1},{1,0},{2,3},{3,2},{4,5},{5,4},{6,7},{7,6},{8,9},{9,8},{10,11... | collective-permute-start | bytes 3833864 | tf_op jit(solution)/shard_map/ppermute | solution.py:41
  76.0 10.3 %copy-start.2 = (f32[624,512]{1,0:T(8,128)}, f32[624,512]{1,0:T(8,128)S(1)}, u32[]{:S(2)}) copy-start(f32[624,512]{1,0:T(8,128)S(1)} %get-tuple-element.14) | copy-start | bytes 3833860
  76.0 1.2 collective-permute-start.5
  77.3 3.6 %collective-permute-start.6 = (f32[624,1]{0,1:T(1,128)S(1)}, f32[624,1]{0,1:T(1,128)S(1)}, u32[]{:S(2)}, u32[]{:S(2)}) collective-permute-start(f32[624,1]{0,1:T(1,128)S(1)} %reshape_add_fusion), channel_id=1, source_target_pairs={{0,2},{2,0},{1,3},{3,1},{4,6},{6,4},{5,7},{7,5},{8,10},{10,8},{9,1... | collective-permute-start | bytes 7496 | tf_op jit(solution)/shard_map/ppermute | solution.py:41
  81.1 5.3 %copy-start.16 = (bf16[2048,1024]{1,0:T(8,128)(2,1)S(1)}, bf16[2048,1024]{1,0:T(8,128)(2,1)}, u32[]{:S(2)}) copy-start(bf16[2048,1024]{1,0:T(8,128)(2,1)} %param.25) | copy-start | bytes 12582916
  81.1 2.1 %collective-permute-start.8 = (bf16[624,512]{1,0:T(8,128)(2,1)S(1)}, bf16[624,512]{1,0:T(8,128)(2,1)S(1)}, u32[]{:S(2)}, u32[]{:S(2)}) collective-permute-start(bf16[624,512]{1,0:T(8,128)(2,1)S(1)} %multiply_convert_fusion.1), channel_id=1, source_target_pairs={{0,1},{1,0},{2,3},{3,2},{4,5},{5,4},{6,7},{7,6},{8,9},{9,8},{10,11... | collective-permute-start | bytes 1916936 | tf_op jit(solution)/shard_map/ppermute | solution.py:41
  81.2 16.8 %collective-permute-start.7 = (bf16[624,512]{1,0:T(8,128)(2,1)S(1)}, bf16[624,512]{1,0:T(8,128)(2,1)S(1)}, u32[]{:S(2)}, u32[]{:S(2)}) collective-permute-start(bf16[624,512]{1,0:T(8,128)(2,1)S(1)} %multiply_convert_fusion.1), channel_id=1, source_target_pairs={{0,2},{2,0},{1,3},{3,1},{4,6},{6,4},{5,7},{7,5},{8,10},{10,8},{9,1... | collective-permute-start | bytes 1916936 | tf_op jit(solution)/shard_map/ppermute | solution.py:41
  87.9 13.7 %copy-start.17 = (bf16[2048,1024]{1,0:T(8,128)(2,1)S(1)}, bf16[2048,1024]{1,0:T(8,128)(2,1)}, u32[]{:S(2)}) copy-start(bf16[2048,1024]{1,0:T(8,128)(2,1)} %param.26) | copy-start | bytes 12582916
  98.0 2.1 %collective-permute-start.9 = (bf16[624,512]{1,0:T(8,128)(2,1)S(1)}, bf16[624,512]{1,0:T(8,128)(2,1)S(1)}, u32[]{:S(2)}, u32[]{:S(2)}) collective-permute-start(bf16[624,512]{1,0:T(8,128)(2,1)S(1)} %collective-permute-done.7), channel_id=1, source_target_pairs={{0,1},{1,0},{2,3},{3,2},{4,5},{5,4},{6,7},{7,6},{8,9},{9,8},{10,11... | collective-permute-start | bytes 1916936 | tf_op jit(solution)/shard_map/ppermute | solution.py:41
  103.1 2.2 %copy-start.18 = (bf16[1024,2048]{1,0:T(8,128)(2,1)S(1)}, bf16[1024,2048]{1,0:T(8,128)(2,1)}, u32[]{:S(2)}) copy-start(bf16[1024,2048]{1,0:T(8,128)(2,1)} %param.27) | copy-start | bytes 12582916
  110.5 1.9 %copy-start.15 = (s32[13]{0:T(128)S(1)}, s32[13]{0:T(128)}, u32[]{:S(2)}) copy-start(s32[13]{0:T(128)} %param.18) | copy-start | bytes 160
  110.5 2.7 %copy-start.10 = (bf16[1,13,4,16,256]{4,3,2,1,0:T(8,128)(2,1)S(1)}, bf16[1,13,4,16,256]{4,3,2,1,0:T(8,128)(2,1)}, u32[]{:S(2)}) copy-start(bf16[1,13,4,16,256]{4,3,2,1,0:T(8,128)(2,1)} %get-tuple-element.30) | copy-start | bytes 1277956
  112.3 8.6 %collective-permute-start.10 = (f32[2,624,512]{2,1,0:T(8,128)}, f32[2,624,512]{2,1,0:T(8,128)}, u32[]{:S(2)}, u32[]{:S(2)}) collective-permute-start(f32[2,624,512]{2,1,0:T(8,128)} %pad_maximum_fusion.1), channel_id=1, source_target_pairs={{0,1},{1,0},{2,3},{3,2},{4,5},{5,4},{6,7},{7,6},{8,9},{9,8},{10,11... | collective-permute-start | bytes 7667720 | tf_op jit(solution)/shard_map/ppermute | solution.py:41
  115.2 33.5 %all-to-all-start.1 = ((bf16[8,2,136,256]{3,2,1,0:T(8,128)(2,1)}), bf16[8,2,136,256]{3,2,1,0:T(8,128)(2,1)}, u32[]{:S(2)}, u32[]{:S(2)}) async-start(bf16[8,2,136,256]{3,2,1,0:T(8,128)(2,1)} %select_select_fusion), calls=%async_computation.1 | async-start | bytes 2228224 | tf_op jit(solution)/shard_map/all_to_all | solution.py:194
  124.9 16.6 %collective-permute-start.11 = (bf16[624,512]{1,0:T(8,128)(2,1)}, bf16[624,512]{1,0:T(8,128)(2,1)S(1)}, u32[]{:S(2)}, u32[]{:S(2)}) collective-permute-start(bf16[624,512]{1,0:T(8,128)(2,1)} %fusion.24), channel_id=1, source_target_pairs={{0,2},{2,0},{1,3},{3,1},{4,6},{6,4},{5,7},{7,5},{8,10},{10,8},{9,1... | collective-permute-start | bytes 1916936 | tf_op jit(solution)/shard_map/ppermute | solution.py:41
  151.6 1.5 copy-start.3
  151.6 2.0 %copy-start.4 = (f32[624,512]{1,0:T(8,128)S(1)}, f32[624,512]{1,0:T(8,128)}, u32[]{:S(2)}) copy-start(f32[624,512]{1,0:T(8,128)} %bitcast_add_fusion) | copy-start | bytes 3833860
  151.7 3.0 %copy-start.1 = (bf16[512,2048]{1,0:T(8,128)(2,1)S(1)}, bf16[512,2048]{1,0:T(8,128)(2,1)}, u32[]{:S(2)}) copy-start(bf16[512,2048]{1,0:T(8,128)(2,1)} %param.23) | copy-start | bytes 6291460
  (4 other events, 4.1 us)

commit v18 on v17

--- a/solution.py
+++ b/solution.py
@@ -164,12 +164,16 @@
     query_groups = local_q // local_kv
 
     past_share = earlier_rotated_keys.shape[1]
-    stacked = jnp.stack([earlier_rotated_keys, earlier_values])
-    stacked = stacked.reshape(2, request_list, past_share, kv_count, local_kv * HEAD_WIDTH)
-    stacked = stacked.transpose(0, 3, 1, 2, 4)
-    arrived = lax.all_to_all(stacked, ("kvy", "core"), split_axis=1, concat_axis=1, tiled=True)
-    head_kv = arrived.transpose(0, 2, 1, 3, 4).reshape(
-        2, request_list, kv_count * past_share, local_kv * HEAD_WIDTH
+    lanes_share = local_kv * HEAD_WIDTH
+    stacked = jnp.stack(
+        [
+            jnp.stack([past[..., j * lanes_share:(j + 1) * lanes_share] for past in (earlier_rotated_keys, earlier_values)])
+            for j in range(kv_count)
+        ]
+    )
+    arrived = lax.all_to_all(stacked, ("kvy", "core"), split_axis=0, concat_axis=0, tiled=True)
+    head_kv = arrived.transpose(1, 2, 0, 3, 4).reshape(
+        2, request_list, kv_count * past_share, lanes_share
     )
     past_size = head_kv.shape[2]
 

time: 156 us -> 156 us (level)
    unnamed x46 -> x48, local copies, waits for them, and re-layouts: 5.28 us -> 6.1 us
  transfers between devices with their start and end apart: 14 -> 14, of which waited for: 11 -> 11; matrix products, arithmetic and copies ran while one was open for 28% -> 27% of each run, Pallas kernels for 0% -> 0%
where the time goes in v18:
time: 156 us; the launch traced here: 155 us
  waiting for transfers between devices  59.7 us (38%)
  other arithmetic  28 us (18%)
  starting transfers between devices  22.1 us (14%)
  matrix products  21.9 us (14%)
  local copies, waits for them, and re-layouts  21.7 us (14%)
    ppermute x12, waiting for transfers between devices, swap(): return lax.ppermute(values, axis_name, [(0, 1), (1, 0)])  49.7 us
    ppermute x12, starting transfers between devices, swap(): return lax.ppermute(values, axis_name, [(0, 1), (1, 0)])  12.1 us
    unnamed x48, local copies, waits for them, and re-layouts  6.1 us
    all_to_all x1, waiting for transfers between devices, local(): lax.all_to_all(packed, 'req', split_axis=0, concat_axis=0, tiled=True)  5.82 us
    all_to_all x1, starting transfers between devices, local(): lax.all_to_all(packed, 'req', split_axis=0, concat_axis=0, tiled=True)  5.72 us
    dot_general x2, matrix products, gather_project(): jnp.dot(local_pair, lax.dynamic_slice_in_dim(weight, chip * half, half, 0...  4.66 us
    all_to_all x1, starting transfers between devices, local(): lax.all_to_all(stacked, ('kvy', 'core'), split_axis=0, concat_axis=0, til...  4.33 us
    all_to_all x1, waiting for transfers between devices, local(): lax.all_to_all(stacked, ('kvy', 'core'), split_axis=0, concat_axis=0, til...  4.16 us
  transfers between devices with their start and end apart: 14, of which 11 were waited for; matrix products, arithmetic and copies ran while one was open for 27% of the time, Pallas kernels for 0%

profile of v18, /device:TPU:0, one launch (start us, length us, event | category | flops | bytes accessed | tf_op | source)
XLA Modules:
  0.0 154.6 jit_solution(2468998121512332210)
XLA Ops:
  0.6 3.0 %collective-permute-start = (bf16[624,512]{1,0:T(8,128)(2,1)}, bf16[624,512]{1,0:T(8,128)(2,1)S(1)}, u32[]{:S(2)}, u32[]{:S(2)}) collective-permute-start(bf16[624,512]{1,0:T(8,128)(2,1)} %param.15), channel_id=1, source_target_pairs={{0,2},{2,0},{1,3},{3,1},{4,6},{6,4},{5,7},{7,5},{8,10},{10,8},{9,1... | collective-permute-start | bytes 1916936 | tf_op jit(solution)/shard_map/ppermute | solution.py:41
  7.0 4.3 %all-to-all-start = ((bf16[4,2,13,16,256]{4,3,2,1,0:T(8,128)(2,1)}), bf16[4,2,13,16,256]{4,3,2,1,0:T(8,128)(2,1)}, u32[]{:S(2)}, u32[]{:S(2)}) async-start(bf16[4,2,13,16,256]{4,3,2,1,0:T(8,128)(2,1)} %pad_maximum_fusion.2), calls=%async_computation | async-start | bytes 1703936 | tf_op jit(solution)/shard_map/all_to_all | solution.py:174
  12.4 1.9 %collective-permute-start.3 = (bf16[512,1024]{1,0:T(8,128)(2,1)}, bf16[512,1024]{1,0:T(8,128)(2,1)}, u32[]{:S(2)}, u32[]{:S(2)}) collective-permute-start(bf16[512,1024]{1,0:T(8,128)(2,1)} %constant_dynamic-slice_fusion.1), channel_id=1, source_target_pairs={{0,2},{2,0},{1,3},{3,1},{4,6},{6,4},{5,7},{7,5},{8,10},{10,8},{9,1... | collective-permute-start | bytes 3145736 | tf_op jit(solution)/shard_map/ppermute | solution.py:41
  14.4 4.7 %collective-permute-done = bf16[624,512]{1,0:T(8,128)(2,1)S(1)} collective-permute-done((bf16[624,512]{1,0:T(8,128)(2,1)}, bf16[624,512]{1,0:T(8,128)(2,1)S(1)}, u32[]{:S(2)}, u32[]{:S(2)}) %collective-permute-start) | collective-permute-done | bytes 639008 | tf_op jit(solution)/shard_map/ppermute | solution.py:41
  19.9 1.9 %maximum_select_fusion = bf16[2,624,512]{2,1,0:T(8,128)(2,1)S(1)} fusion(bf16[1,624,512]{2,1,0:T(8,128)(2,1)} %bitcast.126, bf16[1,624,512]{2,1,0:T(8,128)(2,1)} %bitcast.121, pred[]{:T(512)S(6)} %eq.27), kind=kLoop, calls=%fused_computation.23 | loop fusion | flops 1916928 | bytes 2555905 | tf_op jit(solution)/shard_map/jit(_where)/select_n | solution.py:48
  22.2 2.0 %multiply_cosine_fusion = (f32[13,48,128]{2,1,0:T(8,128)}, f32[13,48,128]{2,1,0:T(8,128)}) fusion(f32[128]{0:T(128)S(1)} %multiply_exponential_fusion, f32[13,48]{1,0:T(8,128)S(1)} %iota_add_fusion), kind=kLoop, calls=%fused_computation.70 | loop fusion | flops 79872 | bytes 641984 | tf_op jit(solution)/shard_map/cos | solution.py:22
  24.2 4.2 %all-to-all-done = bf16[4,2,13,16,256]{4,3,2,1,0:T(8,128)(2,1)} async-done(((bf16[4,2,13,16,256]{4,3,2,1,0:T(8,128)(2,1)}), bf16[4,2,13,16,256]{4,3,2,1,0:T(8,128)(2,1)}, u32[]{:S(2)}, u32[]{:S(2)}) %all-to-all-start) | async-done | bytes 852000 | tf_op jit(solution)/shard_map/all_to_all | solution.py:174
  32.0 2.0 %fusion = f32[624]{0:T(1024)S(1)} fusion(bf16[624,512]{1,0:T(8,128)(2,1)S(1)} %get-tuple-element.21, bf16[624,512]{1,0:T(8,128)(2,1)S(1)} %get-tuple-element.22, bf16[624,512]{1,0:T(8,128)(2,1)S(1)} %get-tuple-element.20, bf16[624,512]{1,0:T(8,128)(2,1)S(1)} %get-tuple-element.19), kind=kLoop, calls=%fused_computation.4 | loop fusion | flops 12778896 | bytes 2558400 | tf_op jit(solution)/shard_map/reduce_sum | solution.py:206
  36.5 2.5 %fusion.61 = f32[624,512]{1,0:T(8,128)} fusion(bf16[624,2048]{1,0:T(8,128)(2,1)S(1)} %fusion.2, bf16[2048,512]{1,0:T(8,128)(2,1)S(1)} %copy-done.20), kind=kOutput, calls=%fused_computation.154 | convolution fusion | flops 1308622848 | bytes 5931008 | tf_op jit(solution)/shard_map/dot_general | solution.py:213
  39.0 2.1 %reshape.329 = f32[13,48,2,256]{3,2,1,0:T(2,128)S(1)} reshape(f32[624,512]{1,0:T(8,128)} %fusion.61) | data formatting | bytes 2555904 | tf_op jit(solution)/shard_map/reshape | solution.py:215
  42.8 2.2 %fusion.60 = f32[624,256]{1,0:T(8,128)S(1)} fusion(bf16[624,2048]{1,0:T(8,128)(2,1)S(1)} %copy-done.6, bf16[2048,256]{1,0:T(8,128)(2,1)} %param.21), kind=kOutput, calls=%fused_computation.153 | convolution fusion | flops 654311424 | bytes 4243456 | tf_op jit(solution)/shard_map/dot_general | solution.py:217
  45.0 1.6 %fusion.34 = (bf16[13,48,1,128]{3,1,0,2:T(8,128)(2,1)S(1)}, bf16[13,48,1,128]{3,1,0,2:T(8,128)(2,1)S(1)}) fusion(f32[13,48,1,256]{3,1,0,2:T(8,128)S(1)} %bitcast.127, f32[128]{0:T(128)S(1)} %multiply_exponential_fusion, f32[13,48]{1,0:T(8,128)S(1)} %iota_add_fusion), kind=kLoop, calls=%fused_computation.78 | loop fusion | flops 718848 | bytes 961472 | tf_op jit(solution)/shard_map/convert.7
  50.7 2.1 %collective-permute-start.2 = (bf16[624,512]{1,0:T(8,128)(2,1)S(1)}, bf16[624,512]{1,0:T(8,128)(2,1)}, u32[]{:S(2)}, u32[]{:S(2)}) collective-permute-start(bf16[624,512]{1,0:T(8,128)(2,1)S(1)} %bitcast.118), channel_id=1, source_target_pairs={{0,2},{2,0},{1,3},{3,1},{4,6},{6,4},{5,7},{7,5},{8,10},{10,8},{9,1... | collective-permute-start | bytes 1916936 | tf_op jit(solution)/shard_map/ppermute | solution.py:41
  53.7 11.9 %collective-permute-done.2 = bf16[624,512]{1,0:T(8,128)(2,1)} collective-permute-done((bf16[624,512]{1,0:T(8,128)(2,1)S(1)}, bf16[624,512]{1,0:T(8,128)(2,1)}, u32[]{:S(2)}, u32[]{:S(2)}) %collective-permute-start.2) | collective-permute-done | bytes 639008 | tf_op jit(solution)/shard_map/ppermute | solution.py:41
  65.6 3.8 %convolution_add_fusion = f32[624,1024]{1,0:T(8,128)} fusion(f32[624,1024]{1,0:T(8,128)S(1)} %fusion.15, bf16[624,512]{1,0:T(8,128)(2,1)} %collective-permute-done.2, bf16[512,1024]{1,0:T(8,128)(2,1)} %collective-permute-done.3), kind=kOutput, calls=%fused_computation.21 | convolution fusion | flops 654950400 | bytes 6799360 | tf_op jit(solution)/shard_map/dot_general | solution.py:121
  70.9 3.1 %collective-permute-done.4 = f32[624,512]{1,0:T(8,128)} collective-permute-done((f32[624,512]{1,0:T(8,128)S(1)}, f32[624,512]{1,0:T(8,128)}, u32[]{:S(2)}, u32[]{:S(2)}) %collective-permute-start.4) | collective-permute-done | bytes 1277984 | tf_op jit(solution)/shard_map/ppermute | solution.py:41
  74.0 2.0 %multiply_reduce_fusion = (f32[624]{0:T(1024)S(1)}, f32[624,512]{1,0:T(8,128)S(1)}) fusion(f32[624,512]{1,0:T(8,128)} %collective-permute-done.4, f32[624,1024]{1,0:T(8,128)} %convolution_add_fusion, s32[]{:T(128)S(6)} %select_n.199, bf16[624,512]{1,0:T(8,128)(2,1)S(1)} %copy-done.7), kind=kLoop, calls=%fused_computation.34 | loop fusion | flops 1596816 | bytes 4475332 | tf_op jit(solution)/shard_map/reduce_sum | solution.py:130
  83.2 3.1 %fusion.7 = f32[624,1024]{1,0:T(8,128)S(1)} fusion(bf16[2048,1024]{1,0:T(8,128)(2,1)} %param.26, s32[]{:T(128)S(6)} %select_n.197, bf16[624,512]{1,0:T(8,128)(2,1)S(1)} %collective-permute-done.8, bf16[624,512]{1,0:T(8,128)(2,1)S(1)} %multiply_convert_fusion.1, pred[]{:T(512)S(6)} %eq.26), kind=kOutput, calls=%fused_computation.15 | convolution fusion | flops 1314373632 | bytes 5931013 | tf_op jit(solution)/shard_map/dot_general | solution.py:69
  86.4 1.5 fusion.9
  87.9 10.0 %collective-permute-done.7 = bf16[624,512]{1,0:T(8,128)(2,1)S(1)} collective-permute-done((bf16[624,512]{1,0:T(8,128)(2,1)S(1)}, bf16[624,512]{1,0:T(8,128)(2,1)S(1)}, u32[]{:S(2)}, u32[]{:S(2)}) %collective-permute-start.7) | collective-permute-done | bytes 639008 | tf_op jit(solution)/shard_map/ppermute | solution.py:41
  98.0 2.1 %collective-permute-done.9 = bf16[624,512]{1,0:T(8,128)(2,1)S(1)} collective-permute-done((bf16[624,512]{1,0:T(8,128)(2,1)S(1)}, bf16[624,512]{1,0:T(8,128)(2,1)S(1)}, u32[]{:S(2)}, u32[]{:S(2)}) %collective-permute-start.9) | collective-permute-done | bytes 639008 | tf_op jit(solution)/shard_map/ppermute | solution.py:41
  100.0 1.5 fusion.5
  101.6 1.5 fusion.3
  105.3 3.1 %fusion.62 = f32[624,2048]{1,0:T(8,128)S(1)} fusion(bf16[624,1024]{1,0:T(8,128)(2,1)S(1)} %multiply_convert_fusion, bf16[1024,2048]{1,0:T(8,128)(2,1)S(1)} %copy-done.19), kind=kOutput, calls=%fused_computation.155 | convolution fusion | flops 2617245696 | bytes 10584064 | tf_op jit(solution)/shard_map/dot_general | solution.py:97
  108.4 2.1 %select_bitcast_fusion.3 = (f32[1,624,512]{2,1,0:T(8,128)}, f32[1,624,512]{2,1,0:T(8,128)}, f32[1,624,512]{2,1,0:T(8,128)S(1)}, f32[1,624,512]{2,1,0:T(8,128)S(1)}) fusion(f32[624,2048]{1,0:T(8,128)S(1)} %fusion.62, pred[]{:T(512)S(6)} %eq.26), kind=kLoop, calls=%fused_computation.32 | loop fusion | flops 1277952 | bytes 10223617 | tf_op jit(solution)/shard_map/stack | solution.py:104
  110.5 1.7 %pad_maximum_fusion.1 = f32[2,624,512]{2,1,0:T(8,128)} fusion(f32[1,624,512]{2,1,0:T(8,128)S(1)} %get-tuple-element.17, f32[1,624,512]{2,1,0:T(8,128)S(1)} %get-tuple-element.18), kind=kLoop, calls=%fused_computation.9 | loop fusion | flops 638976 | bytes 5111808 | tf_op jit(solution)/shard_map/stack | solution.py:105
  115.1 5.7 %all-to-all-start.1 = ((bf16[8,2,136,256]{3,2,1,0:T(8,128)(2,1)}), bf16[8,2,136,256]{3,2,1,0:T(8,128)(2,1)}, u32[]{:S(2)}, u32[]{:S(2)}) async-start(bf16[8,2,136,256]{3,2,1,0:T(8,128)(2,1)} %select_select_fusion), calls=%async_computation.1 | async-start | bytes 2228224 | tf_op jit(solution)/shard_map/all_to_all | solution.py:198
  120.9 3.1 %maximum_add_fusion = f32[2,624,512]{2,1,0:T(8,128)S(1)} fusion(f32[2,624,512]{2,1,0:T(8,128)} %collective-permute-done.10, f32[1,624,512]{2,1,0:T(8,128)} %get-tuple-element.16, f32[1,624,512]{2,1,0:T(8,128)} %get-tuple-element.15), kind=kLoop, calls=%fused_computation.8 | loop fusion | flops 1277952 | bytes 7667712 | tf_op jit(solution)/shard_map/add | solution.py:106
  124.9 1.5 collective-permute-start.11
  126.6 14.9 %collective-permute-done.11 = bf16[624,512]{1,0:T(8,128)(2,1)S(1)} collective-permute-done((bf16[624,512]{1,0:T(8,128)(2,1)}, bf16[624,512]{1,0:T(8,128)(2,1)S(1)}, u32[]{:S(2)}, u32[]{:S(2)}) %collective-permute-start.11) | collective-permute-done | bytes 639008 | tf_op jit(solution)/shard_map/ppermute | solution.py:41
  142.8 5.8 %all-to-all-done.1 = bf16[8,2,136,256]{3,2,1,0:T(8,128)(2,1)} async-done(((bf16[8,2,136,256]{3,2,1,0:T(8,128)(2,1)}), bf16[8,2,136,256]{3,2,1,0:T(8,128)(2,1)}, u32[]{:S(2)}, u32[]{:S(2)}) %all-to-all-start.1) | async-done | bytes 1114144 | tf_op jit(solution)/shard_map/all_to_all | solution.py:198
  149.8 1.9 %gather_fusion.1 = bf16[13,136,256]{2,1,0:T(8,128)(2,1)S(1)} fusion(bf16[16,136,256]{2,1,0:T(8,128)(2,1)} %bitcast.47, s32[1024]{0:T(1024)S(1)} %pad_clamp_fusion), kind=kCustom, calls=%fused_computation.1 | custom fusion | bytes 1810484 | tf_op jit(solution)/shard_map/jit(_take)/gather | solution.py:262
  (126 shorter events, 38.5 us)
Async XLA Ops:
  0.6 10.7 %copy-start = (bf16[512,2048]{1,0:T(8,128)(2,1)S(1)}, bf16[512,2048]{1,0:T(8,128)(2,1)}, u32[]{:S(2)}) copy-start(bf16[512,2048]{1,0:T(8,128)(2,1)} %param.23) | copy-start | bytes 6291460
  0.6 18.5 %collective-permute-start = (bf16[624,512]{1,0:T(8,128)(2,1)}, bf16[624,512]{1,0:T(8,128)(2,1)S(1)}, u32[]{:S(2)}, u32[]{:S(2)}) collective-permute-start(bf16[624,512]{1,0:T(8,128)(2,1)} %param.15), channel_id=1, source_target_pairs={{0,2},{2,0},{1,3},{3,1},{4,6},{6,4},{5,7},{7,5},{8,10},{10,8},{9,1... | collective-permute-start | bytes 1916936 | tf_op jit(solution)/shard_map/ppermute | solution.py:41
  7.0 7.4 %copy-start.22 = (s32[13]{0:T(128)S(1)}, s32[13]{0:T(128)}, u32[]{:S(2)}) copy-start(s32[13]{0:T(128)} %param.17) | copy-start | bytes 160
  7.0 21.4 %all-to-all-start = ((bf16[4,2,13,16,256]{4,3,2,1,0:T(8,128)(2,1)}), bf16[4,2,13,16,256]{4,3,2,1,0:T(8,128)(2,1)}, u32[]{:S(2)}, u32[]{:S(2)}) async-start(bf16[4,2,13,16,256]{4,3,2,1,0:T(8,128)(2,1)} %pad_maximum_fusion.2), calls=%async_computation | async-start | bytes 1703936 | tf_op jit(solution)/shard_map/all_to_all | solution.py:174
  11.3 10.7 %copy-start.15 = (s32[13]{0:T(128)S(1)}, s32[13]{0:T(128)}, u32[]{:S(2)}) copy-start(s32[13]{0:T(128)} %param.16) | copy-start | bytes 160
  12.4 41.2 %collective-permute-start.3 = (bf16[512,1024]{1,0:T(8,128)(2,1)}, bf16[512,1024]{1,0:T(8,128)(2,1)}, u32[]{:S(2)}, u32[]{:S(2)}) collective-permute-start(bf16[512,1024]{1,0:T(8,128)(2,1)} %constant_dynamic-slice_fusion.1), channel_id=1, source_target_pairs={{0,2},{2,0},{1,3},{3,1},{4,6},{6,4},{5,7},{7,5},{8,10},{10,8},{9,1... | collective-permute-start | bytes 3145736 | tf_op jit(solution)/shard_map/ppermute | solution.py:41
  21.9 8.7 %collective-permute-start.1 = (bf16[2,624,512]{2,1,0:T(8,128)(2,1)S(1)}, bf16[2,624,512]{2,1,0:T(8,128)(2,1)}, u32[]{:S(2)}, u32[]{:S(2)}) collective-permute-start(bf16[2,624,512]{2,1,0:T(8,128)(2,1)S(1)} %maximum_select_fusion), channel_id=1, source_target_pairs={{0,1},{1,0},{2,3},{3,2},{4,5},{5,4},{6,7},{7,6},{8,9},{9,8},{10,11... | collective-permute-start | bytes 3833864 | tf_op jit(solution)/shard_map/ppermute | solution.py:41
  32.0 2.1 %copy-start.14 = (f32[2048]{0:T(1024)S(1)}, f32[2048]{0:T(1024)}, u32[]{:S(2)}) copy-start(f32[2048]{0:T(1024)} %param.19) | copy-start | bytes 24580
  34.1 2.4 %copy-start.20 = (bf16[2048,512]{1,0:T(8,128)(2,1)S(1)}, bf16[2048,512]{1,0:T(8,128)(2,1)}, u32[]{:S(2)}) copy-start(bf16[2048,512]{1,0:T(8,128)(2,1)} %param.20) | copy-start | bytes 6291460
  35.0 1.5 copy-start.5
  41.1 1.7 %copy-start.6 = (bf16[624,2048]{1,0:T(8,128)(2,1)S(1)}, bf16[624,2048]{1,0:T(8,128)(2,1)}, u32[]{:S(2)}) copy-start(bf16[624,2048]{1,0:T(8,128)(2,1)} %copy-done.5) | copy-start | bytes 7667716
  42.8 3.7 %copy-start.21 = (bf16[2048,256]{1,0:T(8,128)(2,1)S(1)}, bf16[2048,256]{1,0:T(8,128)(2,1)}, u32[]{:S(2)}) copy-start(bf16[2048,256]{1,0:T(8,128)(2,1)} %param.22) | copy-start | bytes 3145732
  50.7 14.9 %collective-permute-start.2 = (bf16[624,512]{1,0:T(8,128)(2,1)S(1)}, bf16[624,512]{1,0:T(8,128)(2,1)}, u32[]{:S(2)}, u32[]{:S(2)}) collective-permute-start(bf16[624,512]{1,0:T(8,128)(2,1)S(1)} %bitcast.118), channel_id=1, source_target_pairs={{0,2},{2,0},{1,3},{3,1},{4,6},{6,4},{5,7},{7,5},{8,10},{10,8},{9,1... | collective-permute-start | bytes 1916936 | tf_op jit(solution)/shard_map/ppermute | solution.py:41
  69.4 4.7 %copy-start.7 = (bf16[624,512]{1,0:T(8,128)(2,1)S(1)}, bf16[624,512]{1,0:T(8,128)(2,1)}, u32[]{:S(2)}) copy-start(bf16[624,512]{1,0:T(8,128)(2,1)} %param.15) | copy-start | bytes 1916932
  70.9 3.2 %collective-permute-start.4 = (f32[624,512]{1,0:T(8,128)S(1)}, f32[624,512]{1,0:T(8,128)}, u32[]{:S(2)}, u32[]{:S(2)}) collective-permute-start(f32[624,512]{1,0:T(8,128)S(1)} %constant_dynamic-slice_fusion), channel_id=1, source_target_pairs={{0,1},{1,0},{2,3},{3,2},{4,5},{5,4},{6,7},{7,6},{8,9},{9,8},{10,11... | collective-permute-start | bytes 3833864 | tf_op jit(solution)/shard_map/ppermute | solution.py:41
  76.0 10.3 %copy-start.2 = (f32[624,512]{1,0:T(8,128)}, f32[624,512]{1,0:T(8,128)S(1)}, u32[]{:S(2)}) copy-start(f32[624,512]{1,0:T(8,128)S(1)} %get-tuple-element.14) | copy-start | bytes 3833860
  76.0 1.2 collective-permute-start.5
  77.3 3.6 %collective-permute-start.6 = (f32[624,1]{0,1:T(1,128)S(1)}, f32[624,1]{0,1:T(1,128)S(1)}, u32[]{:S(2)}, u32[]{:S(2)}) collective-permute-start(f32[624,1]{0,1:T(1,128)S(1)} %reshape_add_fusion), channel_id=1, source_target_pairs={{0,2},{2,0},{1,3},{3,1},{4,6},{6,4},{5,7},{7,5},{8,10},{10,8},{9,1... | collective-permute-start | bytes 7496 | tf_op jit(solution)/shard_map/ppermute | solution.py:41
  81.1 5.3 %copy-start.17 = (bf16[2048,1024]{1,0:T(8,128)(2,1)S(1)}, bf16[2048,1024]{1,0:T(8,128)(2,1)}, u32[]{:S(2)}) copy-start(bf16[2048,1024]{1,0:T(8,128)(2,1)} %param.25) | copy-start | bytes 12582916
  81.1 2.1 %collective-permute-start.8 = (bf16[624,512]{1,0:T(8,128)(2,1)S(1)}, bf16[624,512]{1,0:T(8,128)(2,1)S(1)}, u32[]{:S(2)}, u32[]{:S(2)}) collective-permute-start(bf16[624,512]{1,0:T(8,128)(2,1)S(1)} %multiply_convert_fusion.1), channel_id=1, source_target_pairs={{0,1},{1,0},{2,3},{3,2},{4,5},{5,4},{6,7},{7,6},{8,9},{9,8},{10,11... | collective-permute-start | bytes 1916936 | tf_op jit(solution)/shard_map/ppermute | solution.py:41
  81.2 16.8 %collective-permute-start.7 = (bf16[624,512]{1,0:T(8,128)(2,1)S(1)}, bf16[624,512]{1,0:T(8,128)(2,1)S(1)}, u32[]{:S(2)}, u32[]{:S(2)}) collective-permute-start(bf16[624,512]{1,0:T(8,128)(2,1)S(1)} %multiply_convert_fusion.1), channel_id=1, source_target_pairs={{0,2},{2,0},{1,3},{3,1},{4,6},{6,4},{5,7},{7,5},{8,10},{10,8},{9,1... | collective-permute-start | bytes 1916936 | tf_op jit(solution)/shard_map/ppermute | solution.py:41
  87.9 13.7 %copy-start.18 = (bf16[2048,1024]{1,0:T(8,128)(2,1)S(1)}, bf16[2048,1024]{1,0:T(8,128)(2,1)}, u32[]{:S(2)}) copy-start(bf16[2048,1024]{1,0:T(8,128)(2,1)} %param.26) | copy-start | bytes 12582916
  98.0 2.1 %collective-permute-start.9 = (bf16[624,512]{1,0:T(8,128)(2,1)S(1)}, bf16[624,512]{1,0:T(8,128)(2,1)S(1)}, u32[]{:S(2)}, u32[]{:S(2)}) collective-permute-start(bf16[624,512]{1,0:T(8,128)(2,1)S(1)} %collective-permute-done.7), channel_id=1, source_target_pairs={{0,1},{1,0},{2,3},{3,2},{4,5},{5,4},{6,7},{7,6},{8,9},{9,8},{10,11... | collective-permute-start | bytes 1916936 | tf_op jit(solution)/shard_map/ppermute | solution.py:41
  103.1 2.2 %copy-start.19 = (bf16[1024,2048]{1,0:T(8,128)(2,1)S(1)}, bf16[1024,2048]{1,0:T(8,128)(2,1)}, u32[]{:S(2)}) copy-start(bf16[1024,2048]{1,0:T(8,128)(2,1)} %param.27) | copy-start | bytes 12582916
  110.5 1.9 %copy-start.16 = (s32[13]{0:T(128)S(1)}, s32[13]{0:T(128)}, u32[]{:S(2)}) copy-start(s32[13]{0:T(128)} %param.18) | copy-start | bytes 160
  110.5 2.7 %copy-start.10 = (bf16[1,13,4,16,256]{4,3,2,1,0:T(8,128)(2,1)S(1)}, bf16[1,13,4,16,256]{4,3,2,1,0:T(8,128)(2,1)}, u32[]{:S(2)}) copy-start(bf16[1,13,4,16,256]{4,3,2,1,0:T(8,128)(2,1)} %get-tuple-element.30) | copy-start | bytes 1277956
  112.2 8.6 %collective-permute-start.10 = (f32[2,624,512]{2,1,0:T(8,128)}, f32[2,624,512]{2,1,0:T(8,128)}, u32[]{:S(2)}, u32[]{:S(2)}) collective-permute-start(f32[2,624,512]{2,1,0:T(8,128)} %pad_maximum_fusion.1), channel_id=1, source_target_pairs={{0,1},{1,0},{2,3},{3,2},{4,5},{5,4},{6,7},{7,6},{8,9},{9,8},{10,11... | collective-permute-start | bytes 7667720 | tf_op jit(solution)/shard_map/ppermute | solution.py:41
  115.1 33.5 %all-to-all-start.1 = ((bf16[8,2,136,256]{3,2,1,0:T(8,128)(2,1)}), bf16[8,2,136,256]{3,2,1,0:T(8,128)(2,1)}, u32[]{:S(2)}, u32[]{:S(2)}) async-start(bf16[8,2,136,256]{3,2,1,0:T(8,128)(2,1)} %select_select_fusion), calls=%async_computation.1 | async-start | bytes 2228224 | tf_op jit(solution)/shard_map/all_to_all | solution.py:198
  124.9 16.6 %collective-permute-start.11 = (bf16[624,512]{1,0:T(8,128)(2,1)}, bf16[624,512]{1,0:T(8,128)(2,1)S(1)}, u32[]{:S(2)}, u32[]{:S(2)}) collective-permute-start(bf16[624,512]{1,0:T(8,128)(2,1)} %fusion.24), channel_id=1, source_target_pairs={{0,2},{2,0},{1,3},{3,1},{4,6},{6,4},{5,7},{7,5},{8,10},{10,8},{9,1... | collective-permute-start | bytes 1916936 | tf_op jit(solution)/shard_map/ppermute | solution.py:41
  151.6 1.5 copy-start.3
  151.6 2.0 %copy-start.4 = (f32[624,512]{1,0:T(8,128)S(1)}, f32[624,512]{1,0:T(8,128)}, u32[]{:S(2)}) copy-start(f32[624,512]{1,0:T(8,128)} %bitcast_add_fusion) | copy-start | bytes 3833860
  151.6 3.0 %copy-start.1 = (bf16[512,2048]{1,0:T(8,128)(2,1)S(1)}, bf16[512,2048]{1,0:T(8,128)(2,1)}, u32[]{:S(2)}) copy-start(bf16[512,2048]{1,0:T(8,128)(2,1)} %param.23) | copy-start | bytes 6291460
  (5 other events, 4.9 us)

commit v19 on v17

--- a/solution.py
+++ b/solution.py
@@ -128,8 +128,13 @@
 
 def row_scale(values, gain_share):
     square_sum = jnp.sum(values * values, axis=-1, keepdims=True)
-    square_sum = square_sum + swap(square_sum, "core")
-    square_sum = square_sum + swap(square_sum, "kvy")
+    diagonal = [(source, 2 * CORES - 1 - source) for source in range(2 * CORES)]
+    square_sum = (
+        square_sum
+        + swap(square_sum, "core")
+        + swap(square_sum, "kvy")
+        + lax.ppermute(square_sum, ("kvy", "core"), diagonal)
+    )
     width = values.shape[-1] * 2 * CORES
     return values * lax.rsqrt(square_sum / width + epsilon) * gain_share
 

time: 156 us -> 155 us (level)
    ppermute x12, starting transfers between devices: 12.1 us -> 10.4 us  [swap(): return lax.ppermute(values, axis_name, [(0, 1), (1, 0)])]
  transfers between devices with their start and end apart: 14 -> 15, of which waited for: 11 -> 11; matrix products, arithmetic and copies ran while one was open for 28% -> 28% of each run, Pallas kernels for 0% -> 0%
where the time goes in v19:
time: 155 us
  waiting for transfers between devices  60.7 us (39%)
  other arithmetic  27.5 us (18%)
  local copies, waits for them, and re-layouts  22.4 us (14%)
  matrix products  21.9 us (14%)
  starting transfers between devices  20.9 us (13%)
    ppermute x12, waiting for transfers between devices, swap(): return lax.ppermute(values, axis_name, [(0, 1), (1, 0)])  49.1 us
    ppermute x12, starting transfers between devices, swap(): return lax.ppermute(values, axis_name, [(0, 1), (1, 0)])  10.4 us
    all_to_all x1, waiting for transfers between devices, local(): lax.all_to_all(packed, 'req', split_axis=0, concat_axis=0, tiled=True)  5.81 us
    all_to_all x1, starting transfers between devices, local(): lax.all_to_all(packed, 'req', split_axis=0, concat_axis=0, tiled=True)  5.81 us
    unnamed x46, local copies, waits for them, and re-layouts  5.28 us
    all_to_all x1, waiting for transfers between devices, local(): lax.all_to_all(stacked, ('kvy', 'core'), split_axis=1, concat_axis=1, til...  4.87 us
    dot_general x2, matrix products, gather_project(): jnp.dot(local_pair, lax.dynamic_slice_in_dim(weight, chip * half, half, 0...  4.66 us
    all_to_all x1, starting transfers between devices, local(): lax.all_to_all(stacked, ('kvy', 'core'), split_axis=1, concat_axis=1, til...  4.33 us
  transfers between devices with their start and end apart: 15, of which 11 were waited for; matrix products, arithmetic and copies ran while one was open for 28% of the time, Pallas kernels for 0%

profile of v19, /device:TPU:0, one launch (start us, length us, event | category | flops | bytes accessed | tf_op | source)
XLA Modules:
  0.0 154.6 jit_solution(14551635193787868228)
XLA Ops:
  0.6 3.0 %collective-permute-start = (bf16[624,512]{1,0:T(8,128)(2,1)}, bf16[624,512]{1,0:T(8,128)(2,1)}, u32[]{:S(2)}, u32[]{:S(2)}) collective-permute-start(bf16[624,512]{1,0:T(8,128)(2,1)} %param.15), channel_id=1, source_target_pairs={{0,2},{2,0},{1,3},{3,1},{4,6},{6,4},{5,7},{7,5},{8,10},{10,8},{9,1... | collective-permute-start | bytes 1916936 | tf_op jit(solution)/shard_map/ppermute | solution.py:41
  8.0 4.3 %all-to-all-start = ((bf16[2,4,13,16,256]{4,3,2,0,1:T(8,128)(2,1)}), bf16[2,4,13,16,256]{4,3,2,0,1:T(8,128)(2,1)}, u32[]{:S(2)}, u32[]{:S(2)}) async-start(bf16[2,4,13,16,256]{4,3,2,0,1:T(8,128)(2,1)} %copy.60), calls=%async_computation | async-start | bytes 1703936 | tf_op jit(solution)/shard_map/all_to_all | solution.py:175
  13.5 1.9 %collective-permute-start.3 = (bf16[512,1024]{1,0:T(8,128)(2,1)}, bf16[512,1024]{1,0:T(8,128)(2,1)}, u32[]{:S(2)}, u32[]{:S(2)}) collective-permute-start(bf16[512,1024]{1,0:T(8,128)(2,1)} %constant_dynamic-slice_fusion.1), channel_id=1, source_target_pairs={{0,2},{2,0},{1,3},{3,1},{4,6},{6,4},{5,7},{7,5},{8,10},{10,8},{9,1... | collective-permute-start | bytes 3145736 | tf_op jit(solution)/shard_map/ppermute | solution.py:41
  15.4 3.8 %collective-permute-done = bf16[624,512]{1,0:T(8,128)(2,1)} collective-permute-done((bf16[624,512]{1,0:T(8,128)(2,1)}, bf16[624,512]{1,0:T(8,128)(2,1)}, u32[]{:S(2)}, u32[]{:S(2)}) %collective-permute-start) | collective-permute-done | bytes 639008 | tf_op jit(solution)/shard_map/ppermute | solution.py:41
  19.2 1.9 %maximum_select_fusion = bf16[2,624,512]{2,1,0:T(8,128)(2,1)S(1)} fusion(bf16[1,624,512]{2,1,0:T(8,128)(2,1)} %bitcast.4, bf16[1,624,512]{2,1,0:T(8,128)(2,1)} %bitcast.99, pred[]{:T(512)S(6)} %eq.27), kind=kLoop, calls=%fused_computation.23 | loop fusion | flops 1916928 | bytes 2555905 | tf_op jit(solution)/shard_map/jit(_where)/select_n | solution.py:48
  21.4 2.0 %multiply_cosine_fusion = (f32[13,48,128]{2,1,0:T(8,128)}, f32[13,48,128]{2,1,0:T(8,128)}) fusion(f32[128]{0:T(128)S(1)} %multiply_exponential_fusion, f32[13,48]{1,0:T(8,128)S(1)} %iota_add_fusion), kind=kLoop, calls=%fused_computation.70 | loop fusion | flops 79872 | bytes 641984 | tf_op jit(solution)/shard_map/cos | solution.py:22
  23.5 4.9 %all-to-all-done = bf16[2,4,13,16,256]{4,3,2,0,1:T(8,128)(2,1)} async-done(((bf16[2,4,13,16,256]{4,3,2,0,1:T(8,128)(2,1)}), bf16[2,4,13,16,256]{4,3,2,0,1:T(8,128)(2,1)}, u32[]{:S(2)}, u32[]{:S(2)}) %all-to-all-start) | async-done | bytes 852000 | tf_op jit(solution)/shard_map/all_to_all | solution.py:175
  32.0 2.0 %fusion = f32[624]{0:T(1024)S(1)} fusion(bf16[624,512]{1,0:T(8,128)(2,1)S(1)} %get-tuple-element.21, bf16[624,512]{1,0:T(8,128)(2,1)S(1)} %get-tuple-element.22, bf16[624,512]{1,0:T(8,128)(2,1)S(1)} %get-tuple-element.20, bf16[624,512]{1,0:T(8,128)(2,1)S(1)} %get-tuple-element.19), kind=kLoop, calls=%fused_computation.4 | loop fusion | flops 12778896 | bytes 2558400 | tf_op jit(solution)/shard_map/reduce_sum | solution.py:207
  35.0 1.5 copy-done.5
  36.5 2.5 %fusion.61 = f32[624,512]{1,0:T(8,128)} fusion(bf16[624,2048]{1,0:T(8,128)(2,1)S(1)} %fusion.2, bf16[2048,512]{1,0:T(8,128)(2,1)S(1)} %copy-done.19), kind=kOutput, calls=%fused_computation.142 | convolution fusion | flops 1308622848 | bytes 5931008 | tf_op jit(solution)/shard_map/dot_general | solution.py:214
  39.0 2.1 %reshape.334 = f32[13,48,2,256]{3,2,1,0:T(2,128)S(1)} reshape(f32[624,512]{1,0:T(8,128)} %fusion.61) | data formatting | bytes 2555904 | tf_op jit(solution)/shard_map/reshape | solution.py:216
  42.8 2.2 %fusion.60 = f32[624,256]{1,0:T(8,128)S(1)} fusion(bf16[624,2048]{1,0:T(8,128)(2,1)S(1)} %copy-done.6, bf16[2048,256]{1,0:T(8,128)(2,1)} %param.21), kind=kOutput, calls=%fused_computation.141 | convolution fusion | flops 654311424 | bytes 4243456 | tf_op jit(solution)/shard_map/dot_general | solution.py:218
  45.0 1.6 %fusion.34 = (bf16[13,48,1,128]{3,1,0,2:T(8,128)(2,1)S(1)}, bf16[13,48,1,128]{3,1,0,2:T(8,128)(2,1)S(1)}) fusion(f32[13,48,1,256]{3,1,0,2:T(8,128)S(1)} %bitcast.104, f32[128]{0:T(128)S(1)} %multiply_exponential_fusion, f32[13,48]{1,0:T(8,128)S(1)} %iota_add_fusion), kind=kLoop, calls=%fused_computation.78 | loop fusion | flops 718848 | bytes 961472 | tf_op jit(solution)/shard_map/convert.7
  50.7 2.1 %collective-permute-start.2 = (bf16[624,512]{1,0:T(8,128)(2,1)S(1)}, bf16[624,512]{1,0:T(8,128)(2,1)}, u32[]{:S(2)}, u32[]{:S(2)}) collective-permute-start(bf16[624,512]{1,0:T(8,128)(2,1)S(1)} %bitcast.96), channel_id=1, source_target_pairs={{0,2},{2,0},{1,3},{3,1},{4,6},{6,4},{5,7},{7,5},{8,10},{10,8},{9,1... | collective-permute-start | bytes 1916936 | tf_op jit(solution)/shard_map/ppermute | solution.py:41
  53.7 11.9 %collective-permute-done.2 = bf16[624,512]{1,0:T(8,128)(2,1)} collective-permute-done((bf16[624,512]{1,0:T(8,128)(2,1)S(1)}, bf16[624,512]{1,0:T(8,128)(2,1)}, u32[]{:S(2)}, u32[]{:S(2)}) %collective-permute-start.2) | collective-permute-done | bytes 639008 | tf_op jit(solution)/shard_map/ppermute | solution.py:41
  65.6 3.8 %convolution_add_fusion = f32[624,1024]{1,0:T(8,128)} fusion(f32[624,1024]{1,0:T(8,128)S(1)} %fusion.15, bf16[624,512]{1,0:T(8,128)(2,1)} %collective-permute-done.2, bf16[512,1024]{1,0:T(8,128)(2,1)} %collective-permute-done.3), kind=kOutput, calls=%fused_computation.21 | convolution fusion | flops 654950400 | bytes 6799360 | tf_op jit(solution)/shard_map/dot_general | solution.py:121
  70.9 3.1 %collective-permute-done.4 = f32[624,512]{1,0:T(8,128)} collective-permute-done((f32[624,512]{1,0:T(8,128)S(1)}, f32[624,512]{1,0:T(8,128)}, u32[]{:S(2)}, u32[]{:S(2)}) %collective-permute-start.4) | collective-permute-done | bytes 1277984 | tf_op jit(solution)/shard_map/ppermute | solution.py:41
  74.0 2.0 %multiply_reduce_fusion = (f32[624]{0:T(1024)S(1)}, f32[624,512]{1,0:T(8,128)S(1)}) fusion(f32[624,512]{1,0:T(8,128)} %collective-permute-done.4, f32[624,1024]{1,0:T(8,128)} %convolution_add_fusion, s32[]{:T(128)S(6)} %select_n.199, bf16[624,512]{1,0:T(8,128)(2,1)S(1)} %copy-done.7), kind=kLoop, calls=%fused_computation.34 | loop fusion | flops 1596816 | bytes 4475332 | tf_op jit(solution)/shard_map/reduce_sum | solution.py:130
  83.1 3.1 %fusion.7 = f32[624,1024]{1,0:T(8,128)S(1)} fusion(bf16[2048,1024]{1,0:T(8,128)(2,1)} %param.26, s32[]{:T(128)S(6)} %select_n.197, bf16[624,512]{1,0:T(8,128)(2,1)S(1)} %collective-permute-done.9, bf16[624,512]{1,0:T(8,128)(2,1)S(1)} %multiply_convert_fusion.1, pred[]{:T(512)S(6)} %eq.26), kind=kOutput, calls=%fused_computation.15 | convolution fusion | flops 1314373632 | bytes 5931013 | tf_op jit(solution)/shard_map/dot_general | solution.py:69
  86.2 1.5 fusion.9
  87.8 10.0 %collective-permute-done.8 = bf16[624,512]{1,0:T(8,128)(2,1)S(1)} collective-permute-done((bf16[624,512]{1,0:T(8,128)(2,1)S(1)}, bf16[624,512]{1,0:T(8,128)(2,1)S(1)}, u32[]{:S(2)}, u32[]{:S(2)}) %collective-permute-start.8) | collective-permute-done | bytes 639008 | tf_op jit(solution)/shard_map/ppermute | solution.py:41
  97.8 2.1 %collective-permute-done.10 = bf16[624,512]{1,0:T(8,128)(2,1)S(1)} collective-permute-done((bf16[624,512]{1,0:T(8,128)(2,1)S(1)}, bf16[624,512]{1,0:T(8,128)(2,1)S(1)}, u32[]{:S(2)}, u32[]{:S(2)}) %collective-permute-start.10) | collective-permute-done | bytes 639008 | tf_op jit(solution)/shard_map/ppermute | solution.py:41
  99.9 1.5 fusion.5
  101.4 1.5 fusion.3
  105.1 3.1 %fusion.62 = f32[624,2048]{1,0:T(8,128)S(1)} fusion(bf16[624,1024]{1,0:T(8,128)(2,1)S(1)} %multiply_convert_fusion, bf16[1024,2048]{1,0:T(8,128)(2,1)S(1)} %copy-done.18), kind=kOutput, calls=%fused_computation.143 | convolution fusion | flops 2617245696 | bytes 10584064 | tf_op jit(solution)/shard_map/dot_general | solution.py:97
  108.2 2.1 %select_bitcast_fusion.3 = (f32[1,624,512]{2,1,0:T(8,128)}, f32[1,624,512]{2,1,0:T(8,128)}, f32[1,624,512]{2,1,0:T(8,128)S(1)}, f32[1,624,512]{2,1,0:T(8,128)S(1)}) fusion(f32[624,2048]{1,0:T(8,128)S(1)} %fusion.62, pred[]{:T(512)S(6)} %eq.26), kind=kLoop, calls=%fused_computation.32 | loop fusion | flops 1277952 | bytes 10223617 | tf_op jit(solution)/shard_map/stack | solution.py:104
  110.3 1.7 %pad_maximum_fusion.1 = f32[2,624,512]{2,1,0:T(8,128)} fusion(f32[1,624,512]{2,1,0:T(8,128)S(1)} %get-tuple-element.17, f32[1,624,512]{2,1,0:T(8,128)S(1)} %get-tuple-element.18), kind=kLoop, calls=%fused_computation.9 | loop fusion | flops 638976 | bytes 5111808 | tf_op jit(solution)/shard_map/stack | solution.py:105
  115.0 5.8 %all-to-all-start.1 = ((bf16[8,2,136,256]{3,2,1,0:T(8,128)(2,1)}), bf16[8,2,136,256]{3,2,1,0:T(8,128)(2,1)}, u32[]{:S(2)}, u32[]{:S(2)}) async-start(bf16[8,2,136,256]{3,2,1,0:T(8,128)(2,1)} %select_select_fusion), calls=%async_computation.1 | async-start | bytes 2228224 | tf_op jit(solution)/shard_map/all_to_all | solution.py:199
  120.8 3.1 %maximum_add_fusion = f32[2,624,512]{2,1,0:T(8,128)S(1)} fusion(f32[2,624,512]{2,1,0:T(8,128)} %collective-permute-done.11, f32[1,624,512]{2,1,0:T(8,128)} %get-tuple-element.16, f32[1,624,512]{2,1,0:T(8,128)} %get-tuple-element.15), kind=kLoop, calls=%fused_computation.8 | loop fusion | flops 1277952 | bytes 7667712 | tf_op jit(solution)/shard_map/add | solution.py:106
  125.6 15.8 %collective-permute-done.12 = bf16[624,512]{1,0:T(8,128)(2,1)S(1)} collective-permute-done((bf16[624,512]{1,0:T(8,128)(2,1)}, bf16[624,512]{1,0:T(8,128)(2,1)S(1)}, u32[]{:S(2)}, u32[]{:S(2)}) %collective-permute-start.12) | collective-permute-done | bytes 639008 | tf_op jit(solution)/shard_map/ppermute | solution.py:41
  142.8 5.8 %all-to-all-done.1 = bf16[8,2,136,256]{3,2,1,0:T(8,128)(2,1)} async-done(((bf16[8,2,136,256]{3,2,1,0:T(8,128)(2,1)}), bf16[8,2,136,256]{3,2,1,0:T(8,128)(2,1)}, u32[]{:S(2)}, u32[]{:S(2)}) %all-to-all-start.1) | async-done | bytes 1114144 | tf_op jit(solution)/shard_map/all_to_all | solution.py:199
  149.7 1.9 %gather_fusion.1 = bf16[13,136,256]{2,1,0:T(8,128)(2,1)S(1)} fusion(bf16[16,136,256]{2,1,0:T(8,128)(2,1)} %bitcast.36, s32[1024]{0:T(1024)S(1)} %pad_clamp_fusion), kind=kCustom, calls=%fused_computation.1 | custom fusion | bytes 1810484 | tf_op jit(solution)/shard_map/jit(_take)/gather | solution.py:263
  (124 shorter events, 37.7 us)
Async XLA Ops:
  0.6 11.7 %copy-start = (bf16[512,2048]{1,0:T(8,128)(2,1)S(1)}, bf16[512,2048]{1,0:T(8,128)(2,1)}, u32[]{:S(2)}) copy-start(bf16[512,2048]{1,0:T(8,128)(2,1)} %param.23) | copy-start | bytes 6291460
  0.6 18.6 %collective-permute-start = (bf16[624,512]{1,0:T(8,128)(2,1)}, bf16[624,512]{1,0:T(8,128)(2,1)}, u32[]{:S(2)}, u32[]{:S(2)}) collective-permute-start(bf16[624,512]{1,0:T(8,128)(2,1)} %param.15), channel_id=1, source_target_pairs={{0,2},{2,0},{1,3},{3,1},{4,6},{6,4},{5,7},{7,5},{8,10},{10,8},{9,1... | collective-permute-start | bytes 1916936 | tf_op jit(solution)/shard_map/ppermute | solution.py:41
  8.0 7.4 %copy-start.21 = (s32[13]{0:T(128)S(1)}, s32[13]{0:T(128)}, u32[]{:S(2)}) copy-start(s32[13]{0:T(128)} %param.17) | copy-start | bytes 160
  8.0 20.4 %all-to-all-start = ((bf16[2,4,13,16,256]{4,3,2,0,1:T(8,128)(2,1)}), bf16[2,4,13,16,256]{4,3,2,0,1:T(8,128)(2,1)}, u32[]{:S(2)}, u32[]{:S(2)}) async-start(bf16[2,4,13,16,256]{4,3,2,0,1:T(8,128)(2,1)} %copy.60), calls=%async_computation | async-start | bytes 1703936 | tf_op jit(solution)/shard_map/all_to_all | solution.py:175
  12.3 9.0 %copy-start.14 = (s32[13]{0:T(128)S(1)}, s32[13]{0:T(128)}, u32[]{:S(2)}) copy-start(s32[13]{0:T(128)} %param.16) | copy-start | bytes 160
  13.5 40.2 %collective-permute-start.3 = (bf16[512,1024]{1,0:T(8,128)(2,1)}, bf16[512,1024]{1,0:T(8,128)(2,1)}, u32[]{:S(2)}, u32[]{:S(2)}) collective-permute-start(bf16[512,1024]{1,0:T(8,128)(2,1)} %constant_dynamic-slice_fusion.1), channel_id=1, source_target_pairs={{0,2},{2,0},{1,3},{3,1},{4,6},{6,4},{5,7},{7,5},{8,10},{10,8},{9,1... | collective-permute-start | bytes 3145736 | tf_op jit(solution)/shard_map/ppermute | solution.py:41
  21.1 9.4 %collective-permute-start.1 = (bf16[2,624,512]{2,1,0:T(8,128)(2,1)S(1)}, bf16[2,624,512]{2,1,0:T(8,128)(2,1)}, u32[]{:S(2)}, u32[]{:S(2)}) collective-permute-start(bf16[2,624,512]{2,1,0:T(8,128)(2,1)S(1)} %maximum_select_fusion), channel_id=1, source_target_pairs={{0,1},{1,0},{2,3},{3,2},{4,5},{5,4},{6,7},{7,6},{8,9},{9,8},{10,11... | collective-permute-start | bytes 3833864 | tf_op jit(solution)/shard_map/ppermute | solution.py:41
  32.0 2.1 %copy-start.13 = (f32[2048]{0:T(1024)S(1)}, f32[2048]{0:T(1024)}, u32[]{:S(2)}) copy-start(f32[2048]{0:T(1024)} %param.19) | copy-start | bytes 24580
  34.1 2.4 %copy-start.19 = (bf16[2048,512]{1,0:T(8,128)(2,1)S(1)}, bf16[2048,512]{1,0:T(8,128)(2,1)}, u32[]{:S(2)}) copy-start(bf16[2048,512]{1,0:T(8,128)(2,1)} %param.20) | copy-start | bytes 6291460
  41.1 1.7 %copy-start.6 = (bf16[624,2048]{1,0:T(8,128)(2,1)S(1)}, bf16[624,2048]{1,0:T(8,128)(2,1)}, u32[]{:S(2)}) copy-start(bf16[624,2048]{1,0:T(8,128)(2,1)} %copy-done.5) | copy-start | bytes 7667716
  42.8 3.7 %copy-start.20 = (bf16[2048,256]{1,0:T(8,128)(2,1)S(1)}, bf16[2048,256]{1,0:T(8,128)(2,1)}, u32[]{:S(2)}) copy-start(bf16[2048,256]{1,0:T(8,128)(2,1)} %param.22) | copy-start | bytes 3145732
  50.7 14.9 %collective-permute-start.2 = (bf16[624,512]{1,0:T(8,128)(2,1)S(1)}, bf16[624,512]{1,0:T(8,128)(2,1)}, u32[]{:S(2)}, u32[]{:S(2)}) collective-permute-start(bf16[624,512]{1,0:T(8,128)(2,1)S(1)} %bitcast.96), channel_id=1, source_target_pairs={{0,2},{2,0},{1,3},{3,1},{4,6},{6,4},{5,7},{7,5},{8,10},{10,8},{9,1... | collective-permute-start | bytes 1916936 | tf_op jit(solution)/shard_map/ppermute | solution.py:41
  69.4 4.7 %copy-start.7 = (bf16[624,512]{1,0:T(8,128)(2,1)S(1)}, bf16[624,512]{1,0:T(8,128)(2,1)}, u32[]{:S(2)}) copy-start(bf16[624,512]{1,0:T(8,128)(2,1)} %param.15) | copy-start | bytes 1916932
  70.8 3.2 %collective-permute-start.4 = (f32[624,512]{1,0:T(8,128)S(1)}, f32[624,512]{1,0:T(8,128)}, u32[]{:S(2)}, u32[]{:S(2)}) collective-permute-start(f32[624,512]{1,0:T(8,128)S(1)} %constant_dynamic-slice_fusion), channel_id=1, source_target_pairs={{0,1},{1,0},{2,3},{3,2},{4,5},{5,4},{6,7},{7,6},{8,9},{9,8},{10,11... | collective-permute-start | bytes 3833864 | tf_op jit(solution)/shard_map/ppermute | solution.py:41
  76.0 10.2 %copy-start.2 = (f32[624,512]{1,0:T(8,128)}, f32[624,512]{1,0:T(8,128)S(1)}, u32[]{:S(2)}) copy-start(f32[624,512]{1,0:T(8,128)S(1)} %get-tuple-element.14) | copy-start | bytes 3833860
  76.0 2.7 %collective-permute-start.5 = (f32[624,1]{0,1:T(1,128)S(1)}, f32[624,1]{0,1:T(1,128)S(1)}, u32[]{:S(2)}, u32[]{:S(2)}) collective-permute-start(f32[624,1]{0,1:T(1,128)S(1)} %broadcast_in_dim.131), channel_id=1, source_target_pairs={{0,1},{1,0},{2,3},{3,2},{4,5},{5,4},{6,7},{7,6},{8,9},{9,8},{10,11... | collective-permute-start | bytes 7496 | tf_op jit(solution)/shard_map/ppermute | solution.py:41
  76.2 3.6 %collective-permute-start.6 = (f32[624,1]{0,1:T(1,128)S(1)}, f32[624,1]{0,1:T(1,128)S(1)}, u32[]{:S(2)}, u32[]{:S(2)}) collective-permute-start(f32[624,1]{0,1:T(1,128)S(1)} %broadcast_in_dim.131), channel_id=1, source_target_pairs={{0,2},{2,0},{1,3},{3,1},{4,6},{6,4},{5,7},{7,5},{8,10},{10,8},{9,1... | collective-permute-start | bytes 7496 | tf_op jit(solution)/shard_map/ppermute | solution.py:41
  77.7 3.0 %collective-permute-start.7 = (f32[624,1]{0,1:T(1,128)S(1)}, f32[624,1]{0,1:T(1,128)S(1)}, u32[]{:S(2)}, u32[]{:S(2)}) collective-permute-start(f32[624,1]{0,1:T(1,128)S(1)} %broadcast_in_dim.131), channel_id=1, source_target_pairs={{0,3},{1,2},{2,1},{3,0},{4,7},{5,6},{6,5},{7,4},{8,11},{9,10},{10,... | collective-permute-start | bytes 7496 | tf_op jit(solution)/shard_map/ppermute | solution.py:136
  80.9 5.3 %copy-start.16 = (bf16[2048,1024]{1,0:T(8,128)(2,1)S(1)}, bf16[2048,1024]{1,0:T(8,128)(2,1)}, u32[]{:S(2)}) copy-start(bf16[2048,1024]{1,0:T(8,128)(2,1)} %param.25) | copy-start | bytes 12582916
  80.9 2.1 %collective-permute-start.9 = (bf16[624,512]{1,0:T(8,128)(2,1)S(1)}, bf16[624,512]{1,0:T(8,128)(2,1)S(1)}, u32[]{:S(2)}, u32[]{:S(2)}) collective-permute-start(bf16[624,512]{1,0:T(8,128)(2,1)S(1)} %multiply_convert_fusion.1), channel_id=1, source_target_pairs={{0,1},{1,0},{2,3},{3,2},{4,5},{5,4},{6,7},{7,6},{8,9},{9,8},{10,11... | collective-permute-start | bytes 1916936 | tf_op jit(solution)/shard_map/ppermute | solution.py:41
  81.1 16.7 %collective-permute-start.8 = (bf16[624,512]{1,0:T(8,128)(2,1)S(1)}, bf16[624,512]{1,0:T(8,128)(2,1)S(1)}, u32[]{:S(2)}, u32[]{:S(2)}) collective-permute-start(bf16[624,512]{1,0:T(8,128)(2,1)S(1)} %multiply_convert_fusion.1), channel_id=1, source_target_pairs={{0,2},{2,0},{1,3},{3,1},{4,6},{6,4},{5,7},{7,5},{8,10},{10,8},{9,1... | collective-permute-start | bytes 1916936 | tf_op jit(solution)/shard_map/ppermute | solution.py:41
  87.7 13.6 %copy-start.17 = (bf16[2048,1024]{1,0:T(8,128)(2,1)S(1)}, bf16[2048,1024]{1,0:T(8,128)(2,1)}, u32[]{:S(2)}) copy-start(bf16[2048,1024]{1,0:T(8,128)(2,1)} %param.26) | copy-start | bytes 12582916
  97.8 2.1 %collective-permute-start.10 = (bf16[624,512]{1,0:T(8,128)(2,1)S(1)}, bf16[624,512]{1,0:T(8,128)(2,1)S(1)}, u32[]{:S(2)}, u32[]{:S(2)}) collective-permute-start(bf16[624,512]{1,0:T(8,128)(2,1)S(1)} %collective-permute-done.8), channel_id=1, source_target_pairs={{0,1},{1,0},{2,3},{3,2},{4,5},{5,4},{6,7},{7,6},{8,9},{9,8},{10,11... | collective-permute-start | bytes 1916936 | tf_op jit(solution)/shard_map/ppermute | solution.py:41
  102.9 2.2 %copy-start.18 = (bf16[1024,2048]{1,0:T(8,128)(2,1)S(1)}, bf16[1024,2048]{1,0:T(8,128)(2,1)}, u32[]{:S(2)}) copy-start(bf16[1024,2048]{1,0:T(8,128)(2,1)} %param.27) | copy-start | bytes 12582916
  110.3 1.9 %copy-start.15 = (s32[13]{0:T(128)S(1)}, s32[13]{0:T(128)}, u32[]{:S(2)}) copy-start(s32[13]{0:T(128)} %param.18) | copy-start | bytes 160
  110.3 2.7 %copy-start.10 = (bf16[1,13,4,16,256]{4,3,2,1,0:T(8,128)(2,1)S(1)}, bf16[1,13,4,16,256]{4,3,2,1,0:T(8,128)(2,1)}, u32[]{:S(2)}) copy-start(bf16[1,13,4,16,256]{4,3,2,1,0:T(8,128)(2,1)} %get-tuple-element.30) | copy-start | bytes 1277956
  112.1 8.7 %collective-permute-start.11 = (f32[2,624,512]{2,1,0:T(8,128)}, f32[2,624,512]{2,1,0:T(8,128)}, u32[]{:S(2)}, u32[]{:S(2)}) collective-permute-start(f32[2,624,512]{2,1,0:T(8,128)} %pad_maximum_fusion.1), channel_id=1, source_target_pairs={{0,1},{1,0},{2,3},{3,2},{4,5},{5,4},{6,7},{7,6},{8,9},{9,8},{10,11... | collective-permute-start | bytes 7667720 | tf_op jit(solution)/shard_map/ppermute | solution.py:41
  115.0 33.6 %all-to-all-start.1 = ((bf16[8,2,136,256]{3,2,1,0:T(8,128)(2,1)}), bf16[8,2,136,256]{3,2,1,0:T(8,128)(2,1)}, u32[]{:S(2)}, u32[]{:S(2)}) async-start(bf16[8,2,136,256]{3,2,1,0:T(8,128)(2,1)} %select_select_fusion), calls=%async_computation.1 | async-start | bytes 2228224 | tf_op jit(solution)/shard_map/all_to_all | solution.py:199
  124.8 16.6 %collective-permute-start.12 = (bf16[624,512]{1,0:T(8,128)(2,1)}, bf16[624,512]{1,0:T(8,128)(2,1)S(1)}, u32[]{:S(2)}, u32[]{:S(2)}) collective-permute-start(bf16[624,512]{1,0:T(8,128)(2,1)} %fusion.24), channel_id=1, source_target_pairs={{0,2},{2,0},{1,3},{3,1},{4,6},{6,4},{5,7},{7,5},{8,10},{10,8},{9,1... | collective-permute-start | bytes 1916936 | tf_op jit(solution)/shard_map/ppermute | solution.py:41
  151.5 1.5 copy-start.3
  151.5 2.0 %copy-start.4 = (f32[624,512]{1,0:T(8,128)S(1)}, f32[624,512]{1,0:T(8,128)}, u32[]{:S(2)}) copy-start(f32[624,512]{1,0:T(8,128)} %bitcast_add_fusion) | copy-start | bytes 3833860
  151.6 3.0 %copy-start.1 = (bf16[512,2048]{1,0:T(8,128)(2,1)S(1)}, bf16[512,2048]{1,0:T(8,128)(2,1)}, u32[]{:S(2)}) copy-start(bf16[512,2048]{1,0:T(8,128)(2,1)} %param.23) | copy-start | bytes 6291460
  (5 other events, 5.6 us)

commit v20 on v19

--- a/solution.py
+++ b/solution.py
@@ -97,12 +97,12 @@
     product = jnp.dot(matrix_in, weight, preferred_element_type=jnp.float32)
     width = product.shape[1] // (2 * CORES)
 
-    def block(chip_block, core_block):
+    def pick(chip_block, core_block):
         start = (chip_block * CORES + core_block) * width
-        return product[:, start:start + width]
-
-    keep = jnp.stack([jnp.where(core == 0, block(k, 0), block(k, 1)) for k in range(2)])
-    give = jnp.stack([jnp.where(core == 0, block(k, 1), block(k, 0)) for k in range(2)])
+        return lax.dynamic_slice_in_dim(product, start, width, 1)
+
+    keep = jnp.stack([pick(k, core) for k in range(2)])
+    give = jnp.stack([pick(k, 1 - core) for k in range(2)])
     chip_sum = keep + swap(give, "core")
     mine = jnp.where(chip == 0, chip_sum[0], chip_sum[1])
     theirs = jnp.where(chip == 0, chip_sum[1], chip_sum[0])

time: 155 us -> 158 us (1.019)
  matrix products: 21.9 us -> 26.4 us
  local copies, waits for them, and re-layouts: 22.4 us -> 25.5 us
  waiting for transfers between devices: 60.7 us -> 57.8 us
  other arithmetic: 27.5 us -> 25.4 us
    dot_general x2, matrix products: 4.66 us -> 7.64 us  [gather_project(): jnp.dot(local_pair, lax.dynamic_slice_in_dim(weight, chip * half, half, 0...]
    ppermute x12, waiting for transfers between devices: 49.1 us -> 46.2 us  [swap(): return lax.ppermute(values, axis_name, [(0, 1), (1, 0)])]
    another operation x4 -> x3, other arithmetic: 5.64 us -> 3.5 us  [the longest x1 2.14 us: scatter_features(): jnp.stack([jnp.where(core == 0, block(k, 0), block(k, 1)) for k in range(...]
    another operation x0 -> x1, local copies, waits for them, and re-layouts: none -> 2.12 us  [scatter_features(): keep = jnp.stack([pick(k, core) for k in range(2)])]
    unnamed x46 -> x50, local copies, waits for them, and re-layouts: 5.28 us -> 6.22 us
  transfers between devices with their start and end apart: 15 -> 15, of which waited for: 11 -> 11; matrix products, arithmetic and copies ran while one was open for 28% -> 29% of each run, Pallas kernels for 0% -> 0%
where the time goes in v20:
time: 158 us; the launch traced here: 157 us
  waiting for transfers between devices  57.8 us (37%)
  matrix products  26.4 us (17%)
  local copies, waits for them, and re-layouts  25.5 us (16%)
  other arithmetic  25.4 us (16%)
  starting transfers between devices  20.9 us (13%)
    ppermute x12, waiting for transfers between devices, swap(): return lax.ppermute(values, axis_name, [(0, 1), (1, 0)])  46.2 us
    ppermute x12, starting transfers between devices, swap(): return lax.ppermute(values, axis_name, [(0, 1), (1, 0)])  10.4 us
    dot_general x2, matrix products, gather_project(): jnp.dot(local_pair, lax.dynamic_slice_in_dim(weight, chip * half, half, 0...  7.64 us
    unnamed x50, local copies, waits for them, and re-layouts  6.22 us
    all_to_all x1, starting transfers between devices, local(): lax.all_to_all(packed, 'req', split_axis=0, concat_axis=0, tiled=True)  5.82 us
    all_to_all x1, waiting for transfers between devices, local(): lax.all_to_all(packed, 'req', split_axis=0, concat_axis=0, tiled=True)  5.82 us
    all_to_all x1, waiting for transfers between devices, local(): lax.all_to_all(stacked, ('kvy', 'core'), split_axis=1, concat_axis=1, til...  4.86 us
    dot_general x2, matrix products, gather_project(): jnp.dot(remote_pair, lax.dynamic_slice_in_dim(weight, (1 - chip) * half,...  4.62 us
  transfers between devices with their start and end apart: 15, of which 11 were waited for; matrix products, arithmetic and copies ran while one was open for 29% of the time, Pallas kernels for 0%

profile of v20, /device:TPU:0, one launch (start us, length us, event | category | flops | bytes accessed | tf_op | source)
XLA Modules:
  0.0 157.0 jit_solution(18176048250070997937)
XLA Ops:
  0.6 3.0 %collective-permute-start = (bf16[624,512]{1,0:T(8,128)(2,1)}, bf16[624,512]{1,0:T(8,128)(2,1)}, u32[]{:S(2)}, u32[]{:S(2)}) collective-permute-start(bf16[624,512]{1,0:T(8,128)(2,1)} %param.15), channel_id=1, source_target_pairs={{0,2},{2,0},{1,3},{3,1},{4,6},{6,4},{5,7},{7,5},{8,10},{10,8},{9,1... | collective-permute-start | bytes 1916936 | tf_op jit(solution)/shard_map/ppermute | solution.py:41
  8.0 4.3 %all-to-all-start = ((bf16[2,4,13,16,256]{4,3,2,0,1:T(8,128)(2,1)}), bf16[2,4,13,16,256]{4,3,2,0,1:T(8,128)(2,1)}, u32[]{:S(2)}, u32[]{:S(2)}) async-start(bf16[2,4,13,16,256]{4,3,2,0,1:T(8,128)(2,1)} %copy.60), calls=%async_computation | async-start | bytes 1703936 | tf_op jit(solution)/shard_map/all_to_all | solution.py:175
  13.5 1.9 %collective-permute-start.3 = (bf16[512,1024]{1,0:T(8,128)(2,1)}, bf16[512,1024]{1,0:T(8,128)(2,1)}, u32[]{:S(2)}, u32[]{:S(2)}) collective-permute-start(bf16[512,1024]{1,0:T(8,128)(2,1)} %constant_dynamic-slice_fusion.1), channel_id=1, source_target_pairs={{0,2},{2,0},{1,3},{3,1},{4,6},{6,4},{5,7},{7,5},{8,10},{10,8},{9,1... | collective-permute-start | bytes 3145736 | tf_op jit(solution)/shard_map/ppermute | solution.py:41
  15.4 3.8 %collective-permute-done = bf16[624,512]{1,0:T(8,128)(2,1)} collective-permute-done((bf16[624,512]{1,0:T(8,128)(2,1)}, bf16[624,512]{1,0:T(8,128)(2,1)}, u32[]{:S(2)}, u32[]{:S(2)}) %collective-permute-start) | collective-permute-done | bytes 639008 | tf_op jit(solution)/shard_map/ppermute | solution.py:41
  19.2 1.9 %maximum_select_fusion = bf16[2,624,512]{2,1,0:T(8,128)(2,1)S(1)} fusion(bf16[1,624,512]{2,1,0:T(8,128)(2,1)} %bitcast.4, bf16[1,624,512]{2,1,0:T(8,128)(2,1)} %bitcast.99, pred[]{:T(512)S(6)} %eq.27), kind=kLoop, calls=%fused_computation.23 | loop fusion | flops 1916928 | bytes 2555905 | tf_op jit(solution)/shard_map/jit(_where)/select_n | solution.py:48
  21.4 2.0 %multiply_cosine_fusion = (f32[13,48,128]{2,1,0:T(8,128)}, f32[13,48,128]{2,1,0:T(8,128)}) fusion(f32[128]{0:T(128)S(1)} %multiply_exponential_fusion, f32[13,48]{1,0:T(8,128)S(1)} %iota_add_fusion), kind=kLoop, calls=%fused_computation.70 | loop fusion | flops 79872 | bytes 641984 | tf_op jit(solution)/shard_map/cos | solution.py:22
  23.5 4.9 %all-to-all-done = bf16[2,4,13,16,256]{4,3,2,0,1:T(8,128)(2,1)} async-done(((bf16[2,4,13,16,256]{4,3,2,0,1:T(8,128)(2,1)}), bf16[2,4,13,16,256]{4,3,2,0,1:T(8,128)(2,1)}, u32[]{:S(2)}, u32[]{:S(2)}) %all-to-all-start) | async-done | bytes 852000 | tf_op jit(solution)/shard_map/all_to_all | solution.py:175
  32.0 2.0 %fusion = f32[624]{0:T(1024)S(1)} fusion(bf16[624,512]{1,0:T(8,128)(2,1)S(1)} %get-tuple-element.21, bf16[624,512]{1,0:T(8,128)(2,1)S(1)} %get-tuple-element.22, bf16[624,512]{1,0:T(8,128)(2,1)S(1)} %get-tuple-element.20, bf16[624,512]{1,0:T(8,128)(2,1)S(1)} %get-tuple-element.19), kind=kLoop, calls=%fused_computation.4 | loop fusion | flops 12778896 | bytes 2558400 | tf_op jit(solution)/shard_map/reduce_sum | solution.py:207
  35.0 1.5 copy-done.7
  36.5 2.5 %fusion.61 = f32[624,512]{1,0:T(8,128)} fusion(bf16[624,2048]{1,0:T(8,128)(2,1)S(1)} %fusion.2, bf16[2048,512]{1,0:T(8,128)(2,1)S(1)} %copy-done.21), kind=kOutput, calls=%fused_computation.142 | convolution fusion | flops 1308622848 | bytes 5931008 | tf_op jit(solution)/shard_map/dot_general | solution.py:214
  39.0 2.1 %reshape.334 = f32[13,48,2,256]{3,2,1,0:T(2,128)S(1)} reshape(f32[624,512]{1,0:T(8,128)} %fusion.61) | data formatting | bytes 2555904 | tf_op jit(solution)/shard_map/reshape | solution.py:216
  42.8 2.1 %fusion.60 = f32[624,256]{1,0:T(8,128)S(1)} fusion(bf16[624,2048]{1,0:T(8,128)(2,1)S(1)} %copy-done.8, bf16[2048,256]{1,0:T(8,128)(2,1)} %param.21), kind=kOutput, calls=%fused_computation.141 | convolution fusion | flops 654311424 | bytes 4243456 | tf_op jit(solution)/shard_map/dot_general | solution.py:218
  45.0 1.6 %fusion.34 = (bf16[13,48,1,128]{3,1,0,2:T(8,128)(2,1)S(1)}, bf16[13,48,1,128]{3,1,0,2:T(8,128)(2,1)S(1)}) fusion(f32[13,48,1,256]{3,1,0,2:T(8,128)S(1)} %bitcast.104, f32[128]{0:T(128)S(1)} %multiply_exponential_fusion, f32[13,48]{1,0:T(8,128)S(1)} %iota_add_fusion), kind=kLoop, calls=%fused_computation.78 | loop fusion | flops 718848 | bytes 961472 | tf_op jit(solution)/shard_map/convert.7
  50.7 2.1 %collective-permute-start.2 = (bf16[624,512]{1,0:T(8,128)(2,1)S(1)}, bf16[624,512]{1,0:T(8,128)(2,1)}, u32[]{:S(2)}, u32[]{:S(2)}) collective-permute-start(bf16[624,512]{1,0:T(8,128)(2,1)S(1)} %bitcast.96), channel_id=1, source_target_pairs={{0,2},{2,0},{1,3},{3,1},{4,6},{6,4},{5,7},{7,5},{8,10},{10,8},{9,1... | collective-permute-start | bytes 1916936 | tf_op jit(solution)/shard_map/ppermute | solution.py:41
  53.7 11.9 %collective-permute-done.2 = bf16[624,512]{1,0:T(8,128)(2,1)} collective-permute-done((bf16[624,512]{1,0:T(8,128)(2,1)S(1)}, bf16[624,512]{1,0:T(8,128)(2,1)}, u32[]{:S(2)}, u32[]{:S(2)}) %collective-permute-start.2) | collective-permute-done | bytes 639008 | tf_op jit(solution)/shard_map/ppermute | solution.py:41
  65.6 3.8 %convolution_add_fusion = f32[624,1024]{1,0:T(8,128)} fusion(f32[624,1024]{1,0:T(8,128)S(1)} %fusion.15, bf16[624,512]{1,0:T(8,128)(2,1)} %collective-permute-done.2, bf16[512,1024]{1,0:T(8,128)(2,1)} %collective-permute-done.3), kind=kOutput, calls=%fused_computation.21 | convolution fusion | flops 654950400 | bytes 6799360 | tf_op jit(solution)/shard_map/dot_general | solution.py:121
  70.9 3.1 %collective-permute-done.4 = f32[624,512]{1,0:T(8,128)} collective-permute-done((f32[624,512]{1,0:T(8,128)S(1)}, f32[624,512]{1,0:T(8,128)}, u32[]{:S(2)}, u32[]{:S(2)}) %collective-permute-start.4) | collective-permute-done | bytes 1277984 | tf_op jit(solution)/shard_map/ppermute | solution.py:41
  74.0 2.0 %multiply_reduce_fusion = (f32[624]{0:T(1024)S(1)}, f32[624,512]{1,0:T(8,128)S(1)}) fusion(f32[624,512]{1,0:T(8,128)} %collective-permute-done.4, f32[624,1024]{1,0:T(8,128)} %convolution_add_fusion, s32[]{:T(128)S(6)} %select_n.193, bf16[624,512]{1,0:T(8,128)(2,1)S(1)} %copy-done.9), kind=kLoop, calls=%fused_computation.34 | loop fusion | flops 1596816 | bytes 4475332 | tf_op jit(solution)/shard_map/reduce_sum | solution.py:130
  83.1 4.6 %fusion.7 = f32[624,1024]{1,0:T(8,128)} fusion(bf16[2048,1024]{1,0:T(8,128)(2,1)} %param.26, s32[]{:T(128)S(6)} %select_n.191, bf16[624,512]{1,0:T(8,128)(2,1)S(1)} %collective-permute-done.9, bf16[624,512]{1,0:T(8,128)(2,1)S(1)} %multiply_convert_fusion.1, pred[]{:T(512)S(6)} %eq.26), kind=kOutput, calls=%fused_computation.15 | convolution fusion | flops 1314373632 | bytes 5931013 | tf_op jit(solution)/shard_map/dot_general | solution.py:69
  87.7 3.0 %fusion.9 = f32[624,1024]{1,0:T(8,128)} fusion(bf16[2048,1024]{1,0:T(8,128)(2,1)S(1)} %copy-done.18, s32[]{:T(128)S(6)} %select_n.191, bf16[624,512]{1,0:T(8,128)(2,1)S(1)} %collective-permute-done.9, bf16[624,512]{1,0:T(8,128)(2,1)S(1)} %multiply_convert_fusion.1, pred[]{:T(512)S(6)} %eq.26), kind=kOutput, calls=%fused_computation.17 | convolution fusion | flops 1314373632 | bytes 5931013 | tf_op jit(solution)/shard_map/dot_general | solution.py:69
  90.7 7.1 %collective-permute-done.8 = bf16[624,512]{1,0:T(8,128)(2,1)S(1)} collective-permute-done((bf16[624,512]{1,0:T(8,128)(2,1)S(1)}, bf16[624,512]{1,0:T(8,128)(2,1)S(1)}, u32[]{:S(2)}, u32[]{:S(2)}) %collective-permute-start.8) | collective-permute-done | bytes 639008 | tf_op jit(solution)/shard_map/ppermute | solution.py:41
  97.8 2.1 %collective-permute-done.10 = bf16[624,512]{1,0:T(8,128)(2,1)S(1)} collective-permute-done((bf16[624,512]{1,0:T(8,128)(2,1)S(1)}, bf16[624,512]{1,0:T(8,128)(2,1)S(1)}, u32[]{:S(2)}, u32[]{:S(2)}) %collective-permute-start.10) | collective-permute-done | bytes 639008 | tf_op jit(solution)/shard_map/ppermute | solution.py:41
  99.9 3.1 %fusion.5 = f32[624,1024]{1,0:T(8,128)S(1)} fusion(bf16[2048,1024]{1,0:T(8,128)(2,1)} %param.25, s32[]{:T(128)S(6)} %select_n.192, bf16[624,512]{1,0:T(8,128)(2,1)S(1)} %collective-permute-done.10, bf16[624,512]{1,0:T(8,128)(2,1)S(1)} %collective-permute-done.8, pred[]{:T(512)S(6)} %eq.26), kind=kOutput, calls=%fused_computation.13 | convolution fusion | flops 1314373632 | bytes 5931013 | tf_op jit(solution)/shard_map/dot_general | solution.py:85
  103.0 1.5 fusion.3
  107.6 3.1 %fusion.62 = f32[624,2048]{1,0:T(8,128)S(1)} fusion(bf16[624,1024]{1,0:T(8,128)(2,1)S(1)} %multiply_convert_fusion, bf16[1024,2048]{1,0:T(8,128)(2,1)S(1)} %copy-done.20), kind=kOutput, calls=%fused_computation.143 | convolution fusion | flops 2617245696 | bytes 10584064 | tf_op jit(solution)/shard_map/dot_general | solution.py:97
  110.7 2.1 %dynamic-slice_bitcast_fusion.3 = (f32[1,624,512]{2,1,0:T(8,128)}, f32[1,624,512]{2,1,0:T(8,128)S(1)}, f32[1,624,512]{2,1,0:T(8,128)S(1)}, f32[1,624,512]{2,1,0:T(8,128)}) fusion(f32[624,2048]{1,0:T(8,128)S(1)} %fusion.62, s32[]{:T(128)S(6)} %select_n.208, s32[]{:T(128)S(6)} %select_n.211, s32[]{:T(128)S(6)} %select_n.210, s32[]{:T(128)S(6)} %select_n.209), kind=kLoop, calls=%fused_computation.32 | loop fusion | bytes 10223632 | tf_op jit(solution)/shard_map/stack | solution.py:104
  112.8 1.7 %pad_maximum_fusion.1 = f32[2,624,512]{2,1,0:T(8,128)} fusion(f32[1,624,512]{2,1,0:T(8,128)S(1)} %get-tuple-element.16, f32[1,624,512]{2,1,0:T(8,128)S(1)} %get-tuple-element.17), kind=kLoop, calls=%fused_computation.9 | loop fusion | flops 638976 | bytes 5111808 | tf_op jit(solution)/shard_map/stack | solution.py:105
  117.4 5.8 %all-to-all-start.1 = ((bf16[8,2,136,256]{3,2,1,0:T(8,128)(2,1)}), bf16[8,2,136,256]{3,2,1,0:T(8,128)(2,1)}, u32[]{:S(2)}, u32[]{:S(2)}) async-start(bf16[8,2,136,256]{3,2,1,0:T(8,128)(2,1)} %select_select_fusion), calls=%async_computation.1 | async-start | bytes 2228224 | tf_op jit(solution)/shard_map/all_to_all | solution.py:199
  123.3 3.1 %maximum_add_fusion = f32[2,624,512]{2,1,0:T(8,128)S(1)} fusion(f32[2,624,512]{2,1,0:T(8,128)} %collective-permute-done.11, f32[1,624,512]{2,1,0:T(8,128)} %get-tuple-element.18, f32[1,624,512]{2,1,0:T(8,128)} %get-tuple-element.15), kind=kLoop, calls=%fused_computation.8 | loop fusion | flops 1277952 | bytes 7667712 | tf_op jit(solution)/shard_map/add | solution.py:106
  128.0 15.8 %collective-permute-done.12 = bf16[624,512]{1,0:T(8,128)(2,1)S(1)} collective-permute-done((bf16[624,512]{1,0:T(8,128)(2,1)}, bf16[624,512]{1,0:T(8,128)(2,1)S(1)}, u32[]{:S(2)}, u32[]{:S(2)}) %collective-permute-start.12) | collective-permute-done | bytes 639008 | tf_op jit(solution)/shard_map/ppermute | solution.py:41
  145.2 5.8 %all-to-all-done.1 = bf16[8,2,136,256]{3,2,1,0:T(8,128)(2,1)} async-done(((bf16[8,2,136,256]{3,2,1,0:T(8,128)(2,1)}), bf16[8,2,136,256]{3,2,1,0:T(8,128)(2,1)}, u32[]{:S(2)}, u32[]{:S(2)}) %all-to-all-start.1) | async-done | bytes 1114144 | tf_op jit(solution)/shard_map/all_to_all | solution.py:199
  152.2 1.9 %gather_fusion.1 = bf16[13,136,256]{2,1,0:T(8,128)(2,1)S(1)} fusion(bf16[16,136,256]{2,1,0:T(8,128)(2,1)} %bitcast.36, s32[1024]{0:T(1024)S(1)} %pad_clamp_fusion), kind=kCustom, calls=%fused_computation.1 | custom fusion | bytes 1810484 | tf_op jit(solution)/shard_map/jit(_take)/gather | solution.py:263
  (128 shorter events, 38.6 us)
Async XLA Ops:
  0.6 11.7 %copy-start = (bf16[512,2048]{1,0:T(8,128)(2,1)S(1)}, bf16[512,2048]{1,0:T(8,128)(2,1)}, u32[]{:S(2)}) copy-start(bf16[512,2048]{1,0:T(8,128)(2,1)} %param.23) | copy-start | bytes 6291460
  0.6 18.6 %collective-permute-start = (bf16[624,512]{1,0:T(8,128)(2,1)}, bf16[624,512]{1,0:T(8,128)(2,1)}, u32[]{:S(2)}, u32[]{:S(2)}) collective-permute-start(bf16[624,512]{1,0:T(8,128)(2,1)} %param.15), channel_id=1, source_target_pairs={{0,2},{2,0},{1,3},{3,1},{4,6},{6,4},{5,7},{7,5},{8,10},{10,8},{9,1... | collective-permute-start | bytes 1916936 | tf_op jit(solution)/shard_map/ppermute | solution.py:41
  8.0 7.4 %copy-start.23 = (s32[13]{0:T(128)S(1)}, s32[13]{0:T(128)}, u32[]{:S(2)}) copy-start(s32[13]{0:T(128)} %param.17) | copy-start | bytes 160
  8.0 20.4 %all-to-all-start = ((bf16[2,4,13,16,256]{4,3,2,0,1:T(8,128)(2,1)}), bf16[2,4,13,16,256]{4,3,2,0,1:T(8,128)(2,1)}, u32[]{:S(2)}, u32[]{:S(2)}) async-start(bf16[2,4,13,16,256]{4,3,2,0,1:T(8,128)(2,1)} %copy.60), calls=%async_computation | async-start | bytes 1703936 | tf_op jit(solution)/shard_map/all_to_all | solution.py:175
  12.3 9.0 %copy-start.16 = (s32[13]{0:T(128)S(1)}, s32[13]{0:T(128)}, u32[]{:S(2)}) copy-start(s32[13]{0:T(128)} %param.16) | copy-start | bytes 160
  13.5 40.2 %collective-permute-start.3 = (bf16[512,1024]{1,0:T(8,128)(2,1)}, bf16[512,1024]{1,0:T(8,128)(2,1)}, u32[]{:S(2)}, u32[]{:S(2)}) collective-permute-start(bf16[512,1024]{1,0:T(8,128)(2,1)} %constant_dynamic-slice_fusion.1), channel_id=1, source_target_pairs={{0,2},{2,0},{1,3},{3,1},{4,6},{6,4},{5,7},{7,5},{8,10},{10,8},{9,1... | collective-permute-start | bytes 3145736 | tf_op jit(solution)/shard_map/ppermute | solution.py:41
  21.1 9.4 %collective-permute-start.1 = (bf16[2,624,512]{2,1,0:T(8,128)(2,1)S(1)}, bf16[2,624,512]{2,1,0:T(8,128)(2,1)}, u32[]{:S(2)}, u32[]{:S(2)}) collective-permute-start(bf16[2,624,512]{2,1,0:T(8,128)(2,1)S(1)} %maximum_select_fusion), channel_id=1, source_target_pairs={{0,1},{1,0},{2,3},{3,2},{4,5},{5,4},{6,7},{7,6},{8,9},{9,8},{10,11... | collective-permute-start | bytes 3833864 | tf_op jit(solution)/shard_map/ppermute | solution.py:41
  32.0 2.1 %copy-start.15 = (f32[2048]{0:T(1024)S(1)}, f32[2048]{0:T(1024)}, u32[]{:S(2)}) copy-start(f32[2048]{0:T(1024)} %param.19) | copy-start | bytes 24580
  34.1 2.4 %copy-start.21 = (bf16[2048,512]{1,0:T(8,128)(2,1)S(1)}, bf16[2048,512]{1,0:T(8,128)(2,1)}, u32[]{:S(2)}) copy-start(bf16[2048,512]{1,0:T(8,128)(2,1)} %param.20) | copy-start | bytes 6291460
  41.1 1.7 %copy-start.8 = (bf16[624,2048]{1,0:T(8,128)(2,1)S(1)}, bf16[624,2048]{1,0:T(8,128)(2,1)}, u32[]{:S(2)}) copy-start(bf16[624,2048]{1,0:T(8,128)(2,1)} %copy-done.7) | copy-start | bytes 7667716
  42.8 3.7 %copy-start.22 = (bf16[2048,256]{1,0:T(8,128)(2,1)S(1)}, bf16[2048,256]{1,0:T(8,128)(2,1)}, u32[]{:S(2)}) copy-start(bf16[2048,256]{1,0:T(8,128)(2,1)} %param.22) | copy-start | bytes 3145732
  50.7 14.9 %collective-permute-start.2 = (bf16[624,512]{1,0:T(8,128)(2,1)S(1)}, bf16[624,512]{1,0:T(8,128)(2,1)}, u32[]{:S(2)}, u32[]{:S(2)}) collective-permute-start(bf16[624,512]{1,0:T(8,128)(2,1)S(1)} %bitcast.96), channel_id=1, source_target_pairs={{0,2},{2,0},{1,3},{3,1},{4,6},{6,4},{5,7},{7,5},{8,10},{10,8},{9,1... | collective-permute-start | bytes 1916936 | tf_op jit(solution)/shard_map/ppermute | solution.py:41
  69.4 4.7 %copy-start.9 = (bf16[624,512]{1,0:T(8,128)(2,1)S(1)}, bf16[624,512]{1,0:T(8,128)(2,1)}, u32[]{:S(2)}) copy-start(bf16[624,512]{1,0:T(8,128)(2,1)} %param.15) | copy-start | bytes 1916932
  70.9 3.2 %collective-permute-start.4 = (f32[624,512]{1,0:T(8,128)S(1)}, f32[624,512]{1,0:T(8,128)}, u32[]{:S(2)}, u32[]{:S(2)}) collective-permute-start(f32[624,512]{1,0:T(8,128)S(1)} %constant_dynamic-slice_fusion), channel_id=1, source_target_pairs={{0,1},{1,0},{2,3},{3,2},{4,5},{5,4},{6,7},{7,6},{8,9},{9,8},{10,11... | collective-permute-start | bytes 3833864 | tf_op jit(solution)/shard_map/ppermute | solution.py:41
  76.0 11.7 %copy-start.2 = (f32[624,512]{1,0:T(8,128)}, f32[624,512]{1,0:T(8,128)S(1)}, u32[]{:S(2)}) copy-start(f32[624,512]{1,0:T(8,128)S(1)} %get-tuple-element.14) | copy-start | bytes 3833860
  76.0 2.7 %collective-permute-start.5 = (f32[624,1]{0,1:T(1,128)S(1)}, f32[624,1]{0,1:T(1,128)S(1)}, u32[]{:S(2)}, u32[]{:S(2)}) collective-permute-start(f32[624,1]{0,1:T(1,128)S(1)} %broadcast_in_dim.131), channel_id=1, source_target_pairs={{0,1},{1,0},{2,3},{3,2},{4,5},{5,4},{6,7},{7,6},{8,9},{9,8},{10,11... | collective-permute-start | bytes 7496 | tf_op jit(solution)/shard_map/ppermute | solution.py:41
  76.2 3.6 %collective-permute-start.6 = (f32[624,1]{0,1:T(1,128)S(1)}, f32[624,1]{0,1:T(1,128)S(1)}, u32[]{:S(2)}, u32[]{:S(2)}) collective-permute-start(f32[624,1]{0,1:T(1,128)S(1)} %broadcast_in_dim.131), channel_id=1, source_target_pairs={{0,2},{2,0},{1,3},{3,1},{4,6},{6,4},{5,7},{7,5},{8,10},{10,8},{9,1... | collective-permute-start | bytes 7496 | tf_op jit(solution)/shard_map/ppermute | solution.py:41
  77.7 3.0 %collective-permute-start.7 = (f32[624,1]{0,1:T(1,128)S(1)}, f32[624,1]{0,1:T(1,128)S(1)}, u32[]{:S(2)}, u32[]{:S(2)}) collective-permute-start(f32[624,1]{0,1:T(1,128)S(1)} %broadcast_in_dim.131), channel_id=1, source_target_pairs={{0,3},{1,2},{2,1},{3,0},{4,7},{5,6},{6,5},{7,4},{8,11},{9,10},{10,... | collective-permute-start | bytes 7496 | tf_op jit(solution)/shard_map/ppermute | solution.py:136
  80.9 6.8 %copy-start.18 = (bf16[2048,1024]{1,0:T(8,128)(2,1)S(1)}, bf16[2048,1024]{1,0:T(8,128)(2,1)}, u32[]{:S(2)}) copy-start(bf16[2048,1024]{1,0:T(8,128)(2,1)} %param.25) | copy-start | bytes 12582916
  80.9 2.1 %collective-permute-start.9 = (bf16[624,512]{1,0:T(8,128)(2,1)S(1)}, bf16[624,512]{1,0:T(8,128)(2,1)S(1)}, u32[]{:S(2)}, u32[]{:S(2)}) collective-permute-start(bf16[624,512]{1,0:T(8,128)(2,1)S(1)} %multiply_convert_fusion.1), channel_id=1, source_target_pairs={{0,1},{1,0},{2,3},{3,2},{4,5},{5,4},{6,7},{7,6},{8,9},{9,8},{10,11... | collective-permute-start | bytes 1916936 | tf_op jit(solution)/shard_map/ppermute | solution.py:41
  81.1 16.7 %collective-permute-start.8 = (bf16[624,512]{1,0:T(8,128)(2,1)S(1)}, bf16[624,512]{1,0:T(8,128)(2,1)S(1)}, u32[]{:S(2)}, u32[]{:S(2)}) collective-permute-start(bf16[624,512]{1,0:T(8,128)(2,1)S(1)} %multiply_convert_fusion.1), channel_id=1, source_target_pairs={{0,2},{2,0},{1,3},{3,1},{4,6},{6,4},{5,7},{7,5},{8,10},{10,8},{9,1... | collective-permute-start | bytes 1916936 | tf_op jit(solution)/shard_map/ppermute | solution.py:41
  97.8 2.1 %collective-permute-start.10 = (bf16[624,512]{1,0:T(8,128)(2,1)S(1)}, bf16[624,512]{1,0:T(8,128)(2,1)S(1)}, u32[]{:S(2)}, u32[]{:S(2)}) collective-permute-start(bf16[624,512]{1,0:T(8,128)(2,1)S(1)} %collective-permute-done.8), channel_id=1, source_target_pairs={{0,1},{1,0},{2,3},{3,2},{4,5},{5,4},{6,7},{7,6},{8,9},{9,8},{10,11... | collective-permute-start | bytes 1916936 | tf_op jit(solution)/shard_map/ppermute | solution.py:41
  97.8 5.2 %copy-start.19 = (bf16[2048,1024]{1,0:T(8,128)(2,1)S(1)}, bf16[2048,1024]{1,0:T(8,128)(2,1)}, u32[]{:S(2)}) copy-start(bf16[2048,1024]{1,0:T(8,128)(2,1)} %param.26) | copy-start | bytes 12582916
  103.0 2.5 %copy-start.6 = (f32[624,1024]{1,0:T(8,128)S(1)}, f32[624,1024]{1,0:T(8,128)}, u32[]{:S(2)}) copy-start(f32[624,1024]{1,0:T(8,128)} %fusion.9) | copy-start | bytes 7667716
  105.4 2.2 %copy-start.20 = (bf16[1024,2048]{1,0:T(8,128)(2,1)S(1)}, bf16[1024,2048]{1,0:T(8,128)(2,1)}, u32[]{:S(2)}) copy-start(bf16[1024,2048]{1,0:T(8,128)(2,1)} %param.27) | copy-start | bytes 12582916
  112.8 1.9 %copy-start.17 = (s32[13]{0:T(128)S(1)}, s32[13]{0:T(128)}, u32[]{:S(2)}) copy-start(s32[13]{0:T(128)} %param.18) | copy-start | bytes 160
  112.8 2.6 %copy-start.12 = (bf16[1,13,4,16,256]{4,3,2,1,0:T(8,128)(2,1)S(1)}, bf16[1,13,4,16,256]{4,3,2,1,0:T(8,128)(2,1)}, u32[]{:S(2)}) copy-start(bf16[1,13,4,16,256]{4,3,2,1,0:T(8,128)(2,1)} %get-tuple-element.30) | copy-start | bytes 1277956
  114.5 8.7 %collective-permute-start.11 = (f32[2,624,512]{2,1,0:T(8,128)}, f32[2,624,512]{2,1,0:T(8,128)}, u32[]{:S(2)}, u32[]{:S(2)}) collective-permute-start(f32[2,624,512]{2,1,0:T(8,128)} %pad_maximum_fusion.1), channel_id=1, source_target_pairs={{0,1},{1,0},{2,3},{3,2},{4,5},{5,4},{6,7},{7,6},{8,9},{9,8},{10,11... | collective-permute-start | bytes 7667720 | tf_op jit(solution)/shard_map/ppermute | solution.py:41
  117.4 33.6 %all-to-all-start.1 = ((bf16[8,2,136,256]{3,2,1,0:T(8,128)(2,1)}), bf16[8,2,136,256]{3,2,1,0:T(8,128)(2,1)}, u32[]{:S(2)}, u32[]{:S(2)}) async-start(bf16[8,2,136,256]{3,2,1,0:T(8,128)(2,1)} %select_select_fusion), calls=%async_computation.1 | async-start | bytes 2228224 | tf_op jit(solution)/shard_map/all_to_all | solution.py:199
  127.3 16.6 %collective-permute-start.12 = (bf16[624,512]{1,0:T(8,128)(2,1)}, bf16[624,512]{1,0:T(8,128)(2,1)S(1)}, u32[]{:S(2)}, u32[]{:S(2)}) collective-permute-start(bf16[624,512]{1,0:T(8,128)(2,1)} %fusion.24), channel_id=1, source_target_pairs={{0,2},{2,0},{1,3},{3,1},{4,6},{6,4},{5,7},{7,5},{8,10},{10,8},{9,1... | collective-permute-start | bytes 1916936 | tf_op jit(solution)/shard_map/ppermute | solution.py:41
  154.0 2.0 %copy-start.4 = (f32[624,512]{1,0:T(8,128)S(1)}, f32[624,512]{1,0:T(8,128)}, u32[]{:S(2)}) copy-start(f32[624,512]{1,0:T(8,128)} %bitcast_add_fusion) | copy-start | bytes 3833860
  154.0 3.0 %copy-start.1 = (bf16[512,2048]{1,0:T(8,128)(2,1)S(1)}, bf16[512,2048]{1,0:T(8,128)(2,1)}, u32[]{:S(2)}) copy-start(bf16[512,2048]{1,0:T(8,128)(2,1)} %param.23) | copy-start | bytes 6291460
  (7 other events, 8.8 us)
